TPU v7x, 32 devices: a whole 2x2x4 slice. The times are simulated.
32 devices in a mesh: seq: 8 (over z, y), fsdp: 4 (over x, core).
Axes of the slice: x: 2, y: 2, z: 4, core: 2. Of those that a mesh axis runs over, the one named last changes fastest.
Arguments:
- inputs: bfloat16 [12288, 1536], P(('seq', 'fsdp')), may hold values from -15 to 15
- layer_norm_gain: float32 [1536], replicated, may hold values from 0.25 to 1.75
- layer_norm_bias: float32 [1536], replicated, may hold values from -4 to 4
- w_in: bfloat16 [1536, 3072], P('fsdp'), may hold values from -0.15625 to 0.15625
- dw_kernel: float32 [32, 1536], replicated, may hold values from -1 to 1
- bn_gain: float32 [1536], replicated, may hold values from 0.25 to 1.75
- bn_bias: float32 [1536], replicated, may hold values from -4 to 4
- cotangent: bfloat16 [12288, 1536], P(('seq', 'fsdp')), may hold values from -6 to 6
Outputs:
- output: bfloat16 [12288, 1536], P(('seq', 'fsdp'))
- input_gradient: bfloat16 [12288, 1536], P(('seq', 'fsdp'))
- grad_w_in: float32 [1536, 3072], P('fsdp')
- grad_kernel: float32 [32, 1536], replicated
- grad_bn_gain: float32 [1536], replicated
- grad_bn_bias: float32 [1536], replicated
- layer_norm_gain_gradient: float32 [1536], replicated
- grad_ln_bias: float32 [1536], replicated
All inputs are finite; a program needn't handle non-finite values.
Results may differ from a plain program's by a relative error of at most 0.012.
The roundings to bfloat16 on the way count: a program that leaves them out, or rounds other values in their place, can miss the bound.
Values may be sent and summed in bfloat16 or wider, within the bound.
No kernel may reach another device: no remote copies, remote signals or barrier semaphores. Data moves between devices by JAX's collectives and lax.ppermute only.
A program may use at most 128 MiB of HBM per device.

v0:
```python
import jax
import jax.numpy as jnp
from jax import lax
from jax.sharding import PartitionSpec as P

epsilon = 1e-05


def from_behind(block, axis, distance):
    devices = range(lax.axis_size(axis))
    route = [(i - distance, i) for i in devices if i - distance in devices]
    return lax.ppermute(block, axis, route)


def on_device(
    inputs, layer_norm_gain, layer_norm_bias, w_in, dw_kernel, bn_gain, bn_bias, cotangent
):
    tok_rows = inputs.shape[0]
    features = inputs.shape[1]
    kernel_len = dw_kernel.shape[0]
    all_frames = tok_rows * lax.axis_size("seq") * lax.axis_size("fsdp")
    frames = inputs.astype(jnp.float32)
    row_mean = jnp.mean(frames, axis=-1, keepdims=True)
    centered_rows = frames - row_mean
    row_inverse_deviation = lax.rsqrt(
        jnp.mean(centered_rows * centered_rows, axis=-1, keepdims=True) + epsilon
    )
    standardized_input = centered_rows * row_inverse_deviation
    normalized_rows = (standardized_input * layer_norm_gain + layer_norm_bias).astype(jnp.bfloat16)
    full_weight = lax.all_gather(w_in, "fsdp", axis=0, tiled=True)
    hidden = jnp.dot(normalized_rows, full_weight, preferred_element_type=jnp.float32)
    value_part = hidden[:, :features]
    gate_sig = jax.nn.sigmoid(hidden[:, features:])
    glu = (value_part * gate_sig).astype(jnp.bfloat16)
    past_rim = from_behind(glu[tok_rows - (kernel_len - 1) :], ("seq", "fsdp"), 1)
    padded_glu = jnp.concatenate([past_rim, glu], axis=0).astype(jnp.float32)
    conv_out = jnp.zeros((tok_rows, features), jnp.float32)
    for offset in range(kernel_len):
        conv_out = (
            conv_out
            + dw_kernel[offset]
            * padded_glu[kernel_len - 1 - offset : kernel_len - 1 - offset + tok_rows]
        )
    chan_mean = lax.psum(jnp.sum(conv_out, axis=0), ("seq", "fsdp")) / all_frames
    conv_centred = conv_out - chan_mean
    chan_var = lax.psum(jnp.sum(conv_centred * conv_centred, axis=0), ("seq", "fsdp")) / all_frames
    bn_rstd = lax.rsqrt(chan_var + epsilon)
    chat = conv_centred * bn_rstd
    z_value = chat * bn_gain + bn_bias
    z_sig = jax.nn.sigmoid(z_value)
    output = (z_value * z_sig).astype(jnp.bfloat16)
    grad_z = cotangent.astype(jnp.float32) * z_sig * (1.0 + z_value * (1.0 - z_sig))
    grad_bn_bias, grad_bn_gain = lax.psum(
        (jnp.sum(grad_z, axis=0), jnp.sum(grad_z * chat, axis=0)), ("seq", "fsdp")
    )
    grad_conv = (
        bn_gain * bn_rstd * (grad_z - grad_bn_bias / all_frames - chat * grad_bn_gain / all_frames)
    )
    future_rim = from_behind(grad_conv[: kernel_len - 1], ("seq", "fsdp"), -1)
    padded_grad = jnp.concatenate([grad_conv, future_rim], axis=0)
    grad_glu = jnp.zeros((tok_rows, features), jnp.float32)
    kernel_rows = []
    for offset in range(kernel_len):
        grad_glu = grad_glu + dw_kernel[offset] * padded_grad[offset : offset + tok_rows]
        kernel_rows.append(
            jnp.sum(
                grad_conv
                * padded_glu[kernel_len - 1 - offset : kernel_len - 1 - offset + tok_rows],
                axis=0,
            )
        )
    kernel_portion = jnp.stack(kernel_rows, axis=0)
    grad_value = grad_glu * gate_sig
    grad_gate = grad_glu * value_part * gate_sig * (1.0 - gate_sig)
    grad_hidden = jnp.concatenate([grad_value, grad_gate], axis=1).astype(jnp.bfloat16)
    normalized_gradient = lax.dot_general(
        grad_hidden, full_weight, (((1,), (1,)), ((), ())), preferred_element_type=jnp.float32
    )
    grad_kernel, layer_norm_gain_gradient, grad_ln_bias = lax.psum(
        (
            kernel_portion,
            jnp.sum(normalized_gradient * standardized_input, axis=0),
            jnp.sum(normalized_gradient, axis=0),
        ),
        ("seq", "fsdp"),
    )
    rescaled_rows = normalized_gradient * layer_norm_gain
    input_gradient = row_inverse_deviation * (
        rescaled_rows
        - jnp.mean(rescaled_rows, axis=-1, keepdims=True)
        - standardized_input * jnp.mean(rescaled_rows * standardized_input, axis=-1, keepdims=True)
    )
    row_share = lax.psum_scatter(
        lax.dot_general(
            normalized_rows,
            grad_hidden,
            (((0,), (0,)), ((), ())),
            preferred_element_type=jnp.float32,
        ),
        "fsdp",
        scatter_dimension=0,
        tiled=True,
    )
    grad_w_in = lax.psum(row_share, "seq")
    return (
        output,
        input_gradient.astype(jnp.bfloat16),
        grad_w_in,
        grad_kernel,
        grad_bn_gain,
        grad_bn_bias,
        layer_norm_gain_gradient,
        grad_ln_bias,
    )


def solution(mesh):
    placed = (
        P(("seq", "fsdp"), None),
        P(),
        P(),
        P("fsdp", None),
        P(),
        P(),
        P(),
        P(("seq", "fsdp"), None),
    )
    return jax.shard_map(
        on_device,
        mesh=mesh,
        in_specs=placed,
        out_specs=(
            P(("seq", "fsdp"), None),
            P(("seq", "fsdp"), None),
            P("fsdp", None),
            P(),
            P(),
            P(),
            P(),
            P(),
        ),
        check_vma=False,
    )
```

profile of v0, /device:TPU:0, one launch (start us, length us, event | category | flops | bytes accessed | tf_op | source)
XLA Modules:
  0.0 759.2 jit_solution(17330102155597915595)
XLA Ops:
  7.3 0.7 all-gather.2.cloned.1.call-update
  9.3 67.3 %all-gather.2.cloned.1.call-done = bf16[1536,3072]{1,0:T(8,128)(2,1)} async-done(((bf16[384,3072]{1,0:T(8,128)(2,1)}), bf16[1536,3072]{1,0:T(8,128)(2,1)}) %all-gather.2.cloned.1.call-update) | async-done | bytes 9437200 | tf_op jit(solution)/shard_map/all_gather | solution.py:30
  76.6 6.7 fusion.115
  83.9 1.5 copy-done
  85.5 2.2 collective-permute-start
  87.9 0.7 collective-permute-done
  88.9 10.2 %fusion.119 = (f32[1536]{0:T(1024)S(1)}, f32[384,1536]{1,0:T(8,128)}) fusion(f32[415,1536]{1,0:T(8,128)S(1)} %maximum_convert_fusion, f32[1536]{0:T(1024)S(1)} %get-tuple-element.76, f32[1536]{0:T(1024)S(1)} %get-tuple-element.77, f32[1536]{0:T(1024)S(1)} %get-tuple-element.47, f32[1536]{0:T(1024)S(1)} %get-tuple-element.48, ...), kind=kLoop, calls=%fused_computation.261 | loop fusion | flops 37747200 | bytes 78059520 | tf_op jit(solution)/shard_map/reduce_sum | solution.py:44
  99.1 44.0 %psum.56 = f32[1536]{0:T(1024)S(1)} all-reduce(f32[1536]{0:T(1024)S(1)} %get-tuple-element.85), channel_id=1, replica_groups=mesh['seq'=8,'fsdp'=4] {'seq','fsdp'}, use_global_device_ids=true, to_apply=%region_3.0 | all-reduce | flops 1536 | bytes 12288 | tf_op jit(solution)/shard_map/psum | solution.py:44
  143.2 1.9 multiply_reduce_fusion.33
  145.1 40.1 %psum.57 = f32[1536]{0:T(1024)S(1)} all-reduce(f32[1536]{0:T(1024)S(1)} %multiply_reduce_fusion.33), channel_id=1, replica_groups=mesh['seq'=8,'fsdp'=4] {'seq','fsdp'}, use_global_device_ids=true, to_apply=%region_5.0 | all-reduce | flops 1536 | bytes 12288 | tf_op jit(solution)/shard_map/psum | solution.py:46
  185.3 4.5 fusion.117
  189.7 40.2 %all-reduce.1 = (f32[1536]{0:T(1024)S(1)}, f32[1536]{0:T(1024)S(1)}) all-reduce(f32[1536]{0:T(1024)S(1)} %get-tuple-element.41, f32[1536]{0:T(1024)S(1)} %get-tuple-element.40), channel_id=1, replica_groups=mesh['seq'=8,'fsdp'=4] {'seq','fsdp'}, use_global_device_ids=true, to_apply=%region_9.0 | all-reduce | flops 3072 | bytes 24576 | tf_op jit(solution)/shard_map/psum | solution.py:53
  230.5 8.2 %multiply_reduce_fusion = (f32[1536]{0:T(1024)S(1)}, f32[1536]{0:T(1024)S(1)}, f32[1536]{0:T(1024)S(1)}, f32[1536]{0:T(1024)S(1)}, f32[1536]{0:T(1024)S(1)}, /*i...) fusion(f32[415,1536]{1,0:T(8,128)S(1)} %maximum_convert_fusion,, ...), kind=kLoop, calls=%fused_computation.169 | loop fusion | flops 31822848 | bytes 48519168 | tf_op jit(solution)/shard_map/reduce_sum | solution.py:66
  238.8 1.4 copy-done.1
  240.2 1.5 collective-permute-start.1
  241.7 1.9 collective-permute-done.1
  243.5 40.4 %multiply_convert_fusion.1 = (bf16[384,1536]{1,0:T(8,128)(2,1)S(1)}, f32[384,1536]{1,0:T(8,128)}) fusion(f32[384,3072]{1,0:T(8,128)} %copy-done, f32[31,1536]{1,0:T(8,128)S(1)} %collective-permute-done.1, f32[384,1536]{1,0:T(8,128)} %copy-done.1, f32[1536]{0:T(1024)S(1)} %get-tuple-element.76, f32[1536]{0:T(1024)S(1)} %get-tuple-element.77, ...), kind=kLoop, calls=%fused_computation.202 | loop fusion | flops 58392576 | bytes 8644608 | tf_op jit(solution)/shard_map/convert
  284.0 4.4 multiply_convert_fusion
  288.4 1.0 copy-done.7
  289.4 9.4 %fusion.109 = f32[1536,3072]{1,0:T(8,128)} fusion(bf16[384,1536]{1,0:T(8,128)(2,1)S(1)} %multiply_convert_fusion, bf16[384,1536]{1,0:T(8,128)(2,1)S(1)} %get-tuple-element.83, bf16[384,1536]{1,0:T(8,128)(2,1)S(1)} %copy-done.3, f32[1536]{0:T(1024)S(1)} %copy-done.12, f32[1536]{0:T(1024)S(1)} %copy-done.11, f32[384]{0:T(512)S(1)} %add_rsqrt_fusion.1, ...), kind=kOutput, calls=%fused_computation.214 | convolution fusion | flops 3632136192 | bytes 22428672 | tf_op jit(solution)/shard_map/dot_general | solution.py:94
  298.9 5.4 multiply_reduce_fusion.18
  304.8 2.8 stack.131
  307.9 134.5 %reduce-scatter.2.cloned.1.call-done = f32[384,3072]{1,0:T(8,128)} async-done(((f32[1536,3072]{1,0:T(8,128)}), f32[384,3072]{1,0:T(8,128)}) %reduce-scatter.2.cloned.1.call-update) | async-done | bytes 4718608 | tf_op jit(solution)/shard_map/reduce_scatter | solution.py:93
  442.4 1.2 copy-done.4
  444.3 10.0 %fusion.12 = (f32[1536]{0:T(1024)}, f32[384]{0:T(512)}, f32[384]{0:T(512)}, f32[1536]{0:T(1024)}, f32[384,1536]{1,0:T(8,128)}) fusion(bf16[384,1536]{1,0:T(8,128)(2,1)S(1)} %copy-done.4, f32[384]{0:T(512)S(1)} %add_rsqrt_fusion.1, f32[384]{0:T(512)S(1)} %broadcast_multiply_fusion.4, f32[1536]{0:T(1024)S(1)} %copy-done.11, ...), kind=kOutput, calls=%fused_computation.44 | convolution fusion | flops 3634491392 | bytes 15360000 | tf_op jit(solution)/shard_map/dot_general | solution.py:76
  454.3 39.7 %all-reduce = (f32[1536]{0:T(1024)}, f32[1536]{0:T(1024)}) all-reduce(f32[1536]{0:T(1024)} %get-tuple-element.42, f32[1536]{0:T(1024)} %get-tuple-element.45), channel_id=1, replica_groups=mesh['seq'=8,'fsdp'=4] {'seq','fsdp'}, use_global_device_ids=true, to_apply=%region_48.0 | all-reduce | flops 3072 | bytes 24576 | tf_op jit(solution)/shard_map/psum | solution.py:79
  494.0 0.7 broadcast_multiply_fusion.2
  494.7 3.4 fusion.11
  498.1 74.3 %all-reduce.7.cloned.1.call-done = f32[32,1536]{1,0:T(8,128)} async-done(((f32[32,1536]{1,0:T(8,128)}), f32[32,1536]{1,0:T(8,128)}) %all-reduce.7.cloned.1.call-update) | async-done | bytes 196624 | tf_op jit(solution)/shard_map/psum | solution.py:79
  572.4 174.5 %all-reduce.5.cloned.1.call-done = f32[384,3072]{1,0:T(8,128)} async-done(((f32[384,3072]{1,0:T(8,128)}), f32[384,3072]{1,0:T(8,128)}) %all-reduce.5.cloned.1.call-update) | async-done | bytes 4718608 | tf_op jit(solution)/shard_map/psum | solution.py:104
  746.9 5.1 copy.18
  752.0 0.7 copy.19
  (82 shorter events, 4.5 us)
Async XLA Ops:
  7.2 0.9 copy-start.10
  7.2 1.4 copy-start.2
  7.2 69.4 %copy-start.11 = (f32[1536]{0:T(1024)S(1)}, f32[1536]{0:T(1024)}, u32[]{:S(2)}) copy-start(f32[1536]{0:T(1024)} %param.9) | copy-start | bytes 18436
  7.2 69.4 %copy-start.12 = (f32[1536]{0:T(1024)S(1)}, f32[1536]{0:T(1024)}, u32[]{:S(2)}) copy-start(f32[1536]{0:T(1024)} %param.10) | copy-start | bytes 18436
  7.2 69.4 %all-gather.2.cloned.1.call-start = ((), (), s32[]{:S(2)}) async-start(), calls=%async_computation.1 | async-start | bytes 11796480 | tf_op jit(solution)/shard_map/all_gather | solution.py:30
  7.9 434.4 %reduce-scatter.2.cloned.1.call-start = ((), (), s32[]{:S(2)}) async-start(), calls=%async_computation.2 | async-start | bytes 23592960 | tf_op jit(solution)/shard_map/reduce_scatter | solution.py:93
  83.2 2.2 copy-start
  85.5 3.1 collective-permute-start
  99.1 86.1 %copy-start.13 = (f32[1536]{0:T(1024)S(1)}, f32[1536]{0:T(1024)}, u32[]{:S(2)}) copy-start(f32[1536]{0:T(1024)} %param.13) | copy-start | bytes 18436
  99.1 86.1 %copy-start.14 = (f32[1536]{0:T(1024)S(1)}, f32[1536]{0:T(1024)}, u32[]{:S(2)}) copy-start(f32[1536]{0:T(1024)} %param.14) | copy-start | bytes 18436
  229.9 0.6 copy-start.16
  229.9 8.9 %copy-start.15 = (f32[1536]{0:T(1024)}, f32[1536]{0:T(1024)S(1)}, u32[]{:S(2)}) copy-start(f32[1536]{0:T(1024)S(1)} %get-tuple-element.97) | copy-start | bytes 18436
  238.8 1.4 copy-start.1
  240.2 3.3 collective-permute-start.1
  283.9 4.5 copy-start.5
  283.9 5.5 copy-start.3
  288.4 1.0 copy-start.7
  298.8 273.6 %all-reduce.7.cloned.1.call-start = ((), (), s32[]{:S(2)}) async-start(), calls=%async_computation.4 | async-start | bytes 393216 | tf_op jit(solution)/shard_map/psum | solution.py:79
  307.6 439.3 %all-reduce.5.cloned.1.call-start = ((), (), s32[]{:S(2)}) async-start(), calls=%async_computation.3 | async-start | bytes 9437184 | tf_op jit(solution)/shard_map/psum | solution.py:104
  442.4 1.3 copy-start.4
  442.4 1.6 copy-start.6
  442.4 2.0 copy-start.8
  746.9 5.1 copy-start.9
Sparse Core Ops, SparseCore 0:
  9.6 66.9 all-gather.1
  298.9 143.3 reduce-scatter.1
  449.4 122.9 all-reduce.6
  576.3 170.5 all-reduce.4
where the time goes:
time: 760 us; the launch traced here: 759 us
  waiting for transfers between devices  454 us (60%)
  blocking collectives  164 us (22%)
  other arithmetic  80.9 us (11%)
  matrix products  26 us (3%)
  local copies, waits for them, and re-layouts  16.1 us (2%)
  between operations  14.2 us (2%)
    psum x1, waiting for transfers between devices, on_device(): grad_w_in = lax.psum(row_share, 'seq')  174 us
    reduce_scatter x1, waiting for transfers between devices, on_device(): lax.psum_scatter(lax.dot_general(normalized_rows, grad_hidden, (((0,), (0...  135 us
    psum x1, waiting for transfers between devices, on_device(): lax.psum((kernel_portion, jnp.sum(normalized_gradient * standardized_inpu...  74.3 us
    all_gather x1, waiting for transfers between devices, on_device(): full_weight = lax.all_gather(w_in, 'fsdp', axis=0, tiled=True)  67.3 us
    another operation x2, other arithmetic  44.8 us
    psum x1, blocking collectives, on_device(): lax.psum(jnp.sum(conv_out, axis=0), ('seq', 'fsdp')) / all_frames  44 us
    psum x1, blocking collectives, on_device(): lax.psum((jnp.sum(grad_z, axis=0), jnp.sum(grad_z * chat, axis=0)), ('seq...  40.2 us
    psum x1, blocking collectives, on_device(): lax.psum(jnp.sum(conv_centred * conv_centred, axis=0), ('seq', 'fsdp'))  40.1 us
  transfers between devices with their start and end apart: 6, of which 6 were waited for; matrix products, arithmetic and copies ran while one was open for 3% of the time, Pallas kernels for 0%

commit v1 on v0

--- a/solution.py
+++ b/solution.py
@@ -10,6 +10,18 @@
     devices = range(lax.axis_size(axis))
     route = [(i - distance, i) for i in devices if i - distance in devices]
     return lax.ppermute(block, axis, route)
+
+
+def tree_sum(tree, axis):
+    count = lax.axis_size(axis)
+    if count & (count - 1):
+        return lax.psum(tree, axis)
+    stride = 1
+    while stride < count:
+        route = [(i, i ^ stride) for i in range(count)]
+        tree = jax.tree.map(lambda x: x + lax.ppermute(x, axis, route), tree)
+        stride *= 2
+    return tree
 
 
 def on_device(
@@ -41,16 +53,16 @@
             + dw_kernel[offset]
             * padded_glu[kernel_len - 1 - offset : kernel_len - 1 - offset + tok_rows]
         )
-    chan_mean = lax.psum(jnp.sum(conv_out, axis=0), ("seq", "fsdp")) / all_frames
+    chan_mean = tree_sum(jnp.sum(conv_out, axis=0), ("seq", "fsdp")) / all_frames
     conv_centred = conv_out - chan_mean
-    chan_var = lax.psum(jnp.sum(conv_centred * conv_centred, axis=0), ("seq", "fsdp")) / all_frames
+    chan_var = tree_sum(jnp.sum(conv_centred * conv_centred, axis=0), ("seq", "fsdp")) / all_frames
     bn_rstd = lax.rsqrt(chan_var + epsilon)
     chat = conv_centred * bn_rstd
     z_value = chat * bn_gain + bn_bias
     z_sig = jax.nn.sigmoid(z_value)
     output = (z_value * z_sig).astype(jnp.bfloat16)
     grad_z = cotangent.astype(jnp.float32) * z_sig * (1.0 + z_value * (1.0 - z_sig))
-    grad_bn_bias, grad_bn_gain = lax.psum(
+    grad_bn_bias, grad_bn_gain = tree_sum(
         (jnp.sum(grad_z, axis=0), jnp.sum(grad_z * chat, axis=0)), ("seq", "fsdp")
     )
     grad_conv = (
@@ -76,7 +88,7 @@
     normalized_gradient = lax.dot_general(
         grad_hidden, full_weight, (((1,), (1,)), ((), ())), preferred_element_type=jnp.float32
     )
-    grad_kernel, layer_norm_gain_gradient, grad_ln_bias = lax.psum(
+    grad_kernel, layer_norm_gain_gradient, grad_ln_bias = tree_sum(
         (
             kernel_portion,
             jnp.sum(normalized_gradient * standardized_input, axis=0),

time: 760 us -> 561 us (0.74)
  blocking collectives: 164 us -> 0 us
  waiting for transfers between devices: 454 us -> 387 us
  starting transfers between devices: 4.03 us -> 48.7 us
    psum x4 -> x0, blocking collectives: 164 us -> none  [the longest x1 44 us: on_device(): lax.psum(jnp.sum(conv_out, axis=0), ('seq', 'fsdp')) / all_frames]
    psum x1 -> x0, waiting for transfers between devices: 74.3 us -> none  [on_device(): lax.psum((kernel_portion, jnp.sum(normalized_gradient * standardized_inpu...]
    ppermute x0 -> x35, waiting for transfers between devices: none -> 66.7 us  [tree_sum(): tree = jax.tree.map(lambda x: x + lax.ppermute(x, axis, route), tree)]
    psum x1, waiting for transfers between devices: 174 us -> 109 us  [on_device(): grad_w_in = lax.psum(row_share, 'seq')]
    ppermute x0 -> x35, starting transfers between devices: none -> 44.7 us  [tree_sum(): tree = jax.tree.map(lambda x: x + lax.ppermute(x, axis, route), tree)]
  transfers between devices with their start and end apart: 6 -> 40, of which waited for: 6 -> 30; matrix products, arithmetic and copies ran while one was open for 3% -> 4% of each run, Pallas kernels for 0% -> 0%
where the time goes in v1:
time: 561 us
  waiting for transfers between devices  387 us (69%)
  other arithmetic  75.8 us (14%)
  starting transfers between devices  48.7 us (9%)
  matrix products  25.2 us (4%)
  between operations  14.3 us (3%)
  local copies, waits for them, and re-layouts  10.4 us (2%)
    reduce_scatter x1, waiting for transfers between devices, on_device(): lax.psum_scatter(lax.dot_general(normalized_rows, grad_hidden, (((0,), (0...  141 us
    psum x1, waiting for transfers between devices, on_device(): grad_w_in = lax.psum(row_share, 'seq')  109 us
    all_gather x1, waiting for transfers between devices, on_device(): full_weight = lax.all_gather(w_in, 'fsdp', axis=0, tiled=True)  67.3 us
    ppermute x35, waiting for transfers between devices, tree_sum(): tree = jax.tree.map(lambda x: x + lax.ppermute(x, axis, route), tree)  66.7 us
    another operation x2, other arithmetic  44.9 us
    ppermute x35, starting transfers between devices, tree_sum(): tree = jax.tree.map(lambda x: x + lax.ppermute(x, axis, route), tree)  44.7 us
    reduce_sum x2, other arithmetic, on_device(): jnp.sum(grad_conv * padded_glu[kernel_len - 1 - offset:kernel_len - 1 - o...  12.6 us
  transfers between devices with their start and end apart: 40, of which 30 were waited for; matrix products, arithmetic and copies ran while one was open for 4% of the time, Pallas kernels for 0%

profile of v1, /device:TPU:0, one launch (start us, length us, event | category | flops | bytes accessed | tf_op | source)
XLA Modules:
  0.0 560.9 jit_solution(14859436354774125420)
XLA Ops:
  9.3 67.3 %all-gather.2.cloned.1.call-done = bf16[1536,3072]{1,0:T(8,128)(2,1)} async-done(((bf16[384,3072]{1,0:T(8,128)(2,1)}), bf16[1536,3072]{1,0:T(8,128)(2,1)}) %all-gather.2.cloned.1.call-update) | async-done | bytes 9437200 | tf_op jit(solution)/shard_map/all_gather | solution.py:42
  76.6 6.7 %fusion.114 = f32[384,3072]{1,0:T(8,128)S(1)} fusion(bf16[1536,3072]{1,0:T(8,128)(2,1)} %all-gather.2.cloned.1.call-done, bf16[384,1536]{1,0:T(8,128)(2,1)S(1)} %copy-done.2, f32[1536]{0:T(1024)S(1)} %copy-done.10, f32[1536]{0:T(1024)S(1)} %copy-done.9, f32[384]{0:T(512)S(1)} %add_rsqrt_fusion.1, f32[384]{0:T(512)S(1)} %broadcast_multiply_fusion.3), kind=kOutput, calls=%fused_computation.258 | convolution fusion | flops 3627417600 | bytes 15350784 | tf_op jit(solution)/shard_map/dot_general | solution.py:43
  85.5 2.2 collective-permute-start
  88.9 9.4 %fusion.119 = (f32[1536]{0:T(1024)S(1)}, f32[384,1536]{1,0:T(8,128)S(1)}) fusion(f32[415,1536]{1,0:T(8,128)S(1)} %maximum_convert_fusion, f32[1536]{0:T(1024)S(1)} %get-tuple-element.76, f32[1536]{0:T(1024)S(1)} %get-tuple-element.77, f32[1536]{0:T(1024)S(1)} %get-tuple-element.47, f32[1536]{0:T(1024)S(1)} %get-tuple-element.48, ...), kind=kLoop, calls=%fused_computation.261 | loop fusion | flops 37747200 | bytes 78059520 | tf_op jit(solution)/shard_map/reduce_sum | solution.py:56
  100.2 2.6 collective-permute-start.2
  104.4 4.1 collective-permute-start.3
  110.2 2.9 collective-permute-start.4
  114.7 2.9 collective-permute-start.5
  120.8 3.6 collective-permute-done.7
  125.6 2.6 collective-permute-done.8
  128.1 2.0 collective-permute-start.9
  131.8 2.9 collective-permute-start.10
  136.4 2.5 fusion.116
  140.2 1.9 collective-permute-start.17
  147.4 2.0 collective-permute-start.14
  151.0 2.9 collective-permute-start.15
  156.2 2.3 collective-permute-done.20
  158.5 7.1 %multiply_reduce_fusion = (f32[1536]{0:T(1024)S(1)}, f32[1536]{0:T(1024)S(1)}, f32[1536]{0:T(1024)S(1)}, f32[1536]{0:T(1024)S(1)}, f32[1536]{0:T(1024)S(1)}, /*i...) fusion(f32[415,1536]{1,0:T(8,128)S(1)} %maximum_convert_fusion,, ...), kind=kLoop, calls=%fused_computation.169 | loop fusion | flops 31822848 | bytes 48519168 | tf_op jit(solution)/shard_map/reduce_sum | solution.py:78
  168.5 1.9 collective-permute-done.21
  170.3 40.4 %multiply_convert_fusion.1 = (bf16[384,1536]{1,0:T(8,128)(2,1)S(1)}, f32[384,1536]{1,0:T(8,128)}) fusion(f32[384,3072]{1,0:T(8,128)} %copy-done, f32[31,1536]{1,0:T(8,128)S(1)} %collective-permute-done.21, f32[384,1536]{1,0:T(8,128)} %copy-done.1, f32[1536]{0:T(1024)S(1)} %get-tuple-element.76, f32[1536]{0:T(1024)S(1)} %get-tuple-element.77, ...), kind=kLoop, calls=%fused_computation.202 | loop fusion | flops 58392576 | bytes 8644608 | tf_op jit(solution)/shard_map/convert
  210.8 4.4 multiply_convert_fusion
  216.3 9.4 %fusion.109 = f32[1536,3072]{1,0:T(8,128)} fusion(bf16[384,1536]{1,0:T(8,128)(2,1)S(1)} %multiply_convert_fusion, bf16[384,1536]{1,0:T(8,128)(2,1)S(1)} %get-tuple-element.79, bf16[384,1536]{1,0:T(8,128)(2,1)S(1)} %copy-done.3, f32[1536]{0:T(1024)S(1)} %copy-done.10, f32[1536]{0:T(1024)S(1)} %copy-done.9, f32[384]{0:T(512)S(1)} %add_rsqrt_fusion.1, ...), kind=kOutput, calls=%fused_computation.214 | convolution fusion | flops 3632136192 | bytes 22428672 | tf_op jit(solution)/shard_map/dot_general | solution.py:106
  226.0 140.8 %reduce-scatter.2.cloned.1.call-done = f32[384,3072]{1,0:T(8,128)} async-done(((f32[1536,3072]{1,0:T(8,128)}), f32[384,3072]{1,0:T(8,128)}) %reduce-scatter.2.cloned.1.call-update) | async-done | bytes 4718608 | tf_op jit(solution)/shard_map/reduce_scatter | solution.py:105
  366.8 5.4 multiply_reduce_fusion.18
  374.9 6.6 %collective-permute-done.23 = f32[32,1536]{1,0:T(8,128)S(1)} collective-permute-done((f32[32,1536]{1,0:T(8,128)S(1)}, f32[32,1536]{1,0:T(8,128)S(1)}, u32[]{:S(2)}, u32[]{:S(2)}) %collective-permute-start.23) | collective-permute-done | bytes 196640 | tf_op jit(solution)/shard_map/ppermute | solution.py:22
  383.1 9.1 %fusion.12 = (f32[1536]{0:T(1024)S(1)}, f32[384]{0:T(512)S(1)}, f32[384]{0:T(512)S(1)}, f32[1536]{0:T(1024)S(1)}, f32[384,1536]{1,0:T(8,128)S(1)}) fusion(bf16[384,1536]{1,0:T(8,128)(2,1)} %param.8, f32[384]{0:T(512)S(1)} %add_rsqrt_fusion.1, f32[384]{0:T(512)S(1)} %broadcast_multiply_fusion.3, f32[1536]{0:T(1024)S(1)} %copy-done.9, ...), kind=kOutput, calls=%fused_computation.44 | convolution fusion | flops 3634491392 | bytes 15360000 | tf_op jit(solution)/shard_map/dot_general | solution.py:88
  404.4 2.2 collective-permute-done.30
  407.1 2.4 collective-permute-start.36
  409.5 17.2 %collective-permute-done.25 = f32[32,1536]{1,0:T(8,128)S(1)} collective-permute-done((f32[32,1536]{1,0:T(8,128)S(1)}, f32[32,1536]{1,0:T(8,128)S(1)}, u32[]{:S(2)}, u32[]{:S(2)}) %collective-permute-start.25) | collective-permute-done | bytes 196640 | tf_op jit(solution)/shard_map/ppermute | solution.py:22
  430.3 9.8 %collective-permute-done.26 = f32[32,1536]{1,0:T(8,128)S(1)} collective-permute-done((f32[32,1536]{1,0:T(8,128)S(1)}, f32[32,1536]{1,0:T(8,128)S(1)}, u32[]{:S(2)}, u32[]{:S(2)}) %collective-permute-start.26) | collective-permute-done | bytes 196640 | tf_op jit(solution)/shard_map/ppermute | solution.py:22
  440.8 108.5 %all-reduce.2.cloned.1.call-done = f32[384,3072]{1,0:T(8,128)} async-done(((f32[384,3072]{1,0:T(8,128)}), f32[384,3072]{1,0:T(8,128)}) %all-reduce.2.cloned.1.call-update) | async-done | bytes 4718608 | tf_op jit(solution)/shard_map/psum | solution.py:116
  549.3 5.1 copy.17
  (170 shorter events, 55.3 us)
Async XLA Ops:
  7.2 69.4 %all-gather.2.cloned.1.call-start = ((), (), s32[]{:S(2)}) async-start(), calls=%async_computation.1 | async-start | bytes 11796480 | tf_op jit(solution)/shard_map/all_gather | solution.py:42
  7.9 358.8 %reduce-scatter.2.cloned.1.call-start = ((), (), s32[]{:S(2)}) async-start(), calls=%async_computation.2 | async-start | bytes 23592960 | tf_op jit(solution)/shard_map/reduce_scatter | solution.py:105
  100.2 4.3 collective-permute-start.2
  104.4 5.7 %collective-permute-start.3 = (f32[1536]{0:T(1024)S(1)}, f32[1536]{0:T(1024)S(1)}, u32[]{:S(2)}, u32[]{:S(2)}) collective-permute-start(f32[1536]{0:T(1024)S(1)} %add.374), channel_id=1, source_target_pairs={{0,4},{1,5},{2,6},{3,7},{4,0},{5,1},{6,2},{7,3},{8,12},{9,13},{10,... | collective-permute-start | bytes 18440 | tf_op jit(solution)/shard_map/ppermute | solution.py:22
  110.2 4.6 collective-permute-start.4
  114.7 4.6 collective-permute-start.5
  120.8 3.7 collective-permute-start.7
  124.5 3.7 collective-permute-start.8
  128.1 3.7 collective-permute-start.9
  131.8 4.6 collective-permute-start.10
  140.0 3.7 collective-permute-start.12
  140.2 4.6 collective-permute-start.17
  143.7 3.7 collective-permute-start.13
  144.8 4.6 collective-permute-start.18
  147.4 3.7 collective-permute-start.14
  149.4 4.6 collective-permute-start.19
  151.0 4.5 collective-permute-start.15
  153.9 4.6 collective-permute-start.20
  167.0 3.3 collective-permute-start.21
  225.7 323.6 %all-reduce.2.cloned.1.call-start = ((), (), s32[]{:S(2)}) async-start(), calls=%async_computation.3 | async-start | bytes 9437184 | tf_op jit(solution)/shard_map/psum | solution.py:116
  374.6 7.0 %collective-permute-start.23 = (f32[32,1536]{1,0:T(8,128)S(1)}, f32[32,1536]{1,0:T(8,128)S(1)}, u32[]{:S(2)}, u32[]{:S(2)}) collective-permute-start(f32[32,1536]{1,0:T(8,128)S(1)} %add.430), channel_id=1, source_target_pairs={{0,2},{1,3},{2,0},{3,1},{4,6},{5,7},{6,4},{7,5},{8,10},{9,11},{10,... | collective-permute-start | bytes 589832 | tf_op jit(solution)/shard_map/ppermute | solution.py:22
  381.6 21.3 %collective-permute-start.24 = (f32[32,1536]{1,0:T(8,128)S(1)}, f32[32,1536]{1,0:T(8,128)S(1)}, u32[]{:S(2)}, u32[]{:S(2)}) collective-permute-start(f32[32,1536]{1,0:T(8,128)S(1)} %add.431), channel_id=1, source_target_pairs={{0,4},{1,5},{2,6},{3,7},{4,0},{5,1},{6,2},{7,3},{8,12},{9,13},{10,... | collective-permute-start | bytes 589832 | tf_op jit(solution)/shard_map/ppermute | solution.py:22
  393.5 3.7 collective-permute-start.28
  394.0 3.7 collective-permute-start.33
  397.1 3.7 collective-permute-start.29
  397.7 4.6 collective-permute-start.34
  400.8 5.8 %collective-permute-start.30 = (f32[1536]{0:T(1024)S(1)}, f32[1536]{0:T(1024)S(1)}, u32[]{:S(2)}, u32[]{:S(2)}) collective-permute-start(f32[1536]{0:T(1024)S(1)} %add.437), channel_id=1, source_target_pairs={{0,8},{1,9},{2,10},{3,11},{4,12},{5,13},{6,14},{7,15},{8,0},{9,1},... | collective-permute-start | bytes 18440 | tf_op jit(solution)/shard_map/ppermute | solution.py:22
  402.3 4.8 collective-permute-start.35
  402.9 23.9 %collective-permute-start.25 = (f32[32,1536]{1,0:T(8,128)S(1)}, f32[32,1536]{1,0:T(8,128)S(1)}, u32[]{:S(2)}, u32[]{:S(2)}) collective-permute-start(f32[32,1536]{1,0:T(8,128)S(1)} %add.432), channel_id=1, source_target_pairs={{0,8},{1,9},{2,10},{3,11},{4,12},{5,13},{6,14},{7,15},{8,0},{9,1},... | collective-permute-start | bytes 589832 | tf_op jit(solution)/shard_map/ppermute | solution.py:22
  406.6 22.5 %collective-permute-start.31 = (f32[1536]{0:T(1024)S(1)}, f32[1536]{0:T(1024)S(1)}, u32[]{:S(2)}, u32[]{:S(2)}) collective-permute-start(f32[1536]{0:T(1024)S(1)} %add.438), channel_id=1, source_target_pairs={{0,16},{1,17},{2,18},{3,19},{4,20},{5,21},{6,22},{7,23},{8,24},{9,... | collective-permute-start | bytes 18440 | tf_op jit(solution)/shard_map/ppermute | solution.py:22
  407.1 22.6 %collective-permute-start.36 = (f32[1536]{0:T(1024)S(1)}, f32[1536]{0:T(1024)S(1)}, u32[]{:S(2)}, u32[]{:S(2)}) collective-permute-start(f32[1536]{0:T(1024)S(1)} %add.443), channel_id=1, source_target_pairs={{0,16},{1,17},{2,18},{3,19},{4,20},{5,21},{6,22},{7,23},{8,24},{9,... | collective-permute-start | bytes 18440 | tf_op jit(solution)/shard_map/ppermute | solution.py:22
  426.8 13.4 %collective-permute-start.26 = (f32[32,1536]{1,0:T(8,128)S(1)}, f32[32,1536]{1,0:T(8,128)S(1)}, u32[]{:S(2)}, u32[]{:S(2)}) collective-permute-start(f32[32,1536]{1,0:T(8,128)S(1)} %add.433), channel_id=1, source_target_pairs={{0,16},{1,17},{2,18},{3,19},{4,20},{5,21},{6,22},{7,23},{8,24},{9,... | collective-permute-start | bytes 589832 | tf_op jit(solution)/shard_map/ppermute | solution.py:22
  (22 other events, 335.4 us)
Sparse Core Ops, SparseCore 0:
  9.6 66.9 all-gather.1
  225.8 140.8 reduce-scatter.1
  370.8 178.4 all-reduce.1

commit v2 on v1

--- a/solution.py
+++ b/solution.py
@@ -40,6 +40,7 @@
     standardized_input = centered_rows * row_inverse_deviation
     normalized_rows = (standardized_input * layer_norm_gain + layer_norm_bias).astype(jnp.bfloat16)
     full_weight = lax.all_gather(w_in, "fsdp", axis=0, tiled=True)
+    group_rows = lax.all_gather(normalized_rows, "fsdp", axis=0, tiled=True)
     hidden = jnp.dot(normalized_rows, full_weight, preferred_element_type=jnp.float32)
     value_part = hidden[:, :features]
     gate_sig = jax.nn.sigmoid(hidden[:, features:])
@@ -102,16 +103,13 @@
         - jnp.mean(rescaled_rows, axis=-1, keepdims=True)
         - standardized_input * jnp.mean(rescaled_rows * standardized_input, axis=-1, keepdims=True)
     )
-    row_share = lax.psum_scatter(
-        lax.dot_general(
-            normalized_rows,
-            grad_hidden,
-            (((0,), (0,)), ((), ())),
-            preferred_element_type=jnp.float32,
-        ),
-        "fsdp",
-        scatter_dimension=0,
-        tiled=True,
+    feature_rows = w_in.shape[0]
+    own_columns = lax.dynamic_slice_in_dim(
+        group_rows, lax.axis_index("fsdp") * feature_rows, feature_rows, axis=1
+    )
+    group_grad = lax.all_gather(grad_hidden, "fsdp", axis=0, tiled=True)
+    row_share = lax.dot_general(
+        own_columns, group_grad, (((0,), (0,)), ((), ())), preferred_element_type=jnp.float32
     )
     grad_w_in = lax.psum(row_share, "seq")
     return (

time: 561 us -> 496 us (0.88)
  waiting for transfers between devices: 387 us -> 311 us
  other arithmetic: 75.8 us -> 85.4 us
    reduce_scatter x1 -> x0, waiting for transfers between devices: 141 us -> none  [on_device(): lax.psum_scatter(lax.dot_general(normalized_rows, grad_hidden, (((0,), (0...]
    all_gather x0 -> x2, waiting for transfers between devices: none -> 69.7 us  [the longest x1 69.7 us: on_device(): group_grad = lax.all_gather(grad_hidden, 'fsdp', axis=0, tiled=True)]
    another operation x2, other arithmetic: 44.9 us -> 51.1 us
  transfers between devices with their start and end apart: 40 -> 41, of which waited for: 30 -> 31; matrix products, arithmetic and copies ran while one was open for 4% -> 17% of each run, Pallas kernels for 0% -> 0%
where the time goes in v2:
time: 496 us
  waiting for transfers between devices  311 us (63%)
  other arithmetic  85.4 us (17%)
  starting transfers between devices  48.4 us (10%)
  matrix products  25.6 us (5%)
  between operations  14.4 us (3%)
  local copies, waits for them, and re-layouts  10.5 us (2%)
    psum x1, waiting for transfers between devices, on_device(): grad_w_in = lax.psum(row_share, 'seq')  106 us
    all_gather x1, waiting for transfers between devices, on_device(): group_grad = lax.all_gather(grad_hidden, 'fsdp', axis=0, tiled=True)  69.7 us
    all_gather x1, waiting for transfers between devices, on_device(): full_weight = lax.all_gather(w_in, 'fsdp', axis=0, tiled=True)  66.8 us
    ppermute x35, waiting for transfers between devices, tree_sum(): tree = jax.tree.map(lambda x: x + lax.ppermute(x, axis, route), tree)  65 us
    another operation x2, other arithmetic  51.1 us
    ppermute x35, starting transfers between devices, tree_sum(): tree = jax.tree.map(lambda x: x + lax.ppermute(x, axis, route), tree)  44.6 us
    reduce_sum x2, other arithmetic, on_device(): jnp.sum(grad_conv * padded_glu[kernel_len - 1 - offset:kernel_len - 1 - o...  13.8 us
    dot_general x1, matrix products, on_device(): lax.dot_general(own_columns, group_grad, (((0,), (0,)), ((), ())), prefer...  10.1 us
  transfers between devices with their start and end apart: 41, of which 31 were waited for; matrix products, arithmetic and copies ran while one was open for 17% of the time, Pallas kernels for 0%

profile of v2, /device:TPU:0, one launch (start us, length us, event | category | flops | bytes accessed | tf_op | source)
XLA Modules:
  0.0 495.6 jit_solution(478660610724217691)
XLA Ops:
  9.8 66.8 %all-gather.4.cloned.1.call-done = bf16[1536,3072]{1,0:T(8,128)(2,1)} async-done(((bf16[384,3072]{1,0:T(8,128)(2,1)}), bf16[1536,3072]{1,0:T(8,128)(2,1)}) %all-gather.4.cloned.1.call-update) | async-done | bytes 9437200 | tf_op jit(solution)/shard_map/all_gather | solution.py:42
  76.6 6.3 %fusion.117 = f32[384,3072]{1,0:T(8,128)S(1)} fusion(bf16[384,1536]{1,0:T(8,128)(2,1)S(1)} %fusion.7, bf16[1536,3072]{1,0:T(8,128)(2,1)} %all-gather.4.cloned.1.call-done), kind=kOutput, calls=%fused_computation.261 | convolution fusion | flops 3623878656 | bytes 15335424 | tf_op jit(solution)/shard_map/dot_general | solution.py:44
  85.1 2.2 collective-permute-start
  88.6 9.4 %fusion.116 = (f32[1536]{0:T(1024)S(1)}, f32[384,1536]{1,0:T(8,128)S(1)}) fusion(f32[415,1536]{1,0:T(8,128)S(1)} %maximum_convert_fusion, f32[1536]{0:T(1024)S(1)} %get-tuple-element.76, f32[1536]{0:T(1024)S(1)} %get-tuple-element.77, f32[1536]{0:T(1024)S(1)} %get-tuple-element.47, f32[1536]{0:T(1024)S(1)} %get-tuple-element.48, ...), kind=kLoop, calls=%fused_computation.260 | loop fusion | flops 37747200 | bytes 78059520 | tf_op jit(solution)/shard_map/reduce_sum | solution.py:57
  99.8 2.6 collective-permute-start.2
  104.1 4.1 collective-permute-start.3
  109.8 2.9 collective-permute-start.4
  114.4 2.9 collective-permute-start.5
  120.5 3.6 collective-permute-done.7
  125.2 2.6 collective-permute-done.8
  127.8 2.0 collective-permute-start.9
  131.5 2.9 collective-permute-start.10
  136.1 2.5 fusion.113
  139.9 1.9 collective-permute-start.17
  147.1 2.0 collective-permute-start.14
  150.7 2.9 collective-permute-start.15
  155.9 2.5 collective-permute-done.20
  158.3 8.3 %multiply_reduce_fusion = (f32[1536]{0:T(1024)S(1)}, f32[1536]{0:T(1024)S(1)}, f32[1536]{0:T(1024)S(1)}, f32[1536]{0:T(1024)S(1)}, f32[1536]{0:T(1024)S(1)}, /*i...) fusion(f32[415,1536]{1,0:T(8,128)S(1)} %maximum_convert_fusion,, ...), kind=kLoop, calls=%fused_computation.169 | loop fusion | flops 31822848 | bytes 48519168 | tf_op jit(solution)/shard_map/reduce_sum | solution.py:79
  169.7 1.9 collective-permute-done.21
  171.5 46.7 %multiply_convert_fusion.1 = (bf16[384,1536]{1,0:T(8,128)(2,1)S(1)}, f32[384,1536]{1,0:T(8,128)}) fusion(f32[384,3072]{1,0:T(8,128)} %copy-done.1, f32[31,1536]{1,0:T(8,128)S(1)} %collective-permute-done.21, f32[384,1536]{1,0:T(8,128)} %copy-done.2, f32[1536]{0:T(1024)S(1)} %get-tuple-element.76, f32[1536]{0:T(1024)S(1)} %get-tuple-element.77, ...), kind=kLoop, calls=%fused_computation.202 | loop fusion | flops 58392576 | bytes 8644608 | tf_op jit(solution)/shard_map/convert
  218.2 4.4 multiply_convert_fusion
  225.4 69.7 %all-gather.8.cloned.1.call-done = bf16[1536,3072]{1,0:T(8,128)(2,1)} async-done(((bf16[384,3072]{1,0:T(8,128)(2,1)}), bf16[1536,3072]{1,0:T(8,128)(2,1)}) %all-gather.8.cloned.1.call-update) | async-done | bytes 9437200 | tf_op jit(solution)/shard_map/all_gather | solution.py:110
  295.2 10.1 %fusion.109 = f32[384,3072]{1,0:T(8,128)} fusion(bf16[1536,3072]{1,0:T(8,128)(2,1)} %all-gather.8.cloned.1.call-done, bf16[1536,1536]{1,0:T(8,128)(2,1)} %all-gather.6.cloned.1.call-done, s32[]{:T(128)S(6)} %select_n.3), kind=kOutput, calls=%fused_computation.215 | convolution fusion | flops 3623878656 | bytes 15335428 | tf_op jit(solution)/shard_map/dot_general | solution.py:111
  305.3 5.4 %multiply_reduce_fusion.18 = (f32[1536]{0:T(1024)S(1)}, f32[1536]{0:T(1024)S(1)}, f32[1536]{0:T(1024)S(1)}, f32[1536]{0:T(1024)S(1)}, f32[1536]{0:T(1024)S(1)}, ...) fusion(f32[384,1536]{1,0:T(8,128)} %copy-done.2, ...), kind=kLoop, calls=%fused_computation.187 | loop fusion | flops 16493568 | bytes 35475456 | tf_op jit(solution)/shard_map/reduce_sum | solution.py:79
  313.5 6.7 %collective-permute-done.23 = f32[32,1536]{1,0:T(8,128)S(1)} collective-permute-done((f32[32,1536]{1,0:T(8,128)S(1)}, f32[32,1536]{1,0:T(8,128)S(1)}, u32[]{:S(2)}, u32[]{:S(2)}) %collective-permute-start.23) | collective-permute-done | bytes 196640 | tf_op jit(solution)/shard_map/ppermute | solution.py:22
  321.8 9.1 %fusion.12 = (f32[1536]{0:T(1024)S(1)}, f32[384]{0:T(512)S(1)}, f32[384]{0:T(512)S(1)}, f32[1536]{0:T(1024)S(1)}, f32[384,1536]{1,0:T(8,128)S(1)}) fusion(bf16[384,1536]{1,0:T(8,128)(2,1)} %param.8, f32[384]{0:T(512)S(1)} %add_rsqrt_fusion.1, f32[384]{0:T(512)S(1)} %broadcast_multiply_fusion.3, f32[1536]{0:T(1024)S(1)} %copy-done.12, ...), kind=kOutput, calls=%fused_computation.44 | convolution fusion | flops 3634491392 | bytes 15360000 | tf_op jit(solution)/shard_map/dot_general | solution.py:89
  343.1 2.5 collective-permute-done.35
  346.1 2.4 collective-permute-start.31
  348.6 14.9 %collective-permute-done.25 = f32[32,1536]{1,0:T(8,128)S(1)} collective-permute-done((f32[32,1536]{1,0:T(8,128)S(1)}, f32[32,1536]{1,0:T(8,128)S(1)}, u32[]{:S(2)}, u32[]{:S(2)}) %collective-permute-start.25) | collective-permute-done | bytes 196640 | tf_op jit(solution)/shard_map/ppermute | solution.py:22
  367.1 9.7 %collective-permute-done.26 = f32[32,1536]{1,0:T(8,128)S(1)} collective-permute-done((f32[32,1536]{1,0:T(8,128)S(1)}, f32[32,1536]{1,0:T(8,128)S(1)}, u32[]{:S(2)}, u32[]{:S(2)}) %collective-permute-start.26) | collective-permute-done | bytes 196640 | tf_op jit(solution)/shard_map/ppermute | solution.py:22
  377.5 106.5 %all-reduce.2.cloned.1.call-done = f32[384,3072]{1,0:T(8,128)} async-done(((f32[384,3072]{1,0:T(8,128)}), f32[384,3072]{1,0:T(8,128)}) %all-reduce.2.cloned.1.call-update) | async-done | bytes 4718608 | tf_op jit(solution)/shard_map/psum | solution.py:114
  484.0 5.1 %copy.17 = f32[384,3072]{1,0:T(8,128)} copy(f32[384,3072]{1,0:T(8,128)} %all-reduce.2.cloned.1.call-done) | data formatting | bytes 9437184
  (177 shorter events, 57.5 us)
Async XLA Ops:
  7.2 69.4 %all-gather.4.cloned.1.call-start = ((), (), s32[]{:S(2)}) async-start(), calls=%async_computation | async-start | bytes 11796480 | tf_op jit(solution)/shard_map/all_gather | solution.py:42
  7.9 217.5 %all-gather.6.cloned.1.call-start = ((), (), s32[]{:S(2)}) async-start(), calls=%async_computation.1 | async-start | bytes 5898240 | tf_op jit(solution)/shard_map/all_gather | solution.py:43
  99.8 4.3 collective-permute-start.2
  104.1 5.7 %collective-permute-start.3 = (f32[1536]{0:T(1024)S(1)}, f32[1536]{0:T(1024)S(1)}, u32[]{:S(2)}, u32[]{:S(2)}) collective-permute-start(f32[1536]{0:T(1024)S(1)} %add.375), channel_id=1, source_target_pairs={{0,4},{1,5},{2,6},{3,7},{4,0},{5,1},{6,2},{7,3},{8,12},{9,13},{10,... | collective-permute-start | bytes 18440 | tf_op jit(solution)/shard_map/ppermute | solution.py:22
  109.8 4.6 collective-permute-start.4
  114.4 4.6 collective-permute-start.5
  120.5 3.7 collective-permute-start.7
  124.2 3.7 collective-permute-start.8
  127.8 3.7 collective-permute-start.9
  131.5 4.6 collective-permute-start.10
  139.7 3.7 collective-permute-start.12
  139.9 4.6 collective-permute-start.17
  143.4 3.7 collective-permute-start.13
  144.5 4.6 collective-permute-start.18
  147.1 3.7 collective-permute-start.14
  149.1 4.7 collective-permute-start.19
  150.7 4.5 collective-permute-start.15
  153.7 141.5 %all-gather.8.cloned.1.call-start = ((), (), s32[]{:S(2)}) async-start(), calls=%async_computation.2 | async-start | bytes 11796480 | tf_op jit(solution)/shard_map/all_gather | solution.py:110
  153.7 4.6 collective-permute-start.20
  225.4 258.7 %all-reduce.2.cloned.1.call-start = ((), (), s32[]{:S(2)}) async-start(), calls=%async_computation.3 | async-start | bytes 9437184 | tf_op jit(solution)/shard_map/psum | solution.py:114
  313.1 7.1 %collective-permute-start.23 = (f32[32,1536]{1,0:T(8,128)S(1)}, f32[32,1536]{1,0:T(8,128)S(1)}, u32[]{:S(2)}, u32[]{:S(2)}) collective-permute-start(f32[32,1536]{1,0:T(8,128)S(1)} %add.432), channel_id=1, source_target_pairs={{0,2},{1,3},{2,0},{3,1},{4,6},{5,7},{6,4},{7,5},{8,10},{9,11},{10,... | collective-permute-start | bytes 589832 | tf_op jit(solution)/shard_map/ppermute | solution.py:22
  320.3 21.3 %collective-permute-start.24 = (f32[32,1536]{1,0:T(8,128)S(1)}, f32[32,1536]{1,0:T(8,128)S(1)}, u32[]{:S(2)}, u32[]{:S(2)}) collective-permute-start(f32[32,1536]{1,0:T(8,128)S(1)} %add.433), channel_id=1, source_target_pairs={{0,4},{1,5},{2,6},{3,7},{4,0},{5,1},{6,2},{7,3},{8,12},{9,13},{10,... | collective-permute-start | bytes 589832 | tf_op jit(solution)/shard_map/ppermute | solution.py:22
  332.2 3.7 collective-permute-start.33
  332.7 3.7 collective-permute-start.28
  335.8 3.7 collective-permute-start.34
  336.4 4.6 collective-permute-start.29
  339.5 6.1 %collective-permute-start.35 = (f32[1536]{0:T(1024)S(1)}, f32[1536]{0:T(1024)S(1)}, u32[]{:S(2)}, u32[]{:S(2)}) collective-permute-start(f32[1536]{0:T(1024)S(1)} %add.444), channel_id=1, source_target_pairs={{0,8},{1,9},{2,10},{3,11},{4,12},{5,13},{6,14},{7,15},{8,0},{9,1},... | collective-permute-start | bytes 18440 | tf_op jit(solution)/shard_map/ppermute | solution.py:22
  341.0 5.1 %collective-permute-start.30 = (f32[1536]{0:T(1024)S(1)}, f32[1536]{0:T(1024)S(1)}, u32[]{:S(2)}, u32[]{:S(2)}) collective-permute-start(f32[1536]{0:T(1024)S(1)} %add.439), channel_id=1, source_target_pairs={{0,8},{1,9},{2,10},{3,11},{4,12},{5,13},{6,14},{7,15},{8,0},{9,1},... | collective-permute-start | bytes 18440 | tf_op jit(solution)/shard_map/ppermute | solution.py:22
  341.6 21.9 %collective-permute-start.25 = (f32[32,1536]{1,0:T(8,128)S(1)}, f32[32,1536]{1,0:T(8,128)S(1)}, u32[]{:S(2)}, u32[]{:S(2)}) collective-permute-start(f32[32,1536]{1,0:T(8,128)S(1)} %add.434), channel_id=1, source_target_pairs={{0,8},{1,9},{2,10},{3,11},{4,12},{5,13},{6,14},{7,15},{8,0},{9,1},... | collective-permute-start | bytes 589832 | tf_op jit(solution)/shard_map/ppermute | solution.py:22
  345.6 20.3 %collective-permute-start.36 = (f32[1536]{0:T(1024)S(1)}, f32[1536]{0:T(1024)S(1)}, u32[]{:S(2)}, u32[]{:S(2)}) collective-permute-start(f32[1536]{0:T(1024)S(1)} %add.445), channel_id=1, source_target_pairs={{0,16},{1,17},{2,18},{3,19},{4,20},{5,21},{6,22},{7,23},{8,24},{9,... | collective-permute-start | bytes 18440 | tf_op jit(solution)/shard_map/ppermute | solution.py:22
  346.1 20.4 %collective-permute-start.31 = (f32[1536]{0:T(1024)S(1)}, f32[1536]{0:T(1024)S(1)}, u32[]{:S(2)}, u32[]{:S(2)}) collective-permute-start(f32[1536]{0:T(1024)S(1)} %add.440), channel_id=1, source_target_pairs={{0,16},{1,17},{2,18},{3,19},{4,20},{5,21},{6,22},{7,23},{8,24},{9,... | collective-permute-start | bytes 18440 | tf_op jit(solution)/shard_map/ppermute | solution.py:22
  363.5 13.3 %collective-permute-start.26 = (f32[32,1536]{1,0:T(8,128)S(1)}, f32[32,1536]{1,0:T(8,128)S(1)}, u32[]{:S(2)}, u32[]{:S(2)}) collective-permute-start(f32[32,1536]{1,0:T(8,128)S(1)} %add.435), channel_id=1, source_target_pairs={{0,16},{1,17},{2,18},{3,19},{4,20},{5,21},{6,22},{7,23},{8,24},{9,... | collective-permute-start | bytes 589832 | tf_op jit(solution)/shard_map/ppermute | solution.py:22
  (24 other events, 311.8 us)
Sparse Core Ops, SparseCore 0:
  9.6 66.9 all-gather.3
  153.8 36.8 all-gather.5
  225.5 69.6 all-gather.7
  305.5 178.5 all-reduce.1

commit v3 on v2

--- a/solution.py
+++ b/solution.py
@@ -16,12 +16,69 @@
     count = lax.axis_size(axis)
     if count & (count - 1):
         return lax.psum(tree, axis)
+    leaves, treedef = jax.tree.flatten(tree)
+    width = leaves[0].shape[-1]
+    packed = jnp.concatenate([leaf.reshape(-1, width) for leaf in leaves], axis=0)
     stride = 1
     while stride < count:
         route = [(i, i ^ stride) for i in range(count)]
-        tree = jax.tree.map(lambda x: x + lax.ppermute(x, axis, route), tree)
+        packed = packed + lax.ppermute(packed, axis, route)
         stride *= 2
-    return tree
+    out, start = [], 0
+    for leaf in leaves:
+        rows = leaf.size // width
+        out.append(packed[start : start + rows].reshape(leaf.shape))
+        start += rows
+    return jax.tree.unflatten(treedef, out)
+
+
+def group_shards(block, axis):
+    far = lax.ppermute(block, axis, [(i, i ^ 2) for i in range(4)])
+    near = lax.ppermute(
+        jnp.concatenate([block, far], axis=0), axis, [(i, i ^ 1) for i in range(4)]
+    )
+    return jnp.concatenate([block, far, near], axis=0)
+
+
+def gather_rows(block, axis):
+    count = lax.axis_size(axis)
+    if count != 4:
+        return lax.all_gather(block, axis, axis=0, tiled=True)
+    rows = block.shape[0]
+    me = lax.axis_index(axis)
+    shards = group_shards(block, axis)
+    whole = jnp.zeros((count * rows,) + block.shape[1:], block.dtype)
+    for slot, owner in enumerate((me, me ^ 2, me ^ 1, me ^ 3)):
+        whole = lax.dynamic_update_slice_in_dim(
+            whole, shards[slot * rows : (slot + 1) * rows], owner * rows, axis=0
+        )
+    return whole
+
+
+def gather_own_columns(rows_block, axis, width):
+    me = lax.axis_index(axis)
+    frames = rows_block.shape[0]
+
+    def cols(owner):
+        return lax.dynamic_slice_in_dim(rows_block, owner * width, width, axis=1)
+
+    if lax.axis_size(axis) != 4:
+        return lax.dynamic_slice_in_dim(
+            lax.all_gather(rows_block, axis, axis=0, tiled=True), me * width, width, axis=1
+        )
+    far = lax.ppermute(
+        jnp.concatenate([cols(me ^ 2), cols(me ^ 3)], axis=0), axis, [(i, i ^ 2) for i in range(4)]
+    )
+    near = lax.ppermute(
+        jnp.concatenate([cols(me ^ 1), far[frames:]], axis=0), axis, [(i, i ^ 1) for i in range(4)]
+    )
+    return jnp.concatenate([cols(me), far[:frames], near], axis=0)
+
+
+def gather_frames(block, axis):
+    if lax.axis_size(axis) != 4:
+        return lax.all_gather(block, axis, axis=0, tiled=True)
+    return group_shards(block, axis)
 
 
 def on_device(
@@ -39,8 +96,7 @@
     )
     standardized_input = centered_rows * row_inverse_deviation
     normalized_rows = (standardized_input * layer_norm_gain + layer_norm_bias).astype(jnp.bfloat16)
-    full_weight = lax.all_gather(w_in, "fsdp", axis=0, tiled=True)
-    group_rows = lax.all_gather(normalized_rows, "fsdp", axis=0, tiled=True)
+    full_weight = gather_rows(w_in, "fsdp")
     hidden = jnp.dot(normalized_rows, full_weight, preferred_element_type=jnp.float32)
     value_part = hidden[:, :features]
     gate_sig = jax.nn.sigmoid(hidden[:, features:])
@@ -104,12 +160,10 @@
         - standardized_input * jnp.mean(rescaled_rows * standardized_input, axis=-1, keepdims=True)
     )
     feature_rows = w_in.shape[0]
-    own_columns = lax.dynamic_slice_in_dim(
-        group_rows, lax.axis_index("fsdp") * feature_rows, feature_rows, axis=1
-    )
-    group_grad = lax.all_gather(grad_hidden, "fsdp", axis=0, tiled=True)
+    group_rows = gather_own_columns(normalized_rows, "fsdp", feature_rows)
+    group_grad = gather_frames(grad_hidden, "fsdp")
     row_share = lax.dot_general(
-        own_columns, group_grad, (((0,), (0,)), ((), ())), preferred_element_type=jnp.float32
+        group_rows, group_grad, (((0,), (0,)), ((), ())), preferred_element_type=jnp.float32
     )
     grad_w_in = lax.psum(row_share, "seq")
     return (

time: 496 us -> 492 us (level)
  waiting for transfers between devices: 311 us -> 273 us
  local copies, waits for them, and re-layouts: 10.5 us -> 47.2 us
  matrix products: 25.6 us -> 17.9 us
    all_gather x3 -> x0, waiting for transfers between devices: 137 us -> none  [the longest x1 69.7 us: on_device(): group_grad = lax.all_gather(grad_hidden, 'fsdp', axis=0, tiled=True)]
    ppermute x35 -> x26, waiting for transfers between devices: 65 us -> 186 us  [the longest x2 102 us: group_shards(): far = lax.ppermute(block, axis, [(i, i ^ 2) for i in range(4)])]
    psum x1, waiting for transfers between devices: 106 us -> 85.6 us  [on_device(): grad_w_in = lax.psum(row_share, 'seq')]
    another operation x33 -> x32, local copies, waits for them, and re-layouts: 0.53 us -> 19.1 us  [on_device(): kernel_portion = jnp.stack(kernel_rows, axis=0)]
    concatenate x0 -> x5, other arithmetic: none -> 13.4 us  [the longest x2 13.2 us: group_shards(): jnp.concatenate([block, far], axis=0)]
    concatenate x0 -> x1, local copies, waits for them, and re-layouts: none -> 7.35 us  [tree_sum(): jnp.concatenate([leaf.reshape(-1, width) for leaf in leaves], axis=0)]
    another operation x2, other arithmetic: 51.1 us -> 45.3 us
    ppermute x35 -> x26, starting transfers between devices: 44.6 us -> 44.6 us  [the longest x20 36.1 us: tree_sum(): packed = packed + lax.ppermute(packed, axis, route)]
  transfers between devices with their start and end apart: 41 -> 29, of which waited for: 31 -> 27; matrix products, arithmetic and copies ran while one was open for 17% -> 11% of each run, Pallas kernels for 0% -> 0%
where the time goes in v3:
time: 492 us; the launch traced here: 491 us
  waiting for transfers between devices  273 us (55%)
  other arithmetic  90.3 us (18%)
  starting transfers between devices  48.4 us (10%)
  local copies, waits for them, and re-layouts  47.2 us (10%)
  matrix products  17.9 us (4%)
  between operations  14.5 us (3%)
    ppermute x2, waiting for transfers between devices, group_shards(): far = lax.ppermute(block, axis, [(i, i ^ 2) for i in range(4)])  102 us
    psum x1, waiting for transfers between devices, on_device(): grad_w_in = lax.psum(row_share, 'seq')  85.6 us
    ppermute x20, waiting for transfers between devices, tree_sum(): packed = packed + lax.ppermute(packed, axis, route)  65.5 us
    another operation x2, other arithmetic  45.3 us
    ppermute x20, starting transfers between devices, tree_sum(): packed = packed + lax.ppermute(packed, axis, route)  36.1 us
    another operation x32, local copies, waits for them, and re-layouts, on_device(): kernel_portion = jnp.stack(kernel_rows, axis=0)  19.1 us
    ppermute x1, waiting for transfers between devices, gather_own_columns(): lax.ppermute(jnp.concatenate([cols(me ^ 2), cols(me ^ 3)], axis=0), axis,...  13.5 us
    concatenate x2, other arithmetic, group_shards(): jnp.concatenate([block, far], axis=0)  13.2 us
  transfers between devices with their start and end apart: 29, of which 27 were waited for; matrix products, arithmetic and copies ran while one was open for 11% of the time, Pallas kernels for 0%

profile of v3, /device:TPU:0, one launch (start us, length us, event | category | flops | bytes accessed | tf_op | source)
XLA Modules:
  0.0 491.2 jit_solution(5277442707779186700)
XLA Ops:
  7.2 3.0 collective-permute-start
  10.2 51.5 %collective-permute-done = bf16[384,3072]{1,0:T(8,128)(2,1)S(1)} collective-permute-done((bf16[384,3072]{1,0:T(8,128)(2,1)}, bf16[384,3072]{1,0:T(8,128)(2,1)S(1)}, u32[]{:S(2)}, u32[]{:S(2)}) %collective-permute-start) | collective-permute-done | bytes 2359328 | tf_op jit(solution)/shard_map/ppermute | solution.py:36
  61.7 4.2 pad_maximum_fusion
  78.0 3.8 fusion.129
  88.2 9.4 %fusion.127 = (f32[1536]{0:T(1024)S(1)}, f32[384,1536]{1,0:T(8,128)S(1)}) fusion(f32[415,1536]{1,0:T(8,128)S(1)} %maximum_convert_fusion, f32[1536]{0:T(1024)S(1)} %get-tuple-element.78, f32[1536]{0:T(1024)S(1)} %get-tuple-element.79, f32[1536]{0:T(1024)S(1)} %get-tuple-element.49, f32[1536]{0:T(1024)S(1)} %get-tuple-element.50, ...), kind=kLoop, calls=%fused_computation.288 | loop fusion | flops 37747200 | bytes 78059520 | tf_op jit(solution)/shard_map/reduce_sum | solution.py:113
  104.5 3.0 collective-permute-start.5
  109.2 3.0 collective-permute-start.6
  113.8 3.1 collective-permute-start.7
  120.2 3.6 collective-permute-done.9
  131.2 3.0 collective-permute-start.12
  139.8 3.7 collective-permute-done.14
  144.5 2.7 collective-permute-done.15
  151.0 3.0 collective-permute-start.17
  156.3 7.1 %multiply_reduce_fusion = (f32[1536]{0:T(1024)S(1)}, f32[1536]{0:T(1024)S(1)}, f32[1536]{0:T(1024)S(1)}, f32[1536]{0:T(1024)S(1)}, f32[1536]{0:T(1024)S(1)}, /*i...) fusion(f32[415,1536]{1,0:T(8,128)S(1)} %maximum_convert_fusion,, ...), kind=kLoop, calls=%fused_computation.181 | loop fusion | flops 31822848 | bytes 48519168 | tf_op jit(solution)/shard_map/reduce_sum | solution.py:135
  168.2 40.9 %multiply_convert_fusion.1 = (bf16[384,1536]{1,0:T(8,128)(2,1)S(1)}, f32[384,1536]{1,0:T(8,128)}) fusion(f32[384,3072]{1,0:T(8,128)} %copy-done, f32[31,1536]{1,0:T(8,128)S(1)} %collective-permute-done.18, f32[384,1536]{1,0:T(8,128)} %copy-done.1, f32[1536]{0:T(1024)S(1)} %get-tuple-element.78, f32[1536]{0:T(1024)S(1)} %get-tuple-element.79, ...), kind=kLoop, calls=%fused_computation.214 | loop fusion | flops 58392576 | bytes 8644608 | tf_op jit(solution)/shard_map/convert
  209.1 4.4 multiply_convert_fusion
  215.6 50.5 %collective-permute-done.21 = bf16[384,3072]{1,0:T(8,128)(2,1)S(1)} collective-permute-done((bf16[384,3072]{1,0:T(8,128)(2,1)S(1)}, bf16[384,3072]{1,0:T(8,128)(2,1)S(1)}, u32[]{:S(2)}, u32[]{:S(2)}) %collective-permute-start.21) | collective-permute-done | bytes 2359328 | tf_op jit(solution)/shard_map/ppermute | solution.py:36
  266.2 9.0 %pad_maximum_fusion.1 = bf16[768,3072]{1,0:T(8,128)(2,1)S(1)} fusion(bf16[384,3072]{1,0:T(8,128)(2,1)S(1)} %collective-permute-done.21, bf16[384,1536]{1,0:T(8,128)(2,1)S(1)} %multiply_convert_fusion, bf16[384,1536]{1,0:T(8,128)(2,1)S(1)} %get-tuple-element.84), kind=kLoop, calls=%fused_computation.39 | loop fusion | flops 14155776 | bytes 9437184 | tf_op jit(solution)/shard_map/concatenate | solution.py:38
  279.0 13.5 %collective-permute-done.19 = bf16[768,384]{1,0:T(8,128)(2,1)S(1)} collective-permute-done((bf16[768,384]{1,0:T(8,128)(2,1)S(1)}, bf16[768,384]{1,0:T(8,128)(2,1)S(1)}, u32[]{:S(2)}, u32[]{:S(2)}) %collective-permute-start.19) | collective-permute-done | bytes 589856 | tf_op jit(solution)/shard_map/ppermute | solution.py:69
  294.7 6.3 %fusion = f32[384,3072]{1,0:T(8,128)} fusion(bf16[768,3072]{1,0:T(8,128)(2,1)S(1)} %collective-permute-done.22, bf16[384,3072]{1,0:T(8,128)(2,1)S(1)} %collective-permute-done.21, bf16[384,1536]{1,0:T(8,128)(2,1)S(1)} %multiply_convert_fusion, bf16[384,1536]{1,0:T(8,128)(2,1)S(1)} %get-tuple-element.84, bf16[768,384]{1,0:T(8,128)(2,1)S(1)} %collective-permute-done.20, ...), kind=kOutput, calls=%fused_computation.30 | convolution fusion | flops 3665166336 | bytes 15335424 | tf_op jit(solution)/shard_map/dot_general | solution.py:165
  301.1 5.6 %multiply_reduce_fusion.18 = (f32[1536]{0:T(1024)S(1)}, f32[1536]{0:T(1024)S(1)}, f32[1536]{0:T(1024)S(1)}, f32[1536]{0:T(1024)S(1)}, f32[1536]{0:T(1024)S(1)}, ...) fusion(f32[384,1536]{1,0:T(8,128)} %copy-done.1, ...), kind=kLoop, calls=%fused_computation.199 | loop fusion | flops 16493568 | bytes 35475456 | tf_op jit(solution)/shard_map/reduce_sum | solution.py:135
  325.8 7.8 %fusion.20 = (f32[1536]{0:T(1024)S(1)}, f32[384]{0:T(512)}, f32[384]{0:T(512)}, f32[1536]{0:T(1024)S(1)}, f32[384,1536]{1,0:T(8,128)S(1)}) fusion(bf16[384,1536]{1,0:T(8,128)(2,1)S(1)} %copy-done.3, f32[384]{0:T(512)S(1)} %add_rsqrt_fusion, f32[384]{0:T(512)S(1)} %broadcast_multiply_fusion.2, f32[1536]{0:T(1024)S(1)} %copy-done.16, ...), kind=kOutput, calls=%fused_computation.54 | convolution fusion | flops 3634491392 | bytes 15360000 | tf_op jit(solution)/shard_map/dot_general | solution.py:145
  334.7 7.3 %concatenate.44 = f32[34,1536]{1,0:T(8,128)} concatenate(f32[1,1536]{1,0:T(1,128)} %stack.96, f32[1,1536]{1,0:T(1,128)} %stack.97, f32[1,1536]{1,0:T(1,128)} %stack.98, f32[1,1536]{1,0:T(1,128)} %stack.99, f32[1,1536]{1,0:T(1,128)} %stack.100, f32[1,1536]{1,0:T(1,128)} %stack.101, f32[1,1536]{1,0:T(1,128)} %stack.102, f32[1,1536]{1,0:T(1,128)} %stack.103, f32[1,1536]{1,0:T(1,128)} %stack.104, ...), dimensions={0} | concatenate | bytes 417792 | tf_op jit(solution)/shard_map/concatenate | solution.py:21
  346.6 6.3 %collective-permute-done.24 = f32[34,1536]{1,0:T(8,128)S(1)} collective-permute-done((f32[34,1536]{1,0:T(8,128)S(1)}, f32[34,1536]{1,0:T(8,128)S(1)}, u32[]{:S(2)}, u32[]{:S(2)}) %collective-permute-start.24) | collective-permute-done | bytes 208928 | tf_op jit(solution)/shard_map/ppermute | solution.py:25
  352.9 2.7 collective-permute-start.25
  355.6 5.5 %collective-permute-done.25 = f32[34,1536]{1,0:T(8,128)S(1)} collective-permute-done((f32[34,1536]{1,0:T(8,128)S(1)}, f32[34,1536]{1,0:T(8,128)S(1)}, u32[]{:S(2)}, u32[]{:S(2)}) %collective-permute-start.25) | collective-permute-done | bytes 208928 | tf_op jit(solution)/shard_map/ppermute | solution.py:25
  361.1 3.1 collective-permute-start.26
  364.9 3.9 collective-permute-done.26
  368.8 2.7 collective-permute-start.27
  373.3 19.1 %collective-permute-done.27 = f32[34,1536]{1,0:T(8,128)S(1)} collective-permute-done((f32[34,1536]{1,0:T(8,128)S(1)}, f32[34,1536]{1,0:T(8,128)S(1)}, u32[]{:S(2)}, u32[]{:S(2)}) %collective-permute-start.27) | collective-permute-done | bytes 208928 | tf_op jit(solution)/shard_map/ppermute | solution.py:25
  393.7 85.6 %all-reduce.2.cloned.1.call-done = f32[384,3072]{1,0:T(8,128)} async-done(((f32[384,3072]{1,0:T(8,128)}), f32[384,3072]{1,0:T(8,128)}) %all-reduce.2.cloned.1.call-update) | async-done | bytes 4718608 | tf_op jit(solution)/shard_map/psum | solution.py:168
  479.3 5.1 %copy.21 = f32[384,3072]{1,0:T(8,128)} copy(f32[384,3072]{1,0:T(8,128)} %all-reduce.2.cloned.1.call-done) | data formatting | bytes 9437184
  (165 shorter events, 93.3 us)
Async XLA Ops:
  7.2 472.1 %all-reduce.2.cloned.1.call-start = ((), (), s32[]{:S(2)}) async-start(), calls=%async_computation | async-start | bytes 9437184 | tf_op jit(solution)/shard_map/psum | solution.py:168
  7.2 54.5 %collective-permute-start = (bf16[384,3072]{1,0:T(8,128)(2,1)}, bf16[384,3072]{1,0:T(8,128)(2,1)S(1)}, u32[]{:S(2)}, u32[]{:S(2)}) collective-permute-start(bf16[384,3072]{1,0:T(8,128)(2,1)} %param.11), channel_id=1, source_target_pairs={{0,2},{1,3},{2,0},{3,1},{4,6},{5,7},{6,4},{7,5},{8,10},{9,11},{10,... | collective-permute-start | bytes 7077896 | tf_op jit(solution)/shard_map/ppermute | solution.py:36
  65.9 8.3 %collective-permute-start.1 = (bf16[768,3072]{1,0:T(8,128)(2,1)}, bf16[768,3072]{1,0:T(8,128)(2,1)}, u32[]{:S(2)}, u32[]{:S(2)}) collective-permute-start(bf16[768,3072]{1,0:T(8,128)(2,1)} %pad_maximum_fusion), channel_id=1, source_target_pairs={{0,1},{1,0},{2,3},{3,2},{4,5},{5,4},{6,7},{7,6},{8,9},{9,8},{10,11... | collective-permute-start | bytes 14155784 | tf_op jit(solution)/shard_map/ppermute | solution.py:37
  84.1 3.8 collective-permute-start.2
  97.7 2.6 collective-permute-start.3
  100.3 4.2 collective-permute-start.4
  104.5 4.6 collective-permute-start.5
  109.2 4.7 collective-permute-start.6
  113.8 4.7 collective-permute-start.7
  118.9 1.2 collective-permute-start.8
  120.1 3.7 collective-permute-start.9
  123.8 3.7 collective-permute-start.10
  127.5 3.7 collective-permute-start.11
  131.2 4.6 collective-permute-start.12
  138.4 1.2 collective-permute-start.13
  139.7 3.8 collective-permute-start.14
  143.5 3.8 collective-permute-start.15
  147.2 3.8 collective-permute-start.16
  151.0 4.7 collective-permute-start.17
  164.8 3.3 collective-permute-start.18
  209.0 85.6 %copy-start.5 = (bf16[384,1536]{1,0:T(8,128)(2,1)}, bf16[384,1536]{1,0:T(8,128)(2,1)S(1)}, u32[]{:S(2)}) copy-start(bf16[384,1536]{1,0:T(8,128)(2,1)S(1)} %get-tuple-element.84) | copy-start | bytes 3538948
  213.5 81.2 %copy-start.7 = (bf16[384,1536]{1,0:T(8,128)(2,1)}, bf16[384,1536]{1,0:T(8,128)(2,1)S(1)}, u32[]{:S(2)}) copy-start(bf16[384,1536]{1,0:T(8,128)(2,1)S(1)} %multiply_convert_fusion) | copy-start | bytes 3538948
  213.8 63.1 %copy-start.13 = (bf16[384,1536]{1,0:T(8,128)(2,1)S(1)}, bf16[384,1536]{1,0:T(8,128)(2,1)}, u32[]{:S(2)}) copy-start(bf16[384,1536]{1,0:T(8,128)(2,1)} %copy-done.12) | copy-start | bytes 3538948
  213.8 52.4 %collective-permute-start.21 = (bf16[384,3072]{1,0:T(8,128)(2,1)S(1)}, bf16[384,3072]{1,0:T(8,128)(2,1)S(1)}, u32[]{:S(2)}, u32[]{:S(2)}) collective-permute-start(bf16[384,3072]{1,0:T(8,128)(2,1)S(1)} %pad_maximum_fusion.3), channel_id=1, source_target_pairs={{0,2},{1,3},{2,0},{3,1},{4,6},{5,7},{6,4},{7,5},{8,10},{9,11},{10,... | collective-permute-start | bytes 7077896 | tf_op jit(solution)/shard_map/ppermute | solution.py:36
  275.2 19.5 %collective-permute-start.22 = (bf16[768,3072]{1,0:T(8,128)(2,1)S(1)}, bf16[768,3072]{1,0:T(8,128)(2,1)S(1)}, u32[]{:S(2)}, u32[]{:S(2)}) collective-permute-start(bf16[768,3072]{1,0:T(8,128)(2,1)S(1)} %pad_maximum_fusion.1), channel_id=1, source_target_pairs={{0,1},{1,0},{2,3},{3,2},{4,5},{5,4},{6,7},{7,6},{8,9},{9,8},{10,11... | collective-permute-start | bytes 14155784 | tf_op jit(solution)/shard_map/ppermute | solution.py:37
  277.1 15.4 %collective-permute-start.19 = (bf16[768,384]{1,0:T(8,128)(2,1)S(1)}, bf16[768,384]{1,0:T(8,128)(2,1)S(1)}, u32[]{:S(2)}, u32[]{:S(2)}) collective-permute-start(bf16[768,384]{1,0:T(8,128)(2,1)S(1)} %pad_maximum_fusion.4), channel_id=1, source_target_pairs={{0,2},{1,3},{2,0},{3,1},{4,6},{5,7},{6,4},{7,5},{8,10},{9,11},{10,... | collective-permute-start | bytes 1769480 | tf_op jit(solution)/shard_map/ppermute | solution.py:69
  292.6 2.1 collective-permute-start.20
  342.1 1.7 collective-permute-start.23
  344.8 8.1 %collective-permute-start.24 = (f32[34,1536]{1,0:T(8,128)S(1)}, f32[34,1536]{1,0:T(8,128)S(1)}, u32[]{:S(2)}, u32[]{:S(2)}) collective-permute-start(f32[34,1536]{1,0:T(8,128)S(1)} %add.400), channel_id=1, source_target_pairs={{0,2},{1,3},{2,0},{3,1},{4,6},{5,7},{6,4},{7,5},{8,10},{9,11},{10,... | collective-permute-start | bytes 626696 | tf_op jit(solution)/shard_map/ppermute | solution.py:25
  352.9 8.2 %collective-permute-start.25 = (f32[34,1536]{1,0:T(8,128)S(1)}, f32[34,1536]{1,0:T(8,128)S(1)}, u32[]{:S(2)}, u32[]{:S(2)}) collective-permute-start(f32[34,1536]{1,0:T(8,128)S(1)} %add.401), channel_id=1, source_target_pairs={{0,4},{1,5},{2,6},{3,7},{4,0},{5,1},{6,2},{7,3},{8,12},{9,13},{10,... | collective-permute-start | bytes 626696 | tf_op jit(solution)/shard_map/ppermute | solution.py:25
  361.1 7.7 %collective-permute-start.26 = (f32[34,1536]{1,0:T(8,128)S(1)}, f32[34,1536]{1,0:T(8,128)S(1)}, u32[]{:S(2)}, u32[]{:S(2)}) collective-permute-start(f32[34,1536]{1,0:T(8,128)S(1)} %add.402), channel_id=1, source_target_pairs={{0,8},{1,9},{2,10},{3,11},{4,12},{5,13},{6,14},{7,15},{8,0},{9,1},... | collective-permute-start | bytes 626696 | tf_op jit(solution)/shard_map/ppermute | solution.py:25
  368.8 23.5 %collective-permute-start.27 = (f32[34,1536]{1,0:T(8,128)S(1)}, f32[34,1536]{1,0:T(8,128)S(1)}, u32[]{:S(2)}, u32[]{:S(2)}) collective-permute-start(f32[34,1536]{1,0:T(8,128)S(1)} %add.403), channel_id=1, source_target_pairs={{0,16},{1,17},{2,18},{3,19},{4,20},{5,21},{6,22},{7,23},{8,24},{9,... | collective-permute-start | bytes 626696 | tf_op jit(solution)/shard_map/ppermute | solution.py:25
  (16 other events, 311.8 us)
Sparse Core Ops, SparseCore 0:
  301.1 178.1 all-reduce.1

commit v4 on v3

--- a/solution.py
+++ b/solution.py
@@ -165,7 +165,10 @@
     row_share = lax.dot_general(
         group_rows, group_grad, (((0,), (0,)), ((), ())), preferred_element_type=jnp.float32
     )
-    grad_w_in = lax.psum(row_share, "seq")
+    reduced = lax.psum_scatter(row_share, "seq", scatter_dimension=0, tiled=True)
+    grad_w_in = lax.all_gather(
+        reduced.astype(jnp.bfloat16), "seq", axis=0, tiled=True
+    ).astype(jnp.float32)
     return (
         output,
         input_gradient.astype(jnp.bfloat16),

time: 492 us -> 493 us (level)
  other arithmetic: 90.3 us -> 98.6 us
  local copies, waits for them, and re-layouts: 47.2 us -> 42.2 us
    reduce_scatter x0 -> x1, waiting for transfers between devices: none -> 97.5 us  [on_device(): lax.psum_scatter(row_share, 'seq', scatter_dimension=0, tiled=True)]
    psum x1 -> x0, waiting for transfers between devices: 85.6 us -> none  [on_device(): grad_w_in = lax.psum(row_share, 'seq')]
    ppermute x20, waiting for transfers between devices: 65.5 us -> 54.8 us  [tree_sum(): packed = packed + lax.ppermute(packed, axis, route)]
    convert_element_type x0 -> x2, other arithmetic: none -> 6.22 us  [the longest x1 4.42 us: on_device(): grad_w_in = lax.all_gather(reduced.astype(jnp.bfloat16), 'seq', axis=0, t...]
    unnamed x39 -> x38, local copies, waits for them, and re-layouts: 8.96 us -> 4.02 us
  transfers between devices with their start and end apart: 29 -> 30, of which waited for: 27 -> 27; matrix products, arithmetic and copies ran while one was open for 11% -> 11% of each run, Pallas kernels for 0% -> 0%
where the time goes in v4:
time: 493 us; the launch traced here: 492 us
  waiting for transfers between devices  274 us (56%)
  other arithmetic  98.6 us (20%)
  starting transfers between devices  45.1 us (9%)
  local copies, waits for them, and re-layouts  42.2 us (9%)
  matrix products  17.8 us (4%)
  between operations  14.6 us (3%)
    ppermute x2, waiting for transfers between devices, group_shards(): far = lax.ppermute(block, axis, [(i, i ^ 2) for i in range(4)])  102 us
    reduce_scatter x1, waiting for transfers between devices, on_device(): lax.psum_scatter(row_share, 'seq', scatter_dimension=0, tiled=True)  97.5 us
    ppermute x20, waiting for transfers between devices, tree_sum(): packed = packed + lax.ppermute(packed, axis, route)  54.8 us
    another operation x2, other arithmetic  47.3 us
    ppermute x20, starting transfers between devices, tree_sum(): packed = packed + lax.ppermute(packed, axis, route)  32.8 us
    another operation x32, local copies, waits for them, and re-layouts, on_device(): kernel_portion = jnp.stack(kernel_rows, axis=0)  19.1 us
    ppermute x1, waiting for transfers between devices, gather_own_columns(): lax.ppermute(jnp.concatenate([cols(me ^ 2), cols(me ^ 3)], axis=0), axis,...  13.5 us
    concatenate x2, other arithmetic, group_shards(): jnp.concatenate([block, far], axis=0)  13.2 us
  transfers between devices with their start and end apart: 30, of which 27 were waited for; matrix products, arithmetic and copies ran while one was open for 11% of the time, Pallas kernels for 0%

profile of v4, /device:TPU:0, one launch (start us, length us, event | category | flops | bytes accessed | tf_op | source)
XLA Modules:
  0.0 492.5 jit_solution(5998431982452889752)
XLA Ops:
  7.2 3.0 collective-permute-start
  10.2 51.5 %collective-permute-done = bf16[384,3072]{1,0:T(8,128)(2,1)S(1)} collective-permute-done((bf16[384,3072]{1,0:T(8,128)(2,1)}, bf16[384,3072]{1,0:T(8,128)(2,1)S(1)}, u32[]{:S(2)}, u32[]{:S(2)}) %collective-permute-start) | collective-permute-done | bytes 2359328 | tf_op jit(solution)/shard_map/ppermute | solution.py:36
  61.7 4.2 pad_maximum_fusion
  71.6 2.5 collective-permute-done.1
  78.0 3.8 fusion.129
  88.2 9.4 %fusion.127 = (f32[1536]{0:T(1024)S(1)}, f32[384,1536]{1,0:T(8,128)S(1)}) fusion(f32[415,1536]{1,0:T(8,128)S(1)} %maximum_convert_fusion, f32[1536]{0:T(1024)S(1)} %get-tuple-element.78, f32[1536]{0:T(1024)S(1)} %get-tuple-element.79, f32[1536]{0:T(1024)S(1)} %get-tuple-element.49, f32[1536]{0:T(1024)S(1)} %get-tuple-element.50, ...), kind=kLoop, calls=%fused_computation.288 | loop fusion | flops 37747200 | bytes 78059520 | tf_op jit(solution)/shard_map/reduce_sum | solution.py:113
  100.3 2.6 collective-permute-start.4
  104.5 3.0 collective-permute-start.5
  109.2 3.0 collective-permute-start.6
  113.8 3.1 collective-permute-start.7
  120.2 3.6 collective-permute-done.9
  124.8 2.7 collective-permute-done.10
  131.2 3.0 collective-permute-start.12
  139.8 3.7 collective-permute-done.14
  144.5 2.7 collective-permute-done.15
  151.0 3.0 collective-permute-start.17
  156.3 7.1 %multiply_reduce_fusion = (f32[1536]{0:T(1024)S(1)}, f32[1536]{0:T(1024)S(1)}, f32[1536]{0:T(1024)S(1)}, f32[1536]{0:T(1024)S(1)}, f32[1536]{0:T(1024)S(1)}, /*i...) fusion(f32[415,1536]{1,0:T(8,128)S(1)} %maximum_convert_fusion,, ...), kind=kLoop, calls=%fused_computation.181 | loop fusion | flops 31822848 | bytes 48519168 | tf_op jit(solution)/shard_map/reduce_sum | solution.py:135
  168.3 42.9 %multiply_convert_fusion.1 = (bf16[384,1536]{1,0:T(8,128)(2,1)S(1)}, f32[384,1536]{1,0:T(8,128)}) fusion(f32[384,3072]{1,0:T(8,128)} %copy-done, f32[31,1536]{1,0:T(8,128)S(1)} %collective-permute-done.18, f32[384,1536]{1,0:T(8,128)} %copy-done.1, f32[1536]{0:T(1024)S(1)} %get-tuple-element.78, f32[1536]{0:T(1024)S(1)} %get-tuple-element.79, ...), kind=kLoop, calls=%fused_computation.214 | loop fusion | flops 58392576 | bytes 8644608 | tf_op jit(solution)/shard_map/convert
  211.2 4.4 multiply_convert_fusion
  217.8 50.5 %collective-permute-done.21 = bf16[384,3072]{1,0:T(8,128)(2,1)S(1)} collective-permute-done((bf16[384,3072]{1,0:T(8,128)(2,1)S(1)}, bf16[384,3072]{1,0:T(8,128)(2,1)S(1)}, u32[]{:S(2)}, u32[]{:S(2)}) %collective-permute-start.21) | collective-permute-done | bytes 2359328 | tf_op jit(solution)/shard_map/ppermute | solution.py:36
  268.3 9.0 %pad_maximum_fusion.1 = bf16[768,3072]{1,0:T(8,128)(2,1)S(1)} fusion(bf16[384,3072]{1,0:T(8,128)(2,1)S(1)} %collective-permute-done.21, bf16[384,1536]{1,0:T(8,128)(2,1)S(1)} %multiply_convert_fusion, bf16[384,1536]{1,0:T(8,128)(2,1)S(1)} %get-tuple-element.84), kind=kLoop, calls=%fused_computation.39 | loop fusion | flops 14155776 | bytes 9437184 | tf_op jit(solution)/shard_map/concatenate | solution.py:38
  281.1 13.5 %collective-permute-done.19 = bf16[768,384]{1,0:T(8,128)(2,1)S(1)} collective-permute-done((bf16[768,384]{1,0:T(8,128)(2,1)S(1)}, bf16[768,384]{1,0:T(8,128)(2,1)S(1)}, u32[]{:S(2)}, u32[]{:S(2)}) %collective-permute-start.19) | collective-permute-done | bytes 589856 | tf_op jit(solution)/shard_map/ppermute | solution.py:69
  296.9 6.3 %fusion = f32[384,3072]{1,0:T(8,128)} fusion(bf16[768,3072]{1,0:T(8,128)(2,1)S(1)} %collective-permute-done.22, bf16[384,3072]{1,0:T(8,128)(2,1)S(1)} %collective-permute-done.21, bf16[384,1536]{1,0:T(8,128)(2,1)S(1)} %multiply_convert_fusion, bf16[384,1536]{1,0:T(8,128)(2,1)S(1)} %get-tuple-element.84, bf16[768,384]{1,0:T(8,128)(2,1)S(1)} %collective-permute-done.20, ...), kind=kOutput, calls=%fused_computation.30 | convolution fusion | flops 3665166336 | bytes 15335424 | tf_op jit(solution)/shard_map/dot_general | solution.py:165
  303.2 97.5 %reduce-scatter.2.cloned.1.call-done = f32[48,3072]{1,0:T(8,128)} async-done(((f32[384,3072]{1,0:T(8,128)}), f32[48,3072]{1,0:T(8,128)}) %reduce-scatter.2.cloned.1.call-update) | async-done | bytes 589840 | tf_op jit(solution)/shard_map/reduce_scatter | solution.py:168
  402.6 5.6 %multiply_reduce_fusion.18 = (f32[1536]{0:T(1024)S(1)}, f32[1536]{0:T(1024)S(1)}, f32[1536]{0:T(1024)S(1)}, f32[1536]{0:T(1024)S(1)}, f32[1536]{0:T(1024)S(1)}, ...) fusion(f32[384,1536]{1,0:T(8,128)} %copy-done.1, ...), kind=kLoop, calls=%fused_computation.199 | loop fusion | flops 16493568 | bytes 35475456 | tf_op jit(solution)/shard_map/reduce_sum | solution.py:135
  427.4 7.7 %fusion.20 = (f32[1536]{0:T(1024)S(1)}, f32[384]{0:T(512)}, f32[384]{0:T(512)}, f32[1536]{0:T(1024)S(1)}, f32[384,1536]{1,0:T(8,128)S(1)}) fusion(bf16[384,1536]{1,0:T(8,128)(2,1)S(1)} %copy-done.3, f32[384]{0:T(512)S(1)} %add_rsqrt_fusion, f32[384]{0:T(512)S(1)} %broadcast_multiply_fusion.2, f32[1536]{0:T(1024)S(1)} %copy-done.16, ...), kind=kOutput, calls=%fused_computation.54 | convolution fusion | flops 3634491392 | bytes 15360000 | tf_op jit(solution)/shard_map/dot_general | solution.py:145
  436.2 7.3 %concatenate.44 = f32[34,1536]{1,0:T(8,128)} concatenate(f32[1,1536]{1,0:T(1,128)} %stack.96, f32[1,1536]{1,0:T(1,128)} %stack.97, f32[1,1536]{1,0:T(1,128)} %stack.98, f32[1,1536]{1,0:T(1,128)} %stack.99, f32[1,1536]{1,0:T(1,128)} %stack.100, f32[1,1536]{1,0:T(1,128)} %stack.101, f32[1,1536]{1,0:T(1,128)} %stack.102, f32[1,1536]{1,0:T(1,128)} %stack.103, f32[1,1536]{1,0:T(1,128)} %stack.104, ...), dimensions={0} | concatenate | bytes 417792 | tf_op jit(solution)/shard_map/concatenate | solution.py:21
  447.8 6.5 %collective-permute-done.24 = f32[34,1536]{1,0:T(8,128)S(1)} collective-permute-done((f32[34,1536]{1,0:T(8,128)S(1)}, f32[34,1536]{1,0:T(8,128)S(1)}, u32[]{:S(2)}, u32[]{:S(2)}) %collective-permute-start.24) | collective-permute-done | bytes 208928 | tf_op jit(solution)/shard_map/ppermute | solution.py:25
  455.9 5.8 %collective-permute-done.25 = f32[34,1536]{1,0:T(8,128)S(1)} collective-permute-done((f32[34,1536]{1,0:T(8,128)S(1)}, f32[34,1536]{1,0:T(8,128)S(1)}, u32[]{:S(2)}, u32[]{:S(2)}) %collective-permute-start.25) | collective-permute-done | bytes 208928 | tf_op jit(solution)/shard_map/ppermute | solution.py:25
  464.1 4.1 collective-permute-done.26
  472.2 7.6 %collective-permute-done.27 = f32[34,1536]{1,0:T(8,128)S(1)} collective-permute-done((f32[34,1536]{1,0:T(8,128)S(1)}, f32[34,1536]{1,0:T(8,128)S(1)}, u32[]{:S(2)}, u32[]{:S(2)}) %collective-permute-start.27) | collective-permute-done | bytes 208928 | tf_op jit(solution)/shard_map/ppermute | solution.py:25
  481.2 4.4 convert_element_type.36
  (169 shorter events, 92.7 us)
Async XLA Ops:
  7.2 393.6 %reduce-scatter.2.cloned.1.call-start = ((), (), s32[]{:S(2)}) async-start(), calls=%async_computation.1 | async-start | bytes 5308416 | tf_op jit(solution)/shard_map/reduce_scatter | solution.py:168
  7.2 54.5 %collective-permute-start = (bf16[384,3072]{1,0:T(8,128)(2,1)}, bf16[384,3072]{1,0:T(8,128)(2,1)S(1)}, u32[]{:S(2)}, u32[]{:S(2)}) collective-permute-start(bf16[384,3072]{1,0:T(8,128)(2,1)} %param.11), channel_id=1, source_target_pairs={{0,2},{1,3},{2,0},{3,1},{4,6},{5,7},{6,4},{7,5},{8,10},{9,11},{10,... | collective-permute-start | bytes 7077896 | tf_op jit(solution)/shard_map/ppermute | solution.py:36
  65.9 8.3 %collective-permute-start.1 = (bf16[768,3072]{1,0:T(8,128)(2,1)}, bf16[768,3072]{1,0:T(8,128)(2,1)}, u32[]{:S(2)}, u32[]{:S(2)}) collective-permute-start(bf16[768,3072]{1,0:T(8,128)(2,1)} %pad_maximum_fusion), channel_id=1, source_target_pairs={{0,1},{1,0},{2,3},{3,2},{4,5},{5,4},{6,7},{7,6},{8,9},{9,8},{10,11... | collective-permute-start | bytes 14155784 | tf_op jit(solution)/shard_map/ppermute | solution.py:37
  84.1 3.8 collective-permute-start.2
  97.7 2.6 collective-permute-start.3
  100.3 4.2 collective-permute-start.4
  104.5 4.6 collective-permute-start.5
  109.2 4.7 collective-permute-start.6
  113.8 4.7 collective-permute-start.7
  118.9 1.2 collective-permute-start.8
  120.1 3.7 collective-permute-start.9
  123.8 3.7 collective-permute-start.10
  127.5 3.7 collective-permute-start.11
  131.2 4.6 collective-permute-start.12
  138.4 1.2 collective-permute-start.13
  139.7 3.8 collective-permute-start.14
  143.5 3.8 collective-permute-start.15
  147.2 3.8 collective-permute-start.16
  151.0 4.7 collective-permute-start.17
  165.0 3.3 collective-permute-start.18
  211.2 85.6 %copy-start.5 = (bf16[384,1536]{1,0:T(8,128)(2,1)}, bf16[384,1536]{1,0:T(8,128)(2,1)S(1)}, u32[]{:S(2)}) copy-start(bf16[384,1536]{1,0:T(8,128)(2,1)S(1)} %get-tuple-element.84) | copy-start | bytes 3538948
  215.6 81.2 %copy-start.7 = (bf16[384,1536]{1,0:T(8,128)(2,1)}, bf16[384,1536]{1,0:T(8,128)(2,1)S(1)}, u32[]{:S(2)}) copy-start(bf16[384,1536]{1,0:T(8,128)(2,1)S(1)} %multiply_convert_fusion) | copy-start | bytes 3538948
  215.9 52.4 %collective-permute-start.21 = (bf16[384,3072]{1,0:T(8,128)(2,1)S(1)}, bf16[384,3072]{1,0:T(8,128)(2,1)S(1)}, u32[]{:S(2)}, u32[]{:S(2)}) collective-permute-start(bf16[384,3072]{1,0:T(8,128)(2,1)S(1)} %pad_maximum_fusion.3), channel_id=1, source_target_pairs={{0,2},{1,3},{2,0},{3,1},{4,6},{5,7},{6,4},{7,5},{8,10},{9,11},{10,... | collective-permute-start | bytes 7077896 | tf_op jit(solution)/shard_map/ppermute | solution.py:36
  277.4 19.5 %collective-permute-start.22 = (bf16[768,3072]{1,0:T(8,128)(2,1)S(1)}, bf16[768,3072]{1,0:T(8,128)(2,1)S(1)}, u32[]{:S(2)}, u32[]{:S(2)}) collective-permute-start(bf16[768,3072]{1,0:T(8,128)(2,1)S(1)} %pad_maximum_fusion.1), channel_id=1, source_target_pairs={{0,1},{1,0},{2,3},{3,2},{4,5},{5,4},{6,7},{7,6},{8,9},{9,8},{10,11... | collective-permute-start | bytes 14155784 | tf_op jit(solution)/shard_map/ppermute | solution.py:37
  279.3 15.4 %collective-permute-start.19 = (bf16[768,384]{1,0:T(8,128)(2,1)S(1)}, bf16[768,384]{1,0:T(8,128)(2,1)S(1)}, u32[]{:S(2)}, u32[]{:S(2)}) collective-permute-start(bf16[768,384]{1,0:T(8,128)(2,1)S(1)} %pad_maximum_fusion.4), channel_id=1, source_target_pairs={{0,2},{1,3},{2,0},{3,1},{4,6},{5,7},{6,4},{7,5},{8,10},{9,11},{10,... | collective-permute-start | bytes 1769480 | tf_op jit(solution)/shard_map/ppermute | solution.py:69
  294.8 2.1 collective-permute-start.20
  303.2 178.0 %all-gather.2.cloned.1.call-start = ((), (), s32[]{:S(2)}) async-start(), calls=%async_computation.2 | async-start | bytes 2654208 | tf_op jit(solution)/shard_map/all_gather | solution.py:169
  443.6 1.7 collective-permute-start.23
  446.3 8.1 %collective-permute-start.24 = (f32[34,1536]{1,0:T(8,128)S(1)}, f32[34,1536]{1,0:T(8,128)S(1)}, u32[]{:S(2)}, u32[]{:S(2)}) collective-permute-start(f32[34,1536]{1,0:T(8,128)S(1)} %add.400), channel_id=1, source_target_pairs={{0,2},{1,3},{2,0},{3,1},{4,6},{5,7},{6,4},{7,5},{8,10},{9,11},{10,... | collective-permute-start | bytes 626696 | tf_op jit(solution)/shard_map/ppermute | solution.py:25
  454.4 7.3 %collective-permute-start.25 = (f32[34,1536]{1,0:T(8,128)S(1)}, f32[34,1536]{1,0:T(8,128)S(1)}, u32[]{:S(2)}, u32[]{:S(2)}) collective-permute-start(f32[34,1536]{1,0:T(8,128)S(1)} %add.401), channel_id=1, source_target_pairs={{0,4},{1,5},{2,6},{3,7},{4,0},{5,1},{6,2},{7,3},{8,12},{9,13},{10,... | collective-permute-start | bytes 626696 | tf_op jit(solution)/shard_map/ppermute | solution.py:25
  461.7 6.4 %collective-permute-start.26 = (f32[34,1536]{1,0:T(8,128)S(1)}, f32[34,1536]{1,0:T(8,128)S(1)}, u32[]{:S(2)}, u32[]{:S(2)}) collective-permute-start(f32[34,1536]{1,0:T(8,128)S(1)} %add.402), channel_id=1, source_target_pairs={{0,8},{1,9},{2,10},{3,11},{4,12},{5,13},{6,14},{7,15},{8,0},{9,1},... | collective-permute-start | bytes 626696 | tf_op jit(solution)/shard_map/ppermute | solution.py:25
  468.2 11.7 %collective-permute-start.27 = (f32[34,1536]{1,0:T(8,128)S(1)}, f32[34,1536]{1,0:T(8,128)S(1)}, u32[]{:S(2)}, u32[]{:S(2)}) collective-permute-start(f32[34,1536]{1,0:T(8,128)S(1)} %add.403), channel_id=1, source_target_pairs={{0,16},{1,17},{2,18},{3,19},{4,20},{5,21},{6,22},{7,23},{8,24},{9,... | collective-permute-start | bytes 626696 | tf_op jit(solution)/shard_map/ppermute | solution.py:25
  (17 other events, 372.3 us)
Sparse Core Ops, SparseCore 0:
  303.3 97.4 reduce-scatter.1
  403.5 51.8 all-gather.1

commit v5 on v3

--- a/solution.py
+++ b/solution.py
@@ -145,27 +145,46 @@
     normalized_gradient = lax.dot_general(
         grad_hidden, full_weight, (((1,), (1,)), ((), ())), preferred_element_type=jnp.float32
     )
-    grad_kernel, layer_norm_gain_gradient, grad_ln_bias = tree_sum(
-        (
-            kernel_portion,
-            jnp.sum(normalized_gradient * standardized_input, axis=0),
-            jnp.sum(normalized_gradient, axis=0),
-        ),
-        ("seq", "fsdp"),
-    )
     rescaled_rows = normalized_gradient * layer_norm_gain
     input_gradient = row_inverse_deviation * (
         rescaled_rows
         - jnp.mean(rescaled_rows, axis=-1, keepdims=True)
         - standardized_input * jnp.mean(rescaled_rows * standardized_input, axis=-1, keepdims=True)
     )
+    local_sums = (
+        kernel_portion,
+        jnp.sum(normalized_gradient * standardized_input, axis=0),
+        jnp.sum(normalized_gradient, axis=0),
+    )
     feature_rows = w_in.shape[0]
     group_rows = gather_own_columns(normalized_rows, "fsdp", feature_rows)
-    group_grad = gather_frames(grad_hidden, "fsdp")
-    row_share = lax.dot_general(
-        group_rows, group_grad, (((0,), (0,)), ((), ())), preferred_element_type=jnp.float32
-    )
-    grad_w_in = lax.psum(row_share, "seq")
+    halves = [grad_hidden[:, :features], grad_hidden[:, features:]]
+    grad_w_parts = []
+    if lax.axis_size("fsdp") == 4:
+        cross = [(i, i ^ 2) for i in range(4)]
+        on_chip = [(i, i ^ 1) for i in range(4)]
+        first_far = lax.ppermute(halves[0], "fsdp", cross)
+        first_far, input_gradient, local_sums = lax.optimization_barrier(
+            (first_far, input_gradient, local_sums)
+        )
+        second_half, first_far = lax.optimization_barrier((halves[1], first_far))
+        second_far = lax.ppermute(second_half, "fsdp", cross)
+        group_grads = []
+        for half, far in ((halves[0], first_far), (second_half, second_far)):
+            near = lax.ppermute(jnp.concatenate([half, far], axis=0), "fsdp", on_chip)
+            group_grads.append(jnp.concatenate([half, far, near], axis=0))
+    else:
+        group_grads = [lax.all_gather(h, "fsdp", axis=0, tiled=True) for h in halves]
+    for group_grad in group_grads:
+        row_share = lax.dot_general(
+            group_rows, group_grad, (((0,), (0,)), ((), ())), preferred_element_type=jnp.float32
+        )
+        reduced = lax.psum_scatter(row_share, "seq", scatter_dimension=0, tiled=True)
+        grad_w_parts.append(
+            lax.all_gather(reduced.astype(jnp.bfloat16), "seq", axis=0, tiled=True)
+        )
+    grad_w_in = jnp.concatenate(grad_w_parts, axis=1).astype(jnp.float32)
+    grad_kernel, layer_norm_gain_gradient, grad_ln_bias = tree_sum(local_sums, ("seq", "fsdp"))
     return (
         output,
         input_gradient.astype(jnp.bfloat16),

time: 492 us -> 512 us (1.041)
  waiting for transfers between devices: 273 us -> 339 us
  local copies, waits for them, and re-layouts: 47.2 us -> 13.7 us
  starting transfers between devices: 48.4 us -> 41.4 us
    reduce_scatter x0 -> x2, waiting for transfers between devices: none -> 103 us  [on_device(): lax.psum_scatter(row_share, 'seq', scatter_dimension=0, tiled=True)]
    psum x1 -> x0, waiting for transfers between devices: 85.6 us -> none  [on_device(): grad_w_in = lax.psum(row_share, 'seq')]
    ppermute x0 -> x4, waiting for transfers between devices: none -> 51.3 us  [the longest x1 27.6 us: on_device(): second_far = lax.ppermute(second_half, 'fsdp', cross)]
    ppermute x2 -> x1, waiting for transfers between devices: 102 us -> 51.5 us  [group_shards(): far = lax.ppermute(block, axis, [(i, i ^ 2) for i in range(4)])]
    another operation x2 -> x0, other arithmetic: 45.3 us -> none
    slice x0 -> x2, other arithmetic: none -> 43.6 us  [on_device(): halves = [grad_hidden[:, :features], grad_hidden[:, features:]]]
    all_gather x0 -> x2, waiting for transfers between devices: none -> 41.6 us  [on_device(): lax.all_gather(reduced.astype(jnp.bfloat16), 'seq', axis=0, tiled=True)]
    another operation x32 -> x33, local copies, waits for them, and re-layouts: 19.1 us -> 0.53 us  [on_device(): kernel_portion = jnp.stack(kernel_rows, axis=0)]
  transfers between devices with their start and end apart: 29 -> 34, of which waited for: 27 -> 31; matrix products, arithmetic and copies ran while one was open for 11% -> 5% of each run, Pallas kernels for 0% -> 0%
where the time goes in v5:
time: 512 us; the launch traced here: 511 us
  waiting for transfers between devices  339 us (66%)
  other arithmetic  85.3 us (17%)
  starting transfers between devices  41.4 us (8%)
  matrix products  17.8 us (3%)
  between operations  14.6 us (3%)
  local copies, waits for them, and re-layouts  13.7 us (3%)
    reduce_scatter x2, waiting for transfers between devices, on_device(): lax.psum_scatter(row_share, 'seq', scatter_dimension=0, tiled=True)  103 us
    ppermute x20, waiting for transfers between devices, tree_sum(): packed = packed + lax.ppermute(packed, axis, route)  70.8 us
    ppermute x1, waiting for transfers between devices, group_shards(): far = lax.ppermute(block, axis, [(i, i ^ 2) for i in range(4)])  51.5 us
    slice x2, other arithmetic, on_device(): halves = [grad_hidden[:, :features], grad_hidden[:, features:]]  43.6 us
    all_gather x2, waiting for transfers between devices, on_device(): lax.all_gather(reduced.astype(jnp.bfloat16), 'seq', axis=0, tiled=True)  41.6 us
    ppermute x20, starting transfers between devices, tree_sum(): packed = packed + lax.ppermute(packed, axis, route)  32.4 us
    ppermute x1, waiting for transfers between devices, on_device(): second_far = lax.ppermute(second_half, 'fsdp', cross)  27.6 us
    ppermute x1, waiting for transfers between devices, on_device(): first_far = lax.ppermute(halves[0], 'fsdp', cross)  19.1 us
  transfers between devices with their start and end apart: 34, of which 31 were waited for; matrix products, arithmetic and copies ran while one was open for 5% of the time, Pallas kernels for 0%

profile of v5, /device:TPU:0, one launch (start us, length us, event | category | flops | bytes accessed | tf_op | source)
XLA Modules:
  0.0 511.4 jit_solution(2086483940265013376)
XLA Ops:
  7.2 3.0 collective-permute-start
  10.2 51.5 %collective-permute-done = bf16[384,3072]{1,0:T(8,128)(2,1)S(1)} collective-permute-done((bf16[384,3072]{1,0:T(8,128)(2,1)}, bf16[384,3072]{1,0:T(8,128)(2,1)S(1)}, u32[]{:S(2)}, u32[]{:S(2)}) %collective-permute-start) | collective-permute-done | bytes 2359328 | tf_op jit(solution)/shard_map/ppermute | solution.py:36
  61.7 5.0 pad_maximum_fusion
  72.1 2.9 collective-permute-done.1
  78.9 3.8 fusion.133
  88.3 9.4 %fusion.131 = (f32[1536]{0:T(1024)S(1)}, f32[384,1536]{1,0:T(8,128)S(1)}) fusion(f32[415,1536]{1,0:T(8,128)S(1)} %maximum_convert_fusion.1, f32[1536]{0:T(1024)S(1)} %get-tuple-element.92, f32[1536]{0:T(1024)S(1)} %get-tuple-element.93, f32[1536]{0:T(1024)S(1)} %get-tuple-element.63, f32[1536]{0:T(1024)S(1)} %get-tuple-element.64, ...), kind=kLoop, calls=%fused_computation.295 | loop fusion | flops 37747200 | bytes 78059520 | tf_op jit(solution)/shard_map/reduce_sum | solution.py:113
  105.4 3.0 collective-permute-start.5
  110.0 3.0 collective-permute-start.6
  114.7 3.1 collective-permute-start.7
  121.1 3.6 collective-permute-done.9
  132.1 3.0 collective-permute-start.12
  140.6 3.7 collective-permute-done.14
  151.9 3.0 collective-permute-start.17
  157.2 7.1 %multiply_reduce_fusion = (f32[1536]{0:T(1024)S(1)}, f32[1536]{0:T(1024)S(1)}, f32[1536]{0:T(1024)S(1)}, f32[1536]{0:T(1024)S(1)}, f32[1536]{0:T(1024)S(1)}, /*i...) fusion(f32[415,1536]{1,0:T(8,128)S(1)} %maximum_convert_fusion., ...), kind=kLoop, calls=%fused_computation.189 | loop fusion | flops 31822848 | bytes 48519168 | tf_op jit(solution)/shard_map/reduce_sum | solution.py:135
  165.9 4.3 multiply_reduce_fusion.18
  171.0 40.5 %multiply_convert_fusion = (bf16[384,1536]{1,0:T(8,128)(2,1)S(1)}, f32[384,1536]{1,0:T(8,128)}) fusion(f32[384,3072]{1,0:T(8,128)} %copy-done, f32[31,1536]{1,0:T(8,128)S(1)} %collective-permute-done.18, f32[384,1536]{1,0:T(8,128)} %copy-done.1, f32[1536]{0:T(1024)S(1)} %get-tuple-element.92, f32[1536]{0:T(1024)S(1)} %get-tuple-element.93, ...), kind=kLoop, calls=%fused_computation.221 | loop fusion | flops 60162048 | bytes 11003904 | tf_op jit(solution)/shard_map/slice | solution.py:161
  211.5 3.1 multiply_convert_fusion.1
  215.3 7.1 %fusion.23 = (f32[1536]{0:T(1024)S(1)}, f32[384]{0:T(512)S(1)}, f32[384]{0:T(512)S(1)}, f32[1536]{0:T(1024)S(1)}, f32[384,1536]{1,0:T(8,128)S(1)}) fusion(bf16[384,1536]{1,0:T(8,128)(2,1)S(1)} %copy-done.3, f32[384]{0:T(512)S(1)} %add_rsqrt_fusion, f32[384]{0:T(512)S(1)} %broadcast_multiply_fusion.2, f32[1536]{0:T(1024)S(1)} %copy-done.14, ...), kind=kOutput, calls=%fused_computation.56 | convolution fusion | flops 3634491392 | bytes 15360000 | tf_op jit(solution)/shard_map/dot_general | solution.py:145
  224.2 19.1 %collective-permute-done.19 = bf16[384,1536]{1,0:T(8,128)(2,1)S(1)} collective-permute-done((bf16[384,1536]{1,0:T(8,128)(2,1)S(1)}, bf16[384,1536]{1,0:T(8,128)(2,1)S(1)}, u32[]{:S(2)}, u32[]{:S(2)}) %collective-permute-start.19) | collective-permute-done | bytes 1179680 | tf_op jit(solution)/shard_map/ppermute | solution.py:166
  245.5 14.7 %collective-permute-done.20 = bf16[768,384]{1,0:T(8,128)(2,1)S(1)} collective-permute-done((bf16[768,384]{1,0:T(8,128)(2,1)S(1)}, bf16[768,384]{1,0:T(8,128)(2,1)S(1)}, u32[]{:S(2)}, u32[]{:S(2)}) %collective-permute-start.20) | collective-permute-done | bytes 589856 | tf_op jit(solution)/shard_map/ppermute | solution.py:69
  263.3 3.5 fusion
  267.2 27.6 %collective-permute-done.23 = bf16[384,1536]{1,0:T(8,128)(2,1)S(1)} collective-permute-done((bf16[384,1536]{1,0:T(8,128)(2,1)S(1)}, bf16[384,1536]{1,0:T(8,128)(2,1)S(1)}, u32[]{:S(2)}, u32[]{:S(2)}) %collective-permute-start.23) | collective-permute-done | bytes 1179680 | tf_op jit(solution)/shard_map/ppermute | solution.py:171
  295.1 4.5 collective-permute-done.24
  299.6 3.4 fusion.6
  303.1 32.9 %reduce-scatter.3.cloned.1.call-done = f32[48,1536]{1,0:T(8,128)} async-done(((f32[384,1536]{1,0:T(8,128)}), f32[48,1536]{1,0:T(8,128)}) %reduce-scatter.3.cloned.1.call-update) | async-done | bytes 294928 | tf_op jit(solution)/shard_map/reduce_scatter | solution.py:182
  337.7 70.4 %reduce-scatter.5.cloned.1.call-done = f32[48,1536]{1,0:T(8,128)} async-done(((f32[384,1536]{1,0:T(8,128)}), f32[48,1536]{1,0:T(8,128)}) %reduce-scatter.5.cloned.1.call-update) | async-done | bytes 294928 | tf_op jit(solution)/shard_map/reduce_scatter | solution.py:182
  413.0 6.5 %collective-permute-done.26 = f32[34,1536]{1,0:T(8,128)S(1)} collective-permute-done((f32[34,1536]{1,0:T(8,128)S(1)}, f32[34,1536]{1,0:T(8,128)S(1)}, u32[]{:S(2)}, u32[]{:S(2)}) %collective-permute-start.26) | collective-permute-done | bytes 208928 | tf_op jit(solution)/shard_map/ppermute | solution.py:25
  420.4 6.5 %collective-permute-done.27 = f32[34,1536]{1,0:T(8,128)S(1)} collective-permute-done((f32[34,1536]{1,0:T(8,128)S(1)}, f32[34,1536]{1,0:T(8,128)S(1)}, u32[]{:S(2)}, u32[]{:S(2)}) %collective-permute-start.27) | collective-permute-done | bytes 208928 | tf_op jit(solution)/shard_map/ppermute | solution.py:25
  428.4 6.4 %collective-permute-done.28 = f32[34,1536]{1,0:T(8,128)S(1)} collective-permute-done((f32[34,1536]{1,0:T(8,128)S(1)}, f32[34,1536]{1,0:T(8,128)S(1)}, u32[]{:S(2)}, u32[]{:S(2)}) %collective-permute-start.28) | collective-permute-done | bytes 208928 | tf_op jit(solution)/shard_map/ppermute | solution.py:25
  436.7 20.9 %collective-permute-done.29 = f32[34,1536]{1,0:T(8,128)S(1)} collective-permute-done((f32[34,1536]{1,0:T(8,128)S(1)}, f32[34,1536]{1,0:T(8,128)S(1)}, u32[]{:S(2)}, u32[]{:S(2)}) %collective-permute-start.29) | collective-permute-done | bytes 208928 | tf_op jit(solution)/shard_map/ppermute | solution.py:25
  458.9 41.6 %all-gather.5.cloned.1.call-done = bf16[384,1536]{1,0:T(8,128)(2,1)} async-done(((bf16[48,1536]{1,0:T(8,128)(2,1)}), bf16[384,1536]{1,0:T(8,128)(2,1)}) %all-gather.5.cloned.1.call-update) | async-done | bytes 1179664 | tf_op jit(solution)/shard_map/all_gather | solution.py:184
  500.5 4.4 maximum_convert_fusion
  (182 shorter events, 74.3 us)
Async XLA Ops:
  7.2 328.8 %reduce-scatter.3.cloned.1.call-start = ((), (), s32[]{:S(2)}) async-start(), calls=%async_computation.2 | async-start | bytes 2654208 | tf_op jit(solution)/shard_map/reduce_scatter | solution.py:182
  7.2 54.5 %collective-permute-start = (bf16[384,3072]{1,0:T(8,128)(2,1)}, bf16[384,3072]{1,0:T(8,128)(2,1)S(1)}, u32[]{:S(2)}, u32[]{:S(2)}) collective-permute-start(bf16[384,3072]{1,0:T(8,128)(2,1)} %param.11), channel_id=1, source_target_pairs={{0,2},{1,3},{2,0},{3,1},{4,6},{5,7},{6,4},{7,5},{8,10},{9,11},{10,... | collective-permute-start | bytes 7077896 | tf_op jit(solution)/shard_map/ppermute | solution.py:36
  66.7 8.3 %collective-permute-start.1 = (bf16[768,3072]{1,0:T(8,128)(2,1)}, bf16[768,3072]{1,0:T(8,128)(2,1)}, u32[]{:S(2)}, u32[]{:S(2)}) collective-permute-start(bf16[768,3072]{1,0:T(8,128)(2,1)} %pad_maximum_fusion), channel_id=1, source_target_pairs={{0,1},{1,0},{2,3},{3,2},{4,5},{5,4},{6,7},{7,6},{8,9},{9,8},{10,11... | collective-permute-start | bytes 14155784 | tf_op jit(solution)/shard_map/ppermute | solution.py:37
  85.0 3.0 collective-permute-start.2
  97.8 3.3 collective-permute-start.3
  101.1 4.3 collective-permute-start.4
  105.4 4.6 collective-permute-start.5
  110.0 4.7 collective-permute-start.6
  114.7 4.7 collective-permute-start.7
  121.0 3.7 collective-permute-start.9
  124.7 3.7 collective-permute-start.10
  128.4 3.7 collective-permute-start.11
  132.1 4.6 collective-permute-start.12
  140.5 3.8 collective-permute-start.14
  144.3 3.8 collective-permute-start.15
  148.1 3.8 collective-permute-start.16
  151.9 4.7 collective-permute-start.17
  164.3 6.7 %collective-permute-start.18 = (f32[31,1536]{1,0:T(8,128)S(1)}, f32[31,1536]{1,0:T(8,128)S(1)}, u32[]{:S(2)}, u32[]{:S(2)}) collective-permute-start(f32[31,1536]{1,0:T(8,128)S(1)} %slice.543), channel_id=1, source_target_pairs={{1,0},{2,1},{3,2},{4,3},{5,4},{6,5},{7,6},{8,7},{9,8},{10,9},{11,1... | collective-permute-start | bytes 571400 | tf_op jit(solution)/shard_map/ppermute | solution.py:12
  214.6 28.7 %collective-permute-start.19 = (bf16[384,1536]{1,0:T(8,128)(2,1)S(1)}, bf16[384,1536]{1,0:T(8,128)(2,1)S(1)}, u32[]{:S(2)}, u32[]{:S(2)}) collective-permute-start(bf16[384,1536]{1,0:T(8,128)(2,1)S(1)} %multiply_convert_fusion.1), channel_id=1, source_target_pairs={{0,2},{1,3},{2,0},{3,1},{4,6},{5,7},{6,4},{7,5},{8,10},{9,11},{10,... | collective-permute-start | bytes 3538952 | tf_op jit(solution)/shard_map/ppermute | solution.py:166
  243.5 18.9 %collective-permute-start.22 = (bf16[768,1536]{1,0:T(8,128)(2,1)S(1)}, bf16[768,1536]{1,0:T(8,128)(2,1)S(1)}, u32[]{:S(2)}, u32[]{:S(2)}) collective-permute-start(bf16[768,1536]{1,0:T(8,128)(2,1)S(1)} %pad_maximum_fusion.2), channel_id=1, source_target_pairs={{0,1},{1,0},{2,3},{3,2},{4,5},{5,4},{6,7},{7,6},{8,9},{9,8},{10,11... | collective-permute-start | bytes 7077896 | tf_op jit(solution)/shard_map/ppermute | solution.py:174
  244.8 15.4 %collective-permute-start.20 = (bf16[768,384]{1,0:T(8,128)(2,1)S(1)}, bf16[768,384]{1,0:T(8,128)(2,1)S(1)}, u32[]{:S(2)}, u32[]{:S(2)}) collective-permute-start(bf16[768,384]{1,0:T(8,128)(2,1)S(1)} %pad_maximum_fusion.5), channel_id=1, source_target_pairs={{0,2},{1,3},{2,0},{3,1},{4,6},{5,7},{6,4},{7,5},{8,10},{9,11},{10,... | collective-permute-start | bytes 1769480 | tf_op jit(solution)/shard_map/ppermute | solution.py:69
  260.4 2.1 collective-permute-start.21
  266.7 141.4 %reduce-scatter.5.cloned.1.call-start = ((), (), s32[]{:S(2)}) async-start(), calls=%async_computation.4 | async-start | bytes 2654208 | tf_op jit(solution)/shard_map/reduce_scatter | solution.py:182
  266.8 28.1 %collective-permute-start.23 = (bf16[384,1536]{1,0:T(8,128)(2,1)S(1)}, bf16[384,1536]{1,0:T(8,128)(2,1)S(1)}, u32[]{:S(2)}, u32[]{:S(2)}) collective-permute-start(bf16[384,1536]{1,0:T(8,128)(2,1)S(1)} %get-tuple-element.18), channel_id=1, source_target_pairs={{0,2},{1,3},{2,0},{3,1},{4,6},{5,7},{6,4},{7,5},{8,10},{9,11},{10,... | collective-permute-start | bytes 3538952 | tf_op jit(solution)/shard_map/ppermute | solution.py:171
  295.0 4.6 collective-permute-start.24
  303.1 155.8 %all-gather.3.cloned.1.call-start = ((), (), s32[]{:S(2)}) async-start(), calls=%async_computation.3 | async-start | bytes 1327104 | tf_op jit(solution)/shard_map/all_gather | solution.py:184
  337.7 162.8 %all-gather.5.cloned.1.call-start = ((), (), s32[]{:S(2)}) async-start(), calls=%async_computation.5 | async-start | bytes 1327104 | tf_op jit(solution)/shard_map/all_gather | solution.py:184
  409.9 1.6 collective-permute-start.25
  411.5 8.1 %collective-permute-start.26 = (f32[34,1536]{1,0:T(8,128)S(1)}, f32[34,1536]{1,0:T(8,128)S(1)}, u32[]{:S(2)}, u32[]{:S(2)}) collective-permute-start(f32[34,1536]{1,0:T(8,128)S(1)} %fusion.128), channel_id=1, source_target_pairs={{0,2},{1,3},{2,0},{3,1},{4,6},{5,7},{6,4},{7,5},{8,10},{9,11},{10,... | collective-permute-start | bytes 626696 | tf_op jit(solution)/shard_map/ppermute | solution.py:25
  419.6 7.3 %collective-permute-start.27 = (f32[34,1536]{1,0:T(8,128)S(1)}, f32[34,1536]{1,0:T(8,128)S(1)}, u32[]{:S(2)}, u32[]{:S(2)}) collective-permute-start(f32[34,1536]{1,0:T(8,128)S(1)} %add.403), channel_id=1, source_target_pairs={{0,4},{1,5},{2,6},{3,7},{4,0},{5,1},{6,2},{7,3},{8,12},{9,13},{10,... | collective-permute-start | bytes 626696 | tf_op jit(solution)/shard_map/ppermute | solution.py:25
  426.9 8.0 %collective-permute-start.28 = (f32[34,1536]{1,0:T(8,128)S(1)}, f32[34,1536]{1,0:T(8,128)S(1)}, u32[]{:S(2)}, u32[]{:S(2)}) collective-permute-start(f32[34,1536]{1,0:T(8,128)S(1)} %add.404), channel_id=1, source_target_pairs={{0,8},{1,9},{2,10},{3,11},{4,12},{5,13},{6,14},{7,15},{8,0},{9,1},... | collective-permute-start | bytes 626696 | tf_op jit(solution)/shard_map/ppermute | solution.py:25
  434.9 22.7 %collective-permute-start.29 = (f32[34,1536]{1,0:T(8,128)S(1)}, f32[34,1536]{1,0:T(8,128)S(1)}, u32[]{:S(2)}, u32[]{:S(2)}) collective-permute-start(f32[34,1536]{1,0:T(8,128)S(1)} %add.405), channel_id=1, source_target_pairs={{0,16},{1,17},{2,18},{3,19},{4,20},{5,21},{6,22},{7,23},{8,24},{9,... | collective-permute-start | bytes 626696 | tf_op jit(solution)/shard_map/ppermute | solution.py:25
  (21 other events, 313.6 us)
Sparse Core Ops, SparseCore 0:
  266.9 69.1 reduce-scatter.2
  340.1 68.0 reduce-scatter.4
  410.3 47.2 all-gather.2
  460.3 40.1 all-gather.4

commit v6 on v4

--- a/solution.py
+++ b/solution.py
@@ -145,23 +145,30 @@
     normalized_gradient = lax.dot_general(
         grad_hidden, full_weight, (((1,), (1,)), ((), ())), preferred_element_type=jnp.float32
     )
-    grad_kernel, layer_norm_gain_gradient, grad_ln_bias = tree_sum(
-        (
-            kernel_portion,
-            jnp.sum(normalized_gradient * standardized_input, axis=0),
-            jnp.sum(normalized_gradient, axis=0),
-        ),
-        ("seq", "fsdp"),
-    )
     rescaled_rows = normalized_gradient * layer_norm_gain
     input_gradient = row_inverse_deviation * (
         rescaled_rows
         - jnp.mean(rescaled_rows, axis=-1, keepdims=True)
         - standardized_input * jnp.mean(rescaled_rows * standardized_input, axis=-1, keepdims=True)
     )
+    local_sums = (
+        kernel_portion,
+        jnp.sum(normalized_gradient * standardized_input, axis=0),
+        jnp.sum(normalized_gradient, axis=0),
+    )
     feature_rows = w_in.shape[0]
     group_rows = gather_own_columns(normalized_rows, "fsdp", feature_rows)
-    group_grad = gather_frames(grad_hidden, "fsdp")
+    if lax.axis_size("fsdp") == 4:
+        far = lax.ppermute(grad_hidden, "fsdp", [(i, i ^ 2) for i in range(4)])
+        far, input_gradient, local_sums = lax.optimization_barrier(
+            (far, input_gradient, local_sums)
+        )
+        near = lax.ppermute(
+            jnp.concatenate([grad_hidden, far], axis=0), "fsdp", [(i, i ^ 1) for i in range(4)]
+        )
+        group_grad = jnp.concatenate([grad_hidden, far, near], axis=0)
+    else:
+        group_grad = lax.all_gather(grad_hidden, "fsdp", axis=0, tiled=True)
     row_share = lax.dot_general(
         group_rows, group_grad, (((0,), (0,)), ((), ())), preferred_element_type=jnp.float32
     )
@@ -169,6 +176,7 @@
     grad_w_in = lax.all_gather(
         reduced.astype(jnp.bfloat16), "seq", axis=0, tiled=True
     ).astype(jnp.float32)
+    grad_kernel, layer_norm_gain_gradient, grad_ln_bias = tree_sum(local_sums, ("seq", "fsdp"))
     return (
         output,
         input_gradient.astype(jnp.bfloat16),

time: 493 us -> 476 us (0.966); the launches traced: 492 us -> 470 us
  local copies, waits for them, and re-layouts: 42.2 us -> 12.2 us
  other arithmetic: 98.6 us -> 82.3 us
  waiting for transfers between devices: 274 us -> 286 us
  matrix products: 17.8 us -> 27.3 us
    ppermute x2 -> x1, waiting for transfers between devices: 102 us -> 51.5 us  [group_shards(): far = lax.ppermute(block, axis, [(i, i ^ 2) for i in range(4)])]
    ppermute x0 -> x2, waiting for transfers between devices: none -> 34.5 us  [the longest x1 34.5 us: on_device(): far = lax.ppermute(grad_hidden, 'fsdp', [(i, i ^ 2) for i in range(4)])]
    ppermute x20, waiting for transfers between devices: 54.8 us -> 76 us  [tree_sum(): packed = packed + lax.ppermute(packed, axis, route)]
    another operation x32 -> x33, local copies, waits for them, and re-layouts: 19.1 us -> 0.53 us  [on_device(): kernel_portion = jnp.stack(kernel_rows, axis=0)]
    another operation x2, other arithmetic: 47.3 us -> 29.5 us
    concatenate x0 -> x1, other arithmetic: none -> 10.4 us  [on_device(): jnp.concatenate([grad_hidden, far], axis=0)]
    concatenate x2 -> x1, other arithmetic: 13.2 us -> 5.02 us  [group_shards(): jnp.concatenate([block, far], axis=0)]
    dot_general x1, matrix products: 6.3 us -> 14.2 us  [on_device(): lax.dot_general(group_rows, group_grad, (((0,), (0,)), ((), ())), preferr...]
  transfers between devices with their start and end apart: 30 -> 30, of which waited for: 27 -> 29; matrix products, arithmetic and copies ran while one was open for 11% -> 5% of each run, Pallas kernels for 0% -> 0%
where the time goes in v6:
time: 476 us; the launch traced here: 470 us
  waiting for transfers between devices  286 us (60%)
  other arithmetic  82.3 us (17%)
  starting transfers between devices  46.3 us (10%)
  matrix products  27.3 us (6%)
  between operations  16 us (3%)
  local copies, waits for them, and re-layouts  12.2 us (3%)
    reduce_scatter x1, waiting for transfers between devices, on_device(): lax.psum_scatter(row_share, 'seq', scatter_dimension=0, tiled=True)  97.5 us
    ppermute x20, waiting for transfers between devices, tree_sum(): packed = packed + lax.ppermute(packed, axis, route)  76 us
    ppermute x1, waiting for transfers between devices, group_shards(): far = lax.ppermute(block, axis, [(i, i ^ 2) for i in range(4)])  51.5 us
    ppermute x1, waiting for transfers between devices, on_device(): far = lax.ppermute(grad_hidden, 'fsdp', [(i, i ^ 2) for i in range(4)])  34.5 us
    ppermute x20, starting transfers between devices, tree_sum(): packed = packed + lax.ppermute(packed, axis, route)  34 us
    another operation x2, other arithmetic  29.5 us
    dot_general x1, matrix products, on_device(): lax.dot_general(group_rows, group_grad, (((0,), (0,)), ((), ())), preferr...  14.2 us
    ppermute x1, waiting for transfers between devices, gather_own_columns(): lax.ppermute(jnp.concatenate([cols(me ^ 2), cols(me ^ 3)], axis=0), axis,...  13.5 us
  transfers between devices with their start and end apart: 30, of which 29 were waited for; matrix products, arithmetic and copies ran while one was open for 5% of the time, Pallas kernels for 0%

profile of v6, /device:TPU:0, one launch (start us, length us, event | category | flops | bytes accessed | tf_op | source)
XLA Modules:
  0.0 469.6 jit_solution(896644516031943627)
XLA Ops:
  7.2 3.0 collective-permute-start
  10.2 51.5 %collective-permute-done = bf16[384,3072]{1,0:T(8,128)(2,1)S(1)} collective-permute-done((bf16[384,3072]{1,0:T(8,128)(2,1)}, bf16[384,3072]{1,0:T(8,128)(2,1)S(1)}, u32[]{:S(2)}, u32[]{:S(2)}) %collective-permute-start) | collective-permute-done | bytes 2359328 | tf_op jit(solution)/shard_map/ppermute | solution.py:36
  61.7 5.0 %pad_maximum_fusion = bf16[768,3072]{1,0:T(8,128)(2,1)} fusion(bf16[384,3072]{1,0:T(8,128)(2,1)S(1)} %collective-permute-done, bf16[384,3072]{1,0:T(8,128)(2,1)} %param.11), kind=kLoop, calls=%fused_computation.38 | loop fusion | flops 9437184 | bytes 9437184 | tf_op jit(solution)/shard_map/concatenate | solution.py:38
  72.3 2.7 collective-permute-done.1
  78.9 3.8 fusion.129
  88.6 9.4 %fusion.127 = (f32[1536]{0:T(1024)S(1)}, f32[384,1536]{1,0:T(8,128)S(1)}) fusion(f32[415,1536]{1,0:T(8,128)S(1)} %maximum_convert_fusion, f32[1536]{0:T(1024)S(1)} %get-tuple-element.88, f32[1536]{0:T(1024)S(1)} %get-tuple-element.89, f32[1536]{0:T(1024)S(1)} %get-tuple-element.59, f32[1536]{0:T(1024)S(1)} %get-tuple-element.60, ...), kind=kLoop, calls=%fused_computation.289 | loop fusion | flops 37747200 | bytes 78059520 | tf_op jit(solution)/shard_map/reduce_sum | solution.py:113
  101.4 2.7 collective-permute-start.4
  105.7 3.0 collective-permute-start.5
  110.3 3.0 collective-permute-start.6
  115.0 3.1 collective-permute-start.7
  121.4 3.6 collective-permute-done.9
  132.4 3.0 collective-permute-start.12
  140.9 3.7 collective-permute-done.14
  145.6 2.7 collective-permute-done.15
  152.2 3.0 collective-permute-start.17
  157.5 7.8 %multiply_reduce_fusion = (f32[1536]{0:T(1024)}, f32[1536]{0:T(1024)}, f32[1536]{0:T(1024)}, f32[1536]{0:T(1024)}, f32[1536]{0:T(1024)}, /*index=5*/f32[1536]{0:...) fusion(f32[415,1536]{1,0:T(8,128)S(1)} %maximum_convert_fusion,, ...), kind=kLoop, calls=%fused_computation.180 | loop fusion | flops 31822848 | bytes 48519168 | tf_op jit(solution)/shard_map/reduce_sum | solution.py:135
  168.6 25.5 %multiply_convert_fusion.1 = (bf16[384,1536]{1,0:T(8,128)(2,1)}, f32[384,1536]{1,0:T(8,128)}) fusion(f32[384,3072]{1,0:T(8,128)} %copy-done, f32[31,1536]{1,0:T(8,128)S(1)} %collective-permute-done.18, f32[384,1536]{1,0:T(8,128)S(1)} %get-tuple-element.93, f32[1536]{0:T(1024)} %copy-done.43, f32[1536]{0:T(1024)} %copy-done.44, ...), kind=kLoop, calls=%fused_computation.213 | loop fusion | flops 58392576 | bytes 8644608 | tf_op jit(solution)/shard_map/convert
  194.0 4.1 multiply_convert_fusion
  201.9 4.3 multiply_reduce_fusion.18
  207.3 9.2 %fusion.19 = (f32[1536]{0:T(1024)S(1)}, f32[384]{0:T(512)S(1)}, f32[384]{0:T(512)S(1)}, f32[1536]{0:T(1024)S(1)}, f32[384,1536]{1,0:T(8,128)S(1)}) fusion(bf16[384,1536]{1,0:T(8,128)(2,1)} %param.8, f32[384]{0:T(512)} %copy-done.67, f32[384]{0:T(512)S(1)} %broadcast_multiply_fusion.2, f32[1536]{0:T(1024)S(1)} %copy-done.47, ...), kind=kOutput, calls=%fused_computation.53 | convolution fusion | flops 3634491392 | bytes 15360000 | tf_op jit(solution)/shard_map/dot_general | solution.py:145
  218.3 34.5 %collective-permute-done.19 = bf16[384,3072]{1,0:T(8,128)(2,1)} collective-permute-done((bf16[384,3072]{1,0:T(8,128)(2,1)}, bf16[384,3072]{1,0:T(8,128)(2,1)}, u32[]{:S(2)}, u32[]{:S(2)}) %collective-permute-start.19) | collective-permute-done | bytes 2359328 | tf_op jit(solution)/shard_map/ppermute | solution.py:162
  252.8 10.4 %pad_maximum_fusion.1 = bf16[768,3072]{1,0:T(8,128)(2,1)S(1)} fusion(bf16[384,3072]{1,0:T(8,128)(2,1)} %collective-permute-done.19, bf16[384,1536]{1,0:T(8,128)(2,1)S(1)} %copy-done.6, bf16[384,1536]{1,0:T(8,128)(2,1)S(1)} %copy-done.4), kind=kLoop, calls=%fused_computation.39 | loop fusion | flops 14155776 | bytes 9437184 | tf_op jit(solution)/shard_map/concatenate | solution.py:167
  267.0 13.5 %collective-permute-done.20 = bf16[768,384]{1,0:T(8,128)(2,1)S(1)} collective-permute-done((bf16[768,384]{1,0:T(8,128)(2,1)S(1)}, bf16[768,384]{1,0:T(8,128)(2,1)S(1)}, u32[]{:S(2)}, u32[]{:S(2)}) %collective-permute-start.20) | collective-permute-done | bytes 589856 | tf_op jit(solution)/shard_map/ppermute | solution.py:69
  282.7 14.2 %fusion = f32[384,3072]{1,0:T(8,128)} fusion(bf16[768,3072]{1,0:T(8,128)(2,1)S(1)} %collective-permute-done.22, bf16[384,3072]{1,0:T(8,128)(2,1)} %collective-permute-done.19, bf16[384,1536]{1,0:T(8,128)(2,1)S(1)} %copy-done.6, bf16[384,1536]{1,0:T(8,128)(2,1)S(1)} %copy-done.4, bf16[768,384]{1,0:T(8,128)(2,1)S(1)} %collective-permute-done.21, ...), kind=kOutput, calls=%fused_computation.30 | convolution fusion | flops 3665166336 | bytes 15335424 | tf_op jit(solution)/shard_map/dot_general | solution.py:172
  297.0 97.5 %reduce-scatter.2.cloned.1.call-done = f32[48,3072]{1,0:T(8,128)} async-done(((f32[384,3072]{1,0:T(8,128)}), f32[48,3072]{1,0:T(8,128)}) %reduce-scatter.2.cloned.1.call-update) | async-done | bytes 589840 | tf_op jit(solution)/shard_map/reduce_scatter | solution.py:175
  399.6 6.5 %collective-permute-done.24 = f32[34,1536]{1,0:T(8,128)S(1)} collective-permute-done((f32[34,1536]{1,0:T(8,128)S(1)}, f32[34,1536]{1,0:T(8,128)S(1)}, u32[]{:S(2)}, u32[]{:S(2)}) %collective-permute-start.24) | collective-permute-done | bytes 208928 | tf_op jit(solution)/shard_map/ppermute | solution.py:25
  407.7 8.5 %collective-permute-done.25 = f32[34,1536]{1,0:T(8,128)S(1)} collective-permute-done((f32[34,1536]{1,0:T(8,128)S(1)}, f32[34,1536]{1,0:T(8,128)S(1)}, u32[]{:S(2)}, u32[]{:S(2)}) %collective-permute-start.25) | collective-permute-done | bytes 208928 | tf_op jit(solution)/shard_map/ppermute | solution.py:25
  417.8 8.0 %collective-permute-done.26 = f32[34,1536]{1,0:T(8,128)S(1)} collective-permute-done((f32[34,1536]{1,0:T(8,128)S(1)}, f32[34,1536]{1,0:T(8,128)S(1)}, u32[]{:S(2)}, u32[]{:S(2)}) %collective-permute-start.26) | collective-permute-done | bytes 208928 | tf_op jit(solution)/shard_map/ppermute | solution.py:25
  425.8 2.7 collective-permute-start.27
  428.5 22.4 %collective-permute-done.27 = f32[34,1536]{1,0:T(8,128)S(1)} collective-permute-done((f32[34,1536]{1,0:T(8,128)S(1)}, f32[34,1536]{1,0:T(8,128)S(1)}, u32[]{:S(2)}, u32[]{:S(2)}) %collective-permute-start.27) | collective-permute-done | bytes 208928 | tf_op jit(solution)/shard_map/ppermute | solution.py:25
  452.2 5.7 %all-gather.2.cloned.1.call-done = bf16[384,3072]{1,0:T(8,128)(2,1)} async-done(((bf16[48,3072]{1,0:T(8,128)(2,1)}), bf16[384,3072]{1,0:T(8,128)(2,1)}) %all-gather.2.cloned.1.call-update) | async-done | bytes 2359312 | tf_op jit(solution)/shard_map/all_gather | solution.py:176
  457.9 4.4 convert_element_type.36
  (272 shorter events, 71.1 us)
Async XLA Ops:
  7.2 59.6 %copy-start.14 = (f32[32,1536]{1,0:T(8,128)S(1)}, f32[32,1536]{1,0:T(8,128)}, u32[]{:S(2)}) copy-start(f32[32,1536]{1,0:T(8,128)} %param.12) | copy-start | bytes 589828
  7.2 59.9 %copy-start.1 = (bf16[384,1536]{1,0:T(8,128)(2,1)S(1)}, bf16[384,1536]{1,0:T(8,128)(2,1)}, u32[]{:S(2)}) copy-start(bf16[384,1536]{1,0:T(8,128)(2,1)} %param.8) | copy-start | bytes 3538948
  7.2 387.3 %reduce-scatter.2.cloned.1.call-start = ((), (), s32[]{:S(2)}) async-start(), calls=%async_computation.1 | async-start | bytes 5308416 | tf_op jit(solution)/shard_map/reduce_scatter | solution.py:175
  7.2 54.5 %collective-permute-start = (bf16[384,3072]{1,0:T(8,128)(2,1)}, bf16[384,3072]{1,0:T(8,128)(2,1)S(1)}, u32[]{:S(2)}, u32[]{:S(2)}) collective-permute-start(bf16[384,3072]{1,0:T(8,128)(2,1)} %param.11), channel_id=1, source_target_pairs={{0,2},{1,3},{2,0},{3,1},{4,6},{5,7},{6,4},{7,5},{8,10},{9,11},{10,... | collective-permute-start | bytes 7077896 | tf_op jit(solution)/shard_map/ppermute | solution.py:36
  66.7 8.3 %collective-permute-start.1 = (bf16[768,3072]{1,0:T(8,128)(2,1)}, bf16[768,3072]{1,0:T(8,128)(2,1)}, u32[]{:S(2)}, u32[]{:S(2)}) collective-permute-start(bf16[768,3072]{1,0:T(8,128)(2,1)} %pad_maximum_fusion), channel_id=1, source_target_pairs={{0,1},{1,0},{2,3},{3,2},{4,5},{5,4},{6,7},{7,6},{8,9},{9,8},{10,11... | collective-permute-start | bytes 14155784 | tf_op jit(solution)/shard_map/ppermute | solution.py:37
  85.0 3.0 collective-permute-start.2
  98.1 3.3 collective-permute-start.3
  101.4 4.3 collective-permute-start.4
  105.7 4.6 collective-permute-start.5
  110.3 4.7 collective-permute-start.6
  115.0 4.7 %collective-permute-start.7 = (f32[1,1536]{1,0:T(1,128)S(1)}, f32[1,1536]{1,0:T(1,128)S(1)}, u32[]{:S(2)}, u32[]{:S(2)}) collective-permute-start(f32[1,1536]{1,0:T(1,128)S(1)} %add.351), channel_id=1, source_target_pairs={{0,16},{1,17},{2,18},{3,19},{4,20},{5,21},{6,22},{7,23},{8,24},{9,... | collective-permute-start | bytes 18440 | tf_op jit(solution)/shard_map/ppermute | solution.py:25
  120.0 1.2 collective-permute-start.8
  121.3 3.7 collective-permute-start.9
  125.0 3.7 collective-permute-start.10
  128.7 3.7 collective-permute-start.11
  132.4 4.6 collective-permute-start.12
  139.6 1.2 collective-permute-start.13
  140.8 3.8 collective-permute-start.14
  144.6 3.8 collective-permute-start.15
  148.4 3.8 collective-permute-start.16
  152.2 4.7 collective-permute-start.17
  165.2 3.3 collective-permute-start.18
  200.1 52.7 %collective-permute-start.19 = (bf16[384,3072]{1,0:T(8,128)(2,1)}, bf16[384,3072]{1,0:T(8,128)(2,1)}, u32[]{:S(2)}, u32[]{:S(2)}) collective-permute-start(bf16[384,3072]{1,0:T(8,128)(2,1)} %pad_maximum_fusion.3), channel_id=1, source_target_pairs={{0,2},{1,3},{2,0},{3,1},{4,6},{5,7},{6,4},{7,5},{8,10},{9,11},{10,... | collective-permute-start | bytes 7077896 | tf_op jit(solution)/shard_map/ppermute | solution.py:162
  263.2 19.5 %collective-permute-start.22 = (bf16[768,3072]{1,0:T(8,128)(2,1)S(1)}, bf16[768,3072]{1,0:T(8,128)(2,1)S(1)}, u32[]{:S(2)}, u32[]{:S(2)}) collective-permute-start(bf16[768,3072]{1,0:T(8,128)(2,1)S(1)} %pad_maximum_fusion.1), channel_id=1, source_target_pairs={{0,1},{1,0},{2,3},{3,2},{4,5},{5,4},{6,7},{7,6},{8,9},{9,8},{10,11... | collective-permute-start | bytes 14155784 | tf_op jit(solution)/shard_map/ppermute | solution.py:166
  265.1 15.4 %collective-permute-start.20 = (bf16[768,384]{1,0:T(8,128)(2,1)S(1)}, bf16[768,384]{1,0:T(8,128)(2,1)S(1)}, u32[]{:S(2)}, u32[]{:S(2)}) collective-permute-start(bf16[768,384]{1,0:T(8,128)(2,1)S(1)} %pad_maximum_fusion.4), channel_id=1, source_target_pairs={{0,2},{1,3},{2,0},{3,1},{4,6},{5,7},{6,4},{7,5},{8,10},{9,11},{10,... | collective-permute-start | bytes 1769480 | tf_op jit(solution)/shard_map/ppermute | solution.py:69
  280.6 2.1 collective-permute-start.21
  297.0 161.0 %all-gather.2.cloned.1.call-start = ((), (), s32[]{:S(2)}) async-start(), calls=%async_computation.2 | async-start | bytes 2654208 | tf_op jit(solution)/shard_map/all_gather | solution.py:176
  396.4 1.6 collective-permute-start.23
  398.0 8.1 %collective-permute-start.24 = (f32[34,1536]{1,0:T(8,128)S(1)}, f32[34,1536]{1,0:T(8,128)S(1)}, u32[]{:S(2)}, u32[]{:S(2)}) collective-permute-start(f32[34,1536]{1,0:T(8,128)S(1)} %fusion.123), channel_id=1, source_target_pairs={{0,2},{1,3},{2,0},{3,1},{4,6},{5,7},{6,4},{7,5},{8,10},{9,11},{10,... | collective-permute-start | bytes 626696 | tf_op jit(solution)/shard_map/ppermute | solution.py:25
  406.1 10.1 %collective-permute-start.25 = (f32[34,1536]{1,0:T(8,128)S(1)}, f32[34,1536]{1,0:T(8,128)S(1)}, u32[]{:S(2)}, u32[]{:S(2)}) collective-permute-start(f32[34,1536]{1,0:T(8,128)S(1)} %add.401), channel_id=1, source_target_pairs={{0,4},{1,5},{2,6},{3,7},{4,0},{5,1},{6,2},{7,3},{8,12},{9,13},{10,... | collective-permute-start | bytes 626696 | tf_op jit(solution)/shard_map/ppermute | solution.py:25
  416.2 9.5 %collective-permute-start.26 = (f32[34,1536]{1,0:T(8,128)S(1)}, f32[34,1536]{1,0:T(8,128)S(1)}, u32[]{:S(2)}, u32[]{:S(2)}) collective-permute-start(f32[34,1536]{1,0:T(8,128)S(1)} %add.402), channel_id=1, source_target_pairs={{0,8},{1,9},{2,10},{3,11},{4,12},{5,13},{6,14},{7,15},{8,0},{9,1},... | collective-permute-start | bytes 626696 | tf_op jit(solution)/shard_map/ppermute | solution.py:25
  425.8 25.1 %collective-permute-start.27 = (f32[34,1536]{1,0:T(8,128)S(1)}, f32[34,1536]{1,0:T(8,128)S(1)}, u32[]{:S(2)}, u32[]{:S(2)}) collective-permute-start(f32[34,1536]{1,0:T(8,128)S(1)} %add.403), channel_id=1, source_target_pairs={{0,16},{1,17},{2,18},{3,19},{4,20},{5,21},{6,22},{7,23},{8,24},{9,... | collective-permute-start | bytes 626696 | tf_op jit(solution)/shard_map/ppermute | solution.py:25
  (68 other events, 739.3 us)
Sparse Core Ops, SparseCore 0:
  297.1 97.4 reduce-scatter.1
  397.3 60.6 all-gather.1

commit v7 on v6

--- a/solution.py
+++ b/solution.py
@@ -34,10 +34,9 @@
 
 def group_shards(block, axis):
     far = lax.ppermute(block, axis, [(i, i ^ 2) for i in range(4)])
-    near = lax.ppermute(
-        jnp.concatenate([block, far], axis=0), axis, [(i, i ^ 1) for i in range(4)]
-    )
-    return jnp.concatenate([block, far, near], axis=0)
+    near = lax.ppermute(block, axis, [(i, i ^ 1) for i in range(4)])
+    near_far = lax.ppermute(far, axis, [(i, i ^ 1) for i in range(4)])
+    return [block, far, near, near_far]
 
 
 def gather_rows(block, axis):
@@ -48,10 +47,8 @@
     me = lax.axis_index(axis)
     shards = group_shards(block, axis)
     whole = jnp.zeros((count * rows,) + block.shape[1:], block.dtype)
-    for slot, owner in enumerate((me, me ^ 2, me ^ 1, me ^ 3)):
-        whole = lax.dynamic_update_slice_in_dim(
-            whole, shards[slot * rows : (slot + 1) * rows], owner * rows, axis=0
-        )
+    for shard, owner in zip(shards, (me, me ^ 2, me ^ 1, me ^ 3)):
+        whole = lax.dynamic_update_slice_in_dim(whole, shard, owner * rows, axis=0)
     return whole
 
 
@@ -73,12 +70,6 @@
         jnp.concatenate([cols(me ^ 1), far[frames:]], axis=0), axis, [(i, i ^ 1) for i in range(4)]
     )
     return jnp.concatenate([cols(me), far[:frames], near], axis=0)
-
-
-def gather_frames(block, axis):
-    if lax.axis_size(axis) != 4:
-        return lax.all_gather(block, axis, axis=0, tiled=True)
-    return group_shards(block, axis)
 
 
 def on_device(
@@ -158,20 +149,29 @@
     )
     feature_rows = w_in.shape[0]
     group_rows = gather_own_columns(normalized_rows, "fsdp", feature_rows)
+    contract = (((0,), (0,)), ((), ()))
     if lax.axis_size("fsdp") == 4:
         far = lax.ppermute(grad_hidden, "fsdp", [(i, i ^ 2) for i in range(4)])
+        near = lax.ppermute(grad_hidden, "fsdp", [(i, i ^ 1) for i in range(4)])
         far, input_gradient, local_sums = lax.optimization_barrier(
             (far, input_gradient, local_sums)
         )
-        near = lax.ppermute(
-            jnp.concatenate([grad_hidden, far], axis=0), "fsdp", [(i, i ^ 1) for i in range(4)]
-        )
-        group_grad = jnp.concatenate([grad_hidden, far, near], axis=0)
+        near_far = lax.ppermute(far, "fsdp", [(i, i ^ 1) for i in range(4)])
+        pieces = (grad_hidden, far, near, near_far)
+        row_share = None
+        for slot, piece in enumerate(pieces):
+            term = lax.dot_general(
+                group_rows[slot * tok_rows : (slot + 1) * tok_rows],
+                piece,
+                contract,
+                preferred_element_type=jnp.float32,
+            )
+            row_share = term if row_share is None else row_share + term
     else:
         group_grad = lax.all_gather(grad_hidden, "fsdp", axis=0, tiled=True)
-    row_share = lax.dot_general(
-        group_rows, group_grad, (((0,), (0,)), ((), ())), preferred_element_type=jnp.float32
-    )
+        row_share = lax.dot_general(
+            group_rows, group_grad, contract, preferred_element_type=jnp.float32
+        )
     reduced = lax.psum_scatter(row_share, "seq", scatter_dimension=0, tiled=True)
     grad_w_in = lax.all_gather(
         reduced.astype(jnp.bfloat16), "seq", axis=0, tiled=True

time: 476 us -> 447 us (0.939); the launches traced: 470 us -> 446 us
  other arithmetic: 82.3 us -> 69.6 us
  waiting for transfers between devices: 286 us -> 276 us
    concatenate x2 -> x0, other arithmetic: 15.5 us -> none  [the longest x1 10.4 us: on_device(): jnp.concatenate([grad_hidden, far], axis=0)]
    dot_general x1 -> x4, matrix products: 14.2 us -> 10 us  [on_device(): lax.dot_general(group_rows[slot * tok_rows:(slot + 1) * tok_rows], piece,...]
  transfers between devices with their start and end apart: 30 -> 32, of which waited for: 29 -> 26; matrix products, arithmetic and copies ran while one was open for 5% -> 8% of each run, Pallas kernels for 0% -> 0%
where the time goes in v7:
time: 447 us; the launch traced here: 446 us
  waiting for transfers between devices  276 us (62%)
  other arithmetic  69.6 us (16%)
  starting transfers between devices  47.5 us (11%)
  matrix products  23 us (5%)
  between operations  15.6 us (3%)
  local copies, waits for them, and re-layouts  14.8 us (3%)
    reduce_scatter x1, waiting for transfers between devices, on_device(): lax.psum_scatter(row_share, 'seq', scatter_dimension=0, tiled=True)  97.6 us
    ppermute x20, waiting for transfers between devices, tree_sum(): packed = packed + lax.ppermute(packed, axis, route)  76 us
    ppermute x1, waiting for transfers between devices, group_shards(): far = lax.ppermute(block, axis, [(i, i ^ 2) for i in range(4)])  48.1 us
    ppermute x20, starting transfers between devices, tree_sum(): packed = packed + lax.ppermute(packed, axis, route)  32.7 us
    ppermute x1, waiting for transfers between devices, on_device(): far = lax.ppermute(grad_hidden, 'fsdp', [(i, i ^ 2) for i in range(4)])  31.9 us
    another operation x2, other arithmetic  29.5 us
    ppermute x1, waiting for transfers between devices, gather_own_columns(): lax.ppermute(jnp.concatenate([cols(me ^ 2), cols(me ^ 3)], axis=0), axis,...  13.5 us
    reduce_sum x2, other arithmetic, on_device(): jnp.sum(grad_conv * padded_glu[kernel_len - 1 - offset:kernel_len - 1 - o...  12.3 us
  transfers between devices with their start and end apart: 32, of which 26 were waited for; matrix products, arithmetic and copies ran while one was open for 8% of the time, Pallas kernels for 0%

profile of v7, /device:TPU:0, one launch (start us, length us, event | category | flops | bytes accessed | tf_op | source)
XLA Modules:
  0.0 446.1 jit_solution(1606725813982369533)
XLA Ops:
  7.2 3.0 collective-permute-start
  13.7 48.1 %collective-permute-done = bf16[384,3072]{1,0:T(8,128)(2,1)} collective-permute-done((bf16[384,3072]{1,0:T(8,128)(2,1)}, bf16[384,3072]{1,0:T(8,128)(2,1)}, u32[]{:S(2)}, u32[]{:S(2)}) %collective-permute-start) | collective-permute-done | bytes 2359328 | tf_op jit(solution)/shard_map/ppermute | solution.py:36
  71.7 3.8 fusion.125
  77.7 2.6 collective-permute-start.3
  82.6 9.4 %fusion.124 = (f32[1536]{0:T(1024)S(1)}, f32[384,1536]{1,0:T(8,128)S(1)}) fusion(f32[415,1536]{1,0:T(8,128)S(1)} %maximum_convert_fusion, f32[1536]{0:T(1024)S(1)} %get-tuple-element.88, f32[1536]{0:T(1024)S(1)} %get-tuple-element.89, f32[1536]{0:T(1024)S(1)} %get-tuple-element.59, f32[1536]{0:T(1024)S(1)} %get-tuple-element.60, ...), kind=kLoop, calls=%fused_computation.282 | loop fusion | flops 37747200 | bytes 78059520 | tf_op jit(solution)/shard_map/reduce_sum | solution.py:104
  98.5 3.0 collective-permute-start.6
  103.1 3.0 collective-permute-start.7
  107.8 3.1 collective-permute-start.8
  114.1 3.6 collective-permute-done.10
  118.8 2.7 collective-permute-done.11
  125.2 3.0 collective-permute-start.13
  129.8 2.5 fusion.122
  133.7 3.7 collective-permute-done.15
  138.4 2.7 collective-permute-done.16
  144.9 3.0 collective-permute-start.18
  150.2 7.8 %multiply_reduce_fusion = (f32[1536]{0:T(1024)}, f32[1536]{0:T(1024)}, f32[1536]{0:T(1024)}, f32[1536]{0:T(1024)}, f32[1536]{0:T(1024)}, /*index=5*/f32[1536]{0:...) fusion(f32[415,1536]{1,0:T(8,128)S(1)} %maximum_convert_fusion,, ...), kind=kLoop, calls=%fused_computation.169 | loop fusion | flops 31822848 | bytes 48519168 | tf_op jit(solution)/shard_map/reduce_sum | solution.py:126
  161.3 25.5 %multiply_convert_fusion.1 = (bf16[384,1536]{1,0:T(8,128)(2,1)}, f32[384,1536]{1,0:T(8,128)}) fusion(f32[384,3072]{1,0:T(8,128)} %copy-done, f32[31,1536]{1,0:T(8,128)S(1)} %collective-permute-done.19, f32[384,1536]{1,0:T(8,128)S(1)} %get-tuple-element.93, f32[1536]{0:T(1024)} %copy-done.40, f32[1536]{0:T(1024)} %copy-done.41, ...), kind=kLoop, calls=%fused_computation.202 | loop fusion | flops 58392576 | bytes 8644608 | tf_op jit(solution)/shard_map/convert
  186.8 4.1 multiply_convert_fusion
  194.7 4.6 %multiply_reduce_fusion.18 = (f32[1536]{0:T(1024)S(1)}, f32[1536]{0:T(1024)S(1)}, f32[1536]{0:T(1024)S(1)}, f32[1536]{0:T(1024)S(1)}, f32[1536]{0:T(1024)S(1)}, ...) fusion(f32[384,1536]{1,0:T(8,128)S(1)} %get-tuple-element.93, ...), kind=kLoop, calls=%fused_computation.187 | loop fusion | flops 16493568 | bytes 35475456 | tf_op jit(solution)/shard_map/reduce_sum | solution.py:126
  202.7 9.1 %fusion.11 = (f32[1536]{0:T(1024)S(1)}, f32[384]{0:T(512)S(1)}, f32[384]{0:T(512)S(1)}, f32[1536]{0:T(1024)S(1)}, f32[384,1536]{1,0:T(8,128)S(1)}) fusion(bf16[384,1536]{1,0:T(8,128)(2,1)} %param.8, f32[384]{0:T(512)} %copy-done.64, f32[384]{0:T(512)S(1)} %broadcast_multiply_fusion.2, f32[1536]{0:T(1024)S(1)} %copy-done.44, ...), kind=kOutput, calls=%fused_computation.44 | convolution fusion | flops 3634491392 | bytes 15360000 | tf_op jit(solution)/shard_map/dot_general | solution.py:136
  213.7 31.9 %collective-permute-done.20 = bf16[384,3072]{1,0:T(8,128)(2,1)} collective-permute-done((bf16[384,3072]{1,0:T(8,128)(2,1)}, bf16[384,3072]{1,0:T(8,128)(2,1)}, u32[]{:S(2)}, u32[]{:S(2)}) %collective-permute-start.20) | collective-permute-done | bytes 2359328 | tf_op jit(solution)/shard_map/ppermute | solution.py:154
  249.2 13.5 %collective-permute-done.21 = bf16[768,384]{1,0:T(8,128)(2,1)S(1)} collective-permute-done((bf16[768,384]{1,0:T(8,128)(2,1)S(1)}, bf16[768,384]{1,0:T(8,128)(2,1)S(1)}, u32[]{:S(2)}, u32[]{:S(2)}) %collective-permute-start.21) | collective-permute-done | bytes 589856 | tf_op jit(solution)/shard_map/ppermute | solution.py:66
  264.3 3.1 fusion.114
  268.9 4.1 add_add_fusion
  273.1 97.6 %reduce-scatter.2.cloned.1.call-done = f32[48,3072]{1,0:T(8,128)} async-done(((f32[384,3072]{1,0:T(8,128)}), f32[48,3072]{1,0:T(8,128)}) %reduce-scatter.2.cloned.1.call-update) | async-done | bytes 589840 | tf_op jit(solution)/shard_map/reduce_scatter | solution.py:175
  375.7 6.5 %collective-permute-done.26 = f32[34,1536]{1,0:T(8,128)S(1)} collective-permute-done((f32[34,1536]{1,0:T(8,128)S(1)}, f32[34,1536]{1,0:T(8,128)S(1)}, u32[]{:S(2)}, u32[]{:S(2)}) %collective-permute-start.26) | collective-permute-done | bytes 208928 | tf_op jit(solution)/shard_map/ppermute | solution.py:25
  383.8 8.5 %collective-permute-done.27 = f32[34,1536]{1,0:T(8,128)S(1)} collective-permute-done((f32[34,1536]{1,0:T(8,128)S(1)}, f32[34,1536]{1,0:T(8,128)S(1)}, u32[]{:S(2)}, u32[]{:S(2)}) %collective-permute-start.27) | collective-permute-done | bytes 208928 | tf_op jit(solution)/shard_map/ppermute | solution.py:25
  393.9 8.0 %collective-permute-done.28 = f32[34,1536]{1,0:T(8,128)S(1)} collective-permute-done((f32[34,1536]{1,0:T(8,128)S(1)}, f32[34,1536]{1,0:T(8,128)S(1)}, u32[]{:S(2)}, u32[]{:S(2)}) %collective-permute-start.28) | collective-permute-done | bytes 208928 | tf_op jit(solution)/shard_map/ppermute | solution.py:25
  401.9 2.7 collective-permute-start.29
  404.6 22.4 %collective-permute-done.29 = f32[34,1536]{1,0:T(8,128)S(1)} collective-permute-done((f32[34,1536]{1,0:T(8,128)S(1)}, f32[34,1536]{1,0:T(8,128)S(1)}, u32[]{:S(2)}, u32[]{:S(2)}) %collective-permute-start.29) | collective-permute-done | bytes 208928 | tf_op jit(solution)/shard_map/ppermute | solution.py:25
  428.4 6.5 %all-gather.2.cloned.1.call-done = bf16[384,3072]{1,0:T(8,128)(2,1)} async-done(((bf16[48,3072]{1,0:T(8,128)(2,1)}), bf16[384,3072]{1,0:T(8,128)(2,1)}) %all-gather.2.cloned.1.call-update) | async-done | bytes 2359312 | tf_op jit(solution)/shard_map/all_gather | solution.py:176
  434.8 4.4 convert_element_type.36
  (271 shorter events, 73.1 us)
Async XLA Ops:
  7.2 363.5 %reduce-scatter.2.cloned.1.call-start = ((), (), s32[]{:S(2)}) async-start(), calls=%async_computation.1 | async-start | bytes 5308416 | tf_op jit(solution)/shard_map/reduce_scatter | solution.py:175
  7.2 54.6 %collective-permute-start = (bf16[384,3072]{1,0:T(8,128)(2,1)}, bf16[384,3072]{1,0:T(8,128)(2,1)}, u32[]{:S(2)}, u32[]{:S(2)}) collective-permute-start(bf16[384,3072]{1,0:T(8,128)(2,1)} %param.11), channel_id=1, source_target_pairs={{0,2},{1,3},{2,0},{3,1},{4,6},{5,7},{6,4},{7,5},{8,10},{9,11},{10,... | collective-permute-start | bytes 7077896 | tf_op jit(solution)/shard_map/ppermute | solution.py:36
  10.2 59.2 %collective-permute-start.1 = (bf16[384,3072]{1,0:T(8,128)(2,1)}, bf16[384,3072]{1,0:T(8,128)(2,1)}, u32[]{:S(2)}, u32[]{:S(2)}) collective-permute-start(bf16[384,3072]{1,0:T(8,128)(2,1)} %param.11), channel_id=1, source_target_pairs={{0,1},{1,0},{2,3},{3,2},{4,5},{5,4},{6,7},{7,6},{8,9},{9,8},{10,11... | collective-permute-start | bytes 7077896 | tf_op jit(solution)/shard_map/ppermute | solution.py:37
  61.8 9.6 %collective-permute-start.2 = (bf16[384,3072]{1,0:T(8,128)(2,1)}, bf16[384,3072]{1,0:T(8,128)(2,1)S(1)}, u32[]{:S(2)}, u32[]{:S(2)}) collective-permute-start(bf16[384,3072]{1,0:T(8,128)(2,1)} %collective-permute-done), channel_id=1, source_target_pairs={{0,1},{1,0},{2,3},{3,2},{4,5},{5,4},{6,7},{7,6},{8,9},{9,8},{10,11... | collective-permute-start | bytes 7077896 | tf_op jit(solution)/shard_map/ppermute | solution.py:38
  77.7 4.3 collective-permute-start.3
  92.1 2.2 collective-permute-start.4
  94.4 4.1 collective-permute-start.5
  98.5 4.6 %collective-permute-start.6 = (f32[1,1536]{1,0:T(1,128)S(1)}, f32[1,1536]{1,0:T(1,128)S(1)}, u32[]{:S(2)}, u32[]{:S(2)}) collective-permute-start(f32[1,1536]{1,0:T(1,128)S(1)} %add.358), channel_id=1, source_target_pairs={{0,4},{1,5},{2,6},{3,7},{4,0},{5,1},{6,2},{7,3},{8,12},{9,13},{10,... | collective-permute-start | bytes 18440 | tf_op jit(solution)/shard_map/ppermute | solution.py:25
  103.1 4.7 %collective-permute-start.7 = (f32[1,1536]{1,0:T(1,128)S(1)}, f32[1,1536]{1,0:T(1,128)S(1)}, u32[]{:S(2)}, u32[]{:S(2)}) collective-permute-start(f32[1,1536]{1,0:T(1,128)S(1)} %add.359), channel_id=1, source_target_pairs={{0,8},{1,9},{2,10},{3,11},{4,12},{5,13},{6,14},{7,15},{8,0},{9,1},... | collective-permute-start | bytes 18440 | tf_op jit(solution)/shard_map/ppermute | solution.py:25
  107.8 4.7 %collective-permute-start.8 = (f32[1,1536]{1,0:T(1,128)S(1)}, f32[1,1536]{1,0:T(1,128)S(1)}, u32[]{:S(2)}, u32[]{:S(2)}) collective-permute-start(f32[1,1536]{1,0:T(1,128)S(1)} %add.360), channel_id=1, source_target_pairs={{0,16},{1,17},{2,18},{3,19},{4,20},{5,21},{6,22},{7,23},{8,24},{9,... | collective-permute-start | bytes 18440 | tf_op jit(solution)/shard_map/ppermute | solution.py:25
  112.8 1.2 collective-permute-start.9
  114.0 3.7 collective-permute-start.10
  117.7 3.7 collective-permute-start.11
  121.5 3.7 collective-permute-start.12
  125.2 4.6 %collective-permute-start.13 = (f32[1,1536]{1,0:T(1,128)S(1)}, f32[1,1536]{1,0:T(1,128)S(1)}, u32[]{:S(2)}, u32[]{:S(2)}) collective-permute-start(f32[1,1536]{1,0:T(1,128)S(1)} %add.365), channel_id=1, source_target_pairs={{0,16},{1,17},{2,18},{3,19},{4,20},{5,21},{6,22},{7,23},{8,24},{9,... | collective-permute-start | bytes 18440 | tf_op jit(solution)/shard_map/ppermute | solution.py:25
  132.3 1.2 collective-permute-start.14
  133.6 3.8 collective-permute-start.15
  137.4 3.8 collective-permute-start.16
  141.2 3.8 collective-permute-start.17
  144.9 4.7 %collective-permute-start.18 = (f32[2,1536]{1,0:T(2,128)S(1)}, f32[2,1536]{1,0:T(2,128)S(1)}, u32[]{:S(2)}, u32[]{:S(2)}) collective-permute-start(f32[2,1536]{1,0:T(2,128)S(1)} %add.376), channel_id=1, source_target_pairs={{0,16},{1,17},{2,18},{3,19},{4,20},{5,21},{6,22},{7,23},{8,24},{9,... | collective-permute-start | bytes 36872 | tf_op jit(solution)/shard_map/ppermute | solution.py:25
  158.0 3.3 collective-permute-start.19
  192.9 52.7 %collective-permute-start.20 = (bf16[384,3072]{1,0:T(8,128)(2,1)}, bf16[384,3072]{1,0:T(8,128)(2,1)}, u32[]{:S(2)}, u32[]{:S(2)}) collective-permute-start(bf16[384,3072]{1,0:T(8,128)(2,1)} %pad_maximum_fusion.1), channel_id=1, source_target_pairs={{0,2},{1,3},{2,0},{3,1},{4,6},{5,7},{6,4},{7,5},{8,10},{9,11},{10,... | collective-permute-start | bytes 7077896 | tf_op jit(solution)/shard_map/ppermute | solution.py:154
  200.3 67.2 %collective-permute-start.23 = (bf16[384,3072]{1,0:T(8,128)(2,1)}, bf16[384,3072]{1,0:T(8,128)(2,1)S(1)}, u32[]{:S(2)}, u32[]{:S(2)}) collective-permute-start(bf16[384,3072]{1,0:T(8,128)(2,1)} %pad_maximum_fusion.1), channel_id=1, source_target_pairs={{0,1},{1,0},{2,3},{3,2},{4,5},{5,4},{6,7},{7,6},{8,9},{9,8},{10,11... | collective-permute-start | bytes 7077896 | tf_op jit(solution)/shard_map/ppermute | solution.py:155
  245.6 23.3 %collective-permute-start.24 = (bf16[384,3072]{1,0:T(8,128)(2,1)}, bf16[384,3072]{1,0:T(8,128)(2,1)S(1)}, u32[]{:S(2)}, u32[]{:S(2)}) collective-permute-start(bf16[384,3072]{1,0:T(8,128)(2,1)} %collective-permute-done.20), channel_id=1, source_target_pairs={{0,1},{1,0},{2,3},{3,2},{4,5},{5,4},{6,7},{7,6},{8,9},{9,8},{10,11... | collective-permute-start | bytes 7077896 | tf_op jit(solution)/shard_map/ppermute | solution.py:159
  247.4 15.4 %collective-permute-start.21 = (bf16[768,384]{1,0:T(8,128)(2,1)S(1)}, bf16[768,384]{1,0:T(8,128)(2,1)S(1)}, u32[]{:S(2)}, u32[]{:S(2)}) collective-permute-start(bf16[768,384]{1,0:T(8,128)(2,1)S(1)} %pad_maximum_fusion.2), channel_id=1, source_target_pairs={{0,2},{1,3},{2,0},{3,1},{4,6},{5,7},{6,4},{7,5},{8,10},{9,11},{10,... | collective-permute-start | bytes 1769480 | tf_op jit(solution)/shard_map/ppermute | solution.py:66
  262.8 4.6 %collective-permute-start.22 = (bf16[768,384]{1,0:T(8,128)(2,1)S(1)}, bf16[768,384]{1,0:T(8,128)(2,1)S(1)}, u32[]{:S(2)}, u32[]{:S(2)}) collective-permute-start(bf16[768,384]{1,0:T(8,128)(2,1)S(1)} %pad_maximum_fusion.3), channel_id=1, source_target_pairs={{0,1},{1,0},{2,3},{3,2},{4,5},{5,4},{6,7},{7,6},{8,9},{9,8},{10,11... | collective-permute-start | bytes 1769480 | tf_op jit(solution)/shard_map/ppermute | solution.py:69
  273.0 161.8 %all-gather.2.cloned.1.call-start = ((), (), s32[]{:S(2)}) async-start(), calls=%async_computation.2 | async-start | bytes 2654208 | tf_op jit(solution)/shard_map/all_gather | solution.py:176
  372.5 1.6 collective-permute-start.25
  374.2 8.1 %collective-permute-start.26 = (f32[34,1536]{1,0:T(8,128)S(1)}, f32[34,1536]{1,0:T(8,128)S(1)}, u32[]{:S(2)}, u32[]{:S(2)}) collective-permute-start(f32[34,1536]{1,0:T(8,128)S(1)} %fusion.120), channel_id=1, source_target_pairs={{0,2},{1,3},{2,0},{3,1},{4,6},{5,7},{6,4},{7,5},{8,10},{9,11},{10,... | collective-permute-start | bytes 626696 | tf_op jit(solution)/shard_map/ppermute | solution.py:25
  382.3 10.1 %collective-permute-start.27 = (f32[34,1536]{1,0:T(8,128)S(1)}, f32[34,1536]{1,0:T(8,128)S(1)}, u32[]{:S(2)}, u32[]{:S(2)}) collective-permute-start(f32[34,1536]{1,0:T(8,128)S(1)} %add.413), channel_id=1, source_target_pairs={{0,4},{1,5},{2,6},{3,7},{4,0},{5,1},{6,2},{7,3},{8,12},{9,13},{10,... | collective-permute-start | bytes 626696 | tf_op jit(solution)/shard_map/ppermute | solution.py:25
  392.4 9.5 %collective-permute-start.28 = (f32[34,1536]{1,0:T(8,128)S(1)}, f32[34,1536]{1,0:T(8,128)S(1)}, u32[]{:S(2)}, u32[]{:S(2)}) collective-permute-start(f32[34,1536]{1,0:T(8,128)S(1)} %add.414), channel_id=1, source_target_pairs={{0,8},{1,9},{2,10},{3,11},{4,12},{5,13},{6,14},{7,15},{8,0},{9,1},... | collective-permute-start | bytes 626696 | tf_op jit(solution)/shard_map/ppermute | solution.py:25
  401.9 25.1 %collective-permute-start.29 = (f32[34,1536]{1,0:T(8,128)S(1)}, f32[34,1536]{1,0:T(8,128)S(1)}, u32[]{:S(2)}, u32[]{:S(2)}) collective-permute-start(f32[34,1536]{1,0:T(8,128)S(1)} %add.415), channel_id=1, source_target_pairs={{0,16},{1,17},{2,18},{3,19},{4,20},{5,21},{6,22},{7,23},{8,24},{9,... | collective-permute-start | bytes 626696 | tf_op jit(solution)/shard_map/ppermute | solution.py:25
  (67 other events, 1506.1 us)
Sparse Core Ops, SparseCore 0:
  273.1 97.4 reduce-scatter.1
  373.4 61.3 all-gather.1

commit v8 on v7

--- a/solution.py
+++ b/solution.py
@@ -32,6 +32,32 @@
     return jax.tree.unflatten(treedef, out)
 
 
+def mean_and_var(block, axis):
+    count = lax.axis_size(axis)
+    frames = block.shape[0]
+    if count & (count - 1):
+        total = count * frames
+        mean = lax.psum(jnp.sum(block, axis=0), axis) / total
+        centred = block - mean
+        return mean, lax.psum(jnp.sum(centred * centred, axis=0), axis) / total
+    mean = jnp.mean(block, axis=0)
+    centred = block - mean
+    spread = jnp.sum(centred * centred, axis=0)
+    stats = jnp.stack([mean, spread])
+    rows, stride = frames, 1
+    while stride < count:
+        other = lax.ppermute(stats, axis, [(i, i ^ stride) for i in range(count)])
+        delta = stats[0] - other[0]
+        stats = jnp.stack(
+            [
+                (stats[0] + other[0]) * 0.5,
+                (stats[1] + other[1]) + (0.5 * rows) * (delta * delta),
+            ]
+        )
+        rows, stride = rows * 2, stride * 2
+    return stats[0], stats[1] / rows
+
+
 def group_shards(block, axis):
     far = lax.ppermute(block, axis, [(i, i ^ 2) for i in range(4)])
     near = lax.ppermute(block, axis, [(i, i ^ 1) for i in range(4)])
@@ -101,9 +127,8 @@
             + dw_kernel[offset]
             * padded_glu[kernel_len - 1 - offset : kernel_len - 1 - offset + tok_rows]
         )
-    chan_mean = tree_sum(jnp.sum(conv_out, axis=0), ("seq", "fsdp")) / all_frames
+    chan_mean, chan_var = mean_and_var(conv_out, ("seq", "fsdp"))
     conv_centred = conv_out - chan_mean
-    chan_var = tree_sum(jnp.sum(conv_centred * conv_centred, axis=0), ("seq", "fsdp")) / all_frames
     bn_rstd = lax.rsqrt(chan_var + epsilon)
     chat = conv_centred * bn_rstd
     z_value = chat * bn_gain + bn_bias

time: 447 us -> 427 us (0.955)
  waiting for transfers between devices: 276 us -> 264 us
  starting transfers between devices: 47.5 us -> 41.3 us
    ppermute x20 -> x10, starting transfers between devices: 32.7 us -> 13.5 us  [tree_sum(): packed = packed + lax.ppermute(packed, axis, route)]
    ppermute x20 -> x10, waiting for transfers between devices: 76 us -> 57.8 us  [tree_sum(): packed = packed + lax.ppermute(packed, axis, route)]
    ppermute x0 -> x5, starting transfers between devices: none -> 13 us  [mean_and_var(): other = lax.ppermute(stats, axis, [(i, i ^ stride) for i in range(count)])]
    ppermute x0 -> x5, waiting for transfers between devices: none -> 7.53 us  [mean_and_var(): other = lax.ppermute(stats, axis, [(i, i ^ stride) for i in range(count)])]
    another operation x2 -> x7, other arithmetic: 29.5 us -> 29.6 us
  transfers between devices with their start and end apart: 32 -> 27, of which waited for: 26 -> 21; matrix products, arithmetic and copies ran while one was open for 8% -> 8% of each run, Pallas kernels for 0% -> 0%
where the time goes in v8:
time: 427 us
  waiting for transfers between devices  264 us (62%)
  other arithmetic  69.9 us (16%)
  starting transfers between devices  41.3 us (10%)
  matrix products  23 us (5%)
  between operations  15.6 us (4%)
  local copies, waits for them, and re-layouts  12.8 us (3%)
    reduce_scatter x1, waiting for transfers between devices, on_device(): lax.psum_scatter(row_share, 'seq', scatter_dimension=0, tiled=True)  97.6 us
    ppermute x10, waiting for transfers between devices, tree_sum(): packed = packed + lax.ppermute(packed, axis, route)  57.8 us
    ppermute x1, waiting for transfers between devices, group_shards(): far = lax.ppermute(block, axis, [(i, i ^ 2) for i in range(4)])  48 us
    ppermute x1, waiting for transfers between devices, on_device(): far = lax.ppermute(grad_hidden, 'fsdp', [(i, i ^ 2) for i in range(4)])  31.9 us
    another operation x2, other arithmetic  29.5 us
    ppermute x1, waiting for transfers between devices, gather_own_columns(): lax.ppermute(jnp.concatenate([cols(me ^ 2), cols(me ^ 3)], axis=0), axis,...  13.5 us
    ppermute x10, starting transfers between devices, tree_sum(): packed = packed + lax.ppermute(packed, axis, route)  13.5 us
    ppermute x5, starting transfers between devices, mean_and_var(): other = lax.ppermute(stats, axis, [(i, i ^ stride) for i in range(count)])  13 us
  transfers between devices with their start and end apart: 27, of which 21 were waited for; matrix products, arithmetic and copies ran while one was open for 8% of the time, Pallas kernels for 0%

profile of v8, /device:TPU:0, one launch (start us, length us, event | category | flops | bytes accessed | tf_op | source)
XLA Modules:
  0.0 426.6 jit_solution(6386529906196035647)
XLA Ops:
  7.2 3.0 collective-permute-start
  13.7 48.0 %collective-permute-done = bf16[384,3072]{1,0:T(8,128)(2,1)S(1)} collective-permute-done((bf16[384,3072]{1,0:T(8,128)(2,1)}, bf16[384,3072]{1,0:T(8,128)(2,1)S(1)}, u32[]{:S(2)}, u32[]{:S(2)}) %collective-permute-start) | collective-permute-done | bytes 2359328 | tf_op jit(solution)/shard_map/ppermute | solution.py:62
  67.2 2.0 constant_dynamic-update-slice_fusion.1
  69.6 3.8 fusion.125
  75.6 2.6 collective-permute-start.3
  80.4 9.4 %fusion.124 = (f32[1536]{0:T(1024)S(1)}, f32[384,1536]{1,0:T(8,128)S(1)}) fusion(f32[415,1536]{1,0:T(8,128)S(1)} %maximum_convert_fusion, f32[1536]{0:T(1024)S(1)} %get-tuple-element.88, f32[1536]{0:T(1024)S(1)} %get-tuple-element.89, f32[1536]{0:T(1024)S(1)} %get-tuple-element.59, f32[1536]{0:T(1024)S(1)} %get-tuple-element.60, ...), kind=kLoop, calls=%fused_computation.307 | loop fusion | flops 37747200 | bytes 78059520 | tf_op jit(solution)/shard_map/reduce_sum | solution.py:43
  92.7 2.5 collective-permute-start.5
  96.9 3.0 collective-permute-start.6
  101.7 3.0 collective-permute-start.7
  106.5 3.1 collective-permute-start.8
  111.3 2.5 fusion.122
  115.2 3.7 collective-permute-done.10
  119.9 2.7 collective-permute-done.11
  126.5 3.0 collective-permute-start.13
  131.8 7.8 %multiply_reduce_fusion = (f32[1536]{0:T(1024)}, f32[1536]{0:T(1024)}, f32[1536]{0:T(1024)}, f32[1536]{0:T(1024)}, f32[1536]{0:T(1024)}, /*index=5*/f32[1536]{0:...) fusion(f32[415,1536]{1,0:T(8,128)S(1)} %maximum_convert_fusion,, ...), kind=kLoop, calls=%fused_computation.169 | loop fusion | flops 31822848 | bytes 48519168 | tf_op jit(solution)/shard_map/reduce_sum | solution.py:151
  142.9 25.5 %multiply_convert_fusion.1 = (bf16[384,1536]{1,0:T(8,128)(2,1)}, f32[384,1536]{1,0:T(8,128)}) fusion(f32[384,3072]{1,0:T(8,128)} %copy-done, f32[31,1536]{1,0:T(8,128)S(1)} %collective-permute-done.14, f32[384,1536]{1,0:T(8,128)S(1)} %get-tuple-element.107, f32[1536]{0:T(1024)} %copy-done.40, f32[1536]{0:T(1024)} %copy-done.41, ...), kind=kLoop, calls=%fused_computation.202 | loop fusion | flops 58392576 | bytes 8644608 | tf_op jit(solution)/shard_map/convert
  168.4 4.1 multiply_convert_fusion
  176.3 4.6 %multiply_reduce_fusion.18 = (f32[1536]{0:T(1024)S(1)}, f32[1536]{0:T(1024)S(1)}, f32[1536]{0:T(1024)S(1)}, f32[1536]{0:T(1024)S(1)}, f32[1536]{0:T(1024)S(1)}, ...) fusion(f32[384,1536]{1,0:T(8,128)S(1)} %get-tuple-element.107, ...), kind=kLoop, calls=%fused_computation.187 | loop fusion | flops 16493568 | bytes 35475456 | tf_op jit(solution)/shard_map/reduce_sum | solution.py:151
  181.8 2.5 collective-permute-start.18
  184.3 9.1 %fusion.11 = (f32[1536]{0:T(1024)S(1)}, f32[384]{0:T(512)S(1)}, f32[384]{0:T(512)S(1)}, f32[1536]{0:T(1024)S(1)}, f32[384,1536]{1,0:T(8,128)S(1)}) fusion(bf16[384,1536]{1,0:T(8,128)(2,1)} %param.8, f32[384]{0:T(512)} %copy-done.64, f32[384]{0:T(512)S(1)} %broadcast_multiply_fusion.3, f32[1536]{0:T(1024)S(1)} %copy-done.44, ...), kind=kOutput, calls=%fused_computation.44 | convolution fusion | flops 3634491392 | bytes 15360000 | tf_op jit(solution)/shard_map/dot_general | solution.py:161
  195.2 31.9 %collective-permute-done.15 = bf16[384,3072]{1,0:T(8,128)(2,1)} collective-permute-done((bf16[384,3072]{1,0:T(8,128)(2,1)}, bf16[384,3072]{1,0:T(8,128)(2,1)}, u32[]{:S(2)}, u32[]{:S(2)}) %collective-permute-start.15) | collective-permute-done | bytes 2359328 | tf_op jit(solution)/shard_map/ppermute | solution.py:179
  230.8 13.5 %collective-permute-done.16 = bf16[768,384]{1,0:T(8,128)(2,1)S(1)} collective-permute-done((bf16[768,384]{1,0:T(8,128)(2,1)S(1)}, bf16[768,384]{1,0:T(8,128)(2,1)S(1)}, u32[]{:S(2)}, u32[]{:S(2)}) %collective-permute-start.16) | collective-permute-done | bytes 589856 | tf_op jit(solution)/shard_map/ppermute | solution.py:92
  245.9 3.1 fusion.114
  250.5 4.1 add_add_fusion
  254.6 97.6 %reduce-scatter.2.cloned.1.call-done = f32[48,3072]{1,0:T(8,128)} async-done(((f32[384,3072]{1,0:T(8,128)}), f32[48,3072]{1,0:T(8,128)}) %reduce-scatter.2.cloned.1.call-update) | async-done | bytes 589840 | tf_op jit(solution)/shard_map/reduce_scatter | solution.py:200
  357.2 6.5 %collective-permute-done.21 = f32[34,1536]{1,0:T(8,128)S(1)} collective-permute-done((f32[34,1536]{1,0:T(8,128)S(1)}, f32[34,1536]{1,0:T(8,128)S(1)}, u32[]{:S(2)}, u32[]{:S(2)}) %collective-permute-start.21) | collective-permute-done | bytes 208928 | tf_op jit(solution)/shard_map/ppermute | solution.py:25
  365.3 8.5 %collective-permute-done.22 = f32[34,1536]{1,0:T(8,128)S(1)} collective-permute-done((f32[34,1536]{1,0:T(8,128)S(1)}, f32[34,1536]{1,0:T(8,128)S(1)}, u32[]{:S(2)}, u32[]{:S(2)}) %collective-permute-start.22) | collective-permute-done | bytes 208928 | tf_op jit(solution)/shard_map/ppermute | solution.py:25
  375.4 8.0 %collective-permute-done.23 = f32[34,1536]{1,0:T(8,128)S(1)} collective-permute-done((f32[34,1536]{1,0:T(8,128)S(1)}, f32[34,1536]{1,0:T(8,128)S(1)}, u32[]{:S(2)}, u32[]{:S(2)}) %collective-permute-start.23) | collective-permute-done | bytes 208928 | tf_op jit(solution)/shard_map/ppermute | solution.py:25
  383.4 2.7 collective-permute-start.24
  386.1 22.3 %collective-permute-done.24 = f32[34,1536]{1,0:T(8,128)S(1)} collective-permute-done((f32[34,1536]{1,0:T(8,128)S(1)}, f32[34,1536]{1,0:T(8,128)S(1)}, u32[]{:S(2)}, u32[]{:S(2)}) %collective-permute-start.24) | collective-permute-done | bytes 208928 | tf_op jit(solution)/shard_map/ppermute | solution.py:25
  409.7 5.6 %all-gather.2.cloned.1.call-done = bf16[384,3072]{1,0:T(8,128)(2,1)} async-done(((bf16[48,3072]{1,0:T(8,128)(2,1)}), bf16[384,3072]{1,0:T(8,128)(2,1)}) %all-gather.2.cloned.1.call-update) | async-done | bytes 2359312 | tf_op jit(solution)/shard_map/all_gather | solution.py:201
  415.4 4.4 %convert_element_type.36 = f32[384,3072]{1,0:T(8,128)} convert(bf16[384,3072]{1,0:T(8,128)(2,1)} %all-gather.2.cloned.1.call-done) | non-fusion elementwise | flops 1179648 | bytes 7077888 | tf_op jit(solution)/shard_map/convert_element_type | solution.py:203
  (262 shorter events, 57.0 us)
Async XLA Ops:
  7.2 345.0 %reduce-scatter.2.cloned.1.call-start = ((), (), s32[]{:S(2)}) async-start(), calls=%async_computation.1 | async-start | bytes 5308416 | tf_op jit(solution)/shard_map/reduce_scatter | solution.py:200
  7.2 54.5 %collective-permute-start = (bf16[384,3072]{1,0:T(8,128)(2,1)}, bf16[384,3072]{1,0:T(8,128)(2,1)S(1)}, u32[]{:S(2)}, u32[]{:S(2)}) collective-permute-start(bf16[384,3072]{1,0:T(8,128)(2,1)} %param.11), channel_id=1, source_target_pairs={{0,2},{1,3},{2,0},{3,1},{4,6},{5,7},{6,4},{7,5},{8,10},{9,11},{10,... | collective-permute-start | bytes 7077896 | tf_op jit(solution)/shard_map/ppermute | solution.py:62
  10.2 57.0 %collective-permute-start.1 = (bf16[384,3072]{1,0:T(8,128)(2,1)}, bf16[384,3072]{1,0:T(8,128)(2,1)}, u32[]{:S(2)}, u32[]{:S(2)}) collective-permute-start(bf16[384,3072]{1,0:T(8,128)(2,1)} %param.11), channel_id=1, source_target_pairs={{0,1},{1,0},{2,3},{3,2},{4,5},{5,4},{6,7},{7,6},{8,9},{9,8},{10,11... | collective-permute-start | bytes 7077896 | tf_op jit(solution)/shard_map/ppermute | solution.py:63
  12.1 68.2 %copy-start.13 = (f32[1536]{0:T(1024)}, f32[1536]{0:T(1024)S(1)}, u32[]{:S(2)}) copy-start(f32[1536]{0:T(1024)S(1)} %get-tuple-element.61) | copy-start | bytes 18436
  12.1 68.2 %copy-start.14 = (f32[1536]{0:T(1024)}, f32[1536]{0:T(1024)S(1)}, u32[]{:S(2)}) copy-start(f32[1536]{0:T(1024)S(1)} %get-tuple-element.62) | copy-start | bytes 18436
  12.1 68.2 %copy-start.15 = (f32[1536]{0:T(1024)}, f32[1536]{0:T(1024)S(1)}, u32[]{:S(2)}) copy-start(f32[1536]{0:T(1024)S(1)} %get-tuple-element.63) | copy-start | bytes 18436
  12.1 68.2 %copy-start.16 = (f32[1536]{0:T(1024)}, f32[1536]{0:T(1024)S(1)}, u32[]{:S(2)}) copy-start(f32[1536]{0:T(1024)S(1)} %get-tuple-element.64) | copy-start | bytes 18436
  12.1 68.2 %copy-start.17 = (f32[1536]{0:T(1024)}, f32[1536]{0:T(1024)S(1)}, u32[]{:S(2)}) copy-start(f32[1536]{0:T(1024)S(1)} %get-tuple-element.65) | copy-start | bytes 18436
  61.7 7.6 %collective-permute-start.2 = (bf16[384,3072]{1,0:T(8,128)(2,1)S(1)}, bf16[384,3072]{1,0:T(8,128)(2,1)S(1)}, u32[]{:S(2)}, u32[]{:S(2)}) collective-permute-start(bf16[384,3072]{1,0:T(8,128)(2,1)S(1)} %collective-permute-done), channel_id=1, source_target_pairs={{0,1},{1,0},{2,3},{3,2},{4,5},{5,4},{6,7},{7,6},{8,9},{9,8},{10,11... | collective-permute-start | bytes 7077896 | tf_op jit(solution)/shard_map/ppermute | solution.py:64
  75.6 4.3 %collective-permute-start.3 = (bf16[31,1536]{1,0:T(8,128)(2,1)S(1)}, bf16[31,1536]{1,0:T(8,128)(2,1)S(1)}, u32[]{:S(2)}, u32[]{:S(2)}) collective-permute-start(bf16[31,1536]{1,0:T(8,128)(2,1)S(1)} %slice.543), channel_id=1, source_target_pairs={{0,1},{1,2},{2,3},{3,4},{4,5},{5,6},{6,7},{7,8},{8,9},{9,10},{10,1... | collective-permute-start | bytes 285704 | tf_op jit(solution)/shard_map/ppermute | solution.py:12
  90.4 2.2 collective-permute-start.4
  92.7 4.1 collective-permute-start.5
  96.9 4.7 %collective-permute-start.6 = (f32[2,1536]{1,0:T(2,128)S(1)}, f32[2,1536]{1,0:T(2,128)S(1)}, u32[]{:S(2)}, u32[]{:S(2)}) collective-permute-start(f32[2,1536]{1,0:T(2,128)S(1)} %pad_maximum_fusion.7), channel_id=1, source_target_pairs={{0,4},{1,5},{2,6},{3,7},{4,0},{5,1},{6,2},{7,3},{8,12},{9,13},{10,... | collective-permute-start | bytes 36872 | tf_op jit(solution)/shard_map/ppermute | solution.py:49
  101.7 4.7 %collective-permute-start.7 = (f32[2,1536]{1,0:T(2,128)S(1)}, f32[2,1536]{1,0:T(2,128)S(1)}, u32[]{:S(2)}, u32[]{:S(2)}) collective-permute-start(f32[2,1536]{1,0:T(2,128)S(1)} %pad_maximum_fusion.8), channel_id=1, source_target_pairs={{0,8},{1,9},{2,10},{3,11},{4,12},{5,13},{6,14},{7,15},{8,0},{9,1},... | collective-permute-start | bytes 36872 | tf_op jit(solution)/shard_map/ppermute | solution.py:49
  106.5 4.8 %collective-permute-start.8 = (f32[2,1536]{1,0:T(2,128)S(1)}, f32[2,1536]{1,0:T(2,128)S(1)}, u32[]{:S(2)}, u32[]{:S(2)}) collective-permute-start(f32[2,1536]{1,0:T(2,128)S(1)} %pad_maximum_fusion.9), channel_id=1, source_target_pairs={{0,16},{1,17},{2,18},{3,19},{4,20},{5,21},{6,22},{7,23},{8,24},{9,... | collective-permute-start | bytes 36872 | tf_op jit(solution)/shard_map/ppermute | solution.py:49
  113.9 1.2 collective-permute-start.9
  115.1 3.8 collective-permute-start.10
  118.9 3.8 collective-permute-start.11
  122.7 3.8 collective-permute-start.12
  126.5 4.7 %collective-permute-start.13 = (f32[2,1536]{1,0:T(2,128)S(1)}, f32[2,1536]{1,0:T(2,128)S(1)}, u32[]{:S(2)}, u32[]{:S(2)}) collective-permute-start(f32[2,1536]{1,0:T(2,128)S(1)} %add.498), channel_id=1, source_target_pairs={{0,16},{1,17},{2,18},{3,19},{4,20},{5,21},{6,22},{7,23},{8,24},{9,... | collective-permute-start | bytes 36872 | tf_op jit(solution)/shard_map/ppermute | solution.py:25
  139.6 3.3 collective-permute-start.14
  174.4 52.7 %collective-permute-start.15 = (bf16[384,3072]{1,0:T(8,128)(2,1)}, bf16[384,3072]{1,0:T(8,128)(2,1)}, u32[]{:S(2)}, u32[]{:S(2)}) collective-permute-start(bf16[384,3072]{1,0:T(8,128)(2,1)} %pad_maximum_fusion.1), channel_id=1, source_target_pairs={{0,2},{1,3},{2,0},{3,1},{4,6},{5,7},{6,4},{7,5},{8,10},{9,11},{10,... | collective-permute-start | bytes 7077896 | tf_op jit(solution)/shard_map/ppermute | solution.py:179
  181.8 67.2 %collective-permute-start.18 = (bf16[384,3072]{1,0:T(8,128)(2,1)}, bf16[384,3072]{1,0:T(8,128)(2,1)S(1)}, u32[]{:S(2)}, u32[]{:S(2)}) collective-permute-start(bf16[384,3072]{1,0:T(8,128)(2,1)} %pad_maximum_fusion.1), channel_id=1, source_target_pairs={{0,1},{1,0},{2,3},{3,2},{4,5},{5,4},{6,7},{7,6},{8,9},{9,8},{10,11... | collective-permute-start | bytes 7077896 | tf_op jit(solution)/shard_map/ppermute | solution.py:180
  227.1 23.3 %collective-permute-start.19 = (bf16[384,3072]{1,0:T(8,128)(2,1)}, bf16[384,3072]{1,0:T(8,128)(2,1)S(1)}, u32[]{:S(2)}, u32[]{:S(2)}) collective-permute-start(bf16[384,3072]{1,0:T(8,128)(2,1)} %collective-permute-done.15), channel_id=1, source_target_pairs={{0,1},{1,0},{2,3},{3,2},{4,5},{5,4},{6,7},{7,6},{8,9},{9,8},{10,11... | collective-permute-start | bytes 7077896 | tf_op jit(solution)/shard_map/ppermute | solution.py:184
  228.9 15.4 %collective-permute-start.16 = (bf16[768,384]{1,0:T(8,128)(2,1)S(1)}, bf16[768,384]{1,0:T(8,128)(2,1)S(1)}, u32[]{:S(2)}, u32[]{:S(2)}) collective-permute-start(bf16[768,384]{1,0:T(8,128)(2,1)S(1)} %pad_maximum_fusion.2), channel_id=1, source_target_pairs={{0,2},{1,3},{2,0},{3,1},{4,6},{5,7},{6,4},{7,5},{8,10},{9,11},{10,... | collective-permute-start | bytes 1769480 | tf_op jit(solution)/shard_map/ppermute | solution.py:92
  244.4 4.6 %collective-permute-start.17 = (bf16[768,384]{1,0:T(8,128)(2,1)S(1)}, bf16[768,384]{1,0:T(8,128)(2,1)S(1)}, u32[]{:S(2)}, u32[]{:S(2)}) collective-permute-start(bf16[768,384]{1,0:T(8,128)(2,1)S(1)} %pad_maximum_fusion.3), channel_id=1, source_target_pairs={{0,1},{1,0},{2,3},{3,2},{4,5},{5,4},{6,7},{7,6},{8,9},{9,8},{10,11... | collective-permute-start | bytes 1769480 | tf_op jit(solution)/shard_map/ppermute | solution.py:95
  254.5 160.8 %all-gather.2.cloned.1.call-start = ((), (), s32[]{:S(2)}) async-start(), calls=%async_computation.2 | async-start | bytes 2654208 | tf_op jit(solution)/shard_map/all_gather | solution.py:201
  354.1 1.6 collective-permute-start.20
  355.7 8.1 %collective-permute-start.21 = (f32[34,1536]{1,0:T(8,128)S(1)}, f32[34,1536]{1,0:T(8,128)S(1)}, u32[]{:S(2)}, u32[]{:S(2)}) collective-permute-start(f32[34,1536]{1,0:T(8,128)S(1)} %fusion.120), channel_id=1, source_target_pairs={{0,2},{1,3},{2,0},{3,1},{4,6},{5,7},{6,4},{7,5},{8,10},{9,11},{10,... | collective-permute-start | bytes 626696 | tf_op jit(solution)/shard_map/ppermute | solution.py:25
  363.8 10.0 %collective-permute-start.22 = (f32[34,1536]{1,0:T(8,128)S(1)}, f32[34,1536]{1,0:T(8,128)S(1)}, u32[]{:S(2)}, u32[]{:S(2)}) collective-permute-start(f32[34,1536]{1,0:T(8,128)S(1)} %add.535), channel_id=1, source_target_pairs={{0,4},{1,5},{2,6},{3,7},{4,0},{5,1},{6,2},{7,3},{8,12},{9,13},{10,... | collective-permute-start | bytes 626696 | tf_op jit(solution)/shard_map/ppermute | solution.py:25
  373.9 9.5 %collective-permute-start.23 = (f32[34,1536]{1,0:T(8,128)S(1)}, f32[34,1536]{1,0:T(8,128)S(1)}, u32[]{:S(2)}, u32[]{:S(2)}) collective-permute-start(f32[34,1536]{1,0:T(8,128)S(1)} %add.536), channel_id=1, source_target_pairs={{0,8},{1,9},{2,10},{3,11},{4,12},{5,13},{6,14},{7,15},{8,0},{9,1},... | collective-permute-start | bytes 626696 | tf_op jit(solution)/shard_map/ppermute | solution.py:25
  383.4 25.0 %collective-permute-start.24 = (f32[34,1536]{1,0:T(8,128)S(1)}, f32[34,1536]{1,0:T(8,128)S(1)}, u32[]{:S(2)}, u32[]{:S(2)}) collective-permute-start(f32[34,1536]{1,0:T(8,128)S(1)} %add.537), channel_id=1, source_target_pairs={{0,16},{1,17},{2,18},{3,19},{4,20},{5,21},{6,22},{7,23},{8,24},{9,... | collective-permute-start | bytes 626696 | tf_op jit(solution)/shard_map/ppermute | solution.py:25
  (62 other events, 1203.2 us)
Sparse Core Ops, SparseCore 0:
  254.7 97.4 reduce-scatter.1
  354.9 60.4 all-gather.1

commit v9 on v7

--- a/solution.py
+++ b/solution.py
@@ -32,6 +32,66 @@
     return jax.tree.unflatten(treedef, out)
 
 
+def exchange(x, axis):
+    count = lax.axis_size(axis)
+    got = [x] + [
+        lax.ppermute(x, axis, [(i, i ^ k) for i in range(count)]) for k in range(1, count)
+    ]
+    return jnp.take(jnp.stack(got), lax.axis_index(axis) ^ jnp.arange(count), axis=0)
+
+
+def combine(x, axes, merge, rows):
+    for axis in axes:
+        count = lax.axis_size(axis)
+        if count in (2, 4, 8):
+            items = list(exchange(x, axis))
+            while len(items) > 1:
+                items = [merge(items[j], items[j + 1], rows) for j in range(0, len(items), 2)]
+                rows *= 2
+            x = items[0]
+        else:
+            stride = 1
+            while stride < count:
+                other = lax.ppermute(x, axis, [(i, i ^ stride) for i in range(count)])
+                x = merge(x, other, rows)
+                rows, stride = rows * 2, stride * 2
+    return x, rows
+
+
+def pair_stats(a, b, rows):
+    delta = a[0] - b[0]
+    return jnp.stack([(a[0] + b[0]) * 0.5, (a[1] + b[1]) + (0.5 * rows) * (delta * delta)])
+
+
+def mean_and_var(block, axes):
+    if any(lax.axis_size(a) & (lax.axis_size(a) - 1) for a in axes):
+        total = block.shape[0] * lax.axis_size(axes)
+        mean = lax.psum(jnp.sum(block, axis=0), axes) / total
+        centred = block - mean
+        return mean, lax.psum(jnp.sum(centred * centred, axis=0), axes) / total
+    mean = jnp.mean(block, axis=0)
+    centred = block - mean
+    stats, rows = combine(
+        jnp.stack([mean, jnp.sum(centred * centred, axis=0)]), axes, pair_stats, block.shape[0]
+    )
+    return stats[0], stats[1] / rows
+
+
+def fast_sum(tree, axes):
+    if any(lax.axis_size(a) & (lax.axis_size(a) - 1) for a in axes):
+        return lax.psum(tree, axes)
+    leaves, treedef = jax.tree.flatten(tree)
+    width = leaves[0].shape[-1]
+    packed = jnp.concatenate([leaf.reshape(-1, width) for leaf in leaves], axis=0)
+    packed, _ = combine(packed, axes, lambda a, b, rows: a + b, 1)
+    out, start = [], 0
+    for leaf in leaves:
+        count = leaf.size // width
+        out.append(packed[start : start + count].reshape(leaf.shape))
+        start += count
+    return jax.tree.unflatten(treedef, out)
+
+
 def group_shards(block, axis):
     far = lax.ppermute(block, axis, [(i, i ^ 2) for i in range(4)])
     near = lax.ppermute(block, axis, [(i, i ^ 1) for i in range(4)])
@@ -101,17 +161,16 @@
             + dw_kernel[offset]
             * padded_glu[kernel_len - 1 - offset : kernel_len - 1 - offset + tok_rows]
         )
-    chan_mean = tree_sum(jnp.sum(conv_out, axis=0), ("seq", "fsdp")) / all_frames
+    chan_mean, chan_var = mean_and_var(conv_out, ("fsdp", "seq"))
     conv_centred = conv_out - chan_mean
-    chan_var = tree_sum(jnp.sum(conv_centred * conv_centred, axis=0), ("seq", "fsdp")) / all_frames
     bn_rstd = lax.rsqrt(chan_var + epsilon)
     chat = conv_centred * bn_rstd
     z_value = chat * bn_gain + bn_bias
     z_sig = jax.nn.sigmoid(z_value)
     output = (z_value * z_sig).astype(jnp.bfloat16)
     grad_z = cotangent.astype(jnp.float32) * z_sig * (1.0 + z_value * (1.0 - z_sig))
-    grad_bn_bias, grad_bn_gain = tree_sum(
-        (jnp.sum(grad_z, axis=0), jnp.sum(grad_z * chat, axis=0)), ("seq", "fsdp")
+    grad_bn_bias, grad_bn_gain = fast_sum(
+        (jnp.sum(grad_z, axis=0), jnp.sum(grad_z * chat, axis=0)), ("fsdp", "seq")
     )
     grad_conv = (
         bn_gain * bn_rstd * (grad_z - grad_bn_bias / all_frames - chat * grad_bn_gain / all_frames)

time: 447 us -> 440 us (0.984)
  waiting for transfers between devices: 276 us -> 259 us
    ppermute x0 -> x20, starting transfers between devices: none -> 29.7 us  [exchange(): lax.ppermute(x, axis, [(i, i ^ k) for i in range(count)])]
    ppermute x20 -> x5, waiting for transfers between devices: 76 us -> 47 us  [tree_sum(): packed = packed + lax.ppermute(packed, axis, route)]
    ppermute x20 -> x5, starting transfers between devices: 32.7 us -> 7.4 us  [tree_sum(): packed = packed + lax.ppermute(packed, axis, route)]
    ppermute x0 -> x20, waiting for transfers between devices: none -> 13.8 us  [exchange(): lax.ppermute(x, axis, [(i, i ^ k) for i in range(count)])]
    another operation x2 -> x7, other arithmetic: 29.5 us -> 29.6 us
  transfers between devices with their start and end apart: 32 -> 37, of which waited for: 26 -> 21; matrix products, arithmetic and copies ran while one was open for 8% -> 8% of each run, Pallas kernels for 0% -> 0%
where the time goes in v9:
time: 440 us; the launch traced here: 439 us
  waiting for transfers between devices  259 us (59%)
  other arithmetic  72.1 us (16%)
  starting transfers between devices  51.6 us (12%)
  matrix products  23 us (5%)
  local copies, waits for them, and re-layouts  18.2 us (4%)
  between operations  15.7 us (4%)
    reduce_scatter x1, waiting for transfers between devices, on_device(): lax.psum_scatter(row_share, 'seq', scatter_dimension=0, tiled=True)  96.9 us
    ppermute x5, waiting for transfers between devices, tree_sum(): packed = packed + lax.ppermute(packed, axis, route)  47 us
    ppermute x1, waiting for transfers between devices, group_shards(): far = lax.ppermute(block, axis, [(i, i ^ 2) for i in range(4)])  46.3 us
    ppermute x1, waiting for transfers between devices, on_device(): far = lax.ppermute(grad_hidden, 'fsdp', [(i, i ^ 2) for i in range(4)])  33.1 us
    ppermute x20, starting transfers between devices, exchange(): lax.ppermute(x, axis, [(i, i ^ k) for i in range(count)])  29.7 us
    another operation x2, other arithmetic  29.5 us
    ppermute x20, waiting for transfers between devices, exchange(): lax.ppermute(x, axis, [(i, i ^ k) for i in range(count)])  13.8 us
    ppermute x1, waiting for transfers between devices, gather_own_columns(): lax.ppermute(jnp.concatenate([cols(me ^ 2), cols(me ^ 3)], axis=0), axis,...  13.5 us
  transfers between devices with their start and end apart: 37, of which 21 were waited for; matrix products, arithmetic and copies ran while one was open for 8% of the time, Pallas kernels for 0%

profile of v9, /device:TPU:0, one launch (start us, length us, event | category | flops | bytes accessed | tf_op | source)
XLA Modules:
  0.0 439.5 jit_solution(12541997392391092798)
XLA Ops:
  7.2 3.0 collective-permute-start
  15.4 46.3 %collective-permute-done = bf16[384,3072]{1,0:T(8,128)(2,1)} collective-permute-done((bf16[384,3072]{1,0:T(8,128)(2,1)}, bf16[384,3072]{1,0:T(8,128)(2,1)}, u32[]{:S(2)}, u32[]{:S(2)}) %collective-permute-start) | collective-permute-done | bytes 2359328 | tf_op jit(solution)/shard_map/ppermute | solution.py:96
  65.2 2.4 constant_dynamic-update-slice_fusion.18
  69.9 3.8 fusion.140
  75.9 2.6 collective-permute-start.3
  79.9 9.4 %fusion.139 = (f32[1536]{0:T(1024)S(1)}, f32[384,1536]{1,0:T(8,128)S(1)}) fusion(f32[415,1536]{1,0:T(8,128)S(1)} %maximum_convert_fusion, f32[1536]{0:T(1024)S(1)} %get-tuple-element.90, f32[1536]{0:T(1024)S(1)} %get-tuple-element.91, f32[1536]{0:T(1024)S(1)} %get-tuple-element.61, f32[1536]{0:T(1024)S(1)} %get-tuple-element.62, ...), kind=kLoop, calls=%fused_computation.353 | loop fusion | flops 37747200 | bytes 78059520 | tf_op jit(solution)/shard_map/reduce_sum | solution.py:72
  91.1 2.1 collective-permute-start.4
  93.2 2.4 collective-permute-start.5
  103.6 3.0 collective-permute-start.10
  107.1 3.6 collective-permute-start.12
  112.6 4.5 %collective-permute-done.13 = f32[2,1536]{1,0:T(2,128)S(1)} collective-permute-done((f32[2,1536]{1,0:T(2,128)S(1)}, f32[2,1536]{1,0:T(2,128)S(1)}, u32[]{:S(2)}, u32[]{:S(2)}) %collective-permute-start.13) | collective-permute-done | bytes 12320 | tf_op jit(solution)/shard_map/ppermute | solution.py:38
  118.1 4.5 %fusion.136 = (f32[1536]{0:T(1024)S(1)}, f32[1536]{0:T(1024)S(1)}, bf16[384,1536]{1,0:T(8,128)(2,1)}) fusion(f32[1536]{0:T(1024)S(1)} %copy-done.42, f32[1536]{0:T(1024)S(1)} %copy-done.12, f32[1536]{0:T(1024)S(1)} %get-tuple-element.96, f32[384,1536]{1,0:T(8,128)} %copy-done, f32[1536]{0:T(1024)S(1)} %get-tuple-element.95, bf16[384,1536]{1,0:T(8,128)(2,1)} %param.19), kind=kLoop, calls=%fused_computation.352 | loop fusion | flops 10613760 | bytes 4755456 | tf_op jit(solution)/shard_map/reduce_sum | solution.py:173
  131.5 3.8 collective-permute-start.21
  135.3 3.8 collective-permute-start.23
  143.2 8.9 %multiply_reduce_fusion = (f32[1536]{0:T(1024)}, f32[1536]{0:T(1024)}, f32[1536]{0:T(1024)}, f32[1536]{0:T(1024)}, f32[1536]{0:T(1024)}, /*index=5*/f32[1536]{0:...) fusion(f32[415,1536]{1,0:T(8,128)S(1)} %maximum_convert_fusion,, ...), kind=kLoop, calls=%fused_computation.173 | loop fusion | flops 31822848 | bytes 48519168 | tf_op jit(solution)/shard_map/reduce_sum | solution.py:185
  155.5 25.5 %multiply_convert_fusion.1 = (bf16[384,1536]{1,0:T(8,128)(2,1)}, f32[384,1536]{1,0:T(8,128)}) fusion(f32[384,3072]{1,0:T(8,128)} %copy-done.1, f32[31,1536]{1,0:T(8,128)S(1)} %collective-permute-done.24, f32[384,1536]{1,0:T(8,128)S(1)} %get-tuple-element.97, f32[1536]{0:T(1024)} %copy-done.21, f32[1536]{0:T(1024)} %copy-done.22, f32[1536]{0:T(1024)} %copy-done.24, ...), kind=kLoop, calls=%fused_computation.206 | loop fusion | flops 58392576 | bytes 8644608 | tf_op jit(solution)/shard_map/convert
  180.9 4.1 multiply_convert_fusion
  187.0 2.5 collective-permute-start.25
  189.5 4.6 %multiply_reduce_fusion.18 = (f32[1536]{0:T(1024)S(1)}, f32[1536]{0:T(1024)S(1)}, f32[1536]{0:T(1024)S(1)}, f32[1536]{0:T(1024)S(1)}, f32[1536]{0:T(1024)S(1)}, ...) fusion(f32[384,1536]{1,0:T(8,128)S(1)} %get-tuple-element.97, ...), kind=kLoop, calls=%fused_computation.191 | loop fusion | flops 16493568 | bytes 35475456 | tf_op jit(solution)/shard_map/reduce_sum | solution.py:185
  196.7 9.1 %fusion.11 = (f32[1536]{0:T(1024)S(1)}, f32[384]{0:T(512)S(1)}, f32[384]{0:T(512)S(1)}, f32[1536]{0:T(1024)S(1)}, f32[384,1536]{1,0:T(8,128)S(1)}) fusion(bf16[384,1536]{1,0:T(8,128)(2,1)} %param.12, f32[384]{0:T(512)} %copy-done.64, f32[384]{0:T(512)S(1)} %broadcast_multiply_fusion.3, f32[1536]{0:T(1024)S(1)} %copy-done.44, ...), kind=kOutput, calls=%fused_computation.48 | convolution fusion | flops 3634491392 | bytes 15360000 | tf_op jit(solution)/shard_map/dot_general | solution.py:195
  207.6 33.1 %collective-permute-done.25 = bf16[384,3072]{1,0:T(8,128)(2,1)} collective-permute-done((bf16[384,3072]{1,0:T(8,128)(2,1)}, bf16[384,3072]{1,0:T(8,128)(2,1)}, u32[]{:S(2)}, u32[]{:S(2)}) %collective-permute-start.25) | collective-permute-done | bytes 2359328 | tf_op jit(solution)/shard_map/ppermute | solution.py:213
  244.0 13.5 %collective-permute-done.26 = bf16[768,384]{1,0:T(8,128)(2,1)S(1)} collective-permute-done((bf16[768,384]{1,0:T(8,128)(2,1)S(1)}, bf16[768,384]{1,0:T(8,128)(2,1)S(1)}, u32[]{:S(2)}, u32[]{:S(2)}) %collective-permute-start.26) | collective-permute-done | bytes 589856 | tf_op jit(solution)/shard_map/ppermute | solution.py:126
  259.1 3.1 fusion.114
  263.7 4.1 add_add_fusion
  267.9 96.9 %reduce-scatter.2.cloned.1.call-done = f32[48,3072]{1,0:T(8,128)} async-done(((f32[384,3072]{1,0:T(8,128)}), f32[48,3072]{1,0:T(8,128)}) %reduce-scatter.2.cloned.1.call-update) | async-done | bytes 589840 | tf_op jit(solution)/shard_map/reduce_scatter | solution.py:234
  369.8 6.5 %collective-permute-done.31 = f32[34,1536]{1,0:T(8,128)S(1)} collective-permute-done((f32[34,1536]{1,0:T(8,128)S(1)}, f32[34,1536]{1,0:T(8,128)S(1)}, u32[]{:S(2)}, u32[]{:S(2)}) %collective-permute-start.31) | collective-permute-done | bytes 208928 | tf_op jit(solution)/shard_map/ppermute | solution.py:25
  377.9 8.5 %collective-permute-done.32 = f32[34,1536]{1,0:T(8,128)S(1)} collective-permute-done((f32[34,1536]{1,0:T(8,128)S(1)}, f32[34,1536]{1,0:T(8,128)S(1)}, u32[]{:S(2)}, u32[]{:S(2)}) %collective-permute-start.32) | collective-permute-done | bytes 208928 | tf_op jit(solution)/shard_map/ppermute | solution.py:25
  388.0 8.0 %collective-permute-done.33 = f32[34,1536]{1,0:T(8,128)S(1)} collective-permute-done((f32[34,1536]{1,0:T(8,128)S(1)}, f32[34,1536]{1,0:T(8,128)S(1)}, u32[]{:S(2)}, u32[]{:S(2)}) %collective-permute-start.33) | collective-permute-done | bytes 208928 | tf_op jit(solution)/shard_map/ppermute | solution.py:25
  396.0 2.7 collective-permute-start.34
  398.7 22.5 %collective-permute-done.34 = f32[34,1536]{1,0:T(8,128)S(1)} collective-permute-done((f32[34,1536]{1,0:T(8,128)S(1)}, f32[34,1536]{1,0:T(8,128)S(1)}, u32[]{:S(2)}, u32[]{:S(2)}) %collective-permute-start.34) | collective-permute-done | bytes 208928 | tf_op jit(solution)/shard_map/ppermute | solution.py:25
  422.5 5.7 %all-gather.2.cloned.1.call-done = bf16[384,3072]{1,0:T(8,128)(2,1)} async-done(((bf16[48,3072]{1,0:T(8,128)(2,1)}), bf16[384,3072]{1,0:T(8,128)(2,1)}) %all-gather.2.cloned.1.call-update) | async-done | bytes 2359312 | tf_op jit(solution)/shard_map/all_gather | solution.py:235
  428.2 4.4 %convert_element_type.36 = f32[384,3072]{1,0:T(8,128)} convert(bf16[384,3072]{1,0:T(8,128)(2,1)} %all-gather.2.cloned.1.call-done) | non-fusion elementwise | flops 1179648 | bytes 7077888 | tf_op jit(solution)/shard_map/convert_element_type | solution.py:237
  (305 shorter events, 65.0 us)
Async XLA Ops:
  7.2 357.6 %reduce-scatter.2.cloned.1.call-start = ((), (), s32[]{:S(2)}) async-start(), calls=%async_computation.1 | async-start | bytes 5308416 | tf_op jit(solution)/shard_map/reduce_scatter | solution.py:234
  7.2 54.6 %collective-permute-start = (bf16[384,3072]{1,0:T(8,128)(2,1)}, bf16[384,3072]{1,0:T(8,128)(2,1)}, u32[]{:S(2)}, u32[]{:S(2)}) collective-permute-start(bf16[384,3072]{1,0:T(8,128)(2,1)} %param.15), channel_id=1, source_target_pairs={{0,2},{1,3},{2,0},{3,1},{4,6},{5,7},{6,4},{7,5},{8,10},{9,11},{10,... | collective-permute-start | bytes 7077896 | tf_op jit(solution)/shard_map/ppermute | solution.py:96
  10.2 57.3 %collective-permute-start.1 = (bf16[384,3072]{1,0:T(8,128)(2,1)}, bf16[384,3072]{1,0:T(8,128)(2,1)}, u32[]{:S(2)}, u32[]{:S(2)}) collective-permute-start(bf16[384,3072]{1,0:T(8,128)(2,1)} %param.15), channel_id=1, source_target_pairs={{0,1},{1,0},{2,3},{3,2},{4,5},{5,4},{6,7},{7,6},{8,9},{9,8},{10,11... | collective-permute-start | bytes 7077896 | tf_op jit(solution)/shard_map/ppermute | solution.py:97
  61.8 7.7 %collective-permute-start.2 = (bf16[384,3072]{1,0:T(8,128)(2,1)}, bf16[384,3072]{1,0:T(8,128)(2,1)S(1)}, u32[]{:S(2)}, u32[]{:S(2)}) collective-permute-start(bf16[384,3072]{1,0:T(8,128)(2,1)} %collective-permute-done), channel_id=1, source_target_pairs={{0,1},{1,0},{2,3},{3,2},{4,5},{5,4},{6,7},{7,6},{8,9},{9,8},{10,11... | collective-permute-start | bytes 7077896 | tf_op jit(solution)/shard_map/ppermute | solution.py:98
  75.9 3.3 collective-permute-start.3
  91.1 4.6 %collective-permute-start.4 = (f32[2,1536]{1,0:T(2,128)S(1)}, f32[2,1536]{1,0:T(2,128)S(1)}, u32[]{:S(2)}, u32[]{:S(2)}) collective-permute-start(f32[2,1536]{1,0:T(2,128)S(1)} %get-tuple-element.115), channel_id=1, source_target_pairs={{0,1},{1,0},{2,3},{3,2},{4,5},{5,4},{6,7},{7,6},{8,9},{9,8},{10,11... | collective-permute-start | bytes 36872 | tf_op jit(solution)/shard_map/ppermute | solution.py:38
  93.2 4.0 collective-permute-start.5
  99.5 7.6 %collective-permute-start.7 = (f32[2,1536]{1,0:T(2,128)S(1)}, f32[2,1536]{1,0:T(2,128)S(1)}, u32[]{:S(2)}, u32[]{:S(2)}) collective-permute-start(f32[2,1536]{1,0:T(2,128)S(1)} %pad_maximum_fusion.8), channel_id=1, source_target_pairs={{0,4},{4,0},{8,12},{12,8},{16,20},{20,16},{24,28},{28,24},{1,5},{5... | collective-permute-start | bytes 36872 | tf_op jit(solution)/shard_map/ppermute | solution.py:38
  101.2 9.5 %collective-permute-start.8 = (f32[2,1536]{1,0:T(2,128)S(1)}, f32[2,1536]{1,0:T(2,128)S(1)}, u32[]{:S(2)}, u32[]{:S(2)}) collective-permute-start(f32[2,1536]{1,0:T(2,128)S(1)} %pad_maximum_fusion.8), channel_id=1, source_target_pairs={{0,8},{4,12},{8,0},{12,4},{16,24},{20,28},{24,16},{28,20},{1,9},{5... | collective-permute-start | bytes 36872 | tf_op jit(solution)/shard_map/ppermute | solution.py:38
  102.8 8.7 %collective-permute-start.9 = (f32[2,1536]{1,0:T(2,128)S(1)}, f32[2,1536]{1,0:T(2,128)S(1)}, u32[]{:S(2)}, u32[]{:S(2)}) collective-permute-start(f32[2,1536]{1,0:T(2,128)S(1)} %pad_maximum_fusion.8), channel_id=1, source_target_pairs={{0,12},{4,8},{8,4},{12,0},{16,28},{20,24},{24,20},{28,16},{1,13},{... | collective-permute-start | bytes 36872 | tf_op jit(solution)/shard_map/ppermute | solution.py:38
  103.6 7.9 %collective-permute-start.10 = (f32[2,1536]{1,0:T(2,128)S(1)}, f32[2,1536]{1,0:T(2,128)S(1)}, u32[]{:S(2)}, u32[]{:S(2)}) collective-permute-start(f32[2,1536]{1,0:T(2,128)S(1)} %pad_maximum_fusion.8), channel_id=1, source_target_pairs={{0,16},{4,20},{8,24},{12,28},{16,0},{20,4},{24,8},{28,12},{1,17},{... | collective-permute-start | bytes 36872 | tf_op jit(solution)/shard_map/ppermute | solution.py:38
  106.6 5.5 %collective-permute-start.11 = (f32[2,1536]{1,0:T(2,128)S(1)}, f32[2,1536]{1,0:T(2,128)S(1)}, u32[]{:S(2)}, u32[]{:S(2)}) collective-permute-start(f32[2,1536]{1,0:T(2,128)S(1)} %pad_maximum_fusion.8), channel_id=1, source_target_pairs={{0,20},{4,16},{8,28},{12,24},{16,4},{20,0},{24,12},{28,8},{1,21},{... | collective-permute-start | bytes 36872 | tf_op jit(solution)/shard_map/ppermute | solution.py:38
  107.1 5.5 %collective-permute-start.12 = (f32[2,1536]{1,0:T(2,128)S(1)}, f32[2,1536]{1,0:T(2,128)S(1)}, u32[]{:S(2)}, u32[]{:S(2)}) collective-permute-start(f32[2,1536]{1,0:T(2,128)S(1)} %pad_maximum_fusion.8), channel_id=1, source_target_pairs={{0,24},{4,28},{8,16},{12,20},{16,8},{20,12},{24,0},{28,4},{1,25},{... | collective-permute-start | bytes 36872 | tf_op jit(solution)/shard_map/ppermute | solution.py:38
  110.7 6.4 %collective-permute-start.13 = (f32[2,1536]{1,0:T(2,128)S(1)}, f32[2,1536]{1,0:T(2,128)S(1)}, u32[]{:S(2)}, u32[]{:S(2)}) collective-permute-start(f32[2,1536]{1,0:T(2,128)S(1)} %pad_maximum_fusion.8), channel_id=1, source_target_pairs={{0,28},{4,24},{8,20},{12,16},{16,12},{20,8},{24,4},{28,0},{1,29},{... | collective-permute-start | bytes 36872 | tf_op jit(solution)/shard_map/ppermute | solution.py:38
  122.7 3.8 collective-permute-start.15
  127.9 7.3 %collective-permute-start.17 = (f32[2,1536]{1,0:T(2,128)S(1)}, f32[2,1536]{1,0:T(2,128)S(1)}, u32[]{:S(2)}, u32[]{:S(2)}) collective-permute-start(f32[2,1536]{1,0:T(2,128)S(1)} %bitcast.51), channel_id=1, source_target_pairs={{0,4},{4,0},{8,12},{12,8},{16,20},{20,16},{24,28},{28,24},{1,5},{5... | collective-permute-start | bytes 36872 | tf_op jit(solution)/shard_map/ppermute | solution.py:38
  129.4 5.9 %collective-permute-start.18 = (f32[2,1536]{1,0:T(2,128)S(1)}, f32[2,1536]{1,0:T(2,128)S(1)}, u32[]{:S(2)}, u32[]{:S(2)}) collective-permute-start(f32[2,1536]{1,0:T(2,128)S(1)} %bitcast.52), channel_id=1, source_target_pairs={{0,8},{4,12},{8,0},{12,4},{16,24},{20,28},{24,16},{28,20},{1,9},{5... | collective-permute-start | bytes 36872 | tf_op jit(solution)/shard_map/ppermute | solution.py:38
  129.4 9.8 %collective-permute-start.19 = (f32[2,1536]{1,0:T(2,128)S(1)}, f32[2,1536]{1,0:T(2,128)S(1)}, u32[]{:S(2)}, u32[]{:S(2)}) collective-permute-start(f32[2,1536]{1,0:T(2,128)S(1)} %bitcast.53), channel_id=1, source_target_pairs={{0,12},{4,8},{8,4},{12,0},{16,28},{20,24},{24,20},{28,16},{1,13},{... | collective-permute-start | bytes 36872 | tf_op jit(solution)/shard_map/ppermute | solution.py:38
  131.5 7.7 %collective-permute-start.20 = (f32[2,1536]{1,0:T(2,128)S(1)}, f32[2,1536]{1,0:T(2,128)S(1)}, u32[]{:S(2)}, u32[]{:S(2)}) collective-permute-start(f32[2,1536]{1,0:T(2,128)S(1)} %bitcast.54), channel_id=1, source_target_pairs={{0,16},{4,20},{8,24},{12,28},{16,0},{20,4},{24,8},{28,12},{1,17},{... | collective-permute-start | bytes 36872 | tf_op jit(solution)/shard_map/ppermute | solution.py:38
  131.5 7.7 %collective-permute-start.21 = (f32[2,1536]{1,0:T(2,128)S(1)}, f32[2,1536]{1,0:T(2,128)S(1)}, u32[]{:S(2)}, u32[]{:S(2)}) collective-permute-start(f32[2,1536]{1,0:T(2,128)S(1)} %bitcast.55), channel_id=1, source_target_pairs={{0,20},{4,16},{8,28},{12,24},{16,4},{20,0},{24,12},{28,8},{1,21},{... | collective-permute-start | bytes 36872 | tf_op jit(solution)/shard_map/ppermute | solution.py:38
  135.3 5.5 %collective-permute-start.22 = (f32[2,1536]{1,0:T(2,128)S(1)}, f32[2,1536]{1,0:T(2,128)S(1)}, u32[]{:S(2)}, u32[]{:S(2)}) collective-permute-start(f32[2,1536]{1,0:T(2,128)S(1)} %bitcast.56), channel_id=1, source_target_pairs={{0,24},{4,28},{8,16},{12,20},{16,8},{20,12},{24,0},{28,4},{1,25},{... | collective-permute-start | bytes 36872 | tf_op jit(solution)/shard_map/ppermute | solution.py:38
  135.3 6.4 %collective-permute-start.23 = (f32[2,1536]{1,0:T(2,128)S(1)}, f32[2,1536]{1,0:T(2,128)S(1)}, u32[]{:S(2)}, u32[]{:S(2)}) collective-permute-start(f32[2,1536]{1,0:T(2,128)S(1)} %bitcast.57), channel_id=1, source_target_pairs={{0,28},{4,24},{8,20},{12,16},{16,12},{20,8},{24,4},{28,0},{1,29},{... | collective-permute-start | bytes 36872 | tf_op jit(solution)/shard_map/ppermute | solution.py:38
  187.0 53.7 %collective-permute-start.25 = (bf16[384,3072]{1,0:T(8,128)(2,1)}, bf16[384,3072]{1,0:T(8,128)(2,1)}, u32[]{:S(2)}, u32[]{:S(2)}) collective-permute-start(bf16[384,3072]{1,0:T(8,128)(2,1)} %pad_maximum_fusion.1), channel_id=1, source_target_pairs={{0,2},{1,3},{2,0},{3,1},{4,6},{5,7},{6,4},{7,5},{8,10},{9,11},{10,... | collective-permute-start | bytes 7077896 | tf_op jit(solution)/shard_map/ppermute | solution.py:213
  195.1 67.2 %collective-permute-start.28 = (bf16[384,3072]{1,0:T(8,128)(2,1)}, bf16[384,3072]{1,0:T(8,128)(2,1)S(1)}, u32[]{:S(2)}, u32[]{:S(2)}) collective-permute-start(bf16[384,3072]{1,0:T(8,128)(2,1)} %pad_maximum_fusion.1), channel_id=1, source_target_pairs={{0,1},{1,0},{2,3},{3,2},{4,5},{5,4},{6,7},{7,6},{8,9},{9,8},{10,11... | collective-permute-start | bytes 7077896 | tf_op jit(solution)/shard_map/ppermute | solution.py:214
  240.7 23.0 %collective-permute-start.29 = (bf16[384,3072]{1,0:T(8,128)(2,1)}, bf16[384,3072]{1,0:T(8,128)(2,1)S(1)}, u32[]{:S(2)}, u32[]{:S(2)}) collective-permute-start(bf16[384,3072]{1,0:T(8,128)(2,1)} %collective-permute-done.25), channel_id=1, source_target_pairs={{0,1},{1,0},{2,3},{3,2},{4,5},{5,4},{6,7},{7,6},{8,9},{9,8},{10,11... | collective-permute-start | bytes 7077896 | tf_op jit(solution)/shard_map/ppermute | solution.py:218
  241.9 15.6 %collective-permute-start.26 = (bf16[768,384]{1,0:T(8,128)(2,1)S(1)}, bf16[768,384]{1,0:T(8,128)(2,1)S(1)}, u32[]{:S(2)}, u32[]{:S(2)}) collective-permute-start(bf16[768,384]{1,0:T(8,128)(2,1)S(1)} %pad_maximum_fusion.2), channel_id=1, source_target_pairs={{0,2},{1,3},{2,0},{3,1},{4,6},{5,7},{6,4},{7,5},{8,10},{9,11},{10,... | collective-permute-start | bytes 1769480 | tf_op jit(solution)/shard_map/ppermute | solution.py:126
  257.6 4.6 %collective-permute-start.27 = (bf16[768,384]{1,0:T(8,128)(2,1)S(1)}, bf16[768,384]{1,0:T(8,128)(2,1)S(1)}, u32[]{:S(2)}, u32[]{:S(2)}) collective-permute-start(bf16[768,384]{1,0:T(8,128)(2,1)S(1)} %pad_maximum_fusion.3), channel_id=1, source_target_pairs={{0,1},{1,0},{2,3},{3,2},{4,5},{5,4},{6,7},{7,6},{8,9},{9,8},{10,11... | collective-permute-start | bytes 1769480 | tf_op jit(solution)/shard_map/ppermute | solution.py:129
  267.8 160.4 %all-gather.2.cloned.1.call-start = ((), (), s32[]{:S(2)}) async-start(), calls=%async_computation.2 | async-start | bytes 2654208 | tf_op jit(solution)/shard_map/all_gather | solution.py:235
  368.3 8.1 %collective-permute-start.31 = (f32[34,1536]{1,0:T(8,128)S(1)}, f32[34,1536]{1,0:T(8,128)S(1)}, u32[]{:S(2)}, u32[]{:S(2)}) collective-permute-start(f32[34,1536]{1,0:T(8,128)S(1)} %fusion.134), channel_id=1, source_target_pairs={{0,2},{1,3},{2,0},{3,1},{4,6},{5,7},{6,4},{7,5},{8,10},{9,11},{10,... | collective-permute-start | bytes 626696 | tf_op jit(solution)/shard_map/ppermute | solution.py:25
  376.4 10.1 %collective-permute-start.32 = (f32[34,1536]{1,0:T(8,128)S(1)}, f32[34,1536]{1,0:T(8,128)S(1)}, u32[]{:S(2)}, u32[]{:S(2)}) collective-permute-start(f32[34,1536]{1,0:T(8,128)S(1)} %add.749), channel_id=1, source_target_pairs={{0,4},{1,5},{2,6},{3,7},{4,0},{5,1},{6,2},{7,3},{8,12},{9,13},{10,... | collective-permute-start | bytes 626696 | tf_op jit(solution)/shard_map/ppermute | solution.py:25
  386.5 9.5 %collective-permute-start.33 = (f32[34,1536]{1,0:T(8,128)S(1)}, f32[34,1536]{1,0:T(8,128)S(1)}, u32[]{:S(2)}, u32[]{:S(2)}) collective-permute-start(f32[34,1536]{1,0:T(8,128)S(1)} %add.750), channel_id=1, source_target_pairs={{0,8},{1,9},{2,10},{3,11},{4,12},{5,13},{6,14},{7,15},{8,0},{9,1},... | collective-permute-start | bytes 626696 | tf_op jit(solution)/shard_map/ppermute | solution.py:25
  396.0 25.2 %collective-permute-start.34 = (f32[34,1536]{1,0:T(8,128)S(1)}, f32[34,1536]{1,0:T(8,128)S(1)}, u32[]{:S(2)}, u32[]{:S(2)}) collective-permute-start(f32[34,1536]{1,0:T(8,128)S(1)} %add.751), channel_id=1, source_target_pairs={{0,16},{1,17},{2,18},{3,19},{4,20},{5,21},{6,22},{7,23},{8,24},{9,... | collective-permute-start | bytes 626696 | tf_op jit(solution)/shard_map/ppermute | solution.py:25
  (72 other events, 2327.1 us)
Sparse Core Ops, SparseCore 0:
  267.9 96.7 reduce-scatter.1
  367.5 60.6 all-gather.1

commit v10 on v8

--- a/solution.py
+++ b/solution.py
@@ -143,10 +143,8 @@
     )
     future_rim = from_behind(grad_conv[: kernel_len - 1], ("seq", "fsdp"), -1)
     padded_grad = jnp.concatenate([grad_conv, future_rim], axis=0)
-    grad_glu = jnp.zeros((tok_rows, features), jnp.float32)
     kernel_rows = []
     for offset in range(kernel_len):
-        grad_glu = grad_glu + dw_kernel[offset] * padded_grad[offset : offset + tok_rows]
         kernel_rows.append(
             jnp.sum(
                 grad_conv
@@ -155,9 +153,18 @@
             )
         )
     kernel_portion = jnp.stack(kernel_rows, axis=0)
-    grad_value = grad_glu * gate_sig
-    grad_gate = grad_glu * value_part * gate_sig * (1.0 - gate_sig)
-    grad_hidden = jnp.concatenate([grad_value, grad_gate], axis=1).astype(jnp.bfloat16)
+    half = tok_rows // 2
+    spans = ((0, half), (half, tok_rows))
+    gh_parts = []
+    for lo, hi in spans:
+        grad_glu = jnp.zeros((hi - lo, features), jnp.float32)
+        for offset in range(kernel_len):
+            grad_glu = grad_glu + dw_kernel[offset] * padded_grad[lo + offset : hi + offset]
+        gate_rows = gate_sig[lo:hi]
+        grad_value = grad_glu * gate_rows
+        grad_gate = grad_glu * value_part[lo:hi] * gate_rows * (1.0 - gate_rows)
+        gh_parts.append(jnp.concatenate([grad_value, grad_gate], axis=1).astype(jnp.bfloat16))
+    grad_hidden = jnp.concatenate(gh_parts, axis=0)
     normalized_gradient = lax.dot_general(
         grad_hidden, full_weight, (((1,), (1,)), ((), ())), preferred_element_type=jnp.float32
     )
@@ -176,22 +183,25 @@
     group_rows = gather_own_columns(normalized_rows, "fsdp", feature_rows)
     contract = (((0,), (0,)), ((), ()))
     if lax.axis_size("fsdp") == 4:
-        far = lax.ppermute(grad_hidden, "fsdp", [(i, i ^ 2) for i in range(4)])
-        near = lax.ppermute(grad_hidden, "fsdp", [(i, i ^ 1) for i in range(4)])
-        far, input_gradient, local_sums = lax.optimization_barrier(
-            (far, input_gradient, local_sums)
-        )
-        near_far = lax.ppermute(far, "fsdp", [(i, i ^ 1) for i in range(4)])
-        pieces = (grad_hidden, far, near, near_far)
+        cross = [(i, i ^ 2) for i in range(4)]
+        on_chip = [(i, i ^ 1) for i in range(4)]
+        fars = [lax.ppermute(part, "fsdp", cross) for part in gh_parts]
+        nears = [lax.ppermute(part, "fsdp", on_chip) for part in gh_parts]
+        last_far, input_gradient, local_sums = lax.optimization_barrier(
+            (fars[-1], input_gradient, local_sums)
+        )
+        fars[-1] = last_far
+        near_fars = [lax.ppermute(far, "fsdp", on_chip) for far in fars]
         row_share = None
-        for slot, piece in enumerate(pieces):
-            term = lax.dot_general(
-                group_rows[slot * tok_rows : (slot + 1) * tok_rows],
-                piece,
-                contract,
-                preferred_element_type=jnp.float32,
-            )
-            row_share = term if row_share is None else row_share + term
+        for slot, parts in enumerate((gh_parts, fars, nears, near_fars)):
+            for (lo, hi), piece in zip(spans, parts):
+                term = lax.dot_general(
+                    group_rows[slot * tok_rows + lo : slot * tok_rows + hi],
+                    piece,
+                    contract,
+                    preferred_element_type=jnp.float32,
+                )
+                row_share = term if row_share is None else row_share + term
     else:
         group_grad = lax.all_gather(grad_hidden, "fsdp", axis=0, tiled=True)
         row_share = lax.dot_general(

time: 427 us -> 464 us (1.087); the launches traced: 427 us -> 458 us
  matrix products: 23 us -> 42.4 us
  other arithmetic: 69.9 us -> 80.2 us
    dot_general x4 -> x8, matrix products: 10 us -> 30.4 us  [on_device(): lax.dot_general(group_rows[slot * tok_rows + lo:slot * tok_rows + hi], pi...]
    ppermute x3 -> x6, waiting for transfers between devices: 31.9 us -> 45.8 us  [the longest x2 45.8 us: on_device(): fars = [lax.ppermute(part, 'fsdp', cross) for part in gh_parts]]
    ppermute x1, waiting for transfers between devices: 13.5 us -> 0.01 us  [gather_own_columns(): lax.ppermute(jnp.concatenate([cols(me ^ 2), cols(me ^ 3)], axis=0), axis,...]
    ppermute x10, waiting for transfers between devices: 57.8 us -> 65.7 us  [tree_sum(): packed = packed + lax.ppermute(packed, axis, route)]
    another operation x2 -> x3, other arithmetic: 29.5 us -> 34.9 us
  transfers between devices with their start and end apart: 27 -> 30, of which waited for: 21 -> 19; matrix products, arithmetic and copies ran while one was open for 8% -> 20% of each run, Pallas kernels for 0% -> 0%
where the time goes in v10:
time: 464 us; the launch traced here: 458 us
  waiting for transfers between devices  268 us (58%)
  other arithmetic  80.2 us (17%)
  matrix products  42.4 us (9%)
  starting transfers between devices  38.8 us (8%)
  between operations  16.3 us (4%)
  local copies, waits for them, and re-layouts  12.3 us (3%)
    reduce_scatter x1, waiting for transfers between devices, on_device(): lax.psum_scatter(row_share, 'seq', scatter_dimension=0, tiled=True)  95.8 us
    ppermute x10, waiting for transfers between devices, tree_sum(): packed = packed + lax.ppermute(packed, axis, route)  65.7 us
    ppermute x1, waiting for transfers between devices, group_shards(): far = lax.ppermute(block, axis, [(i, i ^ 2) for i in range(4)])  47.9 us
    ppermute x2, waiting for transfers between devices, on_device(): fars = [lax.ppermute(part, 'fsdp', cross) for part in gh_parts]  45.8 us
    another operation x3, other arithmetic  34.9 us
    dot_general x8, matrix products, on_device(): lax.dot_general(group_rows[slot * tok_rows + lo:slot * tok_rows + hi], pi...  30.4 us
    ppermute x10, starting transfers between devices, tree_sum(): packed = packed + lax.ppermute(packed, axis, route)  15.1 us
    ppermute x5, starting transfers between devices, mean_and_var(): other = lax.ppermute(stats, axis, [(i, i ^ stride) for i in range(count)])  13.1 us
  transfers between devices with their start and end apart: 30, of which 19 were waited for; matrix products, arithmetic and copies ran while one was open for 20% of the time, Pallas kernels for 0%

profile of v10, /device:TPU:0, one launch (start us, length us, event | category | flops | bytes accessed | tf_op | source)
XLA Modules:
  0.0 458.3 jit_solution(1878820139722116538)
XLA Ops:
  7.2 3.0 collective-permute-start
  13.8 47.9 %collective-permute-done = bf16[384,3072]{1,0:T(8,128)(2,1)S(1)} collective-permute-done((bf16[384,3072]{1,0:T(8,128)(2,1)}, bf16[384,3072]{1,0:T(8,128)(2,1)S(1)}, u32[]{:S(2)}, u32[]{:S(2)}) %collective-permute-start) | collective-permute-done | bytes 2359328 | tf_op jit(solution)/shard_map/ppermute | solution.py:62
  67.8 3.8 fusion.177
  71.6 2.5 fusion.15
  74.5 2.6 collective-permute-start.3
  79.5 9.4 %fusion.176 = (f32[1536]{0:T(1024)S(1)}, f32[384,1536]{1,0:T(8,128)S(1)}) fusion(f32[415,1536]{1,0:T(8,128)S(1)} %maximum_convert_fusion, f32[1536]{0:T(1024)S(1)} %get-tuple-element.88, f32[1536]{0:T(1024)S(1)} %get-tuple-element.89, f32[1536]{0:T(1024)S(1)} %get-tuple-element.59, f32[1536]{0:T(1024)S(1)} %get-tuple-element.60, ...), kind=kLoop, calls=%fused_computation.399 | loop fusion | flops 37747200 | bytes 78059520 | tf_op jit(solution)/shard_map/reduce_sum | solution.py:43
  97.0 3.0 collective-permute-start.6
  102.3 3.0 collective-permute-start.7
  107.7 3.2 collective-permute-start.8
  118.8 14.1 %collective-permute-done.10 = f32[2,1536]{1,0:T(2,128)S(1)} collective-permute-done((f32[2,1536]{1,0:T(2,128)S(1)}, f32[2,1536]{1,0:T(2,128)S(1)}, u32[]{:S(2)}, u32[]{:S(2)}) %collective-permute-start.10) | collective-permute-done | bytes 12320 | tf_op jit(solution)/shard_map/ppermute | solution.py:25
  133.9 2.8 collective-permute-done.11
  140.5 3.0 collective-permute-start.13
  146.1 8.3 %multiply_reduce_fusion = (f32[1536]{0:T(1024)S(1)}, f32[1536]{0:T(1024)S(1)}, f32[1536]{0:T(1024)S(1)}, f32[1536]{0:T(1024)S(1)}, f32[1536]{0:T(1024)S(1)}, /*i...) fusion(f32[415,1536]{1,0:T(8,128)S(1)} %maximum_convert_fusion,, ...), kind=kLoop, calls=%fused_computation.60 | loop fusion | flops 31822848 | bytes 48519168 | tf_op jit(solution)/shard_map/reduce_sum | solution.py:149
  156.3 5.5 %multiply_convert_fusion.1 = (bf16[192,1536]{1,0:T(8,128)(2,1)S(1)}, f32[192,1536]{1,0:T(8,128)}) fusion(f32[384,1536]{1,0:T(8,128)S(1)} %copy-done.2, f32[384,1536]{1,0:T(8,128)S(1)} %get-tuple-element.107, f32[1536]{0:T(1024)S(1)} %copy-done.72, f32[1536]{0:T(1024)S(1)} %copy-done.74, f32[1536]{0:T(1024)S(1)} %get-tuple-element.59, ...), kind=kLoop, calls=%fused_computation.298 | loop fusion | flops 19169280 | bytes 40894464 | tf_op jit(solution)/shard_map/convert
  161.8 4.3 multiply_reduce_fusion.18
  167.0 26.6 %multiply_convert_fusion.2 = (bf16[192,1536]{1,0:T(8,128)(2,1)S(1)}, f32[192,1536]{1,0:T(8,128)}) fusion(f32[384,1536]{1,0:T(8,128)} %get-tuple-element.116, f32[31,1536]{1,0:T(8,128)} %collective-permute-done.14, f32[384,1536]{1,0:T(8,128)} %copy-done, f32[1536]{0:T(1024)} %copy-done.71, f32[1536]{0:T(1024)} %copy-done.73, f32[1536]{0:T(1024)S(1)} %get-tuple-element.59, ...), kind=kLoop, calls=%fused_computation.299 | loop fusion | flops 28311552 | bytes 6942720 | tf_op jit(solution)/shard_map/convert.2
  193.6 2.8 fusion.118
  197.7 8.2 %fusion.11 = (f32[1536]{0:T(1024)S(1)}, f32[384]{0:T(512)S(1)}, f32[384]{0:T(512)S(1)}, f32[1536]{0:T(1024)S(1)}, f32[384,1536]{1,0:T(8,128)S(1)}) fusion(bf16[384,1536]{1,0:T(8,128)(2,1)S(1)} %copy-done.5, f32[384]{0:T(512)S(1)} %copy-done.83, f32[384]{0:T(512)S(1)} %copy-done.80, f32[1536]{0:T(1024)S(1)} %copy-done.78, bf16[1536,3072]{1,0:T(8,128)(2,1)} %copy-done.7, ...), kind=kOutput, calls=%fused_computation.44 | convolution fusion | flops 3639209984 | bytes 15360000 | tf_op jit(solution)/shard_map/dot_general | solution.py:168
  214.3 45.8 %collective-permute-done.15 = bf16[192,3072]{1,0:T(8,128)(2,1)S(1)} collective-permute-done((bf16[192,3072]{1,0:T(8,128)(2,1)S(1)}, bf16[192,3072]{1,0:T(8,128)(2,1)S(1)}, u32[]{:S(2)}, u32[]{:S(2)}) %collective-permute-start.15) | collective-permute-done | bytes 1179680 | tf_op jit(solution)/shard_map/ppermute | solution.py:188
  261.5 2.9 fusion.161
  264.4 4.0 fusion.159
  268.4 3.9 fusion.157
  272.3 3.9 fusion.154
  276.2 11.4 %add_add_fusion = f32[384,3072]{1,0:T(8,128)} fusion(f32[384,3072]{1,0:T(8,128)} %fusion.154, f32[384,3072]{1,0:T(8,128)} %fusion.157, f32[384,3072]{1,0:T(8,128)} %fusion.159, f32[384,3072]{1,0:T(8,128)} %fusion.161, f32[384,3072]{1,0:T(8,128)S(1)} %fusion.163, f32[384,3072]{1,0:T(8,128)S(1)} %fusion.167, f32[384,3072]{1,0:T(8,128)S(1)} %fusion.165, ...), kind=kOutput, calls=%fused_computation.30 | convolution fusion | flops 461242368 | bytes 39075840 | tf_op jit(solution)/shard_map/dot_general | solution.py:198
  287.6 95.8 %reduce-scatter.2.cloned.1.call-done = f32[48,3072]{1,0:T(8,128)} async-done(((f32[384,3072]{1,0:T(8,128)}), f32[48,3072]{1,0:T(8,128)}) %reduce-scatter.2.cloned.1.call-update) | async-done | bytes 589840 | tf_op jit(solution)/shard_map/reduce_scatter | solution.py:210
  388.4 6.5 %collective-permute-done.24 = f32[34,1536]{1,0:T(8,128)S(1)} collective-permute-done((f32[34,1536]{1,0:T(8,128)S(1)}, f32[34,1536]{1,0:T(8,128)S(1)}, u32[]{:S(2)}, u32[]{:S(2)}) %collective-permute-start.24) | collective-permute-done | bytes 208928 | tf_op jit(solution)/shard_map/ppermute | solution.py:25
  396.5 8.5 %collective-permute-done.25 = f32[34,1536]{1,0:T(8,128)S(1)} collective-permute-done((f32[34,1536]{1,0:T(8,128)S(1)}, f32[34,1536]{1,0:T(8,128)S(1)}, u32[]{:S(2)}, u32[]{:S(2)}) %collective-permute-start.25) | collective-permute-done | bytes 208928 | tf_op jit(solution)/shard_map/ppermute | solution.py:25
  406.6 8.0 %collective-permute-done.26 = f32[34,1536]{1,0:T(8,128)S(1)} collective-permute-done((f32[34,1536]{1,0:T(8,128)S(1)}, f32[34,1536]{1,0:T(8,128)S(1)}, u32[]{:S(2)}, u32[]{:S(2)}) %collective-permute-start.26) | collective-permute-done | bytes 208928 | tf_op jit(solution)/shard_map/ppermute | solution.py:25
  414.6 2.7 collective-permute-start.27
  417.3 22.3 %collective-permute-done.27 = f32[34,1536]{1,0:T(8,128)S(1)} collective-permute-done((f32[34,1536]{1,0:T(8,128)S(1)}, f32[34,1536]{1,0:T(8,128)S(1)}, u32[]{:S(2)}, u32[]{:S(2)}) %collective-permute-start.27) | collective-permute-done | bytes 208928 | tf_op jit(solution)/shard_map/ppermute | solution.py:25
  441.0 5.6 %all-gather.2.cloned.1.call-done = bf16[384,3072]{1,0:T(8,128)(2,1)} async-done(((bf16[48,3072]{1,0:T(8,128)(2,1)}), bf16[384,3072]{1,0:T(8,128)(2,1)}) %all-gather.2.cloned.1.call-update) | async-done | bytes 2359312 | tf_op jit(solution)/shard_map/all_gather | solution.py:211
  446.6 4.4 convert_element_type.37
  (310 shorter events, 62.2 us)
Async XLA Ops:
  7.2 376.2 %reduce-scatter.2.cloned.1.call-start = ((), (), s32[]{:S(2)}) async-start(), calls=%async_computation.1 | async-start | bytes 5308416 | tf_op jit(solution)/shard_map/reduce_scatter | solution.py:210
  7.2 54.5 %collective-permute-start = (bf16[384,3072]{1,0:T(8,128)(2,1)}, bf16[384,3072]{1,0:T(8,128)(2,1)S(1)}, u32[]{:S(2)}, u32[]{:S(2)}) collective-permute-start(bf16[384,3072]{1,0:T(8,128)(2,1)} %param.11), channel_id=1, source_target_pairs={{0,2},{1,3},{2,0},{3,1},{4,6},{5,7},{6,4},{7,5},{8,10},{9,11},{10,... | collective-permute-start | bytes 7077896 | tf_op jit(solution)/shard_map/ppermute | solution.py:62
  10.2 55.1 %collective-permute-start.1 = (bf16[384,3072]{1,0:T(8,128)(2,1)}, bf16[384,3072]{1,0:T(8,128)(2,1)}, u32[]{:S(2)}, u32[]{:S(2)}) collective-permute-start(bf16[384,3072]{1,0:T(8,128)(2,1)} %param.11), channel_id=1, source_target_pairs={{0,1},{1,0},{2,3},{3,2},{4,5},{5,4},{6,7},{7,6},{8,9},{9,8},{10,11... | collective-permute-start | bytes 7077896 | tf_op jit(solution)/shard_map/ppermute | solution.py:63
  12.1 67.1 %copy-start.15 = (f32[1536]{0:T(1024)}, f32[1536]{0:T(1024)S(1)}, u32[]{:S(2)}) copy-start(f32[1536]{0:T(1024)S(1)} %get-tuple-element.60) | copy-start | bytes 18436
  12.1 67.1 %copy-start.17 = (f32[1536]{0:T(1024)}, f32[1536]{0:T(1024)S(1)}, u32[]{:S(2)}) copy-start(f32[1536]{0:T(1024)S(1)} %get-tuple-element.61) | copy-start | bytes 18436
  61.7 5.8 %collective-permute-start.2 = (bf16[384,3072]{1,0:T(8,128)(2,1)S(1)}, bf16[384,3072]{1,0:T(8,128)(2,1)S(1)}, u32[]{:S(2)}, u32[]{:S(2)}) collective-permute-start(bf16[384,3072]{1,0:T(8,128)(2,1)S(1)} %collective-permute-done), channel_id=1, source_target_pairs={{0,1},{1,0},{2,3},{3,2},{4,5},{5,4},{6,7},{7,6},{8,9},{9,8},{10,11... | collective-permute-start | bytes 7077896 | tf_op jit(solution)/shard_map/ppermute | solution.py:64
  74.5 4.3 collective-permute-start.3
  89.3 2.3 collective-permute-start.4
  92.2 4.1 collective-permute-start.5
  97.0 4.7 %collective-permute-start.6 = (f32[2,1536]{1,0:T(2,128)S(1)}, f32[2,1536]{1,0:T(2,128)S(1)}, u32[]{:S(2)}, u32[]{:S(2)}) collective-permute-start(f32[2,1536]{1,0:T(2,128)S(1)} %pad_maximum_fusion.8), channel_id=1, source_target_pairs={{0,4},{1,5},{2,6},{3,7},{4,0},{5,1},{6,2},{7,3},{8,12},{9,13},{10,... | collective-permute-start | bytes 36872 | tf_op jit(solution)/shard_map/ppermute | solution.py:49
  102.3 4.7 %collective-permute-start.7 = (f32[2,1536]{1,0:T(2,128)S(1)}, f32[2,1536]{1,0:T(2,128)S(1)}, u32[]{:S(2)}, u32[]{:S(2)}) collective-permute-start(f32[2,1536]{1,0:T(2,128)S(1)} %pad_maximum_fusion.9), channel_id=1, source_target_pairs={{0,8},{1,9},{2,10},{3,11},{4,12},{5,13},{6,14},{7,15},{8,0},{9,1},... | collective-permute-start | bytes 36872 | tf_op jit(solution)/shard_map/ppermute | solution.py:49
  107.7 4.8 %collective-permute-start.8 = (f32[2,1536]{1,0:T(2,128)S(1)}, f32[2,1536]{1,0:T(2,128)S(1)}, u32[]{:S(2)}, u32[]{:S(2)}) collective-permute-start(f32[2,1536]{1,0:T(2,128)S(1)} %pad_maximum_fusion.10), channel_id=1, source_target_pairs={{0,16},{1,17},{2,18},{3,19},{4,20},{5,21},{6,22},{7,23},{8,24},{9,... | collective-permute-start | bytes 36872 | tf_op jit(solution)/shard_map/ppermute | solution.py:49
  115.8 1.2 collective-permute-start.9
  116.7 17.2 %collective-permute-start.16 = (bf16[768,384]{1,0:T(8,128)(2,1)}, bf16[768,384]{1,0:T(8,128)(2,1)S(1)}, u32[]{:S(2)}, u32[]{:S(2)}) collective-permute-start(bf16[768,384]{1,0:T(8,128)(2,1)} %pad_maximum_fusion.3), channel_id=1, source_target_pairs={{0,2},{1,3},{2,0},{3,1},{4,6},{5,7},{6,4},{7,5},{8,10},{9,11},{10,... | collective-permute-start | bytes 1769480 | tf_op jit(solution)/shard_map/ppermute | solution.py:92
  117.0 15.9 %collective-permute-start.10 = (f32[2,1536]{1,0:T(2,128)S(1)}, f32[2,1536]{1,0:T(2,128)S(1)}, u32[]{:S(2)}, u32[]{:S(2)}) collective-permute-start(f32[2,1536]{1,0:T(2,128)S(1)} %fusion.171), channel_id=1, source_target_pairs={{0,2},{1,3},{2,0},{3,1},{4,6},{5,7},{6,4},{7,5},{8,10},{9,11},{10,... | collective-permute-start | bytes 36872 | tf_op jit(solution)/shard_map/ppermute | solution.py:25
  132.9 3.8 collective-permute-start.11
  136.7 3.8 collective-permute-start.12
  139.5 124.9 %collective-permute-start.18 = (bf16[768,384]{1,0:T(8,128)(2,1)}, bf16[768,384]{1,0:T(8,128)(2,1)}, u32[]{:S(2)}, u32[]{:S(2)}) collective-permute-start(bf16[768,384]{1,0:T(8,128)(2,1)} %pad_maximum_fusion.4), channel_id=1, source_target_pairs={{0,1},{1,0},{2,3},{3,2},{4,5},{5,4},{6,7},{7,6},{8,9},{9,8},{10,11... | collective-permute-start | bytes 1769480 | tf_op jit(solution)/shard_map/ppermute | solution.py:95
  140.5 4.7 %collective-permute-start.13 = (f32[2,1536]{1,0:T(2,128)S(1)}, f32[2,1536]{1,0:T(2,128)S(1)}, u32[]{:S(2)}, u32[]{:S(2)}) collective-permute-start(f32[2,1536]{1,0:T(2,128)S(1)} %add.603), channel_id=1, source_target_pairs={{0,16},{1,17},{2,18},{3,19},{4,20},{5,21},{6,22},{7,23},{8,24},{9,... | collective-permute-start | bytes 36872 | tf_op jit(solution)/shard_map/ppermute | solution.py:25
  154.5 12.5 %collective-permute-start.14 = (f32[31,1536]{1,0:T(8,128)S(1)}, f32[31,1536]{1,0:T(8,128)}, u32[]{:S(2)}, u32[]{:S(2)}) collective-permute-start(f32[31,1536]{1,0:T(8,128)S(1)} %slice.794), channel_id=1, source_target_pairs={{1,0},{2,1},{3,2},{4,3},{5,4},{6,5},{7,6},{8,7},{9,8},{10,9},{11,1... | collective-permute-start | bytes 571400 | tf_op jit(solution)/shard_map/ppermute | solution.py:12
  206.1 54.1 %collective-permute-start.17 = (bf16[192,3072]{1,0:T(8,128)(2,1)S(1)}, bf16[192,3072]{1,0:T(8,128)(2,1)S(1)}, u32[]{:S(2)}, u32[]{:S(2)}) collective-permute-start(bf16[192,3072]{1,0:T(8,128)(2,1)S(1)} %pad_maximum_fusion.2), channel_id=1, source_target_pairs={{0,2},{1,3},{2,0},{3,1},{4,6},{5,7},{6,4},{7,5},{8,10},{9,11},{10,... | collective-permute-start | bytes 3538952 | tf_op jit(solution)/shard_map/ppermute | solution.py:188
  207.0 57.4 %collective-permute-start.19 = (bf16[192,3072]{1,0:T(8,128)(2,1)S(1)}, bf16[192,3072]{1,0:T(8,128)(2,1)S(1)}, u32[]{:S(2)}, u32[]{:S(2)}) collective-permute-start(bf16[192,3072]{1,0:T(8,128)(2,1)S(1)} %pad_maximum_fusion.2), channel_id=1, source_target_pairs={{0,1},{1,0},{2,3},{3,2},{4,5},{5,4},{6,7},{7,6},{8,9},{9,8},{10,11... | collective-permute-start | bytes 3538952 | tf_op jit(solution)/shard_map/ppermute | solution.py:189
  207.3 52.7 %collective-permute-start.15 = (bf16[192,3072]{1,0:T(8,128)(2,1)S(1)}, bf16[192,3072]{1,0:T(8,128)(2,1)S(1)}, u32[]{:S(2)}, u32[]{:S(2)}) collective-permute-start(bf16[192,3072]{1,0:T(8,128)(2,1)S(1)} %pad_maximum_fusion.1), channel_id=1, source_target_pairs={{0,2},{1,3},{2,0},{3,1},{4,6},{5,7},{6,4},{7,5},{8,10},{9,11},{10,... | collective-permute-start | bytes 3538952 | tf_op jit(solution)/shard_map/ppermute | solution.py:188
  209.0 59.4 %collective-permute-start.20 = (bf16[192,3072]{1,0:T(8,128)(2,1)S(1)}, bf16[192,3072]{1,0:T(8,128)(2,1)S(1)}, u32[]{:S(2)}, u32[]{:S(2)}) collective-permute-start(bf16[192,3072]{1,0:T(8,128)(2,1)S(1)} %pad_maximum_fusion.1), channel_id=1, source_target_pairs={{0,1},{1,0},{2,3},{3,2},{4,5},{5,4},{6,7},{7,6},{8,9},{9,8},{10,11... | collective-permute-start | bytes 3538952 | tf_op jit(solution)/shard_map/ppermute | solution.py:189
  260.1 12.2 %collective-permute-start.22 = (bf16[192,3072]{1,0:T(8,128)(2,1)S(1)}, bf16[192,3072]{1,0:T(8,128)(2,1)S(1)}, u32[]{:S(2)}, u32[]{:S(2)}) collective-permute-start(bf16[192,3072]{1,0:T(8,128)(2,1)S(1)} %collective-permute-done.15), channel_id=1, source_target_pairs={{0,1},{1,0},{2,3},{3,2},{4,5},{5,4},{6,7},{7,6},{8,9},{9,8},{10,11... | collective-permute-start | bytes 3538952 | tf_op jit(solution)/shard_map/ppermute | solution.py:194
  261.0 15.1 %collective-permute-start.21 = (bf16[192,3072]{1,0:T(8,128)(2,1)S(1)}, bf16[192,3072]{1,0:T(8,128)(2,1)S(1)}, u32[]{:S(2)}, u32[]{:S(2)}) collective-permute-start(bf16[192,3072]{1,0:T(8,128)(2,1)S(1)} %collective-permute-done.17), channel_id=1, source_target_pairs={{0,1},{1,0},{2,3},{3,2},{4,5},{5,4},{6,7},{7,6},{8,9},{9,8},{10,11... | collective-permute-start | bytes 3538952 | tf_op jit(solution)/shard_map/ppermute | solution.py:194
  287.6 159.0 %all-gather.2.cloned.1.call-start = ((), (), s32[]{:S(2)}) async-start(), calls=%async_computation.2 | async-start | bytes 2654208 | tf_op jit(solution)/shard_map/all_gather | solution.py:211
  385.3 1.6 collective-permute-start.23
  386.9 8.1 %collective-permute-start.24 = (f32[34,1536]{1,0:T(8,128)S(1)}, f32[34,1536]{1,0:T(8,128)S(1)}, u32[]{:S(2)}, u32[]{:S(2)}) collective-permute-start(f32[34,1536]{1,0:T(8,128)S(1)} %fusion.172), channel_id=1, source_target_pairs={{0,2},{1,3},{2,0},{3,1},{4,6},{5,7},{6,4},{7,5},{8,10},{9,11},{10,... | collective-permute-start | bytes 626696 | tf_op jit(solution)/shard_map/ppermute | solution.py:25
  395.0 10.1 %collective-permute-start.25 = (f32[34,1536]{1,0:T(8,128)S(1)}, f32[34,1536]{1,0:T(8,128)S(1)}, u32[]{:S(2)}, u32[]{:S(2)}) collective-permute-start(f32[34,1536]{1,0:T(8,128)S(1)} %add.675), channel_id=1, source_target_pairs={{0,4},{1,5},{2,6},{3,7},{4,0},{5,1},{6,2},{7,3},{8,12},{9,13},{10,... | collective-permute-start | bytes 626696 | tf_op jit(solution)/shard_map/ppermute | solution.py:25
  405.1 9.5 %collective-permute-start.26 = (f32[34,1536]{1,0:T(8,128)S(1)}, f32[34,1536]{1,0:T(8,128)S(1)}, u32[]{:S(2)}, u32[]{:S(2)}) collective-permute-start(f32[34,1536]{1,0:T(8,128)S(1)} %add.676), channel_id=1, source_target_pairs={{0,8},{1,9},{2,10},{3,11},{4,12},{5,13},{6,14},{7,15},{8,0},{9,1},... | collective-permute-start | bytes 626696 | tf_op jit(solution)/shard_map/ppermute | solution.py:25
  414.6 25.0 %collective-permute-start.27 = (f32[34,1536]{1,0:T(8,128)S(1)}, f32[34,1536]{1,0:T(8,128)S(1)}, u32[]{:S(2)}, u32[]{:S(2)}) collective-permute-start(f32[34,1536]{1,0:T(8,128)S(1)} %add.677), channel_id=1, source_target_pairs={{0,16},{1,17},{2,18},{3,19},{4,20},{5,21},{6,22},{7,23},{8,24},{9,... | collective-permute-start | bytes 626696 | tf_op jit(solution)/shard_map/ppermute | solution.py:25
  (83 other events, 1696.2 us)
Sparse Core Ops, SparseCore 0:
  287.7 95.6 reduce-scatter.1
  386.1 60.4 all-gather.1

commit v11 on v8

--- a/solution.py
+++ b/solution.py
@@ -78,6 +78,43 @@
     return whole
 
 
+def gather_weight(block, axis, twin):
+    if lax.axis_size(axis) != 4 or lax.axis_size(twin) % 2 or block.shape[1] % 512:
+        return gather_rows(block, axis)
+    rows, width = block.shape
+    piece = width // 4
+    bit = lax.axis_index(twin) % 2
+    cross = [(i, i ^ 2) for i in range(4)]
+    on_chip = [(i, i ^ 1) for i in range(4)]
+    pairs = [(i, i ^ 1) for i in range(lax.axis_size(twin))]
+    near = lax.ppermute(block, axis, on_chip)
+    first = lax.ppermute(
+        lax.dynamic_slice_in_dim(block, bit * piece, piece, axis=1), axis, cross
+    )
+    second_out, first = lax.optimization_barrier(
+        (lax.dynamic_slice_in_dim(block, (bit + 2) * piece, piece, axis=1), first)
+    )
+    second = lax.ppermute(second_out, axis, cross)
+    first_twin = lax.ppermute(first, twin, pairs)
+    second_twin = lax.ppermute(second, twin, pairs)
+    low = bit == 0
+    far = jnp.concatenate(
+        [
+            jnp.where(low, first, first_twin),
+            jnp.where(low, first_twin, first),
+            jnp.where(low, second, second_twin),
+            jnp.where(low, second_twin, second),
+        ],
+        axis=1,
+    )
+    near_far = lax.ppermute(far, axis, on_chip)
+    me = lax.axis_index(axis)
+    whole = jnp.zeros((4 * rows, width), block.dtype)
+    for shard, owner in zip((block, far, near, near_far), (me, me ^ 2, me ^ 1, me ^ 3)):
+        whole = lax.dynamic_update_slice_in_dim(whole, shard, owner * rows, axis=0)
+    return whole
+
+
 def gather_own_columns(rows_block, axis, width):
     me = lax.axis_index(axis)
     frames = rows_block.shape[0]
@@ -113,7 +150,7 @@
     )
     standardized_input = centered_rows * row_inverse_deviation
     normalized_rows = (standardized_input * layer_norm_gain + layer_norm_bias).astype(jnp.bfloat16)
-    full_weight = gather_rows(w_in, "fsdp")
+    full_weight = gather_weight(w_in, "fsdp", "seq")
     hidden = jnp.dot(normalized_rows, full_weight, preferred_element_type=jnp.float32)
     value_part = hidden[:, :features]
     gate_sig = jax.nn.sigmoid(hidden[:, features:])

time: 427 us -> 427 us (level)
  waiting for transfers between devices: 264 us -> 245 us
  local copies, waits for them, and re-layouts: 12.8 us -> 22.9 us
  starting transfers between devices: 41.3 us -> 45.8 us
    ppermute x3 -> x6, waiting for transfers between devices: 48 us -> 29.5 us  [the longest x1 13.3 us: gather_weight(): lax.ppermute(lax.dynamic_slice_in_dim(block, bit * piece, piece, axis=1),...]
    dynamic_update_slice x4 -> x3, local copies, waits for them, and re-layouts: 2.92 us -> 8.48 us  [gather_weight(): whole = lax.dynamic_update_slice_in_dim(whole, shard, owner * rows, axis=0)]
    ppermute x3 -> x6, starting transfers between devices: 3.01 us -> 7.66 us  [the longest x1 2.94 us: gather_weight(): lax.ppermute(lax.dynamic_slice_in_dim(block, bit * piece, piece, axis=1),...]
  transfers between devices with their start and end apart: 27 -> 30, of which waited for: 21 -> 23; matrix products, arithmetic and copies ran while one was open for 8% -> 10% of each run, Pallas kernels for 0% -> 0%
where the time goes in v11:
time: 427 us
  waiting for transfers between devices  245 us (57%)
  other arithmetic  71.9 us (17%)
  starting transfers between devices  45.8 us (11%)
  matrix products  25.4 us (6%)
  local copies, waits for them, and re-layouts  22.9 us (5%)
  between operations  15.6 us (4%)
    reduce_scatter x1, waiting for transfers between devices, on_device(): lax.psum_scatter(row_share, 'seq', scatter_dimension=0, tiled=True)  97.3 us
    ppermute x10, waiting for transfers between devices, tree_sum(): packed = packed + lax.ppermute(packed, axis, route)  57.8 us
    ppermute x1, waiting for transfers between devices, on_device(): far = lax.ppermute(grad_hidden, 'fsdp', [(i, i ^ 2) for i in range(4)])  32 us
    another operation x2, other arithmetic  29.6 us
    ppermute x1, waiting for transfers between devices, gather_own_columns(): lax.ppermute(jnp.concatenate([cols(me ^ 2), cols(me ^ 3)], axis=0), axis,...  13.5 us
    ppermute x10, starting transfers between devices, tree_sum(): packed = packed + lax.ppermute(packed, axis, route)  13.5 us
    ppermute x1, waiting for transfers between devices, gather_weight(): lax.ppermute(lax.dynamic_slice_in_dim(block, bit * piece, piece, axis=1),...  13.3 us
    ppermute x5, starting transfers between devices, mean_and_var(): other = lax.ppermute(stats, axis, [(i, i ^ stride) for i in range(count)])  12.6 us
  transfers between devices with their start and end apart: 30, of which 23 were waited for; matrix products, arithmetic and copies ran while one was open for 10% of the time, Pallas kernels for 0%

profile of v11, /device:TPU:0, one launch (start us, length us, event | category | flops | bytes accessed | tf_op | source)
XLA Modules:
  0.0 426.8 jit_solution(16911879306047089732)
XLA Ops:
  9.5 2.9 collective-permute-start
  12.5 13.3 %collective-permute-done = bf16[384,768]{1,0:T(8,128)(2,1)S(1)} collective-permute-done((bf16[384,768]{1,0:T(8,128)(2,1)S(1)}, bf16[384,768]{1,0:T(8,128)(2,1)S(1)}, u32[]{:S(2)}, u32[]{:S(2)}) %collective-permute-start) | collective-permute-done | bytes 589856 | tf_op jit(solution)/shard_map/ppermute | solution.py:91
  29.1 11.5 %collective-permute-done.2 = bf16[384,768]{1,0:T(8,128)(2,1)S(1)} collective-permute-done((bf16[384,768]{1,0:T(8,128)(2,1)}, bf16[384,768]{1,0:T(8,128)(2,1)S(1)}, u32[]{:S(2)}, u32[]{:S(2)}) %collective-permute-start.2) | collective-permute-done | bytes 589856 | tf_op jit(solution)/shard_map/ppermute | solution.py:97
  42.0 4.8 %broadcast_in_dim.2 = bf16[1536,3072]{1,0:T(8,128)(2,1)} broadcast(bf16[]{:T(256)} %constant.18.clone.1), dimensions={} | broadcast | bytes 9437186 | tf_op jit(solution)/shard_map/broadcast_in_dim | solution.py:112
  49.5 4.7 %collective-permute-done.3 = bf16[384,768]{1,0:T(8,128)(2,1)S(1)} collective-permute-done((bf16[384,768]{1,0:T(8,128)(2,1)S(1)}, bf16[384,768]{1,0:T(8,128)(2,1)S(1)}, u32[]{:S(2)}, u32[]{:S(2)}) %collective-permute-start.3) | collective-permute-done | bytes 589856 | tf_op jit(solution)/shard_map/ppermute | solution.py:99
  60.8 3.6 constant_dynamic-update-slice_fusion.1
  64.5 3.3 constant_dynamic-update-slice_fusion
  67.7 6.3 %fusion.125 = f32[384,3072]{1,0:T(8,128)S(1)} fusion(bf16[384,1536]{1,0:T(8,128)(2,1)S(1)} %fusion.7, bf16[1536,3072]{1,0:T(8,128)(2,1)} %constant_dynamic-update-slice_fusion), kind=kOutput, calls=%fused_computation.315 | convolution fusion | flops 3623878656 | bytes 15335424 | tf_op jit(solution)/shard_map/dot_general | solution.py:154
  81.1 9.4 %fusion.124 = (f32[1536]{0:T(1024)S(1)}, f32[384,1536]{1,0:T(8,128)S(1)}) fusion(f32[415,1536]{1,0:T(8,128)S(1)} %maximum_convert_fusion, f32[1536]{0:T(1024)S(1)} %get-tuple-element.92, f32[1536]{0:T(1024)S(1)} %get-tuple-element.93, f32[1536]{0:T(1024)S(1)} %get-tuple-element.63, f32[1536]{0:T(1024)S(1)} %get-tuple-element.64, ...), kind=kLoop, calls=%fused_computation.314 | loop fusion | flops 37747200 | bytes 78059520 | tf_op jit(solution)/shard_map/reduce_sum | solution.py:43
  97.0 3.2 collective-permute-start.9
  102.0 3.0 collective-permute-start.10
  106.8 3.1 collective-permute-start.11
  115.5 3.7 collective-permute-done.13
  120.2 2.7 collective-permute-done.14
  126.8 3.0 collective-permute-start.16
  132.1 7.8 %multiply_reduce_fusion = (f32[1536]{0:T(1024)}, f32[1536]{0:T(1024)}, f32[1536]{0:T(1024)}, f32[1536]{0:T(1024)}, f32[1536]{0:T(1024)}, /*index=5*/f32[1536]{0:...) fusion(f32[415,1536]{1,0:T(8,128)S(1)} %maximum_convert_fusion,, ...), kind=kLoop, calls=%fused_computation.170 | loop fusion | flops 31822848 | bytes 48519168 | tf_op jit(solution)/shard_map/reduce_sum | solution.py:188
  143.2 25.5 %multiply_convert_fusion.1 = (bf16[384,1536]{1,0:T(8,128)(2,1)}, f32[384,1536]{1,0:T(8,128)}) fusion(f32[384,3072]{1,0:T(8,128)} %copy-done, f32[31,1536]{1,0:T(8,128)S(1)} %collective-permute-done.17, f32[384,1536]{1,0:T(8,128)S(1)} %get-tuple-element.111, f32[1536]{0:T(1024)} %copy-done.41, f32[1536]{0:T(1024)} %copy-done.42, ...), kind=kLoop, calls=%fused_computation.203 | loop fusion | flops 58392576 | bytes 8644608 | tf_op jit(solution)/shard_map/convert
  168.7 4.1 multiply_convert_fusion
  176.6 4.6 %multiply_reduce_fusion.18 = (f32[1536]{0:T(1024)S(1)}, f32[1536]{0:T(1024)S(1)}, f32[1536]{0:T(1024)S(1)}, f32[1536]{0:T(1024)S(1)}, f32[1536]{0:T(1024)S(1)}, ...) fusion(f32[384,1536]{1,0:T(8,128)S(1)} %get-tuple-element.111, ...), kind=kLoop, calls=%fused_computation.188 | loop fusion | flops 16493568 | bytes 35475456 | tf_op jit(solution)/shard_map/reduce_sum | solution.py:188
  184.7 9.0 %fusion.11 = (f32[1536]{0:T(1024)S(1)}, f32[384]{0:T(512)S(1)}, f32[384]{0:T(512)S(1)}, f32[1536]{0:T(1024)S(1)}, f32[384,1536]{1,0:T(8,128)S(1)}) fusion(bf16[384,1536]{1,0:T(8,128)(2,1)} %param.8, f32[384]{0:T(512)S(1)} %copy-done.67, f32[384]{0:T(512)S(1)} %copy-done.46, f32[1536]{0:T(1024)S(1)} %copy-done.44, ...), kind=kOutput, calls=%fused_computation.44 | convolution fusion | flops 3634491392 | bytes 15360000 | tf_op jit(solution)/shard_map/dot_general | solution.py:198
  195.5 32.0 %collective-permute-done.18 = bf16[384,3072]{1,0:T(8,128)(2,1)} collective-permute-done((bf16[384,3072]{1,0:T(8,128)(2,1)}, bf16[384,3072]{1,0:T(8,128)(2,1)}, u32[]{:S(2)}, u32[]{:S(2)}) %collective-permute-start.18) | collective-permute-done | bytes 2359328 | tf_op jit(solution)/shard_map/ppermute | solution.py:216
  231.1 13.5 %collective-permute-done.19 = bf16[768,384]{1,0:T(8,128)(2,1)S(1)} collective-permute-done((bf16[768,384]{1,0:T(8,128)(2,1)S(1)}, bf16[768,384]{1,0:T(8,128)(2,1)S(1)}, u32[]{:S(2)}, u32[]{:S(2)}) %collective-permute-start.19) | collective-permute-done | bytes 589856 | tf_op jit(solution)/shard_map/ppermute | solution.py:129
  246.2 3.1 fusion.114
  250.8 4.1 add_add_fusion
  254.9 97.3 %reduce-scatter.2.cloned.1.call-done = f32[48,3072]{1,0:T(8,128)} async-done(((f32[384,3072]{1,0:T(8,128)}), f32[48,3072]{1,0:T(8,128)}) %reduce-scatter.2.cloned.1.call-update) | async-done | bytes 589840 | tf_op jit(solution)/shard_map/reduce_scatter | solution.py:237
  357.3 6.5 %collective-permute-done.24 = f32[34,1536]{1,0:T(8,128)S(1)} collective-permute-done((f32[34,1536]{1,0:T(8,128)S(1)}, f32[34,1536]{1,0:T(8,128)S(1)}, u32[]{:S(2)}, u32[]{:S(2)}) %collective-permute-start.24) | collective-permute-done | bytes 208928 | tf_op jit(solution)/shard_map/ppermute | solution.py:25
  365.4 8.5 %collective-permute-done.25 = f32[34,1536]{1,0:T(8,128)S(1)} collective-permute-done((f32[34,1536]{1,0:T(8,128)S(1)}, f32[34,1536]{1,0:T(8,128)S(1)}, u32[]{:S(2)}, u32[]{:S(2)}) %collective-permute-start.25) | collective-permute-done | bytes 208928 | tf_op jit(solution)/shard_map/ppermute | solution.py:25
  375.5 8.0 %collective-permute-done.26 = f32[34,1536]{1,0:T(8,128)S(1)} collective-permute-done((f32[34,1536]{1,0:T(8,128)S(1)}, f32[34,1536]{1,0:T(8,128)S(1)}, u32[]{:S(2)}, u32[]{:S(2)}) %collective-permute-start.26) | collective-permute-done | bytes 208928 | tf_op jit(solution)/shard_map/ppermute | solution.py:25
  383.5 2.7 collective-permute-start.27
  386.2 22.3 %collective-permute-done.27 = f32[34,1536]{1,0:T(8,128)S(1)} collective-permute-done((f32[34,1536]{1,0:T(8,128)S(1)}, f32[34,1536]{1,0:T(8,128)S(1)}, u32[]{:S(2)}, u32[]{:S(2)}) %collective-permute-start.27) | collective-permute-done | bytes 208928 | tf_op jit(solution)/shard_map/ppermute | solution.py:25
  409.9 5.6 %all-gather.2.cloned.1.call-done = bf16[384,3072]{1,0:T(8,128)(2,1)} async-done(((bf16[48,3072]{1,0:T(8,128)(2,1)}), bf16[384,3072]{1,0:T(8,128)(2,1)}) %all-gather.2.cloned.1.call-update) | async-done | bytes 2359312 | tf_op jit(solution)/shard_map/all_gather | solution.py:238
  415.5 4.4 %convert_element_type.36 = f32[384,3072]{1,0:T(8,128)} convert(bf16[384,3072]{1,0:T(8,128)(2,1)} %all-gather.2.cloned.1.call-done) | non-fusion elementwise | flops 1179648 | bytes 7077888 | tf_op jit(solution)/shard_map/convert_element_type | solution.py:240
  (273 shorter events, 73.4 us)
Async XLA Ops:
  7.2 345.1 %reduce-scatter.2.cloned.1.call-start = ((), (), s32[]{:S(2)}) async-start(), calls=%async_computation.1 | async-start | bytes 5308416 | tf_op jit(solution)/shard_map/reduce_scatter | solution.py:237
  9.5 16.3 %collective-permute-start = (bf16[384,768]{1,0:T(8,128)(2,1)S(1)}, bf16[384,768]{1,0:T(8,128)(2,1)S(1)}, u32[]{:S(2)}, u32[]{:S(2)}) collective-permute-start(bf16[384,768]{1,0:T(8,128)(2,1)S(1)} %get-tuple-element.119), channel_id=1, source_target_pairs={{0,2},{1,3},{2,0},{3,1},{4,6},{5,7},{6,4},{7,5},{8,10},{9,11},{10,... | collective-permute-start | bytes 1769480 | tf_op jit(solution)/shard_map/ppermute | solution.py:91
  25.8 14.7 %collective-permute-start.2 = (bf16[384,768]{1,0:T(8,128)(2,1)}, bf16[384,768]{1,0:T(8,128)(2,1)S(1)}, u32[]{:S(2)}, u32[]{:S(2)}) collective-permute-start(bf16[384,768]{1,0:T(8,128)(2,1)} %get-tuple-element.16), channel_id=1, source_target_pairs={{0,2},{1,3},{2,0},{3,1},{4,6},{5,7},{6,4},{7,5},{8,10},{9,11},{10,... | collective-permute-start | bytes 1769480 | tf_op jit(solution)/shard_map/ppermute | solution.py:97
  27.5 20.8 %collective-permute-start.1 = (bf16[384,768]{1,0:T(8,128)(2,1)S(1)}, bf16[384,768]{1,0:T(8,128)(2,1)}, u32[]{:S(2)}, u32[]{:S(2)}) collective-permute-start(bf16[384,768]{1,0:T(8,128)(2,1)S(1)} %collective-permute-done), channel_id=1, source_target_pairs={{0,4},{4,0},{8,12},{12,8},{16,20},{20,16},{24,28},{28,24},{1,5},{5... | collective-permute-start | bytes 1769480 | tf_op jit(solution)/shard_map/ppermute | solution.py:98
  29.1 31.7 %collective-permute-start.4 = (bf16[384,3072]{1,0:T(8,128)(2,1)S(1)}, bf16[384,3072]{1,0:T(8,128)(2,1)}, u32[]{:S(2)}, u32[]{:S(2)}) collective-permute-start(bf16[384,3072]{1,0:T(8,128)(2,1)S(1)} %copy-done.7), channel_id=1, source_target_pairs={{0,1},{1,0},{2,3},{3,2},{4,5},{5,4},{6,7},{7,6},{8,9},{9,8},{10,11... | collective-permute-start | bytes 7077896 | tf_op jit(solution)/shard_map/ppermute | solution.py:90
  40.5 13.7 %collective-permute-start.3 = (bf16[384,768]{1,0:T(8,128)(2,1)S(1)}, bf16[384,768]{1,0:T(8,128)(2,1)S(1)}, u32[]{:S(2)}, u32[]{:S(2)}) collective-permute-start(bf16[384,768]{1,0:T(8,128)(2,1)S(1)} %collective-permute-done.2), channel_id=1, source_target_pairs={{0,4},{4,0},{8,12},{12,8},{16,20},{20,16},{24,28},{28,24},{1,5},{5... | collective-permute-start | bytes 1769480 | tf_op jit(solution)/shard_map/ppermute | solution.py:99
  56.8 7.6 %collective-permute-start.5 = (bf16[384,3072]{1,0:T(8,128)(2,1)}, bf16[384,3072]{1,0:T(8,128)(2,1)}, u32[]{:S(2)}, u32[]{:S(2)}) collective-permute-start(bf16[384,3072]{1,0:T(8,128)(2,1)} %get-tuple-element.117), channel_id=1, source_target_pairs={{0,1},{1,0},{2,3},{3,2},{4,5},{5,4},{6,7},{7,6},{8,9},{9,8},{10,11... | collective-permute-start | bytes 7077896 | tf_op jit(solution)/shard_map/ppermute | solution.py:110
  58.7 22.3 %copy-start.12 = (f32[1536]{0:T(1024)}, f32[1536]{0:T(1024)S(1)}, u32[]{:S(2)}) copy-start(f32[1536]{0:T(1024)S(1)} %get-tuple-element.64) | copy-start | bytes 18436
  76.3 4.3 %collective-permute-start.6 = (bf16[31,1536]{1,0:T(8,128)(2,1)S(1)}, bf16[31,1536]{1,0:T(8,128)(2,1)S(1)}, u32[]{:S(2)}, u32[]{:S(2)}) collective-permute-start(bf16[31,1536]{1,0:T(8,128)(2,1)S(1)} %slice.543), channel_id=1, source_target_pairs={{0,1},{1,2},{2,3},{3,4},{4,5},{5,6},{6,7},{7,8},{8,9},{9,10},{10,1... | collective-permute-start | bytes 285704 | tf_op jit(solution)/shard_map/ppermute | solution.py:12
  91.1 1.6 collective-permute-start.7
  92.8 4.1 collective-permute-start.8
  97.0 4.9 %collective-permute-start.9 = (f32[2,1536]{1,0:T(2,128)S(1)}, f32[2,1536]{1,0:T(2,128)S(1)}, u32[]{:S(2)}, u32[]{:S(2)}) collective-permute-start(f32[2,1536]{1,0:T(2,128)S(1)} %pad_maximum_fusion.8), channel_id=1, source_target_pairs={{0,4},{1,5},{2,6},{3,7},{4,0},{5,1},{6,2},{7,3},{8,12},{9,13},{10,... | collective-permute-start | bytes 36872 | tf_op jit(solution)/shard_map/ppermute | solution.py:49
  102.0 4.7 %collective-permute-start.10 = (f32[2,1536]{1,0:T(2,128)S(1)}, f32[2,1536]{1,0:T(2,128)S(1)}, u32[]{:S(2)}, u32[]{:S(2)}) collective-permute-start(f32[2,1536]{1,0:T(2,128)S(1)} %pad_maximum_fusion.9), channel_id=1, source_target_pairs={{0,8},{1,9},{2,10},{3,11},{4,12},{5,13},{6,14},{7,15},{8,0},{9,1},... | collective-permute-start | bytes 36872 | tf_op jit(solution)/shard_map/ppermute | solution.py:49
  106.8 4.8 %collective-permute-start.11 = (f32[2,1536]{1,0:T(2,128)S(1)}, f32[2,1536]{1,0:T(2,128)S(1)}, u32[]{:S(2)}, u32[]{:S(2)}) collective-permute-start(f32[2,1536]{1,0:T(2,128)S(1)} %pad_maximum_fusion.10), channel_id=1, source_target_pairs={{0,16},{1,17},{2,18},{3,19},{4,20},{5,21},{6,22},{7,23},{8,24},{9,... | collective-permute-start | bytes 36872 | tf_op jit(solution)/shard_map/ppermute | solution.py:49
  114.2 1.2 collective-permute-start.12
  115.4 3.8 collective-permute-start.13
  119.2 3.8 collective-permute-start.14
  123.0 3.8 collective-permute-start.15
  126.8 4.7 %collective-permute-start.16 = (f32[2,1536]{1,0:T(2,128)S(1)}, f32[2,1536]{1,0:T(2,128)S(1)}, u32[]{:S(2)}, u32[]{:S(2)}) collective-permute-start(f32[2,1536]{1,0:T(2,128)S(1)} %add.515), channel_id=1, source_target_pairs={{0,16},{1,17},{2,18},{3,19},{4,20},{5,21},{6,22},{7,23},{8,24},{9,... | collective-permute-start | bytes 36872 | tf_op jit(solution)/shard_map/ppermute | solution.py:25
  139.9 3.3 collective-permute-start.17
  174.8 52.7 %collective-permute-start.18 = (bf16[384,3072]{1,0:T(8,128)(2,1)}, bf16[384,3072]{1,0:T(8,128)(2,1)}, u32[]{:S(2)}, u32[]{:S(2)}) collective-permute-start(bf16[384,3072]{1,0:T(8,128)(2,1)} %pad_maximum_fusion.2), channel_id=1, source_target_pairs={{0,2},{1,3},{2,0},{3,1},{4,6},{5,7},{6,4},{7,5},{8,10},{9,11},{10,... | collective-permute-start | bytes 7077896 | tf_op jit(solution)/shard_map/ppermute | solution.py:216
  182.2 67.2 %collective-permute-start.21 = (bf16[384,3072]{1,0:T(8,128)(2,1)}, bf16[384,3072]{1,0:T(8,128)(2,1)S(1)}, u32[]{:S(2)}, u32[]{:S(2)}) collective-permute-start(bf16[384,3072]{1,0:T(8,128)(2,1)} %pad_maximum_fusion.2), channel_id=1, source_target_pairs={{0,1},{1,0},{2,3},{3,2},{4,5},{5,4},{6,7},{7,6},{8,9},{9,8},{10,11... | collective-permute-start | bytes 7077896 | tf_op jit(solution)/shard_map/ppermute | solution.py:217
  193.7 35.4 %copy-start.10 = (bf16[384,1536]{1,0:T(8,128)(2,1)S(1)}, bf16[384,1536]{1,0:T(8,128)(2,1)}, u32[]{:S(2)}) copy-start(bf16[384,1536]{1,0:T(8,128)(2,1)} %copy-done.9) | copy-start | bytes 3538948
  227.5 23.3 %collective-permute-start.22 = (bf16[384,3072]{1,0:T(8,128)(2,1)}, bf16[384,3072]{1,0:T(8,128)(2,1)S(1)}, u32[]{:S(2)}, u32[]{:S(2)}) collective-permute-start(bf16[384,3072]{1,0:T(8,128)(2,1)} %collective-permute-done.18), channel_id=1, source_target_pairs={{0,1},{1,0},{2,3},{3,2},{4,5},{5,4},{6,7},{7,6},{8,9},{9,8},{10,11... | collective-permute-start | bytes 7077896 | tf_op jit(solution)/shard_map/ppermute | solution.py:221
  229.3 15.3 %collective-permute-start.19 = (bf16[768,384]{1,0:T(8,128)(2,1)S(1)}, bf16[768,384]{1,0:T(8,128)(2,1)S(1)}, u32[]{:S(2)}, u32[]{:S(2)}) collective-permute-start(bf16[768,384]{1,0:T(8,128)(2,1)S(1)} %pad_maximum_fusion.3), channel_id=1, source_target_pairs={{0,2},{1,3},{2,0},{3,1},{4,6},{5,7},{6,4},{7,5},{8,10},{9,11},{10,... | collective-permute-start | bytes 1769480 | tf_op jit(solution)/shard_map/ppermute | solution.py:129
  244.7 4.6 %collective-permute-start.20 = (bf16[768,384]{1,0:T(8,128)(2,1)S(1)}, bf16[768,384]{1,0:T(8,128)(2,1)S(1)}, u32[]{:S(2)}, u32[]{:S(2)}) collective-permute-start(bf16[768,384]{1,0:T(8,128)(2,1)S(1)} %pad_maximum_fusion.4), channel_id=1, source_target_pairs={{0,1},{1,0},{2,3},{3,2},{4,5},{5,4},{6,7},{7,6},{8,9},{9,8},{10,11... | collective-permute-start | bytes 1769480 | tf_op jit(solution)/shard_map/ppermute | solution.py:132
  254.9 160.6 %all-gather.2.cloned.1.call-start = ((), (), s32[]{:S(2)}) async-start(), calls=%async_computation.2 | async-start | bytes 2654208 | tf_op jit(solution)/shard_map/all_gather | solution.py:238
  354.2 1.6 collective-permute-start.23
  355.8 8.1 %collective-permute-start.24 = (f32[34,1536]{1,0:T(8,128)S(1)}, f32[34,1536]{1,0:T(8,128)S(1)}, u32[]{:S(2)}, u32[]{:S(2)}) collective-permute-start(f32[34,1536]{1,0:T(8,128)S(1)} %fusion.120), channel_id=1, source_target_pairs={{0,2},{1,3},{2,0},{3,1},{4,6},{5,7},{6,4},{7,5},{8,10},{9,11},{10,... | collective-permute-start | bytes 626696 | tf_op jit(solution)/shard_map/ppermute | solution.py:25
  363.9 10.1 %collective-permute-start.25 = (f32[34,1536]{1,0:T(8,128)S(1)}, f32[34,1536]{1,0:T(8,128)S(1)}, u32[]{:S(2)}, u32[]{:S(2)}) collective-permute-start(f32[34,1536]{1,0:T(8,128)S(1)} %add.552), channel_id=1, source_target_pairs={{0,4},{1,5},{2,6},{3,7},{4,0},{5,1},{6,2},{7,3},{8,12},{9,13},{10,... | collective-permute-start | bytes 626696 | tf_op jit(solution)/shard_map/ppermute | solution.py:25
  374.0 9.5 %collective-permute-start.26 = (f32[34,1536]{1,0:T(8,128)S(1)}, f32[34,1536]{1,0:T(8,128)S(1)}, u32[]{:S(2)}, u32[]{:S(2)}) collective-permute-start(f32[34,1536]{1,0:T(8,128)S(1)} %add.553), channel_id=1, source_target_pairs={{0,8},{1,9},{2,10},{3,11},{4,12},{5,13},{6,14},{7,15},{8,0},{9,1},... | collective-permute-start | bytes 626696 | tf_op jit(solution)/shard_map/ppermute | solution.py:25
  383.5 25.0 %collective-permute-start.27 = (f32[34,1536]{1,0:T(8,128)S(1)}, f32[34,1536]{1,0:T(8,128)S(1)}, u32[]{:S(2)}, u32[]{:S(2)}) collective-permute-start(f32[34,1536]{1,0:T(8,128)S(1)} %add.554), channel_id=1, source_target_pairs={{0,16},{1,17},{2,18},{3,19},{4,20},{5,21},{6,22},{7,23},{8,24},{9,... | collective-permute-start | bytes 626696 | tf_op jit(solution)/shard_map/ppermute | solution.py:25
  (66 other events, 822.1 us)
Sparse Core Ops, SparseCore 0:
  255.0 97.2 reduce-scatter.1
  355.0 60.4 all-gather.1

commit v12 on v8

--- a/solution.py
+++ b/solution.py
@@ -113,8 +113,27 @@
     )
     standardized_input = centered_rows * row_inverse_deviation
     normalized_rows = (standardized_input * layer_norm_gain + layer_norm_bias).astype(jnp.bfloat16)
-    full_weight = gather_rows(w_in, "fsdp")
-    hidden = jnp.dot(normalized_rows, full_weight, preferred_element_type=jnp.float32)
+    if lax.axis_size("fsdp") == 4:
+        weight_rows = w_in.shape[0]
+        me = lax.axis_index("fsdp")
+        shards = group_shards(w_in, "fsdp")
+        owners = (me, me ^ 2, me ^ 1, me ^ 3)
+        hidden = None
+        for shard, owner in zip(shards, owners):
+            term = jnp.dot(
+                lax.dynamic_slice_in_dim(normalized_rows, owner * weight_rows, weight_rows, axis=1),
+                shard,
+                preferred_element_type=jnp.float32,
+            )
+            hidden = term if hidden is None else hidden + term
+        full_weight = jnp.zeros((4 * weight_rows, w_in.shape[1]), w_in.dtype)
+        for shard, owner in zip(shards, owners):
+            full_weight = lax.dynamic_update_slice_in_dim(
+                full_weight, shard, owner * weight_rows, axis=0
+            )
+    else:
+        full_weight = lax.all_gather(w_in, "fsdp", axis=0, tiled=True)
+        hidden = jnp.dot(normalized_rows, full_weight, preferred_element_type=jnp.float32)
     value_part = hidden[:, :features]
     gate_sig = jax.nn.sigmoid(hidden[:, features:])
     glu = (value_part * gate_sig).astype(jnp.bfloat16)

time: 427 us -> 432 us (1.012)
  local copies, waits for them, and re-layouts: 12.8 us -> 18 us
    ppermute x10, waiting for transfers between devices: 57.8 us -> 50.5 us  [tree_sum(): packed = packed + lax.ppermute(packed, axis, route)]
    dynamic_update_slice x4, local copies, waits for them, and re-layouts: 2.92 us -> 7.99 us  [on_device(): lax.dynamic_update_slice_in_dim(full_weight, shard, owner * weight_rows,...]
  transfers between devices with their start and end apart: 27 -> 27, of which waited for: 21 -> 20; matrix products, arithmetic and copies ran while one was open for 8% -> 11% of each run, Pallas kernels for 0% -> 0%
where the time goes in v12:
time: 432 us
  waiting for transfers between devices  260 us (60%)
  other arithmetic  70 us (16%)
  starting transfers between devices  41.1 us (10%)
  matrix products  27.3 us (6%)
  local copies, waits for them, and re-layouts  18 us (4%)
  between operations  15.7 us (4%)
    reduce_scatter x1, waiting for transfers between devices, on_device(): lax.psum_scatter(row_share, 'seq', scatter_dimension=0, tiled=True)  96.8 us
    ppermute x10, waiting for transfers between devices, tree_sum(): packed = packed + lax.ppermute(packed, axis, route)  50.5 us
    ppermute x1, waiting for transfers between devices, group_shards(): far = lax.ppermute(block, axis, [(i, i ^ 2) for i in range(4)])  50 us
    ppermute x1, waiting for transfers between devices, on_device(): far = lax.ppermute(grad_hidden, 'fsdp', [(i, i ^ 2) for i in range(4)])  34.8 us
    another operation x2, other arithmetic  29.5 us
    ppermute x1, waiting for transfers between devices, gather_own_columns(): lax.ppermute(jnp.concatenate([cols(me ^ 2), cols(me ^ 3)], axis=0), axis,...  14 us
    ppermute x5, starting transfers between devices, mean_and_var(): other = lax.ppermute(stats, axis, [(i, i ^ stride) for i in range(count)])  13.9 us
    ppermute x10, starting transfers between devices, tree_sum(): packed = packed + lax.ppermute(packed, axis, route)  13.5 us
  transfers between devices with their start and end apart: 27, of which 20 were waited for; matrix products, arithmetic and copies ran while one was open for 11% of the time, Pallas kernels for 0%

profile of v12, /device:TPU:0, one launch (start us, length us, event | category | flops | bytes accessed | tf_op | source)
XLA Modules:
  0.0 432.0 jit_solution(3602691876482972206)
XLA Ops:
  7.2 3.0 collective-permute-start
  11.8 50.0 %collective-permute-done = bf16[384,3072]{1,0:T(8,128)(2,1)} collective-permute-done((bf16[384,3072]{1,0:T(8,128)(2,1)}, bf16[384,3072]{1,0:T(8,128)(2,1)}, u32[]{:S(2)}, u32[]{:S(2)}) %collective-permute-start) | collective-permute-done | bytes 2359328 | tf_op jit(solution)/shard_map/ppermute | solution.py:62
  66.9 3.1 fusion.128
  75.1 2.6 collective-permute-start.3
  79.0 9.4 %fusion.127 = (f32[1536]{0:T(1024)S(1)}, f32[384,1536]{1,0:T(8,128)S(1)}) fusion(f32[415,1536]{1,0:T(8,128)S(1)} %maximum_convert_fusion, f32[1536]{0:T(1024)S(1)} %get-tuple-element.88, f32[1536]{0:T(1024)S(1)} %get-tuple-element.89, f32[1536]{0:T(1024)S(1)} %get-tuple-element.59, f32[1536]{0:T(1024)S(1)} %get-tuple-element.60, ...), kind=kLoop, calls=%fused_computation.311 | loop fusion | flops 37747200 | bytes 78059520 | tf_op jit(solution)/shard_map/reduce_sum | solution.py:43
  92.0 2.7 collective-permute-start.5
  96.4 3.0 collective-permute-start.6
  101.1 3.0 collective-permute-start.7
  105.9 3.1 collective-permute-start.8
  110.8 2.5 fusion.125
  114.7 4.8 %broadcast_in_dim.2 = bf16[1536,3072]{1,0:T(8,128)(2,1)} broadcast(bf16[]{:T(256)} %constant.50.clone.1), dimensions={} | broadcast | bytes 9437186 | tf_op jit(solution)/shard_map/broadcast_in_dim | solution.py:129
  122.7 3.3 constant_dynamic-update-slice_fusion.2
  129.8 2.7 collective-permute-start.13
  135.1 7.8 %multiply_reduce_fusion = (f32[1536]{0:T(1024)}, f32[1536]{0:T(1024)}, f32[1536]{0:T(1024)}, f32[1536]{0:T(1024)}, f32[1536]{0:T(1024)}, /*index=5*/f32[1536]{0:...) fusion(f32[415,1536]{1,0:T(8,128)S(1)} %maximum_convert_fusion,, ...), kind=kLoop, calls=%fused_computation.170 | loop fusion | flops 31822848 | bytes 48519168 | tf_op jit(solution)/shard_map/reduce_sum | solution.py:170
  146.2 25.5 %multiply_convert_fusion.1 = (bf16[384,1536]{1,0:T(8,128)(2,1)}, f32[384,1536]{1,0:T(8,128)}) fusion(f32[384,3072]{1,0:T(8,128)} %copy-done, f32[31,1536]{1,0:T(8,128)S(1)} %collective-permute-done.14, f32[384,1536]{1,0:T(8,128)S(1)} %get-tuple-element.107, f32[1536]{0:T(1024)} %copy-done.47, f32[1536]{0:T(1024)} %copy-done.48, ...), kind=kLoop, calls=%fused_computation.203 | loop fusion | flops 58392576 | bytes 8644608 | tf_op jit(solution)/shard_map/convert
  171.7 4.1 multiply_convert_fusion
  177.8 3.2 collective-permute-start.15
  181.0 4.6 %multiply_reduce_fusion.18 = (f32[1536]{0:T(1024)S(1)}, f32[1536]{0:T(1024)S(1)}, f32[1536]{0:T(1024)S(1)}, f32[1536]{0:T(1024)S(1)}, f32[1536]{0:T(1024)S(1)}, ...) fusion(f32[384,1536]{1,0:T(8,128)S(1)} %get-tuple-element.107, ...), kind=kLoop, calls=%fused_computation.188 | loop fusion | flops 16493568 | bytes 35475456 | tf_op jit(solution)/shard_map/reduce_sum | solution.py:170
  187.2 9.0 %fusion.11 = (f32[1536]{0:T(1024)S(1)}, f32[384]{0:T(512)S(1)}, f32[384]{0:T(512)S(1)}, f32[1536]{0:T(1024)S(1)}, f32[384,1536]{1,0:T(8,128)S(1)}) fusion(bf16[384,1536]{1,0:T(8,128)(2,1)} %param.8, f32[384]{0:T(512)S(1)} %copy-done.74, f32[384]{0:T(512)S(1)} %copy-done.53, f32[1536]{0:T(1024)S(1)} %copy-done.51, ...), kind=kOutput, calls=%fused_computation.45 | convolution fusion | flops 3634491392 | bytes 15360000 | tf_op jit(solution)/shard_map/dot_general | solution.py:180
  198.1 34.8 %collective-permute-done.15 = bf16[384,3072]{1,0:T(8,128)(2,1)} collective-permute-done((bf16[384,3072]{1,0:T(8,128)(2,1)}, bf16[384,3072]{1,0:T(8,128)(2,1)}, u32[]{:S(2)}, u32[]{:S(2)}) %collective-permute-start.15) | collective-permute-done | bytes 2359328 | tf_op jit(solution)/shard_map/ppermute | solution.py:198
  235.4 14.0 %collective-permute-done.16 = bf16[768,384]{1,0:T(8,128)(2,1)S(1)} collective-permute-done((bf16[768,384]{1,0:T(8,128)(2,1)S(1)}, bf16[768,384]{1,0:T(8,128)(2,1)S(1)}, u32[]{:S(2)}, u32[]{:S(2)}) %collective-permute-start.16) | collective-permute-done | bytes 589856 | tf_op jit(solution)/shard_map/ppermute | solution.py:92
  249.6 2.4 fusion.116
  252.0 3.1 fusion.114
  256.6 4.1 add_add_fusion
  260.7 96.8 %reduce-scatter.2.cloned.1.call-done = f32[48,3072]{1,0:T(8,128)} async-done(((f32[384,3072]{1,0:T(8,128)}), f32[48,3072]{1,0:T(8,128)}) %reduce-scatter.2.cloned.1.call-update) | async-done | bytes 589840 | tf_op jit(solution)/shard_map/reduce_scatter | solution.py:219
  362.5 6.5 %collective-permute-done.21 = f32[34,1536]{1,0:T(8,128)S(1)} collective-permute-done((f32[34,1536]{1,0:T(8,128)S(1)}, f32[34,1536]{1,0:T(8,128)S(1)}, u32[]{:S(2)}, u32[]{:S(2)}) %collective-permute-start.21) | collective-permute-done | bytes 208928 | tf_op jit(solution)/shard_map/ppermute | solution.py:25
  370.6 8.5 %collective-permute-done.22 = f32[34,1536]{1,0:T(8,128)S(1)} collective-permute-done((f32[34,1536]{1,0:T(8,128)S(1)}, f32[34,1536]{1,0:T(8,128)S(1)}, u32[]{:S(2)}, u32[]{:S(2)}) %collective-permute-start.22) | collective-permute-done | bytes 208928 | tf_op jit(solution)/shard_map/ppermute | solution.py:25
  380.7 8.0 %collective-permute-done.23 = f32[34,1536]{1,0:T(8,128)S(1)} collective-permute-done((f32[34,1536]{1,0:T(8,128)S(1)}, f32[34,1536]{1,0:T(8,128)S(1)}, u32[]{:S(2)}, u32[]{:S(2)}) %collective-permute-start.23) | collective-permute-done | bytes 208928 | tf_op jit(solution)/shard_map/ppermute | solution.py:25
  388.7 2.7 collective-permute-start.24
  391.4 22.3 %collective-permute-done.24 = f32[34,1536]{1,0:T(8,128)S(1)} collective-permute-done((f32[34,1536]{1,0:T(8,128)S(1)}, f32[34,1536]{1,0:T(8,128)S(1)}, u32[]{:S(2)}, u32[]{:S(2)}) %collective-permute-start.24) | collective-permute-done | bytes 208928 | tf_op jit(solution)/shard_map/ppermute | solution.py:25
  415.1 5.6 %all-gather.2.cloned.1.call-done = bf16[384,3072]{1,0:T(8,128)(2,1)} async-done(((bf16[48,3072]{1,0:T(8,128)(2,1)}), bf16[384,3072]{1,0:T(8,128)(2,1)}) %all-gather.2.cloned.1.call-update) | async-done | bytes 2359312 | tf_op jit(solution)/shard_map/all_gather | solution.py:220
  420.7 4.4 %convert_element_type.36 = f32[384,3072]{1,0:T(8,128)} convert(bf16[384,3072]{1,0:T(8,128)(2,1)} %all-gather.2.cloned.1.call-done) | non-fusion elementwise | flops 1179648 | bytes 7077888 | tf_op jit(solution)/shard_map/convert_element_type | solution.py:222
  (283 shorter events, 55.8 us)
Async XLA Ops:
  7.2 56.9 %copy-start.1 = (bf16[384,1536]{1,0:T(8,128)(2,1)S(1)}, bf16[384,1536]{1,0:T(8,128)(2,1)}, u32[]{:S(2)}) copy-start(bf16[384,1536]{1,0:T(8,128)(2,1)} %param.8) | copy-start | bytes 3538948
  7.2 56.9 %copy-start.75 = (f32[1536]{0:T(1024)S(1)}, f32[1536]{0:T(1024)}, u32[]{:S(2)}) copy-start(f32[1536]{0:T(1024)} %param.10) | copy-start | bytes 18436
  7.2 56.9 %copy-start.50 = (f32[1536]{0:T(1024)S(1)}, f32[1536]{0:T(1024)}, u32[]{:S(2)}) copy-start(f32[1536]{0:T(1024)} %param.9) | copy-start | bytes 18436
  7.2 350.3 %reduce-scatter.2.cloned.1.call-start = ((), (), s32[]{:S(2)}) async-start(), calls=%async_computation.1 | async-start | bytes 5308416 | tf_op jit(solution)/shard_map/reduce_scatter | solution.py:219
  7.2 54.6 %collective-permute-start = (bf16[384,3072]{1,0:T(8,128)(2,1)}, bf16[384,3072]{1,0:T(8,128)(2,1)}, u32[]{:S(2)}, u32[]{:S(2)}) collective-permute-start(bf16[384,3072]{1,0:T(8,128)(2,1)} %param.11), channel_id=1, source_target_pairs={{0,2},{1,3},{2,0},{3,1},{4,6},{5,7},{6,4},{7,5},{8,10},{9,11},{10,... | collective-permute-start | bytes 7077896 | tf_op jit(solution)/shard_map/ppermute | solution.py:62
  10.2 59.7 %collective-permute-start.1 = (bf16[384,3072]{1,0:T(8,128)(2,1)}, bf16[384,3072]{1,0:T(8,128)(2,1)S(1)}, u32[]{:S(2)}, u32[]{:S(2)}) collective-permute-start(bf16[384,3072]{1,0:T(8,128)(2,1)} %param.11), channel_id=1, source_target_pairs={{0,1},{1,0},{2,3},{3,2},{4,5},{5,4},{6,7},{7,6},{8,9},{9,8},{10,11... | collective-permute-start | bytes 7077896 | tf_op jit(solution)/shard_map/ppermute | solution.py:63
  11.8 51.8 %copy-start.52 = (f32[384]{0:T(512)}, f32[384]{0:T(512)S(1)}, u32[]{:S(2)}) copy-start(f32[384]{0:T(512)S(1)} %broadcast_multiply_fusion.3) | copy-start | bytes 4612
  61.8 9.6 %collective-permute-start.2 = (bf16[384,3072]{1,0:T(8,128)(2,1)}, bf16[384,3072]{1,0:T(8,128)(2,1)S(1)}, u32[]{:S(2)}, u32[]{:S(2)}) collective-permute-start(bf16[384,3072]{1,0:T(8,128)(2,1)} %collective-permute-done), channel_id=1, source_target_pairs={{0,1},{1,0},{2,3},{3,2},{4,5},{5,4},{6,7},{7,6},{8,9},{9,8},{10,11... | collective-permute-start | bytes 7077896 | tf_op jit(solution)/shard_map/ppermute | solution.py:64
  75.1 3.4 collective-permute-start.3
  88.9 3.0 collective-permute-start.4
  92.0 4.4 %collective-permute-start.5 = (f32[2,1536]{1,0:T(2,128)S(1)}, f32[2,1536]{1,0:T(2,128)S(1)}, u32[]{:S(2)}, u32[]{:S(2)}) collective-permute-start(f32[2,1536]{1,0:T(2,128)S(1)} %pad_maximum_fusion.6), channel_id=1, source_target_pairs={{0,2},{1,3},{2,0},{3,1},{4,6},{5,7},{6,4},{7,5},{8,10},{9,11},{10,... | collective-permute-start | bytes 36872 | tf_op jit(solution)/shard_map/ppermute | solution.py:49
  96.4 4.6 %collective-permute-start.6 = (f32[2,1536]{1,0:T(2,128)S(1)}, f32[2,1536]{1,0:T(2,128)S(1)}, u32[]{:S(2)}, u32[]{:S(2)}) collective-permute-start(f32[2,1536]{1,0:T(2,128)S(1)} %pad_maximum_fusion.7), channel_id=1, source_target_pairs={{0,4},{1,5},{2,6},{3,7},{4,0},{5,1},{6,2},{7,3},{8,12},{9,13},{10,... | collective-permute-start | bytes 36872 | tf_op jit(solution)/shard_map/ppermute | solution.py:49
  101.1 4.7 %collective-permute-start.7 = (f32[2,1536]{1,0:T(2,128)S(1)}, f32[2,1536]{1,0:T(2,128)S(1)}, u32[]{:S(2)}, u32[]{:S(2)}) collective-permute-start(f32[2,1536]{1,0:T(2,128)S(1)} %pad_maximum_fusion.8), channel_id=1, source_target_pairs={{0,8},{1,9},{2,10},{3,11},{4,12},{5,13},{6,14},{7,15},{8,0},{9,1},... | collective-permute-start | bytes 36872 | tf_op jit(solution)/shard_map/ppermute | solution.py:49
  105.9 4.8 %collective-permute-start.8 = (f32[2,1536]{1,0:T(2,128)S(1)}, f32[2,1536]{1,0:T(2,128)S(1)}, u32[]{:S(2)}, u32[]{:S(2)}) collective-permute-start(f32[2,1536]{1,0:T(2,128)S(1)} %pad_maximum_fusion.9), channel_id=1, source_target_pairs={{0,16},{1,17},{2,18},{3,19},{4,20},{5,21},{6,22},{7,23},{8,24},{9,... | collective-permute-start | bytes 36872 | tf_op jit(solution)/shard_map/ppermute | solution.py:49
  113.3 1.2 collective-permute-start.9
  114.6 6.5 %collective-permute-start.10 = (f32[2,1536]{1,0:T(2,128)S(1)}, f32[2,1536]{1,0:T(2,128)S(1)}, u32[]{:S(2)}, u32[]{:S(2)}) collective-permute-start(f32[2,1536]{1,0:T(2,128)S(1)} %fusion.122), channel_id=1, source_target_pairs={{0,2},{1,3},{2,0},{3,1},{4,6},{5,7},{6,4},{7,5},{8,10},{9,11},{10,... | collective-permute-start | bytes 36872 | tf_op jit(solution)/shard_map/ppermute | solution.py:25
  121.1 4.9 %collective-permute-start.11 = (f32[2,1536]{1,0:T(2,128)S(1)}, f32[2,1536]{1,0:T(2,128)S(1)}, u32[]{:S(2)}, u32[]{:S(2)}) collective-permute-start(f32[2,1536]{1,0:T(2,128)S(1)} %fusion.141), channel_id=1, source_target_pairs={{0,4},{1,5},{2,6},{3,7},{4,0},{5,1},{6,2},{7,3},{8,12},{9,13},{10,... | collective-permute-start | bytes 36872 | tf_op jit(solution)/shard_map/ppermute | solution.py:25
  126.0 3.8 collective-permute-start.12
  129.8 4.7 %collective-permute-start.13 = (f32[2,1536]{1,0:T(2,128)S(1)}, f32[2,1536]{1,0:T(2,128)S(1)}, u32[]{:S(2)}, u32[]{:S(2)}) collective-permute-start(f32[2,1536]{1,0:T(2,128)S(1)} %add.514), channel_id=1, source_target_pairs={{0,16},{1,17},{2,18},{3,19},{4,20},{5,21},{6,22},{7,23},{8,24},{9,... | collective-permute-start | bytes 36872 | tf_op jit(solution)/shard_map/ppermute | solution.py:25
  142.9 3.3 collective-permute-start.14
  177.8 55.1 %collective-permute-start.15 = (bf16[384,3072]{1,0:T(8,128)(2,1)}, bf16[384,3072]{1,0:T(8,128)(2,1)}, u32[]{:S(2)}, u32[]{:S(2)}) collective-permute-start(bf16[384,3072]{1,0:T(8,128)(2,1)} %pad_maximum_fusion.1), channel_id=1, source_target_pairs={{0,2},{1,3},{2,0},{3,1},{4,6},{5,7},{6,4},{7,5},{8,10},{9,11},{10,... | collective-permute-start | bytes 7077896 | tf_op jit(solution)/shard_map/ppermute | solution.py:198
  186.5 68.6 %collective-permute-start.18 = (bf16[384,3072]{1,0:T(8,128)(2,1)}, bf16[384,3072]{1,0:T(8,128)(2,1)S(1)}, u32[]{:S(2)}, u32[]{:S(2)}) collective-permute-start(bf16[384,3072]{1,0:T(8,128)(2,1)} %pad_maximum_fusion.1), channel_id=1, source_target_pairs={{0,1},{1,0},{2,3},{3,2},{4,5},{5,4},{6,7},{7,6},{8,9},{9,8},{10,11... | collective-permute-start | bytes 7077896 | tf_op jit(solution)/shard_map/ppermute | solution.py:199
  196.3 53.2 %copy-start.11 = (bf16[384,384]{1,0:T(8,128)(2,1)S(1)}, bf16[384,384]{1,0:T(8,128)(2,1)}, u32[]{:S(2)}) copy-start(bf16[384,384]{1,0:T(8,128)(2,1)} %copy-done.10) | copy-start | bytes 884740
  232.8 23.8 %collective-permute-start.19 = (bf16[384,3072]{1,0:T(8,128)(2,1)}, bf16[384,3072]{1,0:T(8,128)(2,1)S(1)}, u32[]{:S(2)}, u32[]{:S(2)}) collective-permute-start(bf16[384,3072]{1,0:T(8,128)(2,1)} %collective-permute-done.15), channel_id=1, source_target_pairs={{0,1},{1,0},{2,3},{3,2},{4,5},{5,4},{6,7},{7,6},{8,9},{9,8},{10,11... | collective-permute-start | bytes 7077896 | tf_op jit(solution)/shard_map/ppermute | solution.py:203
  233.3 16.1 %collective-permute-start.16 = (bf16[768,384]{1,0:T(8,128)(2,1)S(1)}, bf16[768,384]{1,0:T(8,128)(2,1)S(1)}, u32[]{:S(2)}, u32[]{:S(2)}) collective-permute-start(bf16[768,384]{1,0:T(8,128)(2,1)S(1)} %pad_maximum_fusion.2), channel_id=1, source_target_pairs={{0,2},{1,3},{2,0},{3,1},{4,6},{5,7},{6,4},{7,5},{8,10},{9,11},{10,... | collective-permute-start | bytes 1769480 | tf_op jit(solution)/shard_map/ppermute | solution.py:92
  249.5 5.6 %collective-permute-start.17 = (bf16[768,384]{1,0:T(8,128)(2,1)S(1)}, bf16[768,384]{1,0:T(8,128)(2,1)S(1)}, u32[]{:S(2)}, u32[]{:S(2)}) collective-permute-start(bf16[768,384]{1,0:T(8,128)(2,1)S(1)} %pad_maximum_fusion.3), channel_id=1, source_target_pairs={{0,1},{1,0},{2,3},{3,2},{4,5},{5,4},{6,7},{7,6},{8,9},{9,8},{10,11... | collective-permute-start | bytes 1769480 | tf_op jit(solution)/shard_map/ppermute | solution.py:95
  260.7 160.0 %all-gather.2.cloned.1.call-start = ((), (), s32[]{:S(2)}) async-start(), calls=%async_computation.2 | async-start | bytes 2654208 | tf_op jit(solution)/shard_map/all_gather | solution.py:220
  359.4 1.6 collective-permute-start.20
  361.0 8.1 %collective-permute-start.21 = (f32[34,1536]{1,0:T(8,128)S(1)}, f32[34,1536]{1,0:T(8,128)S(1)}, u32[]{:S(2)}, u32[]{:S(2)}) collective-permute-start(f32[34,1536]{1,0:T(8,128)S(1)} %fusion.123), channel_id=1, source_target_pairs={{0,2},{1,3},{2,0},{3,1},{4,6},{5,7},{6,4},{7,5},{8,10},{9,11},{10,... | collective-permute-start | bytes 626696 | tf_op jit(solution)/shard_map/ppermute | solution.py:25
  369.1 10.0 %collective-permute-start.22 = (f32[34,1536]{1,0:T(8,128)S(1)}, f32[34,1536]{1,0:T(8,128)S(1)}, u32[]{:S(2)}, u32[]{:S(2)}) collective-permute-start(f32[34,1536]{1,0:T(8,128)S(1)} %add.551), channel_id=1, source_target_pairs={{0,4},{1,5},{2,6},{3,7},{4,0},{5,1},{6,2},{7,3},{8,12},{9,13},{10,... | collective-permute-start | bytes 626696 | tf_op jit(solution)/shard_map/ppermute | solution.py:25
  379.2 9.5 %collective-permute-start.23 = (f32[34,1536]{1,0:T(8,128)S(1)}, f32[34,1536]{1,0:T(8,128)S(1)}, u32[]{:S(2)}, u32[]{:S(2)}) collective-permute-start(f32[34,1536]{1,0:T(8,128)S(1)} %add.552), channel_id=1, source_target_pairs={{0,8},{1,9},{2,10},{3,11},{4,12},{5,13},{6,14},{7,15},{8,0},{9,1},... | collective-permute-start | bytes 626696 | tf_op jit(solution)/shard_map/ppermute | solution.py:25
  388.7 25.0 %collective-permute-start.24 = (f32[34,1536]{1,0:T(8,128)S(1)}, f32[34,1536]{1,0:T(8,128)S(1)}, u32[]{:S(2)}, u32[]{:S(2)}) collective-permute-start(f32[34,1536]{1,0:T(8,128)S(1)} %add.553), channel_id=1, source_target_pairs={{0,16},{1,17},{2,18},{3,19},{4,20},{5,21},{6,22},{7,23},{8,24},{9,... | collective-permute-start | bytes 626696 | tf_op jit(solution)/shard_map/ppermute | solution.py:25
  (71 other events, 836.8 us)
Sparse Core Ops, SparseCore 0:
  260.8 96.6 reduce-scatter.1
  360.2 60.4 all-gather.1

commit v13 on v8

--- a/solution.py
+++ b/solution.py
@@ -58,20 +58,22 @@
     return stats[0], stats[1] / rows
 
 
-def group_shards(block, axis):
+def group_shards(block, axis, cover=None):
     far = lax.ppermute(block, axis, [(i, i ^ 2) for i in range(4)])
+    if cover is not None:
+        far, _ = lax.optimization_barrier((far, cover))
     near = lax.ppermute(block, axis, [(i, i ^ 1) for i in range(4)])
     near_far = lax.ppermute(far, axis, [(i, i ^ 1) for i in range(4)])
     return [block, far, near, near_far]
 
 
-def gather_rows(block, axis):
+def gather_rows(block, axis, cover=None):
     count = lax.axis_size(axis)
     if count != 4:
         return lax.all_gather(block, axis, axis=0, tiled=True)
     rows = block.shape[0]
     me = lax.axis_index(axis)
-    shards = group_shards(block, axis)
+    shards = group_shards(block, axis, cover)
     whole = jnp.zeros((count * rows,) + block.shape[1:], block.dtype)
     for shard, owner in zip(shards, (me, me ^ 2, me ^ 1, me ^ 3)):
         whole = lax.dynamic_update_slice_in_dim(whole, shard, owner * rows, axis=0)
@@ -113,7 +115,7 @@
     )
     standardized_input = centered_rows * row_inverse_deviation
     normalized_rows = (standardized_input * layer_norm_gain + layer_norm_bias).astype(jnp.bfloat16)
-    full_weight = gather_rows(w_in, "fsdp")
+    full_weight = gather_rows(w_in, "fsdp", normalized_rows)
     hidden = jnp.dot(normalized_rows, full_weight, preferred_element_type=jnp.float32)
     value_part = hidden[:, :features]
     gate_sig = jax.nn.sigmoid(hidden[:, features:])

time: 427 us -> 428 us (level)
  transfers between devices with their start and end apart: 27 -> 27, of which waited for: 21 -> 22; matrix products, arithmetic and copies ran while one was open for 8% -> 8% of each run, Pallas kernels for 0% -> 0%
where the time goes in v13:
time: 428 us; the launch traced here: 427 us
  waiting for transfers between devices  264 us (62%)
  other arithmetic  69.9 us (16%)
  starting transfers between devices  42.3 us (10%)
  matrix products  23 us (5%)
  between operations  15.7 us (4%)
  local copies, waits for them, and re-layouts  12.2 us (3%)
    reduce_scatter x1, waiting for transfers between devices, on_device(): lax.psum_scatter(row_share, 'seq', scatter_dimension=0, tiled=True)  97.6 us
    ppermute x10, waiting for transfers between devices, tree_sum(): packed = packed + lax.ppermute(packed, axis, route)  57.8 us
    ppermute x1, waiting for transfers between devices, group_shards(): far = lax.ppermute(block, axis, [(i, i ^ 2) for i in range(4)])  47.8 us
    ppermute x1, waiting for transfers between devices, on_device(): far = lax.ppermute(grad_hidden, 'fsdp', [(i, i ^ 2) for i in range(4)])  31.9 us
    another operation x2, other arithmetic  29.5 us
    ppermute x5, starting transfers between devices, mean_and_var(): other = lax.ppermute(stats, axis, [(i, i ^ stride) for i in range(count)])  14 us
    ppermute x1, waiting for transfers between devices, gather_own_columns(): lax.ppermute(jnp.concatenate([cols(me ^ 2), cols(me ^ 3)], axis=0), axis,...  13.5 us
    ppermute x10, starting transfers between devices, tree_sum(): packed = packed + lax.ppermute(packed, axis, route)  13.5 us
  transfers between devices with their start and end apart: 27, of which 22 were waited for; matrix products, arithmetic and copies ran while one was open for 8% of the time, Pallas kernels for 0%

profile of v13, /device:TPU:0, one launch (start us, length us, event | category | flops | bytes accessed | tf_op | source)
XLA Modules:
  0.0 427.2 jit_solution(4339340137640025169)
XLA Ops:
  7.3 3.0 collective-permute-start
  14.1 47.8 %collective-permute-done = bf16[384,3072]{1,0:T(8,128)(2,1)} collective-permute-done((bf16[384,3072]{1,0:T(8,128)(2,1)}, bf16[384,3072]{1,0:T(8,128)(2,1)}, u32[]{:S(2)}, u32[]{:S(2)}) %collective-permute-start) | collective-permute-done | bytes 2359328 | tf_op jit(solution)/shard_map/ppermute | solution.py:62
  70.2 3.8 fusion.125
  76.2 2.6 collective-permute-start.3
  80.1 9.4 %fusion.124 = (f32[1536]{0:T(1024)S(1)}, f32[384,1536]{1,0:T(8,128)S(1)}) fusion(f32[415,1536]{1,0:T(8,128)S(1)} %maximum_convert_fusion, f32[1536]{0:T(1024)S(1)} %get-tuple-element.90, f32[1536]{0:T(1024)S(1)} %get-tuple-element.91, f32[1536]{0:T(1024)S(1)} %get-tuple-element.61, f32[1536]{0:T(1024)S(1)} %get-tuple-element.62, ...), kind=kLoop, calls=%fused_computation.307 | loop fusion | flops 37747200 | bytes 78059520 | tf_op jit(solution)/shard_map/reduce_sum | solution.py:43
  90.0 2.1 collective-permute-start.4
  93.1 2.7 collective-permute-start.5
  97.5 3.0 collective-permute-start.6
  102.3 3.0 collective-permute-start.7
  107.0 3.1 collective-permute-start.8
  111.9 2.5 fusion.122
  115.8 3.7 collective-permute-done.10
  120.5 2.7 collective-permute-done.11
  127.0 3.0 collective-permute-start.13
  132.3 7.8 %multiply_reduce_fusion = (f32[1536]{0:T(1024)}, f32[1536]{0:T(1024)}, f32[1536]{0:T(1024)}, f32[1536]{0:T(1024)}, f32[1536]{0:T(1024)}, /*index=5*/f32[1536]{0:...) fusion(f32[415,1536]{1,0:T(8,128)S(1)} %maximum_convert_fusion,, ...), kind=kLoop, calls=%fused_computation.169 | loop fusion | flops 31822848 | bytes 48519168 | tf_op jit(solution)/shard_map/reduce_sum | solution.py:153
  143.5 25.5 %multiply_convert_fusion.1 = (bf16[384,1536]{1,0:T(8,128)(2,1)}, f32[384,1536]{1,0:T(8,128)}) fusion(f32[384,3072]{1,0:T(8,128)} %copy-done, f32[31,1536]{1,0:T(8,128)S(1)} %collective-permute-done.14, f32[384,1536]{1,0:T(8,128)S(1)} %get-tuple-element.109, f32[1536]{0:T(1024)} %copy-done.41, f32[1536]{0:T(1024)} %copy-done.42, ...), kind=kLoop, calls=%fused_computation.202 | loop fusion | flops 58392576 | bytes 8644608 | tf_op jit(solution)/shard_map/convert
  169.0 4.1 multiply_convert_fusion
  176.9 4.6 %multiply_reduce_fusion.18 = (f32[1536]{0:T(1024)S(1)}, f32[1536]{0:T(1024)S(1)}, f32[1536]{0:T(1024)S(1)}, f32[1536]{0:T(1024)S(1)}, f32[1536]{0:T(1024)S(1)}, ...) fusion(f32[384,1536]{1,0:T(8,128)S(1)} %get-tuple-element.109, ...), kind=kLoop, calls=%fused_computation.187 | loop fusion | flops 16493568 | bytes 35475456 | tf_op jit(solution)/shard_map/reduce_sum | solution.py:153
  182.4 2.5 collective-permute-start.18
  184.9 9.1 %fusion.11 = (f32[1536]{0:T(1024)S(1)}, f32[384]{0:T(512)S(1)}, f32[384]{0:T(512)S(1)}, f32[1536]{0:T(1024)S(1)}, f32[384,1536]{1,0:T(8,128)S(1)}) fusion(bf16[384,1536]{1,0:T(8,128)(2,1)} %param.8, f32[384]{0:T(512)} %copy-done.65, f32[384]{0:T(512)S(1)} %broadcast_multiply_fusion.3, f32[1536]{0:T(1024)S(1)} %copy-done.45, ...), kind=kOutput, calls=%fused_computation.44 | convolution fusion | flops 3634491392 | bytes 15360000 | tf_op jit(solution)/shard_map/dot_general | solution.py:163
  195.8 31.9 %collective-permute-done.15 = bf16[384,3072]{1,0:T(8,128)(2,1)} collective-permute-done((bf16[384,3072]{1,0:T(8,128)(2,1)}, bf16[384,3072]{1,0:T(8,128)(2,1)}, u32[]{:S(2)}, u32[]{:S(2)}) %collective-permute-start.15) | collective-permute-done | bytes 2359328 | tf_op jit(solution)/shard_map/ppermute | solution.py:181
  231.4 13.5 %collective-permute-done.16 = bf16[768,384]{1,0:T(8,128)(2,1)S(1)} collective-permute-done((bf16[768,384]{1,0:T(8,128)(2,1)S(1)}, bf16[768,384]{1,0:T(8,128)(2,1)S(1)}, u32[]{:S(2)}, u32[]{:S(2)}) %collective-permute-start.16) | collective-permute-done | bytes 589856 | tf_op jit(solution)/shard_map/ppermute | solution.py:94
  246.5 3.1 fusion.114
  251.1 4.1 add_add_fusion
  255.2 97.6 %reduce-scatter.2.cloned.1.call-done = f32[48,3072]{1,0:T(8,128)} async-done(((f32[384,3072]{1,0:T(8,128)}), f32[48,3072]{1,0:T(8,128)}) %reduce-scatter.2.cloned.1.call-update) | async-done | bytes 589840 | tf_op jit(solution)/shard_map/reduce_scatter | solution.py:202
  357.8 6.5 %collective-permute-done.21 = f32[34,1536]{1,0:T(8,128)S(1)} collective-permute-done((f32[34,1536]{1,0:T(8,128)S(1)}, f32[34,1536]{1,0:T(8,128)S(1)}, u32[]{:S(2)}, u32[]{:S(2)}) %collective-permute-start.21) | collective-permute-done | bytes 208928 | tf_op jit(solution)/shard_map/ppermute | solution.py:25
  365.9 8.5 %collective-permute-done.22 = f32[34,1536]{1,0:T(8,128)S(1)} collective-permute-done((f32[34,1536]{1,0:T(8,128)S(1)}, f32[34,1536]{1,0:T(8,128)S(1)}, u32[]{:S(2)}, u32[]{:S(2)}) %collective-permute-start.22) | collective-permute-done | bytes 208928 | tf_op jit(solution)/shard_map/ppermute | solution.py:25
  376.0 8.0 %collective-permute-done.23 = f32[34,1536]{1,0:T(8,128)S(1)} collective-permute-done((f32[34,1536]{1,0:T(8,128)S(1)}, f32[34,1536]{1,0:T(8,128)S(1)}, u32[]{:S(2)}, u32[]{:S(2)}) %collective-permute-start.23) | collective-permute-done | bytes 208928 | tf_op jit(solution)/shard_map/ppermute | solution.py:25
  384.0 2.7 collective-permute-start.24
  386.7 22.3 %collective-permute-done.24 = f32[34,1536]{1,0:T(8,128)S(1)} collective-permute-done((f32[34,1536]{1,0:T(8,128)S(1)}, f32[34,1536]{1,0:T(8,128)S(1)}, u32[]{:S(2)}, u32[]{:S(2)}) %collective-permute-start.24) | collective-permute-done | bytes 208928 | tf_op jit(solution)/shard_map/ppermute | solution.py:25
  410.3 5.6 %all-gather.2.cloned.1.call-done = bf16[384,3072]{1,0:T(8,128)(2,1)} async-done(((bf16[48,3072]{1,0:T(8,128)(2,1)}), bf16[384,3072]{1,0:T(8,128)(2,1)}) %all-gather.2.cloned.1.call-update) | async-done | bytes 2359312 | tf_op jit(solution)/shard_map/all_gather | solution.py:203
  416.0 4.4 %convert_element_type.36 = f32[384,3072]{1,0:T(8,128)} convert(bf16[384,3072]{1,0:T(8,128)(2,1)} %all-gather.2.cloned.1.call-done) | non-fusion elementwise | flops 1179648 | bytes 7077888 | tf_op jit(solution)/shard_map/convert_element_type | solution.py:205
  (264 shorter events, 57.5 us)
Async XLA Ops:
  7.2 54.6 %copy-start.12 = (f32[32,1536]{1,0:T(8,128)S(1)}, f32[32,1536]{1,0:T(8,128)}, u32[]{:S(2)}) copy-start(f32[32,1536]{1,0:T(8,128)} %param.12) | copy-start | bytes 589828
  7.2 345.6 %reduce-scatter.2.cloned.1.call-start = ((), (), s32[]{:S(2)}) async-start(), calls=%async_computation.1 | async-start | bytes 5308416 | tf_op jit(solution)/shard_map/reduce_scatter | solution.py:202
  7.3 54.6 %collective-permute-start = (bf16[384,3072]{1,0:T(8,128)(2,1)}, bf16[384,3072]{1,0:T(8,128)(2,1)}, u32[]{:S(2)}, u32[]{:S(2)}) collective-permute-start(bf16[384,3072]{1,0:T(8,128)(2,1)} %param.11), channel_id=1, source_target_pairs={{0,2},{1,3},{2,0},{3,1},{4,6},{5,7},{6,4},{7,5},{8,10},{9,11},{10,... | collective-permute-start | bytes 7077896 | tf_op jit(solution)/shard_map/ppermute | solution.py:62
  10.3 56.0 %collective-permute-start.1 = (bf16[384,3072]{1,0:T(8,128)(2,1)}, bf16[384,3072]{1,0:T(8,128)(2,1)}, u32[]{:S(2)}, u32[]{:S(2)}) collective-permute-start(bf16[384,3072]{1,0:T(8,128)(2,1)} %param.11), channel_id=1, source_target_pairs={{0,1},{1,0},{2,3},{3,2},{4,5},{5,4},{6,7},{7,6},{8,9},{9,8},{10,11... | collective-permute-start | bytes 7077896 | tf_op jit(solution)/shard_map/ppermute | solution.py:65
  13.5 48.3 %copy-start.65 = (f32[384]{0:T(512)}, f32[384]{0:T(512)S(1)}, u32[]{:S(2)}) copy-start(f32[384]{0:T(512)S(1)} %add_rsqrt_fusion) | copy-start | bytes 4612
  14.1 56.1 %copy-start.9 = (bf16[384,1536]{1,0:T(8,128)(2,1)}, bf16[384,1536]{1,0:T(8,128)(2,1)S(1)}, u32[]{:S(2)}) copy-start(bf16[384,1536]{1,0:T(8,128)(2,1)S(1)} %fusion.7) | copy-start | bytes 3538948
  61.8 6.4 %collective-permute-start.2 = (bf16[384,3072]{1,0:T(8,128)(2,1)}, bf16[384,3072]{1,0:T(8,128)(2,1)}, u32[]{:S(2)}, u32[]{:S(2)}) collective-permute-start(bf16[384,3072]{1,0:T(8,128)(2,1)} %collective-permute-done), channel_id=1, source_target_pairs={{0,1},{1,0},{2,3},{3,2},{4,5},{5,4},{6,7},{7,6},{8,9},{9,8},{10,11... | collective-permute-start | bytes 7077896 | tf_op jit(solution)/shard_map/ppermute | solution.py:66
  76.2 3.3 collective-permute-start.3
  89.7 22.3 %copy-start.8 = (bf16[384,1536]{1,0:T(8,128)(2,1)S(1)}, bf16[384,1536]{1,0:T(8,128)(2,1)}, u32[]{:S(2)}) copy-start(bf16[384,1536]{1,0:T(8,128)(2,1)} %param.15) | copy-start | bytes 3538948
  90.0 2.9 collective-permute-start.4
  93.1 4.4 %collective-permute-start.5 = (f32[2,1536]{1,0:T(2,128)S(1)}, f32[2,1536]{1,0:T(2,128)S(1)}, u32[]{:S(2)}, u32[]{:S(2)}) collective-permute-start(f32[2,1536]{1,0:T(2,128)S(1)} %pad_maximum_fusion.6), channel_id=1, source_target_pairs={{0,2},{1,3},{2,0},{3,1},{4,6},{5,7},{6,4},{7,5},{8,10},{9,11},{10,... | collective-permute-start | bytes 36872 | tf_op jit(solution)/shard_map/ppermute | solution.py:49
  97.5 4.7 %collective-permute-start.6 = (f32[2,1536]{1,0:T(2,128)S(1)}, f32[2,1536]{1,0:T(2,128)S(1)}, u32[]{:S(2)}, u32[]{:S(2)}) collective-permute-start(f32[2,1536]{1,0:T(2,128)S(1)} %pad_maximum_fusion.7), channel_id=1, source_target_pairs={{0,4},{1,5},{2,6},{3,7},{4,0},{5,1},{6,2},{7,3},{8,12},{9,13},{10,... | collective-permute-start | bytes 36872 | tf_op jit(solution)/shard_map/ppermute | solution.py:49
  102.3 4.7 %collective-permute-start.7 = (f32[2,1536]{1,0:T(2,128)S(1)}, f32[2,1536]{1,0:T(2,128)S(1)}, u32[]{:S(2)}, u32[]{:S(2)}) collective-permute-start(f32[2,1536]{1,0:T(2,128)S(1)} %pad_maximum_fusion.8), channel_id=1, source_target_pairs={{0,8},{1,9},{2,10},{3,11},{4,12},{5,13},{6,14},{7,15},{8,0},{9,1},... | collective-permute-start | bytes 36872 | tf_op jit(solution)/shard_map/ppermute | solution.py:49
  107.0 4.8 %collective-permute-start.8 = (f32[2,1536]{1,0:T(2,128)S(1)}, f32[2,1536]{1,0:T(2,128)S(1)}, u32[]{:S(2)}, u32[]{:S(2)}) collective-permute-start(f32[2,1536]{1,0:T(2,128)S(1)} %pad_maximum_fusion.9), channel_id=1, source_target_pairs={{0,16},{1,17},{2,18},{3,19},{4,20},{5,21},{6,22},{7,23},{8,24},{9,... | collective-permute-start | bytes 36872 | tf_op jit(solution)/shard_map/ppermute | solution.py:49
  114.5 1.2 collective-permute-start.9
  115.7 3.8 collective-permute-start.10
  119.5 3.8 collective-permute-start.11
  123.3 3.8 collective-permute-start.12
  127.0 4.7 %collective-permute-start.13 = (f32[2,1536]{1,0:T(2,128)S(1)}, f32[2,1536]{1,0:T(2,128)S(1)}, u32[]{:S(2)}, u32[]{:S(2)}) collective-permute-start(f32[2,1536]{1,0:T(2,128)S(1)} %add.498), channel_id=1, source_target_pairs={{0,16},{1,17},{2,18},{3,19},{4,20},{5,21},{6,22},{7,23},{8,24},{9,... | collective-permute-start | bytes 36872 | tf_op jit(solution)/shard_map/ppermute | solution.py:25
  140.2 3.3 collective-permute-start.14
  175.0 52.7 %collective-permute-start.15 = (bf16[384,3072]{1,0:T(8,128)(2,1)}, bf16[384,3072]{1,0:T(8,128)(2,1)}, u32[]{:S(2)}, u32[]{:S(2)}) collective-permute-start(bf16[384,3072]{1,0:T(8,128)(2,1)} %pad_maximum_fusion.1), channel_id=1, source_target_pairs={{0,2},{1,3},{2,0},{3,1},{4,6},{5,7},{6,4},{7,5},{8,10},{9,11},{10,... | collective-permute-start | bytes 7077896 | tf_op jit(solution)/shard_map/ppermute | solution.py:181
  182.4 67.2 %collective-permute-start.18 = (bf16[384,3072]{1,0:T(8,128)(2,1)}, bf16[384,3072]{1,0:T(8,128)(2,1)S(1)}, u32[]{:S(2)}, u32[]{:S(2)}) collective-permute-start(bf16[384,3072]{1,0:T(8,128)(2,1)} %pad_maximum_fusion.1), channel_id=1, source_target_pairs={{0,1},{1,0},{2,3},{3,2},{4,5},{5,4},{6,7},{7,6},{8,9},{9,8},{10,11... | collective-permute-start | bytes 7077896 | tf_op jit(solution)/shard_map/ppermute | solution.py:182
  194.0 35.3 %copy-start.10 = (bf16[384,1536]{1,0:T(8,128)(2,1)S(1)}, bf16[384,1536]{1,0:T(8,128)(2,1)}, u32[]{:S(2)}) copy-start(bf16[384,1536]{1,0:T(8,128)(2,1)} %copy-done.9) | copy-start | bytes 3538948
  227.7 23.3 %collective-permute-start.19 = (bf16[384,3072]{1,0:T(8,128)(2,1)}, bf16[384,3072]{1,0:T(8,128)(2,1)S(1)}, u32[]{:S(2)}, u32[]{:S(2)}) collective-permute-start(bf16[384,3072]{1,0:T(8,128)(2,1)} %collective-permute-done.15), channel_id=1, source_target_pairs={{0,1},{1,0},{2,3},{3,2},{4,5},{5,4},{6,7},{7,6},{8,9},{9,8},{10,11... | collective-permute-start | bytes 7077896 | tf_op jit(solution)/shard_map/ppermute | solution.py:186
  229.5 15.4 %collective-permute-start.16 = (bf16[768,384]{1,0:T(8,128)(2,1)S(1)}, bf16[768,384]{1,0:T(8,128)(2,1)S(1)}, u32[]{:S(2)}, u32[]{:S(2)}) collective-permute-start(bf16[768,384]{1,0:T(8,128)(2,1)S(1)} %pad_maximum_fusion.2), channel_id=1, source_target_pairs={{0,2},{1,3},{2,0},{3,1},{4,6},{5,7},{6,4},{7,5},{8,10},{9,11},{10,... | collective-permute-start | bytes 1769480 | tf_op jit(solution)/shard_map/ppermute | solution.py:94
  245.0 4.6 %collective-permute-start.17 = (bf16[768,384]{1,0:T(8,128)(2,1)S(1)}, bf16[768,384]{1,0:T(8,128)(2,1)S(1)}, u32[]{:S(2)}, u32[]{:S(2)}) collective-permute-start(bf16[768,384]{1,0:T(8,128)(2,1)S(1)} %pad_maximum_fusion.3), channel_id=1, source_target_pairs={{0,1},{1,0},{2,3},{3,2},{4,5},{5,4},{6,7},{7,6},{8,9},{9,8},{10,11... | collective-permute-start | bytes 1769480 | tf_op jit(solution)/shard_map/ppermute | solution.py:97
  255.2 160.8 %all-gather.2.cloned.1.call-start = ((), (), s32[]{:S(2)}) async-start(), calls=%async_computation.2 | async-start | bytes 2654208 | tf_op jit(solution)/shard_map/all_gather | solution.py:203
  354.7 1.6 collective-permute-start.20
  356.3 8.1 %collective-permute-start.21 = (f32[34,1536]{1,0:T(8,128)S(1)}, f32[34,1536]{1,0:T(8,128)S(1)}, u32[]{:S(2)}, u32[]{:S(2)}) collective-permute-start(f32[34,1536]{1,0:T(8,128)S(1)} %fusion.120), channel_id=1, source_target_pairs={{0,2},{1,3},{2,0},{3,1},{4,6},{5,7},{6,4},{7,5},{8,10},{9,11},{10,... | collective-permute-start | bytes 626696 | tf_op jit(solution)/shard_map/ppermute | solution.py:25
  364.4 10.0 %collective-permute-start.22 = (f32[34,1536]{1,0:T(8,128)S(1)}, f32[34,1536]{1,0:T(8,128)S(1)}, u32[]{:S(2)}, u32[]{:S(2)}) collective-permute-start(f32[34,1536]{1,0:T(8,128)S(1)} %add.535), channel_id=1, source_target_pairs={{0,4},{1,5},{2,6},{3,7},{4,0},{5,1},{6,2},{7,3},{8,12},{9,13},{10,... | collective-permute-start | bytes 626696 | tf_op jit(solution)/shard_map/ppermute | solution.py:25
  374.5 9.5 %collective-permute-start.23 = (f32[34,1536]{1,0:T(8,128)S(1)}, f32[34,1536]{1,0:T(8,128)S(1)}, u32[]{:S(2)}, u32[]{:S(2)}) collective-permute-start(f32[34,1536]{1,0:T(8,128)S(1)} %add.536), channel_id=1, source_target_pairs={{0,8},{1,9},{2,10},{3,11},{4,12},{5,13},{6,14},{7,15},{8,0},{9,1},... | collective-permute-start | bytes 626696 | tf_op jit(solution)/shard_map/ppermute | solution.py:25
  384.0 25.0 %collective-permute-start.24 = (f32[34,1536]{1,0:T(8,128)S(1)}, f32[34,1536]{1,0:T(8,128)S(1)}, u32[]{:S(2)}, u32[]{:S(2)}) collective-permute-start(f32[34,1536]{1,0:T(8,128)S(1)} %add.537), channel_id=1, source_target_pairs={{0,16},{1,17},{2,18},{3,19},{4,20},{5,21},{6,22},{7,23},{8,24},{9,... | collective-permute-start | bytes 626696 | tf_op jit(solution)/shard_map/ppermute | solution.py:25
  (63 other events, 697.8 us)
Sparse Core Ops, SparseCore 0:
  255.3 97.4 reduce-scatter.1
  355.5 60.3 all-gather.1

commit v14 on v8

--- a/solution.py
+++ b/solution.py
@@ -144,20 +144,24 @@
     future_rim = from_behind(grad_conv[: kernel_len - 1], ("seq", "fsdp"), -1)
     padded_grad = jnp.concatenate([grad_conv, future_rim], axis=0)
     grad_glu = jnp.zeros((tok_rows, features), jnp.float32)
-    kernel_rows = []
     for offset in range(kernel_len):
         grad_glu = grad_glu + dw_kernel[offset] * padded_grad[offset : offset + tok_rows]
-        kernel_rows.append(
-            jnp.sum(
-                grad_conv
-                * padded_glu[kernel_len - 1 - offset : kernel_len - 1 - offset + tok_rows],
-                axis=0,
-            )
-        )
-    kernel_portion = jnp.stack(kernel_rows, axis=0)
     grad_value = grad_glu * gate_sig
     grad_gate = grad_glu * value_part * gate_sig * (1.0 - gate_sig)
     grad_hidden = jnp.concatenate([grad_value, grad_gate], axis=1).astype(jnp.bfloat16)
+    late_grad_conv, late_glu, grad_hidden = lax.optimization_barrier(
+        (grad_conv, padded_glu, grad_hidden)
+    )
+    kernel_rows = []
+    for offset in range(kernel_len):
+        kernel_rows.append(
+            jnp.sum(
+                late_grad_conv
+                * late_glu[kernel_len - 1 - offset : kernel_len - 1 - offset + tok_rows],
+                axis=0,
+            )
+        )
+    kernel_portion = jnp.stack(kernel_rows, axis=0)
     normalized_gradient = lax.dot_general(
         grad_hidden, full_weight, (((1,), (1,)), ((), ())), preferred_element_type=jnp.float32
     )

time: 427 us -> 422 us (0.988)
  waiting for transfers between devices: 264 us -> 259 us
    ppermute x1, waiting for transfers between devices: 31.9 us -> 26.7 us  [on_device(): far = lax.ppermute(grad_hidden, 'fsdp', [(i, i ^ 2) for i in range(4)])]
  transfers between devices with their start and end apart: 27 -> 27, of which waited for: 21 -> 21; matrix products, arithmetic and copies ran while one was open for 8% -> 10% of each run, Pallas kernels for 0% -> 0%
where the time goes in v14:
time: 422 us
  waiting for transfers between devices  259 us (61%)
  other arithmetic  68.9 us (16%)
  starting transfers between devices  41.5 us (10%)
  matrix products  24.6 us (6%)
  between operations  15.3 us (4%)
  local copies, waits for them, and re-layouts  12.7 us (3%)
    reduce_scatter x1, waiting for transfers between devices, on_device(): lax.psum_scatter(row_share, 'seq', scatter_dimension=0, tiled=True)  97.7 us
    ppermute x10, waiting for transfers between devices, tree_sum(): packed = packed + lax.ppermute(packed, axis, route)  57.8 us
    ppermute x1, waiting for transfers between devices, group_shards(): far = lax.ppermute(block, axis, [(i, i ^ 2) for i in range(4)])  48 us
    another operation x2, other arithmetic  29.5 us
    ppermute x1, waiting for transfers between devices, on_device(): far = lax.ppermute(grad_hidden, 'fsdp', [(i, i ^ 2) for i in range(4)])  26.7 us
    ppermute x10, starting transfers between devices, tree_sum(): packed = packed + lax.ppermute(packed, axis, route)  13.5 us
    ppermute x1, waiting for transfers between devices, gather_own_columns(): lax.ppermute(jnp.concatenate([cols(me ^ 2), cols(me ^ 3)], axis=0), axis,...  13.5 us
    ppermute x5, starting transfers between devices, mean_and_var(): other = lax.ppermute(stats, axis, [(i, i ^ stride) for i in range(count)])  13 us
  transfers between devices with their start and end apart: 27, of which 21 were waited for; matrix products, arithmetic and copies ran while one was open for 10% of the time, Pallas kernels for 0%

profile of v14, /device:TPU:0, one launch (start us, length us, event | category | flops | bytes accessed | tf_op | source)
XLA Modules:
  0.0 421.8 jit_solution(3457630862127815939)
XLA Ops:
  7.2 3.0 collective-permute-start
  13.7 48.0 %collective-permute-done = bf16[384,3072]{1,0:T(8,128)(2,1)S(1)} collective-permute-done((bf16[384,3072]{1,0:T(8,128)(2,1)}, bf16[384,3072]{1,0:T(8,128)(2,1)S(1)}, u32[]{:S(2)}, u32[]{:S(2)}) %collective-permute-start) | collective-permute-done | bytes 2359328 | tf_op jit(solution)/shard_map/ppermute | solution.py:62
  69.6 3.8 fusion.156
  75.6 2.6 collective-permute-start.3
  80.4 9.4 %fusion.154 = (f32[1536]{0:T(1024)S(1)}, f32[384,1536]{1,0:T(8,128)S(1)}) fusion(f32[415,1536]{1,0:T(8,128)S(1)} %maximum_convert_fusion, f32[1536]{0:T(1024)S(1)} %get-tuple-element.94, f32[1536]{0:T(1024)S(1)} %get-tuple-element.95, f32[1536]{0:T(1024)S(1)} %get-tuple-element.65, f32[1536]{0:T(1024)S(1)} %get-tuple-element.66, ...), kind=kLoop, calls=%fused_computation.368 | loop fusion | flops 37747200 | bytes 78059520 | tf_op jit(solution)/shard_map/reduce_sum | solution.py:43
  92.7 2.5 collective-permute-start.5
  96.9 3.0 collective-permute-start.6
  101.7 3.0 collective-permute-start.7
  106.5 3.1 collective-permute-start.8
  114.1 3.7 collective-permute-done.10
  118.8 2.7 collective-permute-done.11
  125.3 3.0 collective-permute-start.13
  130.6 2.6 subtract_multiply_fusion
  136.6 25.4 %multiply_convert_fusion.1 = (bf16[384,1536]{1,0:T(8,128)(2,1)}, f32[384,1536]{1,0:T(8,128)}) fusion(f32[384,3072]{1,0:T(8,128)} %copy-done, f32[31,1536]{1,0:T(8,128)S(1)} %collective-permute-done.14, f32[384,1536]{1,0:T(8,128)S(1)} %get-tuple-element.17, f32[1536]{0:T(1024)} %copy-done.37, f32[1536]{0:T(1024)} %copy-done.38, ...), kind=kLoop, calls=%fused_computation.265 | loop fusion | flops 58392576 | bytes 8644608 | tf_op jit(solution)/shard_map/convert
  162.0 4.1 multiply_convert_fusion
  169.6 5.3 %multiply_reduce_fusion = (f32[1536]{0:T(1024)S(1)}, f32[1536]{0:T(1024)S(1)}, f32[1536]{0:T(1024)S(1)}, f32[1536]{0:T(1024)S(1)}, f32[1536]{0:T(1024)S(1)}, /*i...) fusion(f32[384,1536]{1,0:T(8,128)S(1)} %get-tuple-element.17, ...), kind=kLoop, calls=%fused_computation.232 | loop fusion | flops 21206016 | bytes 44937216 | tf_op jit(solution)/shard_map/reduce_sum | solution.py:158
  175.0 4.6 %multiply_reduce_fusion.18 = (f32[1536]{0:T(1024)S(1)}, f32[1536]{0:T(1024)S(1)}, f32[1536]{0:T(1024)S(1)}, f32[1536]{0:T(1024)S(1)}, f32[1536]{0:T(1024)S(1)}, ...) fusion(f32[384,1536]{1,0:T(8,128)S(1)} %get-tuple-element.17, ...), kind=kLoop, calls=%fused_computation.250 | loop fusion | flops 16493568 | bytes 35475456 | tf_op jit(solution)/shard_map/reduce_sum | solution.py:158
  179.6 2.5 collective-permute-start.18
  182.8 9.1 %fusion.11 = (f32[1536]{0:T(1024)S(1)}, f32[384]{0:T(512)S(1)}, f32[384]{0:T(512)S(1)}, f32[1536]{0:T(1024)S(1)}, f32[384,1536]{1,0:T(8,128)S(1)}) fusion(bf16[384,1536]{1,0:T(8,128)(2,1)} %param.8, f32[384]{0:T(512)} %copy-done.43, f32[384]{0:T(512)S(1)} %broadcast_multiply_fusion.3, f32[1536]{0:T(1024)S(1)} %copy-done.40, ...), kind=kOutput, calls=%fused_computation.44 | convolution fusion | flops 3629772800 | bytes 15360000 | tf_op jit(solution)/shard_map/dot_general | solution.py:165
  193.8 26.7 %collective-permute-done.15 = bf16[384,3072]{1,0:T(8,128)(2,1)} collective-permute-done((bf16[384,3072]{1,0:T(8,128)(2,1)}, bf16[384,3072]{1,0:T(8,128)(2,1)}, u32[]{:S(2)}, u32[]{:S(2)}) %collective-permute-start.15) | collective-permute-done | bytes 2359328 | tf_op jit(solution)/shard_map/ppermute | solution.py:183
  224.1 13.5 %collective-permute-done.16 = bf16[768,384]{1,0:T(8,128)(2,1)S(1)} collective-permute-done((bf16[768,384]{1,0:T(8,128)(2,1)S(1)}, bf16[768,384]{1,0:T(8,128)(2,1)S(1)}, u32[]{:S(2)}, u32[]{:S(2)}) %collective-permute-start.16) | collective-permute-done | bytes 589856 | tf_op jit(solution)/shard_map/ppermute | solution.py:92
  237.8 3.1 fusion.147
  240.9 3.1 fusion.145
  245.5 4.1 add_add_fusion
  249.6 97.7 %reduce-scatter.2.cloned.1.call-done = f32[48,3072]{1,0:T(8,128)} async-done(((f32[384,3072]{1,0:T(8,128)}), f32[48,3072]{1,0:T(8,128)}) %reduce-scatter.2.cloned.1.call-update) | async-done | bytes 589840 | tf_op jit(solution)/shard_map/reduce_scatter | solution.py:204
  352.4 6.5 %collective-permute-done.21 = f32[34,1536]{1,0:T(8,128)S(1)} collective-permute-done((f32[34,1536]{1,0:T(8,128)S(1)}, f32[34,1536]{1,0:T(8,128)S(1)}, u32[]{:S(2)}, u32[]{:S(2)}) %collective-permute-start.21) | collective-permute-done | bytes 208928 | tf_op jit(solution)/shard_map/ppermute | solution.py:25
  360.5 8.5 %collective-permute-done.22 = f32[34,1536]{1,0:T(8,128)S(1)} collective-permute-done((f32[34,1536]{1,0:T(8,128)S(1)}, f32[34,1536]{1,0:T(8,128)S(1)}, u32[]{:S(2)}, u32[]{:S(2)}) %collective-permute-start.22) | collective-permute-done | bytes 208928 | tf_op jit(solution)/shard_map/ppermute | solution.py:25
  370.5 8.0 %collective-permute-done.23 = f32[34,1536]{1,0:T(8,128)S(1)} collective-permute-done((f32[34,1536]{1,0:T(8,128)S(1)}, f32[34,1536]{1,0:T(8,128)S(1)}, u32[]{:S(2)}, u32[]{:S(2)}) %collective-permute-start.23) | collective-permute-done | bytes 208928 | tf_op jit(solution)/shard_map/ppermute | solution.py:25
  378.5 2.7 collective-permute-start.24
  381.2 22.3 %collective-permute-done.24 = f32[34,1536]{1,0:T(8,128)S(1)} collective-permute-done((f32[34,1536]{1,0:T(8,128)S(1)}, f32[34,1536]{1,0:T(8,128)S(1)}, u32[]{:S(2)}, u32[]{:S(2)}) %collective-permute-start.24) | collective-permute-done | bytes 208928 | tf_op jit(solution)/shard_map/ppermute | solution.py:25
  404.9 5.6 %all-gather.2.cloned.1.call-done = bf16[384,3072]{1,0:T(8,128)(2,1)} async-done(((bf16[48,3072]{1,0:T(8,128)(2,1)}), bf16[384,3072]{1,0:T(8,128)(2,1)}) %all-gather.2.cloned.1.call-update) | async-done | bytes 2359312 | tf_op jit(solution)/shard_map/all_gather | solution.py:205
  410.5 4.4 %convert_element_type.36 = f32[384,3072]{1,0:T(8,128)} convert(bf16[384,3072]{1,0:T(8,128)(2,1)} %all-gather.2.cloned.1.call-done) | non-fusion elementwise | flops 1179648 | bytes 7077888 | tf_op jit(solution)/shard_map/convert_element_type | solution.py:207
  (221 shorter events, 58.8 us)
Async XLA Ops:
  7.2 340.2 %reduce-scatter.2.cloned.1.call-start = ((), (), s32[]{:S(2)}) async-start(), calls=%async_computation.1 | async-start | bytes 5308416 | tf_op jit(solution)/shard_map/reduce_scatter | solution.py:204
  7.2 54.5 %collective-permute-start = (bf16[384,3072]{1,0:T(8,128)(2,1)}, bf16[384,3072]{1,0:T(8,128)(2,1)S(1)}, u32[]{:S(2)}, u32[]{:S(2)}) collective-permute-start(bf16[384,3072]{1,0:T(8,128)(2,1)} %param.11), channel_id=1, source_target_pairs={{0,2},{1,3},{2,0},{3,1},{4,6},{5,7},{6,4},{7,5},{8,10},{9,11},{10,... | collective-permute-start | bytes 7077896 | tf_op jit(solution)/shard_map/ppermute | solution.py:62
  10.2 57.0 %collective-permute-start.1 = (bf16[384,3072]{1,0:T(8,128)(2,1)}, bf16[384,3072]{1,0:T(8,128)(2,1)}, u32[]{:S(2)}, u32[]{:S(2)}) collective-permute-start(bf16[384,3072]{1,0:T(8,128)(2,1)} %param.11), channel_id=1, source_target_pairs={{0,1},{1,0},{2,3},{3,2},{4,5},{5,4},{6,7},{7,6},{8,9},{9,8},{10,11... | collective-permute-start | bytes 7077896 | tf_op jit(solution)/shard_map/ppermute | solution.py:63
  12.1 68.2 %copy-start.10 = (f32[1536]{0:T(1024)}, f32[1536]{0:T(1024)S(1)}, u32[]{:S(2)}) copy-start(f32[1536]{0:T(1024)S(1)} %get-tuple-element.67) | copy-start | bytes 18436
  12.1 68.2 %copy-start.11 = (f32[1536]{0:T(1024)}, f32[1536]{0:T(1024)S(1)}, u32[]{:S(2)}) copy-start(f32[1536]{0:T(1024)S(1)} %get-tuple-element.68) | copy-start | bytes 18436
  12.1 68.2 %copy-start.12 = (f32[1536]{0:T(1024)}, f32[1536]{0:T(1024)S(1)}, u32[]{:S(2)}) copy-start(f32[1536]{0:T(1024)S(1)} %get-tuple-element.69) | copy-start | bytes 18436
  12.1 68.2 %copy-start.13 = (f32[1536]{0:T(1024)}, f32[1536]{0:T(1024)S(1)}, u32[]{:S(2)}) copy-start(f32[1536]{0:T(1024)S(1)} %get-tuple-element.70) | copy-start | bytes 18436
  12.1 68.2 %copy-start.14 = (f32[1536]{0:T(1024)}, f32[1536]{0:T(1024)S(1)}, u32[]{:S(2)}) copy-start(f32[1536]{0:T(1024)S(1)} %get-tuple-element.71) | copy-start | bytes 18436
  61.7 7.6 %collective-permute-start.2 = (bf16[384,3072]{1,0:T(8,128)(2,1)S(1)}, bf16[384,3072]{1,0:T(8,128)(2,1)S(1)}, u32[]{:S(2)}, u32[]{:S(2)}) collective-permute-start(bf16[384,3072]{1,0:T(8,128)(2,1)S(1)} %collective-permute-done), channel_id=1, source_target_pairs={{0,1},{1,0},{2,3},{3,2},{4,5},{5,4},{6,7},{7,6},{8,9},{9,8},{10,11... | collective-permute-start | bytes 7077896 | tf_op jit(solution)/shard_map/ppermute | solution.py:64
  75.6 4.3 %collective-permute-start.3 = (bf16[31,1536]{1,0:T(8,128)(2,1)S(1)}, bf16[31,1536]{1,0:T(8,128)(2,1)S(1)}, u32[]{:S(2)}, u32[]{:S(2)}) collective-permute-start(bf16[31,1536]{1,0:T(8,128)(2,1)S(1)} %slice.639), channel_id=1, source_target_pairs={{0,1},{1,2},{2,3},{3,4},{4,5},{5,6},{6,7},{7,8},{8,9},{9,10},{10,1... | collective-permute-start | bytes 285704 | tf_op jit(solution)/shard_map/ppermute | solution.py:12
  90.4 2.2 collective-permute-start.4
  92.7 4.1 collective-permute-start.5
  96.9 4.7 %collective-permute-start.6 = (f32[2,1536]{1,0:T(2,128)S(1)}, f32[2,1536]{1,0:T(2,128)S(1)}, u32[]{:S(2)}, u32[]{:S(2)}) collective-permute-start(f32[2,1536]{1,0:T(2,128)S(1)} %pad_maximum_fusion.7), channel_id=1, source_target_pairs={{0,4},{1,5},{2,6},{3,7},{4,0},{5,1},{6,2},{7,3},{8,12},{9,13},{10,... | collective-permute-start | bytes 36872 | tf_op jit(solution)/shard_map/ppermute | solution.py:49
  101.7 4.7 %collective-permute-start.7 = (f32[2,1536]{1,0:T(2,128)S(1)}, f32[2,1536]{1,0:T(2,128)S(1)}, u32[]{:S(2)}, u32[]{:S(2)}) collective-permute-start(f32[2,1536]{1,0:T(2,128)S(1)} %pad_maximum_fusion.8), channel_id=1, source_target_pairs={{0,8},{1,9},{2,10},{3,11},{4,12},{5,13},{6,14},{7,15},{8,0},{9,1},... | collective-permute-start | bytes 36872 | tf_op jit(solution)/shard_map/ppermute | solution.py:49
  106.5 4.8 %collective-permute-start.8 = (f32[2,1536]{1,0:T(2,128)S(1)}, f32[2,1536]{1,0:T(2,128)S(1)}, u32[]{:S(2)}, u32[]{:S(2)}) collective-permute-start(f32[2,1536]{1,0:T(2,128)S(1)} %pad_maximum_fusion.9), channel_id=1, source_target_pairs={{0,16},{1,17},{2,18},{3,19},{4,20},{5,21},{6,22},{7,23},{8,24},{9,... | collective-permute-start | bytes 36872 | tf_op jit(solution)/shard_map/ppermute | solution.py:49
  112.7 1.2 collective-permute-start.9
  114.0 3.8 collective-permute-start.10
  117.8 3.8 collective-permute-start.11
  121.6 3.8 collective-permute-start.12
  125.3 4.7 %collective-permute-start.13 = (f32[2,1536]{1,0:T(2,128)S(1)}, f32[2,1536]{1,0:T(2,128)S(1)}, u32[]{:S(2)}, u32[]{:S(2)}) collective-permute-start(f32[2,1536]{1,0:T(2,128)S(1)} %add.498), channel_id=1, source_target_pairs={{0,16},{1,17},{2,18},{3,19},{4,20},{5,21},{6,22},{7,23},{8,24},{9,... | collective-permute-start | bytes 36872 | tf_op jit(solution)/shard_map/ppermute | solution.py:25
  133.2 3.3 collective-permute-start.14
  167.9 52.6 %collective-permute-start.15 = (bf16[384,3072]{1,0:T(8,128)(2,1)}, bf16[384,3072]{1,0:T(8,128)(2,1)}, u32[]{:S(2)}, u32[]{:S(2)}) collective-permute-start(bf16[384,3072]{1,0:T(8,128)(2,1)} %pad_maximum_fusion.1), channel_id=1, source_target_pairs={{0,2},{1,3},{2,0},{3,1},{4,6},{5,7},{6,4},{7,5},{8,10},{9,11},{10,... | collective-permute-start | bytes 7077896 | tf_op jit(solution)/shard_map/ppermute | solution.py:183
  179.6 64.5 %collective-permute-start.18 = (bf16[384,3072]{1,0:T(8,128)(2,1)}, bf16[384,3072]{1,0:T(8,128)(2,1)S(1)}, u32[]{:S(2)}, u32[]{:S(2)}) collective-permute-start(bf16[384,3072]{1,0:T(8,128)(2,1)} %pad_maximum_fusion.1), channel_id=1, source_target_pairs={{0,1},{1,0},{2,3},{3,2},{4,5},{5,4},{6,7},{7,6},{8,9},{9,8},{10,11... | collective-permute-start | bytes 7077896 | tf_op jit(solution)/shard_map/ppermute | solution.py:184
  220.5 25.0 %collective-permute-start.19 = (bf16[384,3072]{1,0:T(8,128)(2,1)}, bf16[384,3072]{1,0:T(8,128)(2,1)S(1)}, u32[]{:S(2)}, u32[]{:S(2)}) collective-permute-start(bf16[384,3072]{1,0:T(8,128)(2,1)} %collective-permute-done.15), channel_id=1, source_target_pairs={{0,1},{1,0},{2,3},{3,2},{4,5},{5,4},{6,7},{7,6},{8,9},{9,8},{10,11... | collective-permute-start | bytes 7077896 | tf_op jit(solution)/shard_map/ppermute | solution.py:188
  222.3 15.3 %collective-permute-start.16 = (bf16[768,384]{1,0:T(8,128)(2,1)S(1)}, bf16[768,384]{1,0:T(8,128)(2,1)S(1)}, u32[]{:S(2)}, u32[]{:S(2)}) collective-permute-start(bf16[768,384]{1,0:T(8,128)(2,1)S(1)} %pad_maximum_fusion.2), channel_id=1, source_target_pairs={{0,2},{1,3},{2,0},{3,1},{4,6},{5,7},{6,4},{7,5},{8,10},{9,11},{10,... | collective-permute-start | bytes 1769480 | tf_op jit(solution)/shard_map/ppermute | solution.py:92
  237.7 6.3 %collective-permute-start.17 = (bf16[768,384]{1,0:T(8,128)(2,1)S(1)}, bf16[768,384]{1,0:T(8,128)(2,1)S(1)}, u32[]{:S(2)}, u32[]{:S(2)}) collective-permute-start(bf16[768,384]{1,0:T(8,128)(2,1)S(1)} %pad_maximum_fusion.3), channel_id=1, source_target_pairs={{0,1},{1,0},{2,3},{3,2},{4,5},{5,4},{6,7},{7,6},{8,9},{9,8},{10,11... | collective-permute-start | bytes 1769480 | tf_op jit(solution)/shard_map/ppermute | solution.py:95
  249.6 161.0 %all-gather.2.cloned.1.call-start = ((), (), s32[]{:S(2)}) async-start(), calls=%async_computation.2 | async-start | bytes 2654208 | tf_op jit(solution)/shard_map/all_gather | solution.py:205
  349.2 1.6 collective-permute-start.20
  350.8 8.1 %collective-permute-start.21 = (f32[34,1536]{1,0:T(8,128)S(1)}, f32[34,1536]{1,0:T(8,128)S(1)}, u32[]{:S(2)}, u32[]{:S(2)}) collective-permute-start(f32[34,1536]{1,0:T(8,128)S(1)} %fusion.151), channel_id=1, source_target_pairs={{0,2},{1,3},{2,0},{3,1},{4,6},{5,7},{6,4},{7,5},{8,10},{9,11},{10,... | collective-permute-start | bytes 626696 | tf_op jit(solution)/shard_map/ppermute | solution.py:25
  358.9 10.0 %collective-permute-start.22 = (f32[34,1536]{1,0:T(8,128)S(1)}, f32[34,1536]{1,0:T(8,128)S(1)}, u32[]{:S(2)}, u32[]{:S(2)}) collective-permute-start(f32[34,1536]{1,0:T(8,128)S(1)} %add.535), channel_id=1, source_target_pairs={{0,4},{1,5},{2,6},{3,7},{4,0},{5,1},{6,2},{7,3},{8,12},{9,13},{10,... | collective-permute-start | bytes 626696 | tf_op jit(solution)/shard_map/ppermute | solution.py:25
  369.0 9.5 %collective-permute-start.23 = (f32[34,1536]{1,0:T(8,128)S(1)}, f32[34,1536]{1,0:T(8,128)S(1)}, u32[]{:S(2)}, u32[]{:S(2)}) collective-permute-start(f32[34,1536]{1,0:T(8,128)S(1)} %add.536), channel_id=1, source_target_pairs={{0,8},{1,9},{2,10},{3,11},{4,12},{5,13},{6,14},{7,15},{8,0},{9,1},... | collective-permute-start | bytes 626696 | tf_op jit(solution)/shard_map/ppermute | solution.py:25
  378.5 25.0 %collective-permute-start.24 = (f32[34,1536]{1,0:T(8,128)S(1)}, f32[34,1536]{1,0:T(8,128)S(1)}, u32[]{:S(2)}, u32[]{:S(2)}) collective-permute-start(f32[34,1536]{1,0:T(8,128)S(1)} %add.537), channel_id=1, source_target_pairs={{0,16},{1,17},{2,18},{3,19},{4,20},{5,21},{6,22},{7,23},{8,24},{9,... | collective-permute-start | bytes 626696 | tf_op jit(solution)/shard_map/ppermute | solution.py:25
  (41 other events, 1024.8 us)
Sparse Core Ops, SparseCore 0:
  249.7 97.6 reduce-scatter.1
  350.1 60.4 all-gather.1

commit v15 on v14

--- a/solution.py
+++ b/solution.py
@@ -202,10 +202,12 @@
             group_rows, group_grad, contract, preferred_element_type=jnp.float32
         )
     reduced = lax.psum_scatter(row_share, "seq", scatter_dimension=0, tiled=True)
+    parameter_grads = tree_sum(local_sums, ("seq", "fsdp"))
+    reduced, parameter_grads = lax.optimization_barrier((reduced, parameter_grads))
+    grad_kernel, layer_norm_gain_gradient, grad_ln_bias = parameter_grads
     grad_w_in = lax.all_gather(
         reduced.astype(jnp.bfloat16), "seq", axis=0, tiled=True
     ).astype(jnp.float32)
-    grad_kernel, layer_norm_gain_gradient, grad_ln_bias = tree_sum(local_sums, ("seq", "fsdp"))
     return (
         output,
         input_gradient.astype(jnp.bfloat16),

time: 422 us -> 427 us (1.012)
  waiting for transfers between devices: 259 us -> 264 us
    reduce_scatter x1, waiting for transfers between devices: 97.7 us -> 44.3 us  [on_device(): lax.psum_scatter(row_share, 'seq', scatter_dimension=0, tiled=True)]
    all_gather x1, waiting for transfers between devices: 5.65 us -> 52.8 us  [on_device(): lax.all_gather(reduced.astype(jnp.bfloat16), 'seq', axis=0, tiled=True)]
    ppermute x10, waiting for transfers between devices: 57.8 us -> 69.6 us  [tree_sum(): packed = packed + lax.ppermute(packed, axis, route)]
where the time goes in v15:
time: 427 us
  waiting for transfers between devices  264 us (62%)
  other arithmetic  68.9 us (16%)
  starting transfers between devices  40.9 us (10%)
  matrix products  24.6 us (6%)
  between operations  15.3 us (4%)
  local copies, waits for them, and re-layouts  12.7 us (3%)
    ppermute x10, waiting for transfers between devices, tree_sum(): packed = packed + lax.ppermute(packed, axis, route)  69.6 us
    all_gather x1, waiting for transfers between devices, on_device(): lax.all_gather(reduced.astype(jnp.bfloat16), 'seq', axis=0, tiled=True)  52.8 us
    ppermute x1, waiting for transfers between devices, group_shards(): far = lax.ppermute(block, axis, [(i, i ^ 2) for i in range(4)])  48 us
    reduce_scatter x1, waiting for transfers between devices, on_device(): lax.psum_scatter(row_share, 'seq', scatter_dimension=0, tiled=True)  44.3 us
    another operation x2, other arithmetic  29.5 us
    ppermute x1, waiting for transfers between devices, on_device(): far = lax.ppermute(grad_hidden, 'fsdp', [(i, i ^ 2) for i in range(4)])  26.7 us
    ppermute x1, waiting for transfers between devices, gather_own_columns(): lax.ppermute(jnp.concatenate([cols(me ^ 2), cols(me ^ 3)], axis=0), axis,...  13.5 us
    ppermute x5, starting transfers between devices, mean_and_var(): other = lax.ppermute(stats, axis, [(i, i ^ stride) for i in range(count)])  13 us
  transfers between devices with their start and end apart: 27, of which 21 were waited for; matrix products, arithmetic and copies ran while one was open for 10% of the time, Pallas kernels for 0%

profile of v15, /device:TPU:0, one launch (start us, length us, event | category | flops | bytes accessed | tf_op | source)
XLA Modules:
  0.0 426.7 jit_solution(15852678041607067747)
XLA Ops:
  7.2 3.0 collective-permute-start
  13.7 48.0 %collective-permute-done = bf16[384,3072]{1,0:T(8,128)(2,1)S(1)} collective-permute-done((bf16[384,3072]{1,0:T(8,128)(2,1)}, bf16[384,3072]{1,0:T(8,128)(2,1)S(1)}, u32[]{:S(2)}, u32[]{:S(2)}) %collective-permute-start) | collective-permute-done | bytes 2359328 | tf_op jit(solution)/shard_map/ppermute | solution.py:62
  69.6 3.8 fusion.156
  75.6 2.6 collective-permute-start.3
  80.4 9.4 %fusion.154 = (f32[1536]{0:T(1024)S(1)}, f32[384,1536]{1,0:T(8,128)S(1)}) fusion(f32[415,1536]{1,0:T(8,128)S(1)} %maximum_convert_fusion, f32[1536]{0:T(1024)S(1)} %get-tuple-element.102, f32[1536]{0:T(1024)S(1)} %get-tuple-element.103, f32[1536]{0:T(1024)S(1)} %get-tuple-element.73, f32[1536]{0:T(1024)S(1)} %get-tuple-element.74, ...), kind=kLoop, calls=%fused_computation.368 | loop fusion | flops 37747200 | bytes 78059520 | tf_op jit(solution)/shard_map/reduce_sum | solution.py:43
  92.7 2.5 collective-permute-start.5
  96.9 3.0 collective-permute-start.6
  101.7 3.0 collective-permute-start.7
  106.5 3.1 collective-permute-start.8
  114.1 3.7 collective-permute-done.10
  118.8 2.7 collective-permute-done.11
  125.3 3.0 collective-permute-start.13
  130.6 2.6 subtract_multiply_fusion
  136.6 25.4 %multiply_convert_fusion.1 = (bf16[384,1536]{1,0:T(8,128)(2,1)}, f32[384,1536]{1,0:T(8,128)}) fusion(f32[384,3072]{1,0:T(8,128)} %copy-done, f32[31,1536]{1,0:T(8,128)S(1)} %collective-permute-done.14, f32[384,1536]{1,0:T(8,128)S(1)} %get-tuple-element.21, f32[1536]{0:T(1024)} %copy-done.37, f32[1536]{0:T(1024)} %copy-done.38, ...), kind=kLoop, calls=%fused_computation.265 | loop fusion | flops 58392576 | bytes 8644608 | tf_op jit(solution)/shard_map/convert
  162.0 4.1 multiply_convert_fusion
  169.6 5.3 %multiply_reduce_fusion = (f32[1536]{0:T(1024)S(1)}, f32[1536]{0:T(1024)S(1)}, f32[1536]{0:T(1024)S(1)}, f32[1536]{0:T(1024)S(1)}, f32[1536]{0:T(1024)S(1)}, /*i...) fusion(f32[384,1536]{1,0:T(8,128)S(1)} %get-tuple-element.21, ...), kind=kLoop, calls=%fused_computation.232 | loop fusion | flops 21206016 | bytes 44937216 | tf_op jit(solution)/shard_map/reduce_sum | solution.py:158
  175.0 4.6 %multiply_reduce_fusion.18 = (f32[1536]{0:T(1024)S(1)}, f32[1536]{0:T(1024)S(1)}, f32[1536]{0:T(1024)S(1)}, f32[1536]{0:T(1024)S(1)}, f32[1536]{0:T(1024)S(1)}, ...) fusion(f32[384,1536]{1,0:T(8,128)S(1)} %get-tuple-element.21, ...), kind=kLoop, calls=%fused_computation.250 | loop fusion | flops 16493568 | bytes 35475456 | tf_op jit(solution)/shard_map/reduce_sum | solution.py:158
  179.6 2.5 collective-permute-start.18
  182.8 9.1 %fusion.11 = (f32[1536]{0:T(1024)S(1)}, f32[384]{0:T(512)S(1)}, f32[384]{0:T(512)S(1)}, f32[1536]{0:T(1024)S(1)}, f32[384,1536]{1,0:T(8,128)S(1)}) fusion(bf16[384,1536]{1,0:T(8,128)(2,1)} %param.8, f32[384]{0:T(512)} %copy-done.43, f32[384]{0:T(512)S(1)} %broadcast_multiply_fusion.3, f32[1536]{0:T(1024)S(1)} %copy-done.40, ...), kind=kOutput, calls=%fused_computation.44 | convolution fusion | flops 3629772800 | bytes 15360000 | tf_op jit(solution)/shard_map/dot_general | solution.py:165
  193.8 26.7 %collective-permute-done.15 = bf16[384,3072]{1,0:T(8,128)(2,1)} collective-permute-done((bf16[384,3072]{1,0:T(8,128)(2,1)}, bf16[384,3072]{1,0:T(8,128)(2,1)}, u32[]{:S(2)}, u32[]{:S(2)}) %collective-permute-start.15) | collective-permute-done | bytes 2359328 | tf_op jit(solution)/shard_map/ppermute | solution.py:183
  224.1 13.5 %collective-permute-done.16 = bf16[768,384]{1,0:T(8,128)(2,1)S(1)} collective-permute-done((bf16[768,384]{1,0:T(8,128)(2,1)S(1)}, bf16[768,384]{1,0:T(8,128)(2,1)S(1)}, u32[]{:S(2)}, u32[]{:S(2)}) %collective-permute-start.16) | collective-permute-done | bytes 589856 | tf_op jit(solution)/shard_map/ppermute | solution.py:92
  237.8 3.1 fusion.147
  240.9 3.1 fusion.145
  245.5 4.1 add_add_fusion
  253.2 6.5 %collective-permute-done.21 = f32[34,1536]{1,0:T(8,128)S(1)} collective-permute-done((f32[34,1536]{1,0:T(8,128)S(1)}, f32[34,1536]{1,0:T(8,128)S(1)}, u32[]{:S(2)}, u32[]{:S(2)}) %collective-permute-start.21) | collective-permute-done | bytes 208928 | tf_op jit(solution)/shard_map/ppermute | solution.py:25
  259.7 2.7 collective-permute-start.22
  262.5 10.2 %collective-permute-done.22 = f32[34,1536]{1,0:T(8,128)S(1)} collective-permute-done((f32[34,1536]{1,0:T(8,128)S(1)}, f32[34,1536]{1,0:T(8,128)S(1)}, u32[]{:S(2)}, u32[]{:S(2)}) %collective-permute-start.22) | collective-permute-done | bytes 208928 | tf_op jit(solution)/shard_map/ppermute | solution.py:25
  274.2 19.5 %collective-permute-done.23 = f32[34,1536]{1,0:T(8,128)S(1)} collective-permute-done((f32[34,1536]{1,0:T(8,128)S(1)}, f32[34,1536]{1,0:T(8,128)S(1)}, u32[]{:S(2)}, u32[]{:S(2)}) %collective-permute-start.23) | collective-permute-done | bytes 208928 | tf_op jit(solution)/shard_map/ppermute | solution.py:25
  293.9 21.3 %collective-permute-done.24 = f32[34,1536]{1,0:T(8,128)S(1)} collective-permute-done((f32[34,1536]{1,0:T(8,128)S(1)}, f32[34,1536]{1,0:T(8,128)S(1)}, u32[]{:S(2)}, u32[]{:S(2)}) %collective-permute-start.24) | collective-permute-done | bytes 208928 | tf_op jit(solution)/shard_map/ppermute | solution.py:25
  316.5 44.3 %reduce-scatter.2.cloned.1.call-done = f32[48,3072]{1,0:T(8,128)} async-done(((f32[384,3072]{1,0:T(8,128)}), f32[48,3072]{1,0:T(8,128)}) %reduce-scatter.2.cloned.1.call-update) | async-done | bytes 589840 | tf_op jit(solution)/shard_map/reduce_scatter | solution.py:204
  362.6 52.8 %all-gather.2.cloned.1.call-done = bf16[384,3072]{1,0:T(8,128)(2,1)} async-done(((bf16[48,3072]{1,0:T(8,128)(2,1)}), bf16[384,3072]{1,0:T(8,128)(2,1)}) %all-gather.2.cloned.1.call-update) | async-done | bytes 2359312 | tf_op jit(solution)/shard_map/all_gather | solution.py:208
  415.4 4.4 %convert_element_type.36 = f32[384,3072]{1,0:T(8,128)} convert(bf16[384,3072]{1,0:T(8,128)(2,1)} %all-gather.2.cloned.1.call-done) | non-fusion elementwise | flops 1179648 | bytes 7077888 | tf_op jit(solution)/shard_map/convert_element_type | solution.py:210
  (221 shorter events, 57.8 us)
Async XLA Ops:
  7.2 353.6 %reduce-scatter.2.cloned.1.call-start = ((), (), s32[]{:S(2)}) async-start(), calls=%async_computation.1 | async-start | bytes 5308416 | tf_op jit(solution)/shard_map/reduce_scatter | solution.py:204
  7.2 54.5 %collective-permute-start = (bf16[384,3072]{1,0:T(8,128)(2,1)}, bf16[384,3072]{1,0:T(8,128)(2,1)S(1)}, u32[]{:S(2)}, u32[]{:S(2)}) collective-permute-start(bf16[384,3072]{1,0:T(8,128)(2,1)} %param.11), channel_id=1, source_target_pairs={{0,2},{1,3},{2,0},{3,1},{4,6},{5,7},{6,4},{7,5},{8,10},{9,11},{10,... | collective-permute-start | bytes 7077896 | tf_op jit(solution)/shard_map/ppermute | solution.py:62
  10.2 57.0 %collective-permute-start.1 = (bf16[384,3072]{1,0:T(8,128)(2,1)}, bf16[384,3072]{1,0:T(8,128)(2,1)}, u32[]{:S(2)}, u32[]{:S(2)}) collective-permute-start(bf16[384,3072]{1,0:T(8,128)(2,1)} %param.11), channel_id=1, source_target_pairs={{0,1},{1,0},{2,3},{3,2},{4,5},{5,4},{6,7},{7,6},{8,9},{9,8},{10,11... | collective-permute-start | bytes 7077896 | tf_op jit(solution)/shard_map/ppermute | solution.py:63
  12.1 68.2 %copy-start.10 = (f32[1536]{0:T(1024)}, f32[1536]{0:T(1024)S(1)}, u32[]{:S(2)}) copy-start(f32[1536]{0:T(1024)S(1)} %get-tuple-element.75) | copy-start | bytes 18436
  12.1 68.2 %copy-start.11 = (f32[1536]{0:T(1024)}, f32[1536]{0:T(1024)S(1)}, u32[]{:S(2)}) copy-start(f32[1536]{0:T(1024)S(1)} %get-tuple-element.76) | copy-start | bytes 18436
  12.1 68.2 %copy-start.12 = (f32[1536]{0:T(1024)}, f32[1536]{0:T(1024)S(1)}, u32[]{:S(2)}) copy-start(f32[1536]{0:T(1024)S(1)} %get-tuple-element.77) | copy-start | bytes 18436
  12.1 68.2 %copy-start.13 = (f32[1536]{0:T(1024)}, f32[1536]{0:T(1024)S(1)}, u32[]{:S(2)}) copy-start(f32[1536]{0:T(1024)S(1)} %get-tuple-element.78) | copy-start | bytes 18436
  12.1 68.2 %copy-start.14 = (f32[1536]{0:T(1024)}, f32[1536]{0:T(1024)S(1)}, u32[]{:S(2)}) copy-start(f32[1536]{0:T(1024)S(1)} %get-tuple-element.79) | copy-start | bytes 18436
  61.7 7.6 %collective-permute-start.2 = (bf16[384,3072]{1,0:T(8,128)(2,1)S(1)}, bf16[384,3072]{1,0:T(8,128)(2,1)S(1)}, u32[]{:S(2)}, u32[]{:S(2)}) collective-permute-start(bf16[384,3072]{1,0:T(8,128)(2,1)S(1)} %collective-permute-done), channel_id=1, source_target_pairs={{0,1},{1,0},{2,3},{3,2},{4,5},{5,4},{6,7},{7,6},{8,9},{9,8},{10,11... | collective-permute-start | bytes 7077896 | tf_op jit(solution)/shard_map/ppermute | solution.py:64
  75.6 4.3 %collective-permute-start.3 = (bf16[31,1536]{1,0:T(8,128)(2,1)S(1)}, bf16[31,1536]{1,0:T(8,128)(2,1)S(1)}, u32[]{:S(2)}, u32[]{:S(2)}) collective-permute-start(bf16[31,1536]{1,0:T(8,128)(2,1)S(1)} %slice.639), channel_id=1, source_target_pairs={{0,1},{1,2},{2,3},{3,4},{4,5},{5,6},{6,7},{7,8},{8,9},{9,10},{10,1... | collective-permute-start | bytes 285704 | tf_op jit(solution)/shard_map/ppermute | solution.py:12
  90.4 2.2 collective-permute-start.4
  92.7 4.1 collective-permute-start.5
  96.9 4.7 %collective-permute-start.6 = (f32[2,1536]{1,0:T(2,128)S(1)}, f32[2,1536]{1,0:T(2,128)S(1)}, u32[]{:S(2)}, u32[]{:S(2)}) collective-permute-start(f32[2,1536]{1,0:T(2,128)S(1)} %pad_maximum_fusion.7), channel_id=1, source_target_pairs={{0,4},{1,5},{2,6},{3,7},{4,0},{5,1},{6,2},{7,3},{8,12},{9,13},{10,... | collective-permute-start | bytes 36872 | tf_op jit(solution)/shard_map/ppermute | solution.py:49
  101.7 4.7 %collective-permute-start.7 = (f32[2,1536]{1,0:T(2,128)S(1)}, f32[2,1536]{1,0:T(2,128)S(1)}, u32[]{:S(2)}, u32[]{:S(2)}) collective-permute-start(f32[2,1536]{1,0:T(2,128)S(1)} %pad_maximum_fusion.8), channel_id=1, source_target_pairs={{0,8},{1,9},{2,10},{3,11},{4,12},{5,13},{6,14},{7,15},{8,0},{9,1},... | collective-permute-start | bytes 36872 | tf_op jit(solution)/shard_map/ppermute | solution.py:49
  106.5 4.8 %collective-permute-start.8 = (f32[2,1536]{1,0:T(2,128)S(1)}, f32[2,1536]{1,0:T(2,128)S(1)}, u32[]{:S(2)}, u32[]{:S(2)}) collective-permute-start(f32[2,1536]{1,0:T(2,128)S(1)} %pad_maximum_fusion.9), channel_id=1, source_target_pairs={{0,16},{1,17},{2,18},{3,19},{4,20},{5,21},{6,22},{7,23},{8,24},{9,... | collective-permute-start | bytes 36872 | tf_op jit(solution)/shard_map/ppermute | solution.py:49
  112.7 1.2 collective-permute-start.9
  114.0 3.8 collective-permute-start.10
  117.8 3.8 collective-permute-start.11
  121.6 3.8 collective-permute-start.12
  125.3 4.7 %collective-permute-start.13 = (f32[2,1536]{1,0:T(2,128)S(1)}, f32[2,1536]{1,0:T(2,128)S(1)}, u32[]{:S(2)}, u32[]{:S(2)}) collective-permute-start(f32[2,1536]{1,0:T(2,128)S(1)} %add.498), channel_id=1, source_target_pairs={{0,16},{1,17},{2,18},{3,19},{4,20},{5,21},{6,22},{7,23},{8,24},{9,... | collective-permute-start | bytes 36872 | tf_op jit(solution)/shard_map/ppermute | solution.py:25
  133.2 3.3 collective-permute-start.14
  167.9 52.6 %collective-permute-start.15 = (bf16[384,3072]{1,0:T(8,128)(2,1)}, bf16[384,3072]{1,0:T(8,128)(2,1)}, u32[]{:S(2)}, u32[]{:S(2)}) collective-permute-start(bf16[384,3072]{1,0:T(8,128)(2,1)} %pad_maximum_fusion.1), channel_id=1, source_target_pairs={{0,2},{1,3},{2,0},{3,1},{4,6},{5,7},{6,4},{7,5},{8,10},{9,11},{10,... | collective-permute-start | bytes 7077896 | tf_op jit(solution)/shard_map/ppermute | solution.py:183
  179.6 64.5 %collective-permute-start.18 = (bf16[384,3072]{1,0:T(8,128)(2,1)}, bf16[384,3072]{1,0:T(8,128)(2,1)S(1)}, u32[]{:S(2)}, u32[]{:S(2)}) collective-permute-start(bf16[384,3072]{1,0:T(8,128)(2,1)} %pad_maximum_fusion.1), channel_id=1, source_target_pairs={{0,1},{1,0},{2,3},{3,2},{4,5},{5,4},{6,7},{7,6},{8,9},{9,8},{10,11... | collective-permute-start | bytes 7077896 | tf_op jit(solution)/shard_map/ppermute | solution.py:184
  220.5 25.0 %collective-permute-start.19 = (bf16[384,3072]{1,0:T(8,128)(2,1)}, bf16[384,3072]{1,0:T(8,128)(2,1)S(1)}, u32[]{:S(2)}, u32[]{:S(2)}) collective-permute-start(bf16[384,3072]{1,0:T(8,128)(2,1)} %collective-permute-done.15), channel_id=1, source_target_pairs={{0,1},{1,0},{2,3},{3,2},{4,5},{5,4},{6,7},{7,6},{8,9},{9,8},{10,11... | collective-permute-start | bytes 7077896 | tf_op jit(solution)/shard_map/ppermute | solution.py:188
  222.3 15.3 %collective-permute-start.16 = (bf16[768,384]{1,0:T(8,128)(2,1)S(1)}, bf16[768,384]{1,0:T(8,128)(2,1)S(1)}, u32[]{:S(2)}, u32[]{:S(2)}) collective-permute-start(bf16[768,384]{1,0:T(8,128)(2,1)S(1)} %pad_maximum_fusion.2), channel_id=1, source_target_pairs={{0,2},{1,3},{2,0},{3,1},{4,6},{5,7},{6,4},{7,5},{8,10},{9,11},{10,... | collective-permute-start | bytes 1769480 | tf_op jit(solution)/shard_map/ppermute | solution.py:92
  237.7 6.3 %collective-permute-start.17 = (bf16[768,384]{1,0:T(8,128)(2,1)S(1)}, bf16[768,384]{1,0:T(8,128)(2,1)S(1)}, u32[]{:S(2)}, u32[]{:S(2)}) collective-permute-start(bf16[768,384]{1,0:T(8,128)(2,1)S(1)} %pad_maximum_fusion.3), channel_id=1, source_target_pairs={{0,1},{1,0},{2,3},{3,2},{4,5},{5,4},{6,7},{7,6},{8,9},{9,8},{10,11... | collective-permute-start | bytes 1769480 | tf_op jit(solution)/shard_map/ppermute | solution.py:95
  249.6 165.8 %all-gather.2.cloned.1.call-start = ((), (), s32[]{:S(2)}) async-start(), calls=%async_computation.2 | async-start | bytes 2654208 | tf_op jit(solution)/shard_map/all_gather | solution.py:208
  249.7 1.7 collective-permute-start.20
  251.4 8.3 %collective-permute-start.21 = (f32[34,1536]{1,0:T(8,128)S(1)}, f32[34,1536]{1,0:T(8,128)S(1)}, u32[]{:S(2)}, u32[]{:S(2)}) collective-permute-start(f32[34,1536]{1,0:T(8,128)S(1)} %fusion.151), channel_id=1, source_target_pairs={{0,2},{1,3},{2,0},{3,1},{4,6},{5,7},{6,4},{7,5},{8,10},{9,11},{10,... | collective-permute-start | bytes 626696 | tf_op jit(solution)/shard_map/ppermute | solution.py:25
  259.7 12.9 %collective-permute-start.22 = (f32[34,1536]{1,0:T(8,128)S(1)}, f32[34,1536]{1,0:T(8,128)S(1)}, u32[]{:S(2)}, u32[]{:S(2)}) collective-permute-start(f32[34,1536]{1,0:T(8,128)S(1)} %add.535), channel_id=1, source_target_pairs={{0,4},{1,5},{2,6},{3,7},{4,0},{5,1},{6,2},{7,3},{8,12},{9,13},{10,... | collective-permute-start | bytes 626696 | tf_op jit(solution)/shard_map/ppermute | solution.py:25
  272.7 21.1 %collective-permute-start.23 = (f32[34,1536]{1,0:T(8,128)S(1)}, f32[34,1536]{1,0:T(8,128)S(1)}, u32[]{:S(2)}, u32[]{:S(2)}) collective-permute-start(f32[34,1536]{1,0:T(8,128)S(1)} %add.536), channel_id=1, source_target_pairs={{0,8},{1,9},{2,10},{3,11},{4,12},{5,13},{6,14},{7,15},{8,0},{9,1},... | collective-permute-start | bytes 626696 | tf_op jit(solution)/shard_map/ppermute | solution.py:25
  293.8 21.3 %collective-permute-start.24 = (f32[34,1536]{1,0:T(8,128)S(1)}, f32[34,1536]{1,0:T(8,128)S(1)}, u32[]{:S(2)}, u32[]{:S(2)}) collective-permute-start(f32[34,1536]{1,0:T(8,128)S(1)} %add.537), channel_id=1, source_target_pairs={{0,16},{1,17},{2,18},{3,19},{4,20},{5,21},{6,22},{7,23},{8,24},{9,... | collective-permute-start | bytes 626696 | tf_op jit(solution)/shard_map/ppermute | solution.py:25
  (41 other events, 1024.8 us)
Sparse Core Ops, SparseCore 0:
  249.7 111.0 reduce-scatter.1
  363.5 51.8 all-gather.1

commit v16 on v14

--- a/solution.py
+++ b/solution.py
@@ -135,9 +135,12 @@
     z_sig = jax.nn.sigmoid(z_value)
     output = (z_value * z_sig).astype(jnp.bfloat16)
     grad_z = cotangent.astype(jnp.float32) * z_sig * (1.0 + z_value * (1.0 - z_sig))
-    grad_bn_bias, grad_bn_gain = tree_sum(
-        (jnp.sum(grad_z, axis=0), jnp.sum(grad_z * chat, axis=0)), ("seq", "fsdp")
-    )
+    late_rows, _ = lax.optimization_barrier((normalized_rows, hidden))
+    group_rows = gather_own_columns(late_rows, "fsdp", w_in.shape[0])
+    group_rows, bn_partials = lax.optimization_barrier(
+        (group_rows, (jnp.sum(grad_z, axis=0), jnp.sum(grad_z * chat, axis=0)))
+    )
+    grad_bn_bias, grad_bn_gain = tree_sum(bn_partials, ("seq", "fsdp"))
     grad_conv = (
         bn_gain * bn_rstd * (grad_z - grad_bn_bias / all_frames - chat * grad_bn_gain / all_frames)
     )
@@ -177,7 +180,6 @@
         jnp.sum(normalized_gradient, axis=0),
     )
     feature_rows = w_in.shape[0]
-    group_rows = gather_own_columns(normalized_rows, "fsdp", feature_rows)
     contract = (((0,), (0,)), ((), ()))
     if lax.axis_size("fsdp") == 4:
         far = lax.ppermute(grad_hidden, "fsdp", [(i, i ^ 2) for i in range(4)])

time: 422 us -> 413 us (0.979)
  waiting for transfers between devices: 259 us -> 253 us
  starting transfers between devices: 41.5 us -> 37.2 us
    ppermute x1, waiting for transfers between devices: 13.5 us -> 6.35 us  [gather_own_columns(): lax.ppermute(jnp.concatenate([cols(me ^ 2), cols(me ^ 3)], axis=0), axis,...]
  transfers between devices with their start and end apart: 27 -> 27, of which waited for: 21 -> 22; matrix products, arithmetic and copies ran while one was open for 10% -> 10% of each run, Pallas kernels for 0% -> 0%
where the time goes in v16:
time: 413 us; the launch traced here: 412 us
  waiting for transfers between devices  253 us (61%)
  other arithmetic  70.1 us (17%)
  starting transfers between devices  37.2 us (9%)
  matrix products  24.6 us (6%)
  between operations  15.3 us (4%)
  local copies, waits for them, and re-layouts  12.7 us (3%)
    reduce_scatter x1, waiting for transfers between devices, on_device(): lax.psum_scatter(row_share, 'seq', scatter_dimension=0, tiled=True)  95.8 us
    ppermute x10, waiting for transfers between devices, tree_sum(): packed = packed + lax.ppermute(packed, axis, route)  59.7 us
    ppermute x1, waiting for transfers between devices, group_shards(): far = lax.ppermute(block, axis, [(i, i ^ 2) for i in range(4)])  48 us
    another operation x2, other arithmetic  29.5 us
    ppermute x1, waiting for transfers between devices, on_device(): far = lax.ppermute(grad_hidden, 'fsdp', [(i, i ^ 2) for i in range(4)])  27.4 us
    ppermute x5, starting transfers between devices, mean_and_var(): other = lax.ppermute(stats, axis, [(i, i ^ stride) for i in range(count)])  13 us
    dot_general x4, matrix products, on_device(): lax.dot_general(group_rows[slot * tok_rows:(slot + 1) * tok_rows], piece,...  11.7 us
    ppermute x10, starting transfers between devices, tree_sum(): packed = packed + lax.ppermute(packed, axis, route)  11.6 us
  transfers between devices with their start and end apart: 27, of which 22 were waited for; matrix products, arithmetic and copies ran while one was open for 10% of the time, Pallas kernels for 0%

profile of v16, /device:TPU:0, one launch (start us, length us, event | category | flops | bytes accessed | tf_op | source)
XLA Modules:
  0.0 412.3 jit_solution(4355087717745387895)
XLA Ops:
  7.2 3.0 collective-permute-start
  13.7 48.0 %collective-permute-done = bf16[384,3072]{1,0:T(8,128)(2,1)S(1)} collective-permute-done((bf16[384,3072]{1,0:T(8,128)(2,1)}, bf16[384,3072]{1,0:T(8,128)(2,1)S(1)}, u32[]{:S(2)}, u32[]{:S(2)}) %collective-permute-start) | collective-permute-done | bytes 2359328 | tf_op jit(solution)/shard_map/ppermute | solution.py:62
  69.5 3.8 fusion.156
  75.5 2.6 collective-permute-start.3
  80.3 9.4 %fusion.153 = (f32[1536]{0:T(1024)S(1)}, f32[384,1536]{1,0:T(8,128)S(1)}) fusion(f32[415,1536]{1,0:T(8,128)S(1)} %maximum_convert_fusion, f32[1536]{0:T(1024)S(1)} %get-tuple-element.102, f32[1536]{0:T(1024)S(1)} %get-tuple-element.103, f32[1536]{0:T(1024)S(1)} %get-tuple-element.73, f32[1536]{0:T(1024)S(1)} %get-tuple-element.74, ...), kind=kLoop, calls=%fused_computation.369 | loop fusion | flops 37747200 | bytes 78059520 | tf_op jit(solution)/shard_map/reduce_sum | solution.py:43
  92.6 2.5 collective-permute-start.5
  96.8 3.0 collective-permute-start.6
  101.5 3.0 collective-permute-start.7
  106.3 3.1 collective-permute-start.8
  111.2 6.3 %collective-permute-done.9 = bf16[768,384]{1,0:T(8,128)(2,1)S(1)} collective-permute-done((bf16[768,384]{1,0:T(8,128)(2,1)S(1)}, bf16[768,384]{1,0:T(8,128)(2,1)S(1)}, u32[]{:S(2)}, u32[]{:S(2)}) %collective-permute-start.9) | collective-permute-done | bytes 589856 | tf_op jit(solution)/shard_map/ppermute | solution.py:92
  122.5 3.4 collective-permute-done.12
  126.6 3.1 collective-permute-done.13
  130.1 3.4 collective-permute-done.14
  133.5 2.7 collective-permute-start.15
  138.8 2.6 subtract_multiply_fusion
  144.8 25.4 %multiply_convert_fusion.1 = (bf16[384,1536]{1,0:T(8,128)(2,1)}, f32[384,1536]{1,0:T(8,128)}) fusion(f32[384,3072]{1,0:T(8,128)} %copy-done, f32[31,1536]{1,0:T(8,128)S(1)} %collective-permute-done.16, f32[384,1536]{1,0:T(8,128)S(1)} %get-tuple-element.24, f32[1536]{0:T(1024)} %copy-done.36, f32[1536]{0:T(1024)} %copy-done.37, ...), kind=kLoop, calls=%fused_computation.265 | loop fusion | flops 58392576 | bytes 8644608 | tf_op jit(solution)/shard_map/convert
  170.2 4.1 multiply_convert_fusion
  178.1 5.3 %multiply_reduce_fusion = (f32[1536]{0:T(1024)S(1)}, f32[1536]{0:T(1024)S(1)}, f32[1536]{0:T(1024)S(1)}, f32[1536]{0:T(1024)S(1)}, f32[1536]{0:T(1024)S(1)}, /*i...) fusion(f32[384,1536]{1,0:T(8,128)S(1)} %get-tuple-element.24, ...), kind=kLoop, calls=%fused_computation.232 | loop fusion | flops 21206016 | bytes 44937216 | tf_op jit(solution)/shard_map/reduce_sum | solution.py:161
  183.4 4.6 %multiply_reduce_fusion.18 = (f32[1536]{0:T(1024)S(1)}, f32[1536]{0:T(1024)S(1)}, f32[1536]{0:T(1024)S(1)}, f32[1536]{0:T(1024)S(1)}, f32[1536]{0:T(1024)S(1)}, ...) fusion(f32[384,1536]{1,0:T(8,128)S(1)} %get-tuple-element.24, ...), kind=kLoop, calls=%fused_computation.250 | loop fusion | flops 16493568 | bytes 35475456 | tf_op jit(solution)/shard_map/reduce_sum | solution.py:161
  190.7 9.1 %fusion.11 = (f32[1536]{0:T(1024)S(1)}, f32[384]{0:T(512)S(1)}, f32[384]{0:T(512)S(1)}, f32[1536]{0:T(1024)S(1)}, f32[384,1536]{1,0:T(8,128)S(1)}) fusion(bf16[384,1536]{1,0:T(8,128)(2,1)} %param.8, f32[384]{0:T(512)} %copy-done.42, f32[384]{0:T(512)S(1)} %broadcast_multiply_fusion.3, f32[1536]{0:T(1024)S(1)} %copy-done.39, ...), kind=kOutput, calls=%fused_computation.44 | convolution fusion | flops 3629772800 | bytes 15360000 | tf_op jit(solution)/shard_map/dot_general | solution.py:168
  201.6 27.4 %collective-permute-done.17 = bf16[384,3072]{1,0:T(8,128)(2,1)} collective-permute-done((bf16[384,3072]{1,0:T(8,128)(2,1)}, bf16[384,3072]{1,0:T(8,128)(2,1)}, u32[]{:S(2)}, u32[]{:S(2)}) %collective-permute-start.17) | collective-permute-done | bytes 2359328 | tf_op jit(solution)/shard_map/ppermute | solution.py:185
  230.3 3.1 fusion.147
  233.4 3.1 fusion.145
  238.0 4.1 add_add_fusion
  242.1 95.8 %reduce-scatter.2.cloned.1.call-done = f32[48,3072]{1,0:T(8,128)} async-done(((f32[384,3072]{1,0:T(8,128)}), f32[48,3072]{1,0:T(8,128)}) %reduce-scatter.2.cloned.1.call-update) | async-done | bytes 589840 | tf_op jit(solution)/shard_map/reduce_scatter | solution.py:206
  343.0 6.5 %collective-permute-done.21 = f32[34,1536]{1,0:T(8,128)S(1)} collective-permute-done((f32[34,1536]{1,0:T(8,128)S(1)}, f32[34,1536]{1,0:T(8,128)S(1)}, u32[]{:S(2)}, u32[]{:S(2)}) %collective-permute-start.21) | collective-permute-done | bytes 208928 | tf_op jit(solution)/shard_map/ppermute | solution.py:25
  351.0 8.5 %collective-permute-done.22 = f32[34,1536]{1,0:T(8,128)S(1)} collective-permute-done((f32[34,1536]{1,0:T(8,128)S(1)}, f32[34,1536]{1,0:T(8,128)S(1)}, u32[]{:S(2)}, u32[]{:S(2)}) %collective-permute-start.22) | collective-permute-done | bytes 208928 | tf_op jit(solution)/shard_map/ppermute | solution.py:25
  361.1 8.0 %collective-permute-done.23 = f32[34,1536]{1,0:T(8,128)S(1)} collective-permute-done((f32[34,1536]{1,0:T(8,128)S(1)}, f32[34,1536]{1,0:T(8,128)S(1)}, u32[]{:S(2)}, u32[]{:S(2)}) %collective-permute-start.23) | collective-permute-done | bytes 208928 | tf_op jit(solution)/shard_map/ppermute | solution.py:25
  369.1 2.7 collective-permute-start.24
  371.8 22.3 %collective-permute-done.24 = f32[34,1536]{1,0:T(8,128)S(1)} collective-permute-done((f32[34,1536]{1,0:T(8,128)S(1)}, f32[34,1536]{1,0:T(8,128)S(1)}, u32[]{:S(2)}, u32[]{:S(2)}) %collective-permute-start.24) | collective-permute-done | bytes 208928 | tf_op jit(solution)/shard_map/ppermute | solution.py:25
  395.4 5.6 %all-gather.2.cloned.1.call-done = bf16[384,3072]{1,0:T(8,128)(2,1)} async-done(((bf16[48,3072]{1,0:T(8,128)(2,1)}), bf16[384,3072]{1,0:T(8,128)(2,1)}) %all-gather.2.cloned.1.call-update) | async-done | bytes 2359312 | tf_op jit(solution)/shard_map/all_gather | solution.py:207
  401.1 4.4 %convert_element_type.36 = f32[384,3072]{1,0:T(8,128)} convert(bf16[384,3072]{1,0:T(8,128)(2,1)} %all-gather.2.cloned.1.call-done) | non-fusion elementwise | flops 1179648 | bytes 7077888 | tf_op jit(solution)/shard_map/convert_element_type | solution.py:209
  (220 shorter events, 57.1 us)
Async XLA Ops:
  7.2 330.7 %reduce-scatter.2.cloned.1.call-start = ((), (), s32[]{:S(2)}) async-start(), calls=%async_computation.1 | async-start | bytes 5308416 | tf_op jit(solution)/shard_map/reduce_scatter | solution.py:206
  7.2 54.5 %collective-permute-start = (bf16[384,3072]{1,0:T(8,128)(2,1)}, bf16[384,3072]{1,0:T(8,128)(2,1)S(1)}, u32[]{:S(2)}, u32[]{:S(2)}) collective-permute-start(bf16[384,3072]{1,0:T(8,128)(2,1)} %param.11), channel_id=1, source_target_pairs={{0,2},{1,3},{2,0},{3,1},{4,6},{5,7},{6,4},{7,5},{8,10},{9,11},{10,... | collective-permute-start | bytes 7077896 | tf_op jit(solution)/shard_map/ppermute | solution.py:62
  10.2 57.0 %collective-permute-start.1 = (bf16[384,3072]{1,0:T(8,128)(2,1)}, bf16[384,3072]{1,0:T(8,128)(2,1)}, u32[]{:S(2)}, u32[]{:S(2)}) collective-permute-start(bf16[384,3072]{1,0:T(8,128)(2,1)} %param.11), channel_id=1, source_target_pairs={{0,1},{1,0},{2,3},{3,2},{4,5},{5,4},{6,7},{7,6},{8,9},{9,8},{10,11... | collective-permute-start | bytes 7077896 | tf_op jit(solution)/shard_map/ppermute | solution.py:63
  12.1 68.1 %copy-start.9 = (f32[1536]{0:T(1024)}, f32[1536]{0:T(1024)S(1)}, u32[]{:S(2)}) copy-start(f32[1536]{0:T(1024)S(1)} %get-tuple-element.75) | copy-start | bytes 18436
  12.1 68.1 %copy-start.10 = (f32[1536]{0:T(1024)}, f32[1536]{0:T(1024)S(1)}, u32[]{:S(2)}) copy-start(f32[1536]{0:T(1024)S(1)} %get-tuple-element.76) | copy-start | bytes 18436
  12.1 68.1 %copy-start.11 = (f32[1536]{0:T(1024)}, f32[1536]{0:T(1024)S(1)}, u32[]{:S(2)}) copy-start(f32[1536]{0:T(1024)S(1)} %get-tuple-element.77) | copy-start | bytes 18436
  12.1 68.1 %copy-start.12 = (f32[1536]{0:T(1024)}, f32[1536]{0:T(1024)S(1)}, u32[]{:S(2)}) copy-start(f32[1536]{0:T(1024)S(1)} %get-tuple-element.78) | copy-start | bytes 18436
  12.1 68.1 %copy-start.13 = (f32[1536]{0:T(1024)}, f32[1536]{0:T(1024)S(1)}, u32[]{:S(2)}) copy-start(f32[1536]{0:T(1024)S(1)} %get-tuple-element.79) | copy-start | bytes 18436
  61.7 7.5 %collective-permute-start.2 = (bf16[384,3072]{1,0:T(8,128)(2,1)S(1)}, bf16[384,3072]{1,0:T(8,128)(2,1)S(1)}, u32[]{:S(2)}, u32[]{:S(2)}) collective-permute-start(bf16[384,3072]{1,0:T(8,128)(2,1)S(1)} %collective-permute-done), channel_id=1, source_target_pairs={{0,1},{1,0},{2,3},{3,2},{4,5},{5,4},{6,7},{7,6},{8,9},{9,8},{10,11... | collective-permute-start | bytes 7077896 | tf_op jit(solution)/shard_map/ppermute | solution.py:64
  75.5 4.3 %collective-permute-start.3 = (bf16[31,1536]{1,0:T(8,128)(2,1)S(1)}, bf16[31,1536]{1,0:T(8,128)(2,1)S(1)}, u32[]{:S(2)}, u32[]{:S(2)}) collective-permute-start(bf16[31,1536]{1,0:T(8,128)(2,1)S(1)} %slice.647), channel_id=1, source_target_pairs={{0,1},{1,2},{2,3},{3,4},{4,5},{5,6},{6,7},{7,8},{8,9},{9,10},{10,1... | collective-permute-start | bytes 285704 | tf_op jit(solution)/shard_map/ppermute | solution.py:12
  90.2 2.2 collective-permute-start.4
  92.6 4.1 %collective-permute-start.5 = (f32[2,1536]{1,0:T(2,128)S(1)}, f32[2,1536]{1,0:T(2,128)S(1)}, u32[]{:S(2)}, u32[]{:S(2)}) collective-permute-start(f32[2,1536]{1,0:T(2,128)S(1)} %pad_maximum_fusion.7), channel_id=1, source_target_pairs={{0,2},{1,3},{2,0},{3,1},{4,6},{5,7},{6,4},{7,5},{8,10},{9,11},{10,... | collective-permute-start | bytes 36872 | tf_op jit(solution)/shard_map/ppermute | solution.py:49
  96.8 4.7 %collective-permute-start.6 = (f32[2,1536]{1,0:T(2,128)S(1)}, f32[2,1536]{1,0:T(2,128)S(1)}, u32[]{:S(2)}, u32[]{:S(2)}) collective-permute-start(f32[2,1536]{1,0:T(2,128)S(1)} %pad_maximum_fusion.8), channel_id=1, source_target_pairs={{0,4},{1,5},{2,6},{3,7},{4,0},{5,1},{6,2},{7,3},{8,12},{9,13},{10,... | collective-permute-start | bytes 36872 | tf_op jit(solution)/shard_map/ppermute | solution.py:49
  101.5 4.7 %collective-permute-start.7 = (f32[2,1536]{1,0:T(2,128)S(1)}, f32[2,1536]{1,0:T(2,128)S(1)}, u32[]{:S(2)}, u32[]{:S(2)}) collective-permute-start(f32[2,1536]{1,0:T(2,128)S(1)} %pad_maximum_fusion.9), channel_id=1, source_target_pairs={{0,8},{1,9},{2,10},{3,11},{4,12},{5,13},{6,14},{7,15},{8,0},{9,1},... | collective-permute-start | bytes 36872 | tf_op jit(solution)/shard_map/ppermute | solution.py:49
  104.6 12.9 %collective-permute-start.9 = (bf16[768,384]{1,0:T(8,128)(2,1)S(1)}, bf16[768,384]{1,0:T(8,128)(2,1)S(1)}, u32[]{:S(2)}, u32[]{:S(2)}) collective-permute-start(bf16[768,384]{1,0:T(8,128)(2,1)S(1)} %pad_maximum_fusion.3), channel_id=1, source_target_pairs={{0,2},{1,3},{2,0},{3,1},{4,6},{5,7},{6,4},{7,5},{8,10},{9,11},{10,... | collective-permute-start | bytes 1769480 | tf_op jit(solution)/shard_map/ppermute | solution.py:92
  106.3 4.8 %collective-permute-start.8 = (f32[2,1536]{1,0:T(2,128)S(1)}, f32[2,1536]{1,0:T(2,128)S(1)}, u32[]{:S(2)}, u32[]{:S(2)}) collective-permute-start(f32[2,1536]{1,0:T(2,128)S(1)} %pad_maximum_fusion.10), channel_id=1, source_target_pairs={{0,16},{1,17},{2,18},{3,19},{4,20},{5,21},{6,22},{7,23},{8,24},{9,... | collective-permute-start | bytes 36872 | tf_op jit(solution)/shard_map/ppermute | solution.py:49
  117.6 2.1 collective-permute-start.10
  120.9 1.2 collective-permute-start.11
  122.2 3.8 collective-permute-start.12
  126.0 3.8 collective-permute-start.13
  129.7 3.8 collective-permute-start.14
  133.5 4.7 %collective-permute-start.15 = (f32[2,1536]{1,0:T(2,128)S(1)}, f32[2,1536]{1,0:T(2,128)S(1)}, u32[]{:S(2)}, u32[]{:S(2)}) collective-permute-start(f32[2,1536]{1,0:T(2,128)S(1)} %add.498), channel_id=1, source_target_pairs={{0,16},{1,17},{2,18},{3,19},{4,20},{5,21},{6,22},{7,23},{8,24},{9,... | collective-permute-start | bytes 36872 | tf_op jit(solution)/shard_map/ppermute | solution.py:25
  141.4 3.3 collective-permute-start.16
  176.0 53.0 %collective-permute-start.17 = (bf16[384,3072]{1,0:T(8,128)(2,1)}, bf16[384,3072]{1,0:T(8,128)(2,1)}, u32[]{:S(2)}, u32[]{:S(2)}) collective-permute-start(bf16[384,3072]{1,0:T(8,128)(2,1)} %pad_maximum_fusion.1), channel_id=1, source_target_pairs={{0,2},{1,3},{2,0},{3,1},{4,6},{5,7},{6,4},{7,5},{8,10},{9,11},{10,... | collective-permute-start | bytes 7077896 | tf_op jit(solution)/shard_map/ppermute | solution.py:185
  188.0 48.5 %collective-permute-start.18 = (bf16[384,3072]{1,0:T(8,128)(2,1)}, bf16[384,3072]{1,0:T(8,128)(2,1)S(1)}, u32[]{:S(2)}, u32[]{:S(2)}) collective-permute-start(bf16[384,3072]{1,0:T(8,128)(2,1)} %pad_maximum_fusion.1), channel_id=1, source_target_pairs={{0,1},{1,0},{2,3},{3,2},{4,5},{5,4},{6,7},{7,6},{8,9},{9,8},{10,11... | collective-permute-start | bytes 7077896 | tf_op jit(solution)/shard_map/ppermute | solution.py:186
  229.0 8.9 %collective-permute-start.19 = (bf16[384,3072]{1,0:T(8,128)(2,1)}, bf16[384,3072]{1,0:T(8,128)(2,1)S(1)}, u32[]{:S(2)}, u32[]{:S(2)}) collective-permute-start(bf16[384,3072]{1,0:T(8,128)(2,1)} %collective-permute-done.17), channel_id=1, source_target_pairs={{0,1},{1,0},{2,3},{3,2},{4,5},{5,4},{6,7},{7,6},{8,9},{9,8},{10,11... | collective-permute-start | bytes 7077896 | tf_op jit(solution)/shard_map/ppermute | solution.py:190
  242.0 159.0 %all-gather.2.cloned.1.call-start = ((), (), s32[]{:S(2)}) async-start(), calls=%async_computation.2 | async-start | bytes 2654208 | tf_op jit(solution)/shard_map/all_gather | solution.py:207
  339.8 1.6 collective-permute-start.20
  341.4 8.1 %collective-permute-start.21 = (f32[34,1536]{1,0:T(8,128)S(1)}, f32[34,1536]{1,0:T(8,128)S(1)}, u32[]{:S(2)}, u32[]{:S(2)}) collective-permute-start(f32[34,1536]{1,0:T(8,128)S(1)} %fusion.150), channel_id=1, source_target_pairs={{0,2},{1,3},{2,0},{3,1},{4,6},{5,7},{6,4},{7,5},{8,10},{9,11},{10,... | collective-permute-start | bytes 626696 | tf_op jit(solution)/shard_map/ppermute | solution.py:25
  349.5 10.0 %collective-permute-start.22 = (f32[34,1536]{1,0:T(8,128)S(1)}, f32[34,1536]{1,0:T(8,128)S(1)}, u32[]{:S(2)}, u32[]{:S(2)}) collective-permute-start(f32[34,1536]{1,0:T(8,128)S(1)} %add.535), channel_id=1, source_target_pairs={{0,4},{1,5},{2,6},{3,7},{4,0},{5,1},{6,2},{7,3},{8,12},{9,13},{10,... | collective-permute-start | bytes 626696 | tf_op jit(solution)/shard_map/ppermute | solution.py:25
  359.6 9.5 %collective-permute-start.23 = (f32[34,1536]{1,0:T(8,128)S(1)}, f32[34,1536]{1,0:T(8,128)S(1)}, u32[]{:S(2)}, u32[]{:S(2)}) collective-permute-start(f32[34,1536]{1,0:T(8,128)S(1)} %add.536), channel_id=1, source_target_pairs={{0,8},{1,9},{2,10},{3,11},{4,12},{5,13},{6,14},{7,15},{8,0},{9,1},... | collective-permute-start | bytes 626696 | tf_op jit(solution)/shard_map/ppermute | solution.py:25
  369.1 25.0 %collective-permute-start.24 = (f32[34,1536]{1,0:T(8,128)S(1)}, f32[34,1536]{1,0:T(8,128)S(1)}, u32[]{:S(2)}, u32[]{:S(2)}) collective-permute-start(f32[34,1536]{1,0:T(8,128)S(1)} %add.537), channel_id=1, source_target_pairs={{0,16},{1,17},{2,18},{3,19},{4,20},{5,21},{6,22},{7,23},{8,24},{9,... | collective-permute-start | bytes 626696 | tf_op jit(solution)/shard_map/ppermute | solution.py:25
  (40 other events, 1010.1 us)
Sparse Core Ops, SparseCore 0:
  242.2 95.6 reduce-scatter.1
  340.7 60.3 all-gather.1
